TPU v7x, 32 devices: a whole 2x2x4 slice. The times are simulated.
32 devices in a mesh: req: 16 (over z, x, core), kv: 2 (over y).
Axes of the slice: x: 2, y: 2, z: 4, core: 2. Of those that a mesh axis runs over, the one named last changes fastest.
Arguments:
- hidden: bfloat16 [32, 256, 1024], P('req', 'kv'), may hold values from -6 to 6
- queries: bfloat16 [32, 256, 1024], P('req', 'kv'), may hold values from -24 to 24
- span_kv: bfloat16 [32, 256, 8, 128], P('req', 'kv'), may hold values from -48 to 48
- cache: bfloat16 [32, 2048, 8, 128], P('req', 'kv'), may hold values from -48 to 48
- req_order: int32 [32], replicated, may hold values from 0 to 31, each once
- cached_len: int32 [32], replicated, may hold values from 8 to 2048, as said below
- out_weight: bfloat16 [1024, 1024], replicated, may hold values from -0.1875 to 0.1875
- norm_gain: float32 [1024], replicated, may hold values from 0.1 to 1.9
- expert_ids: int32 [8192, 8], P(('req', 'kv')), may hold values from 0 to 15, all different within a row; in each aligned block of 256 rows (0 to 255, 256 to 511, ...) at most 256 rows name the same one
- expert_weights: float32 [8192, 8], P(('req', 'kv')), may hold values from 0.05 to 0.5
- w_experts: bfloat16 [16, 3, 1024, 512], P('req', None, None, 'kv'), may hold values from -0.25 to 0.25
- block_map: int32 [32, 128], P('req'), may hold values from 0 to 4095, as said below
Outputs:
- layer_out: bfloat16 [32, 256, 1024], P('req', 'kv')
- decode_pool: bfloat16 [4096, 8, 16, 128], P('req', 'kv')
Inputs may be any that keep to these rules, and one draw needn't show every extreme that they name: `cached_len`: some request fills its cache. `block_map`: a permutation of the 4096 pool pages; pool page s belongs to req index s // 256; the pages that one kv index holds of the slots of one req index (positions of its cache share) go to every req index equally often. `expert_ids`: in the rows of one device no expert is named more than 256 times.
All inputs are finite; a program needn't handle non-finite values.
Results may differ from a plain program's by a relative error of at most 0.023.
Values may be sent and summed in bfloat16 or wider, within the bound.
No kernel may reach another device: no remote copies, remote signals or barrier semaphores. Data moves between devices by JAX's collectives and lax.ppermute only.
A program may use at most 128 MiB of HBM per device.

v0:
```python
import math

import jax
import jax.numpy as jnp
from jax import lax
from jax.sharding import PartitionSpec as P

BLOCK = 16


def lookup_lengths(req_order, cached_len, count):
    start = lax.axis_index("req") * count
    mine = lax.dynamic_slice_in_dim(req_order, start, count)
    match = mine[:, None] == jnp.arange(cached_len.shape[0], dtype=jnp.int32)[None, :]
    return jnp.sum(jnp.where(match, cached_len[None, :], 0), axis=1)


def score_block(query_rows, cache_rows, span_rows):
    span_count, group_count, width = query_rows.shape
    head_dim = cache_rows.shape[-1] // 2
    per_group = width // head_dim
    query_split = query_rows.reshape(span_count, group_count, per_group, head_dim)
    key_rows = jnp.concatenate([cache_rows[..., :head_dim], span_rows[..., :head_dim]], axis=0)
    value_rows = jnp.concatenate([cache_rows[..., head_dim:], span_rows[..., head_dim:]], axis=0)
    scores = jnp.einsum(
        "igsd,pgd->gsip", query_split, key_rows, preferred_element_type=jnp.float32
    ) * (1.0 / math.sqrt(head_dim))
    return (scores, value_rows)


def soft_weights(scores, allowed, value_rows):
    masked = jnp.where(allowed, scores, -1e30)
    row_max = jnp.max(masked, axis=-1, keepdims=True)
    probability = jnp.where(allowed, jnp.exp(masked - row_max), 0.0)
    prob_sum = jnp.sum(probability, axis=-1)
    weighted = jnp.einsum(
        "gsip,pgd->igsd",
        probability.astype(jnp.bfloat16),
        value_rows,
        preferred_element_type=jnp.float32,
    )
    return (weighted, jnp.transpose(row_max[..., 0], (2, 0, 1)), jnp.transpose(prob_sum, (2, 0, 1)))


def whole_request(operands):
    query_rows, cache_rows, span_rows, length = operands
    scores, value_rows = score_block(query_rows, cache_rows, span_rows)
    cached = cache_rows.shape[0]
    position = jnp.arange(scores.shape[-1])[None, :]
    query_pos = jnp.arange(query_rows.shape[0])[:, None]
    allowed = jnp.where(position < cached, position < length, position - cached <= query_pos)
    weighted, row_max, prob_sum = soft_weights(scores, allowed, value_rows)
    result = weighted / prob_sum[..., None]
    return result.reshape(query_rows.shape).astype(jnp.bfloat16)


def place_pages(page_rows, slot_numbers, slots_dev):
    owner_index = slot_numbers // slots_dev
    arrangement = jnp.argsort(owner_index, stable=True)
    return (page_rows[arrangement], (slot_numbers % slots_dev)[arrangement])


def body(
    hidden,
    queries,
    span_kv,
    cache,
    req_order,
    cached_len,
    out_weight,
    norm_gain,
    expert_ids,
    expert_weights,
    w_experts,
    block_map,
):
    local_reqs, local_tokens, width_model = hidden.shape
    row_count = local_reqs * local_tokens
    req_count = lax.axis_size("req")
    kv_count = lax.axis_size("kv")
    kv_heads = span_kv.shape[2]
    head_pair = span_kv.shape[3]
    group_width = queries.shape[2] // kv_heads
    group_count = kv_heads // kv_count
    slots_dev = local_reqs * block_map.shape[1]
    lengths = lookup_lengths(req_order, cached_len, local_reqs)
    queries_grouped = queries.reshape(local_reqs, local_tokens, kv_heads, group_width)
    cache_heads, span_heads, query_heads = (
        lax.all_to_all(cache, "kv", split_axis=2, concat_axis=1, tiled=True),
        lax.all_to_all(span_kv, "kv", split_axis=2, concat_axis=1, tiled=True),
        lax.all_to_all(queries_grouped, "kv", split_axis=2, concat_axis=1, tiled=True),
    )
    attn_heads = lax.map(whole_request, (query_heads, cache_heads, span_heads, lengths))
    attn = lax.all_to_all(attn_heads, "kv", split_axis=1, concat_axis=2, tiled=True).reshape(
        row_count, kv_heads * group_width
    )
    page_total = block_map.shape[1]
    visible = jnp.arange(cache_heads.shape[1])[None, :] < lengths[:, None]
    visible_cache = jnp.where(visible[:, :, None, None], cache_heads, jnp.zeros((), jnp.bfloat16))
    page_rows = (
        visible_cache.reshape(local_reqs, page_total, BLOCK, group_count, head_pair)
        .transpose(0, 1, 3, 2, 4)
        .reshape(local_reqs * page_total, group_count, BLOCK, head_pair)
    )
    sorted_pages, local_slot = place_pages(page_rows, block_map.reshape(-1), slots_dev)
    per_owner = sorted_pages.shape[0] // req_count
    outgoing = sorted_pages.reshape(req_count, per_owner, group_count, BLOCK, head_pair)
    arrived, where_to = (
        lax.all_to_all(outgoing, "req", split_axis=0, concat_axis=0, tiled=True),
        lax.all_to_all(
            local_slot.reshape(req_count, per_owner), "req", split_axis=0, concat_axis=0, tiled=True
        ),
    )
    decode_pool = (
        jnp.zeros((slots_dev, group_count, BLOCK, head_pair), jnp.bfloat16)
        .at[where_to.reshape(-1)]
        .set(arrived.reshape(-1, group_count, BLOCK, head_pair))
    )
    residual = hidden.reshape(row_count, width_model).astype(jnp.float32) + jnp.dot(
        attn, out_weight, preferred_element_type=jnp.float32
    )
    inverse_rms = lax.rsqrt(jnp.mean(residual * residual, axis=-1, keepdims=True) + 1e-05)
    normed = (residual * inverse_rms * norm_gain).astype(jnp.bfloat16)
    top_count = expert_ids.shape[1]
    exp_dev = w_experts.shape[0]
    experts = exp_dev * req_count
    capacity = min(row_count, 2 * row_count * top_count // experts)
    chosen = expert_ids.reshape(-1)
    onehot = (chosen[:, None] == jnp.arange(experts, dtype=jnp.int32)[None, :]).astype(jnp.int32)
    slot_rank = jnp.sum(onehot * (jnp.cumsum(onehot, axis=0) - 1), axis=1)
    target = chosen * capacity + slot_rank
    source_row = jnp.arange(chosen.shape[0]) // top_count
    buffer = (
        jnp.zeros((experts * capacity, width_model), jnp.bfloat16)
        .at[target]
        .set(normed[source_row])
        .reshape(experts, capacity, width_model)
    )
    full_weights = lax.all_gather(w_experts, "kv", axis=3, tiled=True)
    slot_block = lax.all_to_all(buffer, "req", split_axis=0, concat_axis=0, tiled=True)
    source_count = slot_block.shape[0] // exp_dev
    grouped = slot_block.reshape(source_count, exp_dev, slot_block.shape[1], width_model)
    gate_act = jnp.einsum(
        "sejd,edf->sejf", grouped, full_weights[:, 0], preferred_element_type=jnp.float32
    )
    up_act = jnp.einsum(
        "sejd,edf->sejf", grouped, full_weights[:, 1], preferred_element_type=jnp.float32
    )
    activated = (jax.nn.silu(gate_act) * up_act).astype(jnp.bfloat16)
    expert_out = jnp.einsum(
        "sejf,edf->sejd", activated, full_weights[:, 2], preferred_element_type=jnp.float32
    ).astype(jnp.bfloat16)
    returned = lax.all_to_all(
        expert_out.reshape(slot_block.shape), "req", split_axis=0, concat_axis=0, tiled=True
    )
    picked = returned.reshape(experts * capacity, width_model)[target].reshape(
        row_count, top_count, width_model
    )
    expert_sum = jnp.sum(expert_weights[..., None] * picked.astype(jnp.float32), axis=1)
    layer_out = (
        (residual + expert_sum).astype(jnp.bfloat16).reshape(local_reqs, local_tokens, width_model)
    )
    return (layer_out, decode_pool)


def solution(mesh):
    return jax.shard_map(
        body,
        mesh=mesh,
        in_specs=(
            P("req", "kv", None),
            P("req", "kv", None),
            P("req", "kv", None, None),
            P("req", "kv", None, None),
            P(),
            P(),
            P(),
            P(),
            P(("req", "kv"), None),
            P(("req", "kv"), None),
            P("req", None, None, "kv"),
            P("req", None),
        ),
        out_specs=(P("req", "kv", None), P("req", "kv", None, None)),
        check_vma=False,
    )
```

profile of v0, /device:TPU:16, one launch (start us, length us, event | category | flops | bytes accessed | tf_op | source)
XLA Modules:
  0.0 748.1 jit_solution(12969157909613193286)
XLA Ops:
  14.9 6.1 all-to-all-done.1
  24.9 5.0 copy.78
  31.9 5.6 all-to-all-start
  53.8 29.6 %all-to-all-done = bf16[2,1024,8,128]{3,1,0,2:T(8,128)(2,1)} async-done(((bf16[2,1024,8,128]{3,1,0,2:T(8,128)(2,1)}), bf16[2,1024,8,128]{3,1,0,2:T(8,128)(2,1)}, u32[]{:S(2)}, u32[]{:S(2)}) %all-to-all-start) | async-done | bytes 4194336 | tf_op jit(solution)/shard_map/all_to_all | solution.py:89
  88.0 104.1 %while.12 = (s32[]{:T(128)}, bf16[2,256,4,128]{3,2,0,1:T(4,128)(2,1)}, bf16[2,2048,4,128]{3,1,2,0:T(8,128)(2,1)}, bf16[2,256,4,128]{1,3,2,0:T(8,128)(2,1)}, s32[...) while((s32[]{:T(128)}, bf16[2,256,4,128]{3,2,0,1:T(4,128)(2,1)}, ...), condition=%wide.region_4.5_spmd, body=%wide.region_1.4_spmd.sunk | while | flops 1251877888 | bytes 80653984 | solution.py:93
  100.3 9.2 %fusion.65 = f32[4,2304,256,2]{2,1,3,0:T(8,128)} fusion(bf16[256,4,2,64]{0,3,2,1:T(8,128)(2,1)S(1)} %bitcast.190, bf16[256,4,64]{0,2,1:T(8,128)(2,1)} %get-tuple-element.183, bf16[2048,4,64]{0,2,1:T(8,128)(2,1)} %get-tuple-element.184), kind=kOutput, calls=%fused_computation.24.clone.1 | convolution fusion | flops 606339072 | bytes 20316160 | tf_op jit(solution)/shard_map/while/body/eval_jaxpr/igsd,pgd->gsip/dot_general | solution.py:25
  114.1 19.4 %fusion.67 = (f32[4,2,256]{2,1,0:T(2,128)S(1)}, bf16[4,2,256,2304]{2,3,1,0:T(8,128)(2,1)}) fusion(f32[4,2304,256,2]{2,1,3,0:T(8,128)} %fusion.65, pred[256,2304]{0,1:T(8,128)(4,1)} %fusion.66), kind=kOutput, calls=%fused_computation.99.clone.1 | output fusion | flops 37751040 | bytes 28909568 | tf_op jit(solution)/shard_map/while/body/eval_jaxpr/sub | solution.py:34
  133.6 5.5 fusion.68
  152.4 9.2 %fusion.65 = f32[4,2304,256,2]{2,1,3,0:T(8,128)} fusion(bf16[256,4,2,64]{0,3,2,1:T(8,128)(2,1)S(1)} %bitcast.190, bf16[256,4,64]{0,2,1:T(8,128)(2,1)} %get-tuple-element.183, bf16[2048,4,64]{0,2,1:T(8,128)(2,1)} %get-tuple-element.184), kind=kOutput, calls=%fused_computation.24.clone.1 | convolution fusion | flops 606339072 | bytes 20316160 | tf_op jit(solution)/shard_map/while/body/eval_jaxpr/igsd,pgd->gsip/dot_general | solution.py:25
  166.2 19.4 %fusion.67 = (f32[4,2,256]{2,1,0:T(2,128)S(1)}, bf16[4,2,256,2304]{2,3,1,0:T(8,128)(2,1)}) fusion(f32[4,2304,256,2]{2,1,3,0:T(8,128)} %fusion.65, pred[256,2304]{0,1:T(8,128)(4,1)} %fusion.66), kind=kOutput, calls=%fused_computation.99.clone.1 | output fusion | flops 37751040 | bytes 28909568 | tf_op jit(solution)/shard_map/while/body/eval_jaxpr/sub | solution.py:34
  185.6 5.5 fusion.68
  202.3 6.6 all-to-all-start.6
  213.2 33.0 %scatter_custom_fusion = bf16[4096,1024]{1,0:T(8,128)(2,1)} fusion(s32[2048]{0:T(1024)S(1)} %bitcast.205, bf16[256,1024]{1,0:T(8,128)(2,1)} %multiply_convert_fusion, s32[2048]{0:T(1024)S(1)} %broadcast_clamp_fusion.1, bf16[]{:T(256)} %constant.114.clone.1), kind=kCustom, calls=%fused_computation.49 | custom fusion | bytes 8389120 | tf_op jit(solution)/shard_map/scatter | solution.py:136
  246.2 6.3 all-to-all-start.4
  259.2 5.2 gather_fusion.2
  264.4 170.6 %all-to-all-done.4 = bf16[16,256,1024]{2,1,0:T(8,128)(2,1)} async-done(((bf16[16,256,1024]{2,1,0:T(8,128)(2,1)}), bf16[16,256,1024]{2,1,0:T(8,128)(2,1)}, u32[]{:S(2)}, u32[]{:S(2)}) %all-to-all-start.4) | async-done | bytes 8388640 | tf_op jit(solution)/shard_map/all_to_all | solution.py:140
  440.4 46.5 %all-gather.2.cloned.1.call-done = bf16[1,3,1024,512]{3,2,1,0:T(8,128)(2,1)} async-done(((bf16[1,3,1024,256]{3,2,1,0:T(8,128)(2,1)}), bf16[1,3,1024,512]{3,2,1,0:T(8,128)(2,1)}) %all-gather.2.cloned.1.call-update) | async-done | bytes 3145744 | tf_op jit(solution)/shard_map/all_gather | solution.py:139
  486.9 11.4 %fusion.38 = f32[16,256,512]{2,1,0:T(8,128)} fusion(bf16[16,256,1024]{2,1,0:T(8,128)(2,1)} %all-to-all-done.4, bf16[1,3,1024,512]{3,2,1,0:T(8,128)(2,1)} %all-gather.2.cloned.1.call-done), kind=kOutput, calls=%fused_computation.58 | convolution fusion | flops 4294967296 | bytes 17825792 | tf_op jit(solution)/shard_map/sejd,edf->sejf/dot_general | solution.py:143
  498.3 16.0 %convolution_convert_fusion = bf16[16,256,1024]{2,1,0:T(8,128)(2,1)} fusion(f32[16,256,512]{2,1,0:T(8,128)} %fusion.38, bf16[16,256,1024]{2,1,0:T(8,128)(2,1)} %all-to-all-done.4, bf16[1,3,1024,512]{3,2,1,0:T(8,128)(2,1)} %all-gather.2.cloned.1.call-done), kind=kOutput, calls=%fused_computation.47 | convolution fusion | flops 8606711808 | bytes 27262976 | tf_op jit(solution)/shard_map/sejf,edf->sejd/dot_general | solution.py:150
  514.3 18.1 %all-to-all-done.7 = bf16[16,16,4,16,128]{4,3,2,1,0:T(8,128)(2,1)} async-done(((bf16[16,16,4,16,128]{4,3,2,1,0:T(8,128)(2,1)}), bf16[16,16,4,16,128]{4,3,2,1,0:T(8,128)(2,1)}, u32[]{:S(2)}, u32[]{:S(2)}) %all-to-all-start.7) | async-done | bytes 4194336 | tf_op jit(solution)/shard_map/all_to_all | solution.py:109
  532.3 5.0 all-to-all-start.5
  541.9 33.5 %scatter_fusion = bf16[256,4,16,128]{3,2,1,0:T(8,128)(2,1)} fusion(bf16[256,4,16,128]{3,2,1,0:T(8,128)(2,1)} %broadcast_in_dim.106, s32[256]{0:T(256)S(1)} %bitcast.209, bf16[256,4,16,128]{3,2,1,0:T(8,128)(2,1)} %bitcast.57), kind=kCustom, calls=%fused_computation.5 | custom fusion | bytes 12583936 | tf_op jit(solution)/shard_map/scatter | solution.py:117
  575.4 144.4 %all-to-all-done.5 = bf16[16,256,1024]{2,1,0:T(8,128)(2,1)} async-done(((bf16[16,256,1024]{2,1,0:T(8,128)(2,1)}), bf16[16,256,1024]{2,1,0:T(8,128)(2,1)}, u32[]{:S(2)}, u32[]{:S(2)}) %all-to-all-start.5) | async-done | bytes 8388640 | tf_op jit(solution)/shard_map/all_to_all | solution.py:153
  719.8 15.5 %gather_fusion = bf16[2048,1024]{1,0:T(8,128)(2,1)} fusion(bf16[4096,1024]{1,0:T(8,128)(2,1)} %bitcast.46, s32[2048]{0:T(1024)S(1)} %broadcast_clamp_fusion), kind=kCustom, calls=%fused_computation.1 | custom fusion | bytes 8396800 | tf_op jit(solution)/shard_map/gather | solution.py:156
  (113 shorter events, 106.8 us)
Async XLA Ops:
  7.2 203.1 %copy-start = (bf16[1024,1024]{1,0:T(8,128)(2,1)S(1)}, bf16[1024,1024]{1,0:T(8,128)(2,1)}, u32[]{:S(2)}) copy-start(bf16[1024,1024]{1,0:T(8,128)(2,1)} %param.20) | copy-start | bytes 6291460
  7.2 17.3 %copy-start.4 = (s32[256,8]{0,1:T(8,128)S(1)}, s32[256,8]{0,1:T(8,128)}, u32[]{:S(2)}) copy-start(s32[256,8]{0,1:T(8,128)} %param.22) | copy-start | bytes 24580
  9.3 11.7 %all-to-all-start.1 = ((bf16[2,128,8,128]{3,1,0,2:T(8,128)(2,1)}), bf16[2,128,8,128]{3,1,0,2:T(8,128)(2,1)S(1)}, u32[]{:S(2)}, u32[]{:S(2)}) async-start(bf16[2,128,8,128]{3,1,0,2:T(8,128)(2,1)} %copy.81), calls=%async_computation.1 | async-start | bytes 1048576 | tf_op jit(solution)/shard_map/all_to_all | solution.py:90
  21.0 10.9 %all-to-all-start.2 = ((bf16[2,128,8,128]{1,3,0,2:T(8,128)(2,1)}), bf16[2,128,8,128]{1,3,0,2:T(8,128)(2,1)S(1)}, u32[]{:S(2)}, u32[]{:S(2)}) async-start(bf16[2,128,8,128]{1,3,0,2:T(8,128)(2,1)} %copy.84), calls=%async_computation.2 | async-start | bytes 1048576 | tf_op jit(solution)/shard_map/all_to_all | solution.py:91
  29.9 13.0 %copy-start.10 = (s32[32]{0:T(128)S(1)}, s32[32]{0:T(128)}, u32[]{:S(2)}) copy-start(s32[32]{0:T(128)} %param.18) | copy-start | bytes 388
  29.9 13.1 %copy-start.9 = (s32[2,128]{1,0:T(2,128)S(1)}, s32[2,128]{1,0:T(2,128)}, u32[]{:S(2)}) copy-start(s32[2,128]{1,0:T(2,128)} %param.25) | copy-start | bytes 3076
  29.9 16.9 %copy-start.11 = (s32[32]{0:T(128)S(1)}, s32[32]{0:T(128)}, u32[]{:S(2)}) copy-start(s32[32]{0:T(128)} %param.19) | copy-start | bytes 388
  31.9 51.5 %all-to-all-start = ((bf16[2,1024,8,128]{3,1,0,2:T(8,128)(2,1)}), bf16[2,1024,8,128]{3,1,0,2:T(8,128)(2,1)}, u32[]{:S(2)}, u32[]{:S(2)}) async-start(bf16[2,1024,8,128]{3,1,0,2:T(8,128)(2,1)} %copy.78), calls=%async_computation | async-start | bytes 8388608 | tf_op jit(solution)/shard_map/all_to_all | solution.py:89
  88.0 107.8 %copy-start.8 = (s32[256]{0:T(256)S(1)}, s32[256]{0:T(256)}, u32[]{:S(2)}) copy-start(s32[256]{0:T(256)} %compare_select_fusion.3) | copy-start | bytes 3076
  88.0 107.8 %copy-start.1 = (s32[256]{0:T(256)S(1)}, s32[256]{0:T(256)}, u32[]{:S(2)}) copy-start(s32[256]{0:T(256)} %get-tuple-element.133) | copy-start | bytes 3076
  95.0 2.8 copy-start.2
  95.0 3.5 copy-start.3
  147.1 2.8 copy-start.2
  147.1 3.5 copy-start.3
  192.1 20.2 %copy-start.7 = (f32[1024]{0:T(1024)S(1)}, f32[1024]{0:T(1024)}, u32[]{:S(2)}) copy-start(f32[1024]{0:T(1024)} %param.21) | copy-start | bytes 12292
  192.1 10.2 %all-to-all-start.3 = ((bf16[2,256,4,128]{3,2,0,1:T(4,128)(2,1)}), bf16[2,256,4,128]{3,2,0,1:T(4,128)(2,1)S(1)}, u32[]{:S(2)}, u32[]{:S(2)}) async-start(bf16[2,256,4,128]{3,2,0,1:T(4,128)(2,1)} %get-tuple-element.80), calls=%async_computation.3 | async-start | bytes 1048576 | tf_op jit(solution)/shard_map/all_to_all | solution.py:94
  197.7 15.5 %copy-start.5 = (s32[2048,1]{0,1:T(1,128)S(1)}, s32[2048,1]{0,1:T(1,128)}, u32[]{:S(2)}) copy-start(s32[2048,1]{0,1:T(1,128)} %compare_select_fusion.1) | copy-start | bytes 24580
  202.3 43.9 %all-to-all-start.6 = ((s32[16,1,16]{2,1,0:T(1,128)}), s32[16,1,16]{2,1,0:T(1,128)S(1)}, u32[]{:S(2)}, u32[]{:S(2)}) async-start(s32[16,1,16]{2,1,0:T(1,128)} %all_to_all.84), calls=%async_computation.6 | async-start | bytes 16384 | tf_op jit(solution)/shard_map/all_to_all | solution.py:110
  246.2 188.8 %all-to-all-start.4 = ((bf16[16,256,1024]{2,1,0:T(8,128)(2,1)}), bf16[16,256,1024]{2,1,0:T(8,128)(2,1)}, u32[]{:S(2)}, u32[]{:S(2)}) async-start(bf16[16,256,1024]{2,1,0:T(8,128)(2,1)} %bitcast.189), calls=%async_computation.4 | async-start | bytes 16777216 | tf_op jit(solution)/shard_map/all_to_all | solution.py:140
  435.0 97.4 %all-to-all-start.7 = ((bf16[16,16,4,16,128]{4,3,2,1,0:T(8,128)(2,1)}), bf16[16,16,4,16,128]{4,3,2,1,0:T(8,128)(2,1)}, u32[]{:S(2)}, u32[]{:S(2)}) async-start(bf16[16,16,4,16,128]{4,3,2,1,0:T(8,128)(2,1)} %bitcast.192), calls=%async_computation.7 | async-start | bytes 8388608 | tf_op jit(solution)/shard_map/all_to_all | solution.py:109
  439.6 47.3 %all-gather.2.cloned.1.call-start = ((), (), s32[]{:S(2)}) async-start(), calls=%async_computation.8 | async-start | bytes 4718592 | tf_op jit(solution)/shard_map/all_gather | solution.py:139
  514.3 23.1 %copy-start.6 = (f32[256,8]{0,1:T(8,128)S(1)}, f32[256,8]{0,1:T(8,128)}, u32[]{:S(2)}) copy-start(f32[256,8]{0,1:T(8,128)} %param.23) | copy-start | bytes 24580
  532.3 187.5 %all-to-all-start.5 = ((bf16[16,256,1024]{2,1,0:T(8,128)(2,1)}), bf16[16,256,1024]{2,1,0:T(8,128)(2,1)}, u32[]{:S(2)}, u32[]{:S(2)}) async-start(bf16[16,256,1024]{2,1,0:T(8,128)(2,1)} %convolution_convert_fusion), calls=%async_computation.5 | async-start | bytes 16777216 | tf_op jit(solution)/shard_map/all_to_all | solution.py:153
Sparse Core Ops, SparseCore 0:
  442.0 44.8 all-gather.1
where the time goes:
time: 760 us; the launch traced here: 748 us
  waiting for transfers between devices  421 us (55%)
  local copies, waits for them, and re-layouts  147 us (19%)
  other arithmetic  68.1 us (9%)
  matrix products  58.8 us (8%)
  starting transfers between devices  38.9 us (5%)
  between operations  14.6 us (2%)
    all_to_all x1, waiting for transfers between devices, body(): lax.all_to_all(buffer, 'req', split_axis=0, concat_axis=0, tiled=True)  171 us
    all_to_all x1, waiting for transfers between devices, body(): lax.all_to_all(expert_out.reshape(slot_block.shape), 'req', split_axis=0,...  144 us
    all_gather x1, waiting for transfers between devices, body(): full_weights = lax.all_gather(w_experts, 'kv', axis=3, tiled=True)  46.5 us
    sub x2, other arithmetic, soft_weights(): probability = jnp.where(allowed, jnp.exp(masked - row_max), 0.0)  38.9 us
    scatter x1, local copies, waits for them, and re-layouts, body(): decode_pool = jnp.zeros((slots_dev, group_count, BLOCK, head_pair), jnp.b...  33.5 us
    scatter x1, local copies, waits for them, and re-layouts, body(): buffer = jnp.zeros((experts * capacity, width_model), jnp.bfloat16).at[ta...  33 us
    all_to_all x1, waiting for transfers between devices, body(): lax.all_to_all(cache, 'kv', split_axis=2, concat_axis=1, tiled=True)  29.6 us
    dynamic_slice x10, local copies, waits for them, and re-layouts, body(): lax.map(whole_request, (query_heads, cache_heads, span_heads, lengths))  20.2 us
  transfers between devices with their start and end apart: 9, of which 8 were waited for; matrix products, arithmetic and copies ran while one was open for 19% of the time, Pallas kernels for 0%

commit v1 on v0

--- a/solution.py
+++ b/solution.py
@@ -1,8 +1,11 @@
+import functools
 import math
 
 import jax
 import jax.numpy as jnp
 from jax import lax
+from jax.experimental import pallas as pl
+from jax.experimental.pallas import tpu as pltpu
 from jax.sharding import PartitionSpec as P
 
 BLOCK = 16
@@ -15,43 +18,91 @@
     return jnp.sum(jnp.where(match, cached_len[None, :], 0), axis=1)
 
 
-def score_block(query_rows, cache_rows, span_rows):
-    span_count, group_count, width = query_rows.shape
-    head_dim = cache_rows.shape[-1] // 2
-    per_group = width // head_dim
-    query_split = query_rows.reshape(span_count, group_count, per_group, head_dim)
-    key_rows = jnp.concatenate([cache_rows[..., :head_dim], span_rows[..., :head_dim]], axis=0)
-    value_rows = jnp.concatenate([cache_rows[..., head_dim:], span_rows[..., head_dim:]], axis=0)
-    scores = jnp.einsum(
-        "igsd,pgd->gsip", query_split, key_rows, preferred_element_type=jnp.float32
-    ) * (1.0 / math.sqrt(head_dim))
-    return (scores, value_rows)
-
-
-def soft_weights(scores, allowed, value_rows):
-    masked = jnp.where(allowed, scores, -1e30)
-    row_max = jnp.max(masked, axis=-1, keepdims=True)
-    probability = jnp.where(allowed, jnp.exp(masked - row_max), 0.0)
-    prob_sum = jnp.sum(probability, axis=-1)
-    weighted = jnp.einsum(
-        "gsip,pgd->igsd",
-        probability.astype(jnp.bfloat16),
-        value_rows,
-        preferred_element_type=jnp.float32,
-    )
-    return (weighted, jnp.transpose(row_max[..., 0], (2, 0, 1)), jnp.transpose(prob_sum, (2, 0, 1)))
-
-
-def whole_request(operands):
-    query_rows, cache_rows, span_rows, length = operands
-    scores, value_rows = score_block(query_rows, cache_rows, span_rows)
-    cached = cache_rows.shape[0]
-    position = jnp.arange(scores.shape[-1])[None, :]
-    query_pos = jnp.arange(query_rows.shape[0])[:, None]
-    allowed = jnp.where(position < cached, position < length, position - cached <= query_pos)
-    weighted, row_max, prob_sum = soft_weights(scores, allowed, value_rows)
-    result = weighted / prob_sum[..., None]
-    return result.reshape(query_rows.shape).astype(jnp.bfloat16)
+def attend_kernel(len_ref, q_ref, c_ref, s_ref, o_ref, *, tk, head_dim):
+    b = pl.program_id(0)
+    length = len_ref[b]
+    span = q_ref.shape[1]
+    lanes = q_ref.shape[2]
+    per_group = lanes // head_dim
+    scale = 1.0 / math.sqrt(head_dim)
+    lane = lax.broadcasted_iota(jnp.int32, (span, lanes), 1)
+    q_all = q_ref[0].astype(jnp.float32)
+    nblk = (length + tk - 1) // tk
+    row = lax.broadcasted_iota(jnp.int32, (span, span), 0)
+    col = lax.broadcasted_iota(jnp.int32, (span, span), 1)
+    causal = col <= row
+    span_keys = s_ref[0]
+    dims = (((1,), (1,)), ((), ()))
+    outs = []
+    for j in range(per_group):
+        shifted = q_all if j == 0 else pltpu.roll(q_all, lanes - j * head_dim, 1)
+        qj = jnp.where(lane < head_dim, shifted, 0.0).astype(jnp.bfloat16)
+
+        def block_scores(kb):
+            start = pl.multiple_of(kb * tk, tk)
+            keys = c_ref[0, pl.ds(start, tk), :]
+            s = lax.dot_general(qj, keys, dims, preferred_element_type=jnp.float32) * scale
+            pos = start + lax.broadcasted_iota(jnp.int32, (span, tk), 1)
+            return keys, pos < length, s
+
+        def max_body(kb, m):
+            _, ok, s = block_scores(kb)
+            return jnp.maximum(m, jnp.max(jnp.where(ok, s, -1e30), axis=1, keepdims=True))
+
+        s_span = lax.dot_general(qj, span_keys, dims, preferred_element_type=jnp.float32) * scale
+        m0 = jnp.max(jnp.where(causal, s_span, -1e30), axis=1, keepdims=True)
+        m = lax.fori_loop(0, nblk, max_body, m0)
+
+        def sum_body(kb, carry):
+            l, acc = carry
+            keys, ok, s = block_scores(kb)
+            p = jnp.where(ok, jnp.exp(s - m), 0.0)
+            l = l + jnp.sum(p, axis=1, keepdims=True)
+            acc = acc + jnp.dot(p.astype(jnp.bfloat16), keys, preferred_element_type=jnp.float32)
+            return l, acc
+
+        p_span = jnp.where(causal, jnp.exp(s_span - m), 0.0)
+        l0 = jnp.sum(p_span, axis=1, keepdims=True)
+        acc0 = jnp.dot(p_span.astype(jnp.bfloat16), span_keys, preferred_element_type=jnp.float32)
+        l, acc = lax.fori_loop(0, nblk, sum_body, (l0, acc0))
+        res = acc / l
+        shift = (j * head_dim - head_dim) % lanes
+        outs.append(res if shift == 0 else pltpu.roll(res, shift, 1))
+    out = outs[0]
+    for j in range(1, per_group):
+        out = jnp.where(lane >= j * head_dim, outs[j], out)
+    o_ref[0] = out.astype(o_ref.dtype)
+
+
+def attend(query_heads, cache_heads, span_heads, lengths):
+    local_reqs, span, groups, lanes = query_heads.shape
+    cached = cache_heads.shape[1]
+    head_dim = cache_heads.shape[-1] // 2
+    tk = 256 if cached % 256 == 0 else cached
+    q2 = query_heads.reshape(local_reqs, span, groups * lanes)
+    c2 = cache_heads.reshape(local_reqs, cached, groups * lanes)
+    s2 = span_heads.reshape(local_reqs, span, groups * lanes)
+    flops = 2 * local_reqs * groups * (lanes // head_dim) * span * (cached + span) * lanes * 3
+    out = pl.pallas_call(
+        functools.partial(attend_kernel, tk=tk, head_dim=head_dim),
+        out_shape=jax.ShapeDtypeStruct(q2.shape, jnp.bfloat16),
+        grid_spec=pltpu.PrefetchScalarGridSpec(
+            num_scalar_prefetch=1,
+            grid=(local_reqs, groups),
+            in_specs=[
+                pl.BlockSpec((1, span, lanes), lambda b, g, n: (b, 0, g)),
+                pl.BlockSpec((1, cached, lanes), lambda b, g, n: (b, 0, g)),
+                pl.BlockSpec((1, span, lanes), lambda b, g, n: (b, 0, g)),
+            ],
+            out_specs=pl.BlockSpec((1, span, lanes), lambda b, g, n: (b, 0, g)),
+        ),
+        cost_estimate=pl.CostEstimate(
+            flops=flops,
+            transcendentals=local_reqs * groups * 2 * span * (cached + span),
+            bytes_accessed=2 * (2 * q2.size + c2.size + s2.size),
+        ),
+    )(lengths.astype(jnp.int32), q2, c2, s2)
+    return out.reshape(local_reqs, span, groups, lanes)
 
 
 def place_pages(page_rows, slot_numbers, slots_dev):
@@ -90,7 +141,7 @@
         lax.all_to_all(span_kv, "kv", split_axis=2, concat_axis=1, tiled=True),
         lax.all_to_all(queries_grouped, "kv", split_axis=2, concat_axis=1, tiled=True),
     )
-    attn_heads = lax.map(whole_request, (query_heads, cache_heads, span_heads, lengths))
+    attn_heads = attend(query_heads, cache_heads, span_heads, lengths)
     attn = lax.all_to_all(attn_heads, "kv", split_axis=1, concat_axis=2, tiled=True).reshape(
         row_count, kv_heads * group_width
     )
@@ -111,11 +162,14 @@
             local_slot.reshape(req_count, per_owner), "req", split_axis=0, concat_axis=0, tiled=True
         ),
     )
-    decode_pool = (
-        jnp.zeros((slots_dev, group_count, BLOCK, head_pair), jnp.bfloat16)
-        .at[where_to.reshape(-1)]
-        .set(arrived.reshape(-1, group_count, BLOCK, head_pair))
-    )
+    placement = (
+        where_to.reshape(1, -1) == jnp.arange(slots_dev, dtype=jnp.int32)[:, None]
+    ).astype(jnp.bfloat16)
+    decode_pool = jnp.dot(
+        placement,
+        arrived.reshape(slots_dev, group_count * BLOCK * head_pair),
+        preferred_element_type=jnp.float32,
+    ).astype(jnp.bfloat16).reshape(slots_dev, group_count, BLOCK, head_pair)
     residual = hidden.reshape(row_count, width_model).astype(jnp.float32) + jnp.dot(
         attn, out_weight, preferred_element_type=jnp.float32
     )
@@ -125,17 +179,15 @@
     exp_dev = w_experts.shape[0]
     experts = exp_dev * req_count
     capacity = min(row_count, 2 * row_count * top_count // experts)
-    chosen = expert_ids.reshape(-1)
-    onehot = (chosen[:, None] == jnp.arange(experts, dtype=jnp.int32)[None, :]).astype(jnp.int32)
-    slot_rank = jnp.sum(onehot * (jnp.cumsum(onehot, axis=0) - 1), axis=1)
-    target = chosen * capacity + slot_rank
-    source_row = jnp.arange(chosen.shape[0]) // top_count
-    buffer = (
-        jnp.zeros((experts * capacity, width_model), jnp.bfloat16)
-        .at[target]
-        .set(normed[source_row])
-        .reshape(experts, capacity, width_model)
-    )
+    match = expert_ids[:, :, None] == jnp.arange(experts, dtype=jnp.int32)[None, None, :]
+    picks = jnp.sum(match.astype(jnp.int32), axis=1)
+    pick_weight = jnp.sum(jnp.where(match, expert_weights[:, :, None], 0.0), axis=1)
+    rank = jnp.cumsum(picks, axis=0) - 1
+    slot_of = jnp.where(picks > 0, rank, -1).T
+    selector = slot_of[:, None, :] == jnp.arange(capacity, dtype=jnp.int32)[None, :, None]
+    buffer = jnp.einsum(
+        "ect,td->ecd", selector.astype(jnp.bfloat16), normed, preferred_element_type=jnp.float32
+    ).astype(jnp.bfloat16)
     full_weights = lax.all_gather(w_experts, "kv", axis=3, tiled=True)
     slot_block = lax.all_to_all(buffer, "req", split_axis=0, concat_axis=0, tiled=True)
     source_count = slot_block.shape[0] // exp_dev
@@ -153,10 +205,13 @@
     returned = lax.all_to_all(
         expert_out.reshape(slot_block.shape), "req", split_axis=0, concat_axis=0, tiled=True
     )
-    picked = returned.reshape(experts * capacity, width_model)[target].reshape(
-        row_count, top_count, width_model
-    )
-    expert_sum = jnp.sum(expert_weights[..., None] * picked.astype(jnp.float32), axis=1)
+    combine = jnp.where(selector, pick_weight.T[:, None, :], 0.0)
+    combine_hi = combine.astype(jnp.bfloat16)
+    combine_lo = (combine - combine_hi.astype(jnp.float32)).astype(jnp.bfloat16)
+    returned = returned.reshape(experts, capacity, width_model)
+    expert_sum = jnp.einsum(
+        "ect,ecd->td", combine_hi, returned, preferred_element_type=jnp.float32
+    ) + jnp.einsum("ect,ecd->td", combine_lo, returned, preferred_element_type=jnp.float32)
     layer_out = (
         (residual + expert_sum).astype(jnp.bfloat16).reshape(local_reqs, local_tokens, width_model)
     )

time: 760 us -> 699 us (0.920); the launches traced: 748 us -> 703 us
  local copies, waits for them, and re-layouts: 147 us -> 51.5 us
  starting transfers between devices: 38.9 us -> 101 us
  other arithmetic: 68.1 us -> 9.51 us
  waiting for transfers between devices: 421 us -> 456 us
  Pallas kernels: 0 us -> 20.6 us
  matrix products: 58.8 us -> 50.5 us
    scatter x2 -> x0, local copies, waits for them, and re-layouts: 66.5 us -> none  [the longest x1 33.5 us: body(): decode_pool = jnp.zeros((slots_dev, group_count, BLOCK, head_pair), jnp.b...]
    all_to_all x1, starting transfers between devices: 6.59 us -> 69 us  [body(): lax.all_to_all(local_slot.reshape(req_count, per_owner), 'req', split_axi...]
    sub x5 -> x0, other arithmetic: 39 us -> none  [the longest x2 38.9 us: soft_weights(): probability = jnp.where(allowed, jnp.exp(masked - row_max), 0.0)]
    all_to_all x1, waiting for transfers between devices: 144 us -> 167 us  [body(): lax.all_to_all(expert_out.reshape(slot_block.shape), 'req', split_axis=0,...]
    pallas_call x0 -> x1, Pallas kernels: none -> 20.6 us  [attend(): pl.pallas_call(functools.partial(attend_kernel, tk=tk, head_dim=head_dim)...]
    dynamic_slice x10 -> x0, local copies, waits for them, and re-layouts: 20.2 us -> none  [body(): lax.map(whole_request, (query_heads, cache_heads, span_heads, lengths))]
    reshape x1 -> x7, local copies, waits for them, and re-layouts: 0.08 us -> 19.6 us  [the longest x1 7.27 us: body(): arrived.reshape(slots_dev, group_count * BLOCK * head_pair)]
    gather x1 -> x0, local copies, waits for them, and re-layouts: 15.5 us -> none  [body(): returned.reshape(experts * capacity, width_model)[target]]
  transfers between devices with their start and end apart: 9 -> 9, of which waited for: 8 -> 8; matrix products, arithmetic and copies ran while one was open for 19% -> 11% of each run, Pallas kernels for 0% -> 0%
where the time goes in v1:
time: 699 us; the launch traced here: 703 us
  waiting for transfers between devices  456 us (65%)
  starting transfers between devices  101 us (14%)
  local copies, waits for them, and re-layouts  51.5 us (7%)
  matrix products  50.5 us (7%)
  Pallas kernels  20.6 us (3%)
  between operations  14.3 us (2%)
  other arithmetic  9.51 us (1%)
    all_to_all x1, waiting for transfers between devices, body(): lax.all_to_all(buffer, 'req', split_axis=0, concat_axis=0, tiled=True)  173 us
    all_to_all x1, waiting for transfers between devices, body(): lax.all_to_all(expert_out.reshape(slot_block.shape), 'req', split_axis=0,...  167 us
    all_to_all x1, starting transfers between devices, body(): lax.all_to_all(local_slot.reshape(req_count, per_owner), 'req', split_axi...  69 us
    all_gather x1, waiting for transfers between devices, body(): full_weights = lax.all_gather(w_experts, 'kv', axis=3, tiled=True)  46.5 us
    all_to_all x1, waiting for transfers between devices, body(): lax.all_to_all(cache, 'kv', split_axis=2, concat_axis=1, tiled=True)  36.6 us
    pallas_call x1, Pallas kernels, attend(): pl.pallas_call(functools.partial(attend_kernel, tk=tk, head_dim=head_dim)...  20.6 us
    all_to_all x1, waiting for transfers between devices, body(): lax.all_to_all(outgoing, 'req', split_axis=0, concat_axis=0, tiled=True)  18.1 us
    dot_general x1, matrix products, body(): jnp.einsum('sejf,edf->sejd', activated, full_weights[:, 2], preferred_ele...  16 us
  transfers between devices with their start and end apart: 9, of which 8 were waited for; matrix products, arithmetic and copies ran while one was open for 11% of the time, Pallas kernels for 0%

profile of v1, /device:TPU:16, one launch (start us, length us, event | category | flops | bytes accessed | tf_op | source)
XLA Modules:
  0.0 703.2 jit_solution(10273815264189693166)
XLA Ops:
  14.9 6.3 all-to-all-done
  24.7 5.0 copy.61
  32.1 5.6 all-to-all-start.1
  47.0 36.6 %all-to-all-done.1 = bf16[2,1024,8,128]{3,1,0,2:T(8,128)(2,1)} async-done(((bf16[2,1024,8,128]{3,1,0,2:T(8,128)(2,1)}), bf16[2,1024,8,128]{3,1,0,2:T(8,128)(2,1)}, u32[]{:S(2)}, u32[]{:S(2)}) %all-to-all-start.1) | async-done | bytes 4194336 | tf_op jit(solution)/shard_map/all_to_all | solution.py:140
  83.6 7.4 %copy.84 = bf16[2,1024,2,4,128]{4,3,1,2,0:T(4,128)(2,1)} copy(bf16[2,1024,2,4,128]{4,1,0,3,2:T(8,128)(2,1)} %bitcast.5) | data formatting | bytes 8388608 | tf_op jit(solution)/shard_map/all_to_all | solution.py:140
  91.0 7.2 %reshape.133.c_ref = bf16[2,2048,512]{2,1,0:T(8,128)(2,1)} reshape(bf16[2,2,1024,4,128]{4,3,2,1,0:T(4,128)(2,1)} %bitcast.134) | data formatting | bytes 8388608 | tf_op jit(solution)/shard_map/reshape | solution.py:83
  98.2 20.6 %shard_map.131 = bf16[2,256,512]{2,1,0:T(8,128)(2,1)} custom-call(s32[2]{0:T(128)} %fusion.33.len_ref, bf16[2,256,512]{2,1,0:T(8,128)(2,1)} %reshape.132.q_ref, bf16[2,2048,512]{2,1,0:T(8,128)(2,1)} %reshape.133.c_ref, bf16[2,256,512]{2,1,0:T(8,128)(2,1)} %reshape.134.s_ref), custom_call_target="tpu_custom_call" | custom-call | flops 7247757312 | bytes 5767168 | tf_op jit(solution)/shard_map/pallas_call | solution.py:86
  127.2 5.5 all-to-all-done.3
  132.7 69.0 %all-to-all-start.6 = ((s32[16,1,16]{2,1,0:T(1,128)}), s32[16,1,16]{2,1,0:T(1,128)S(1)}, u32[]{:S(2)}, u32[]{:S(2)}) async-start(s32[16,1,16]{2,1,0:T(1,128)} %all_to_all.75), calls=%async_computation.6 | async-start | bytes 16384 | tf_op jit(solution)/shard_map/all_to_all | solution.py:161
  205.3 5.2 convolution_convert_fusion.1
  210.6 6.0 all-to-all-start.4
  216.7 4.1 copy_select_fusion
  220.8 5.3 gather_fusion.1
  226.1 173.1 %all-to-all-done.4 = bf16[16,256,1024]{2,1,0:T(8,128)(2,1)} async-done(((bf16[16,256,1024]{2,1,0:T(8,128)(2,1)}), bf16[16,256,1024]{2,1,0:T(8,128)(2,1)}, u32[]{:S(2)}, u32[]{:S(2)}) %all-to-all-start.4) | async-done | bytes 8388640 | tf_op jit(solution)/shard_map/all_to_all | solution.py:192
  399.2 4.7 all-to-all-start.7
  404.6 46.5 %all-gather.2.cloned.1.call-done = bf16[1,3,1024,512]{3,2,1,0:T(8,128)(2,1)} async-done(((bf16[1,3,1024,256]{3,2,1,0:T(8,128)(2,1)}), bf16[1,3,1024,512]{3,2,1,0:T(8,128)(2,1)}) %all-gather.2.cloned.1.call-update) | async-done | bytes 3145744 | tf_op jit(solution)/shard_map/all_gather | solution.py:191
  451.1 11.4 %fusion.27 = f32[16,256,512]{2,1,0:T(8,128)} fusion(bf16[16,256,1024]{2,1,0:T(8,128)(2,1)} %all-to-all-done.4, bf16[1,3,1024,512]{3,2,1,0:T(8,128)(2,1)} %all-gather.2.cloned.1.call-done), kind=kOutput, calls=%fused_computation.38 | convolution fusion | flops 4294967296 | bytes 17825792 | tf_op jit(solution)/shard_map/sejd,edf->sejf/dot_general | solution.py:195
  462.5 16.0 %convolution_convert_fusion.2 = bf16[16,256,1024]{2,1,0:T(8,128)(2,1)} fusion(f32[16,256,512]{2,1,0:T(8,128)} %fusion.27, bf16[16,256,1024]{2,1,0:T(8,128)(2,1)} %all-to-all-done.4, bf16[1,3,1024,512]{3,2,1,0:T(8,128)(2,1)} %all-gather.2.cloned.1.call-done), kind=kOutput, calls=%fused_computation.11 | convolution fusion | flops 8606711808 | bytes 27262976 | tf_op jit(solution)/shard_map/sejf,edf->sejd/dot_general | solution.py:202
  478.5 18.1 %all-to-all-done.7 = bf16[16,16,4,16,128]{4,3,2,1,0:T(8,128)(2,1)} async-done(((bf16[16,16,4,16,128]{4,3,2,1,0:T(8,128)(2,1)}), bf16[16,16,4,16,128]{4,3,2,1,0:T(8,128)(2,1)}, u32[]{:S(2)}, u32[]{:S(2)}) %all-to-all-start.7) | async-done | bytes 4194336 | tf_op jit(solution)/shard_map/all_to_all | solution.py:160
  496.6 4.9 all-to-all-start.5
  502.7 7.3 %reshape.147 = bf16[256,8192]{1,0:T(8,128)(2,1)} reshape(bf16[16,16,4,16,128]{4,3,2,1,0:T(8,128)(2,1)} %all-to-all-done.7) | data formatting | bytes 8388608 | tf_op jit(solution)/shard_map/reshape | solution.py:170
  516.7 167.1 %all-to-all-done.5 = bf16[16,256,1024]{2,1,0:T(8,128)(2,1)} async-done(((bf16[16,256,1024]{2,1,0:T(8,128)(2,1)}), bf16[16,256,1024]{2,1,0:T(8,128)(2,1)}, u32[]{:S(2)}, u32[]{:S(2)}) %all-to-all-start.5) | async-done | bytes 8388640 | tf_op jit(solution)/shard_map/all_to_all | solution.py:205
  683.8 5.7 fusion.20
  689.6 6.8 fusion.26
  (63 shorter events, 43.6 us)
Async XLA Ops:
  7.2 196.1 %copy-start = (bf16[1024,1024]{1,0:T(8,128)(2,1)S(1)}, bf16[1024,1024]{1,0:T(8,128)(2,1)}, u32[]{:S(2)}) copy-start(bf16[1024,1024]{1,0:T(8,128)(2,1)} %param.18) | copy-start | bytes 6291460
  9.5 11.7 %all-to-all-start = ((bf16[2,128,8,128]{1,3,0,2:T(8,128)(2,1)}), bf16[2,128,8,128]{1,3,0,2:T(8,128)(2,1)S(1)}, u32[]{:S(2)}, u32[]{:S(2)}) async-start(bf16[2,128,8,128]{1,3,0,2:T(8,128)(2,1)} %copy.58), calls=%async_computation | async-start | bytes 1048576 | tf_op jit(solution)/shard_map/all_to_all | solution.py:142
  21.2 10.9 %all-to-all-start.2 = ((bf16[2,128,8,128]{3,1,0,2:T(8,128)(2,1)}), bf16[2,128,8,128]{3,1,0,2:T(8,128)(2,1)S(1)}, u32[]{:S(2)}, u32[]{:S(2)}) async-start(bf16[2,128,8,128]{3,1,0,2:T(8,128)(2,1)} %copy.63), calls=%async_computation.2 | async-start | bytes 1048576 | tf_op jit(solution)/shard_map/all_to_all | solution.py:141
  29.7 8.0 %copy-start.2 = (s32[256,8]{0,1:T(8,128)S(1)}, s32[256,8]{0,1:T(8,128)}, u32[]{:S(2)}) copy-start(s32[256,8]{0,1:T(8,128)} %param.20) | copy-start | bytes 24580
  29.7 8.6 %copy-start.7 = (s32[32]{0:T(128)S(1)}, s32[32]{0:T(128)}, u32[]{:S(2)}) copy-start(s32[32]{0:T(128)} %param.16) | copy-start | bytes 388
  29.7 8.7 %copy-start.5 = (s32[2,128]{1,0:T(2,128)S(1)}, s32[2,128]{1,0:T(2,128)}, u32[]{:S(2)}) copy-start(s32[2,128]{1,0:T(2,128)} %param.23) | copy-start | bytes 3076
  29.7 12.1 %copy-start.8 = (s32[32]{0:T(128)S(1)}, s32[32]{0:T(128)}, u32[]{:S(2)}) copy-start(s32[32]{0:T(128)} %param.17) | copy-start | bytes 388
  32.1 51.5 %all-to-all-start.1 = ((bf16[2,1024,8,128]{3,1,0,2:T(8,128)(2,1)}), bf16[2,1024,8,128]{3,1,0,2:T(8,128)(2,1)}, u32[]{:S(2)}, u32[]{:S(2)}) async-start(bf16[2,1024,8,128]{3,1,0,2:T(8,128)(2,1)} %copy.61), calls=%async_computation.1 | async-start | bytes 8388608 | tf_op jit(solution)/shard_map/all_to_all | solution.py:140
  121.0 11.7 %all-to-all-start.3 = ((bf16[2,256,4,128]{3,2,0,1:T(4,128)(2,1)}), bf16[2,256,4,128]{3,2,0,1:T(4,128)(2,1)S(1)}, u32[]{:S(2)}, u32[]{:S(2)}) async-start(bf16[2,256,4,128]{3,2,0,1:T(4,128)(2,1)} %copy.65), calls=%async_computation.3 | async-start | bytes 1048576 | tf_op jit(solution)/shard_map/all_to_all | solution.py:145
  124.5 80.8 %copy-start.4 = (f32[1024]{0:T(1024)S(1)}, f32[1024]{0:T(1024)}, u32[]{:S(2)}) copy-start(f32[1024]{0:T(1024)} %param.19) | copy-start | bytes 12292
  132.7 77.9 %all-to-all-start.6 = ((s32[16,1,16]{2,1,0:T(1,128)}), s32[16,1,16]{2,1,0:T(1,128)S(1)}, u32[]{:S(2)}, u32[]{:S(2)}) async-start(s32[16,1,16]{2,1,0:T(1,128)} %all_to_all.75), calls=%async_computation.6 | async-start | bytes 16384 | tf_op jit(solution)/shard_map/all_to_all | solution.py:161
  210.6 6.0 copy-start.6
  210.6 188.6 %all-to-all-start.4 = ((bf16[16,256,1024]{2,1,0:T(8,128)(2,1)}), bf16[16,256,1024]{2,1,0:T(8,128)(2,1)}, u32[]{:S(2)}, u32[]{:S(2)}) async-start(bf16[16,256,1024]{2,1,0:T(8,128)(2,1)} %convolution_convert_fusion.1), calls=%async_computation.4 | async-start | bytes 16777216 | tf_op jit(solution)/shard_map/all_to_all | solution.py:192
  399.2 97.4 %all-to-all-start.7 = ((bf16[16,16,4,16,128]{4,3,2,1,0:T(8,128)(2,1)}), bf16[16,16,4,16,128]{4,3,2,1,0:T(8,128)(2,1)}, u32[]{:S(2)}, u32[]{:S(2)}) async-start(bf16[16,16,4,16,128]{4,3,2,1,0:T(8,128)(2,1)} %bitcast.136), calls=%async_computation.7 | async-start | bytes 8388608 | tf_op jit(solution)/shard_map/all_to_all | solution.py:160
  403.9 47.3 %all-gather.2.cloned.1.call-start = ((), (), s32[]{:S(2)}) async-start(), calls=%async_computation.8 | async-start | bytes 4718592 | tf_op jit(solution)/shard_map/all_gather | solution.py:191
  478.5 23.0 %copy-start.3 = (f32[256,8]{0,1:T(8,128)S(1)}, f32[256,8]{0,1:T(8,128)}, u32[]{:S(2)}) copy-start(f32[256,8]{0,1:T(8,128)} %param.21) | copy-start | bytes 24580
  496.6 187.3 %all-to-all-start.5 = ((bf16[16,256,1024]{2,1,0:T(8,128)(2,1)}), bf16[16,256,1024]{2,1,0:T(8,128)(2,1)}, u32[]{:S(2)}, u32[]{:S(2)}) async-start(bf16[16,256,1024]{2,1,0:T(8,128)(2,1)} %convolution_convert_fusion.2), calls=%async_computation.5 | async-start | bytes 16777216 | tf_op jit(solution)/shard_map/all_to_all | solution.py:205
  689.5 6.8 copy-start.1
Sparse Core Ops, SparseCore 0:
  406.2 44.8 all-gather.1

commit v2 on v1

--- a/solution.py
+++ b/solution.py
@@ -11,8 +11,11 @@
 BLOCK = 16
 
 
+REQ = ("zhi", "rlow")
+
+
 def lookup_lengths(req_order, cached_len, count):
-    start = lax.axis_index("req") * count
+    start = lax.axis_index(REQ) * count
     mine = lax.dynamic_slice_in_dim(req_order, start, count)
     match = mine[:, None] == jnp.arange(cached_len.shape[0], dtype=jnp.int32)[None, :]
     return jnp.sum(jnp.where(match, cached_len[None, :], 0), axis=1)
@@ -127,7 +130,7 @@
 ):
     local_reqs, local_tokens, width_model = hidden.shape
     row_count = local_reqs * local_tokens
-    req_count = lax.axis_size("req")
+    req_count = lax.axis_size(REQ)
     kv_count = lax.axis_size("kv")
     kv_heads = span_kv.shape[2]
     head_pair = span_kv.shape[3]
@@ -157,9 +160,9 @@
     per_owner = sorted_pages.shape[0] // req_count
     outgoing = sorted_pages.reshape(req_count, per_owner, group_count, BLOCK, head_pair)
     arrived, where_to = (
-        lax.all_to_all(outgoing, "req", split_axis=0, concat_axis=0, tiled=True),
+        lax.all_to_all(outgoing, REQ, split_axis=0, concat_axis=0, tiled=True),
         lax.all_to_all(
-            local_slot.reshape(req_count, per_owner), "req", split_axis=0, concat_axis=0, tiled=True
+            local_slot.reshape(req_count, per_owner), REQ, split_axis=0, concat_axis=0, tiled=True
         ),
     )
     placement = (
@@ -179,19 +182,33 @@
     exp_dev = w_experts.shape[0]
     experts = exp_dev * req_count
     capacity = min(row_count, 2 * row_count * top_count // experts)
+    halves = lax.axis_size("zhi")
+    side = lax.axis_size("rlow")
     match = expert_ids[:, :, None] == jnp.arange(experts, dtype=jnp.int32)[None, None, :]
     picks = jnp.sum(match.astype(jnp.int32), axis=1)
     pick_weight = jnp.sum(jnp.where(match, expert_weights[:, :, None], 0.0), axis=1)
     rank = jnp.cumsum(picks, axis=0) - 1
-    slot_of = jnp.where(picks > 0, rank, -1).T
+
+    def side_major(table):
+        return (
+            table.reshape(halves, side, exp_dev, row_count)
+            .transpose(1, 0, 2, 3)
+            .reshape(experts, row_count)
+        )
+
+    slot_of = side_major(jnp.where(picks > 0, rank, -1).T)
+    weight_of = side_major(pick_weight.T)
     selector = slot_of[:, None, :] == jnp.arange(capacity, dtype=jnp.int32)[None, :, None]
     buffer = jnp.einsum(
         "ect,td->ecd", selector.astype(jnp.bfloat16), normed, preferred_element_type=jnp.float32
     ).astype(jnp.bfloat16)
-    full_weights = lax.all_gather(w_experts, "kv", axis=3, tiled=True)
-    slot_block = lax.all_to_all(buffer, "req", split_axis=0, concat_axis=0, tiled=True)
-    source_count = slot_block.shape[0] // exp_dev
-    grouped = slot_block.reshape(source_count, exp_dev, slot_block.shape[1], width_model)
+    pair_weights = lax.all_gather(w_experts, "zhi", axis=0, tiled=True)
+    full_weights = lax.all_gather(pair_weights, "kv", axis=3, tiled=True)
+    per_dev = halves * exp_dev
+    slot_block = lax.all_to_all(
+        buffer.reshape(side, per_dev * capacity, width_model), "rlow", split_axis=0, concat_axis=0, tiled=True
+    )
+    grouped = slot_block.reshape(side, per_dev, capacity, width_model)
     gate_act = jnp.einsum(
         "sejd,edf->sejf", grouped, full_weights[:, 0], preferred_element_type=jnp.float32
     )
@@ -203,9 +220,9 @@
         "sejf,edf->sejd", activated, full_weights[:, 2], preferred_element_type=jnp.float32
     ).astype(jnp.bfloat16)
     returned = lax.all_to_all(
-        expert_out.reshape(slot_block.shape), "req", split_axis=0, concat_axis=0, tiled=True
-    )
-    combine = jnp.where(selector, pick_weight.T[:, None, :], 0.0)
+        expert_out.reshape(side, per_dev * capacity, width_model), "rlow", split_axis=0, concat_axis=0, tiled=True
+    )
+    combine = jnp.where(selector, weight_of[:, None, :], 0.0)
     combine_hi = combine.astype(jnp.bfloat16)
     combine_lo = (combine - combine_hi.astype(jnp.float32)).astype(jnp.bfloat16)
     returned = returned.reshape(experts, capacity, width_model)
@@ -219,23 +236,28 @@
 
 
 def solution(mesh):
+    devices = mesh.devices
+    req_total, kv_total = devices.shape
+    split_mesh = jax.sharding.Mesh(
+        devices.reshape(2, req_total // 2, kv_total), ("zhi", "rlow", "kv")
+    )
     return jax.shard_map(
         body,
-        mesh=mesh,
+        mesh=split_mesh,
         in_specs=(
-            P("req", "kv", None),
-            P("req", "kv", None),
-            P("req", "kv", None, None),
-            P("req", "kv", None, None),
-            P(),
-            P(),
-            P(),
-            P(),
-            P(("req", "kv"), None),
-            P(("req", "kv"), None),
-            P("req", None, None, "kv"),
-            P("req", None),
-        ),
-        out_specs=(P("req", "kv", None), P("req", "kv", None, None)),
+            P(REQ, "kv", None),
+            P(REQ, "kv", None),
+            P(REQ, "kv", None, None),
+            P(REQ, "kv", None, None),
+            P(),
+            P(),
+            P(),
+            P(),
+            P((*REQ, "kv"), None),
+            P((*REQ, "kv"), None),
+            P(REQ, None, None, "kv"),
+            P(REQ, None),
+        ),
+        out_specs=(P(REQ, "kv", None), P(REQ, "kv", None, None)),
         check_vma=False,
     )

time: 699 us -> 558 us (0.80); the launches traced: 703 us -> 555 us
  waiting for transfers between devices: 456 us -> 300 us
  starting transfers between devices: 101 us -> 84.4 us
  Pallas kernels: 20.6 us -> 35.5 us
  local copies, waits for them, and re-layouts: 51.5 us -> 59.5 us
    all_to_all x4, waiting for transfers between devices: 358 us -> 140 us  [the longest x1 77.6 us: body(): lax.all_to_all(expert_out.reshape(side, per_dev * capacity, width_model),...]
    all_gather x1 -> x2, waiting for transfers between devices: 46.5 us -> 111 us  [the longest x1 79.6 us: body(): pair_weights = lax.all_gather(w_experts, 'zhi', axis=0, tiled=True)]
    all_to_all x4, starting transfers between devices: 84.5 us -> 68.2 us  [the longest x1 52.8 us: body(): lax.all_to_all(local_slot.reshape(req_count, per_owner), REQ, split_axis=...]
    pallas_call x1, Pallas kernels: 20.6 us -> 35.5 us  [attend(): pl.pallas_call(functools.partial(attend_kernel, tk=tk, head_dim=head_dim)...]
    convert_element_type x0 -> x1, local copies, waits for them, and re-layouts: none -> 7.94 us  [body(): expert_out = jnp.einsum('sejf,edf->sejd', activated, full_weights[:, 2],...]
  transfers between devices with their start and end apart: 9 -> 10, of which waited for: 8 -> 9; matrix products, arithmetic and copies ran while one was open for 11% -> 16% of each run, Pallas kernels for 0% -> 0%
where the time goes in v2:
time: 558 us; the launch traced here: 555 us
  waiting for transfers between devices  300 us (54%)
  starting transfers between devices  84.4 us (15%)
  local copies, waits for them, and re-layouts  59.5 us (11%)
  matrix products  51.3 us (9%)
  Pallas kernels  35.5 us (6%)
  between operations  14.3 us (3%)
  other arithmetic  9.58 us (2%)
    all_gather x1, waiting for transfers between devices, body(): pair_weights = lax.all_gather(w_experts, 'zhi', axis=0, tiled=True)  79.6 us
    all_to_all x1, waiting for transfers between devices, body(): lax.all_to_all(expert_out.reshape(side, per_dev * capacity, width_model),...  77.6 us
    all_to_all x1, starting transfers between devices, body(): lax.all_to_all(local_slot.reshape(req_count, per_owner), REQ, split_axis=...  52.8 us
    all_to_all x1, waiting for transfers between devices, body(): lax.all_to_all(buffer.reshape(side, per_dev * capacity, width_model), 'rl...  36.9 us
    all_to_all x1, waiting for transfers between devices, body(): lax.all_to_all(cache, 'kv', split_axis=2, concat_axis=1, tiled=True)  36.3 us
    pallas_call x1, Pallas kernels, attend(): pl.pallas_call(functools.partial(attend_kernel, tk=tk, head_dim=head_dim)...  35.5 us
    all_gather x1, waiting for transfers between devices, body(): full_weights = lax.all_gather(pair_weights, 'kv', axis=3, tiled=True)  31.6 us
    all_to_all x1, waiting for transfers between devices, body(): lax.all_to_all(outgoing, REQ, split_axis=0, concat_axis=0, tiled=True)  25.1 us
  transfers between devices with their start and end apart: 10, of which 9 were waited for; matrix products, arithmetic and copies ran while one was open for 16% of the time, Pallas kernels for 0%

profile of v2, /device:TPU:16, one launch (start us, length us, event | category | flops | bytes accessed | tf_op | source)
XLA Modules:
  0.0 554.9 jit_solution(16088782041148907240)
XLA Ops:
  14.9 6.3 %all-to-all-done = bf16[2,128,8,128]{1,3,0,2:T(8,128)(2,1)S(1)} async-done(((bf16[2,128,8,128]{1,3,0,2:T(8,128)(2,1)}), bf16[2,128,8,128]{1,3,0,2:T(8,128)(2,1)S(1)}, u32[]{:S(2)}, u32[]{:S(2)}) %all-to-all-start) | async-done | bytes 524320 | tf_op jit(solution)/shard_map/all_to_all | solution.py:145
  24.7 5.0 copy.77
  32.1 5.6 %all-to-all-start.1 = ((bf16[2,1024,8,128]{3,1,0,2:T(8,128)(2,1)}), bf16[2,1024,8,128]{3,1,0,2:T(8,128)(2,1)}, u32[]{:S(2)}, u32[]{:S(2)}) async-start(bf16[2,1024,8,128]{3,1,0,2:T(8,128)(2,1)} %copy.77), calls=%async_computation.1 | async-start | bytes 8388608 | tf_op jit(solution)/shard_map/all_to_all | solution.py:143
  47.2 36.3 %all-to-all-done.1 = bf16[2,1024,8,128]{3,1,0,2:T(8,128)(2,1)} async-done(((bf16[2,1024,8,128]{3,1,0,2:T(8,128)(2,1)}), bf16[2,1024,8,128]{3,1,0,2:T(8,128)(2,1)}, u32[]{:S(2)}, u32[]{:S(2)}) %all-to-all-start.1) | async-done | bytes 4194336 | tf_op jit(solution)/shard_map/all_to_all | solution.py:143
  83.6 7.4 %copy.117 = bf16[2,1024,2,4,128]{4,3,1,2,0:T(4,128)(2,1)} copy(bf16[2,1024,2,4,128]{4,1,0,3,2:T(8,128)(2,1)} %bitcast.5) | data formatting | bytes 8388608 | tf_op jit(solution)/shard_map/all_to_all | solution.py:143
  91.0 7.2 %reshape.126.c_ref = bf16[2,2048,512]{2,1,0:T(8,128)(2,1)} reshape(bf16[2,2,1024,4,128]{4,3,2,1,0:T(4,128)(2,1)} %bitcast.141) | data formatting | bytes 8388608 | tf_op jit(solution)/shard_map/reshape | solution.py:86
  98.2 35.5 %shard_map.131 = bf16[2,256,512]{2,1,0:T(8,128)(2,1)} custom-call(s32[2]{0:T(128)} %fusion.39.len_ref, bf16[2,256,512]{2,1,0:T(8,128)(2,1)} %reshape.125.q_ref, bf16[2,2048,512]{2,1,0:T(8,128)(2,1)} %reshape.126.c_ref, bf16[2,256,512]{2,1,0:T(8,128)(2,1)} %reshape.127.s_ref), custom_call_target="tpu_custom_call" | custom-call | flops 7247757312 | bytes 5767168 | tf_op jit(solution)/shard_map/pallas_call | solution.py:89
  145.9 52.8 %all-to-all-start.6 = ((s32[16,1,16]{2,1,0:T(1,128)}), s32[16,1,16]{2,1,0:T(1,128)S(1)}, u32[]{:S(2)}, u32[]{:S(2)}) async-start(s32[16,1,16]{2,1,0:T(1,128)} %all_to_all.75), calls=%async_computation.6 | async-start | bytes 16384 | tf_op jit(solution)/shard_map/all_to_all | solution.py:164
  202.4 5.2 convolution_convert_fusion.1
  207.6 4.9 all-to-all-start.4
  213.4 79.6 %all-gather.3.cloned.1.call-done = bf16[2,3,1024,256]{3,2,0,1:T(8,128)(2,1)} async-done(((bf16[1,3,1024,256]{3,2,0,1:T(8,128)(2,1)}), bf16[2,3,1024,256]{3,2,0,1:T(8,128)(2,1)}) %all-gather.3.cloned.1.call-update) | async-done | bytes 3145744 | tf_op jit(solution)/shard_map/all_gather | solution.py:205
  297.2 5.3 gather_fusion.1
  302.5 36.9 %all-to-all-done.4 = bf16[8,512,1024]{2,1,0:T(8,128)(2,1)} async-done(((bf16[8,512,1024]{2,1,0:T(8,128)(2,1)}), bf16[8,512,1024]{2,1,0:T(8,128)(2,1)}, u32[]{:S(2)}, u32[]{:S(2)}) %all-to-all-start.4) | async-done | bytes 8388640 | tf_op jit(solution)/shard_map/all_to_all | solution.py:208
  339.4 5.1 all-to-all-start.7
  344.5 31.6 %all-gather.5.cloned.1.call-done = bf16[2,3,1024,512]{3,2,0,1:T(8,128)(2,1)} async-done(((bf16[2,3,1024,256]{3,2,0,1:T(8,128)(2,1)}), bf16[2,3,1024,512]{3,2,0,1:T(8,128)(2,1)}) %all-gather.5.cloned.1.call-update) | async-done | bytes 6291472 | tf_op jit(solution)/shard_map/all_gather | solution.py:206
  376.1 11.7 %fusion.4 = f32[2,8,256,512]{3,2,1,0:T(8,128)} fusion(bf16[8,2,256,1024]{3,2,1,0:T(8,128)(2,1)} %bitcast.19, bf16[2,3,1024,512]{3,2,0,1:T(8,128)(2,1)} %all-gather.5.cloned.1.call-done), kind=kOutput, calls=%fused_computation.11 | convolution fusion | flops 4294967296 | bytes 18874368 | tf_op jit(solution)/shard_map/sejd,edf->sejf/dot_general | solution.py:215
  387.8 16.4 %convert_bitcast_fusion = bf16[8,2,256,1024]{3,2,0,1:T(8,128)(2,1)} fusion(f32[2,8,256,512]{3,2,1,0:T(8,128)} %fusion.4, bf16[8,2,256,1024]{3,2,1,0:T(8,128)(2,1)} %bitcast.19, bf16[2,3,1024,512]{3,2,0,1:T(8,128)(2,1)} %all-gather.5.cloned.1.call-done), kind=kOutput, calls=%fused_computation.10 | convolution fusion | flops 8606711808 | bytes 29360128 | tf_op jit(solution)/shard_map/sejf,edf->sejd/dot_general | solution.py:219
  404.2 7.9 %copy.92 = bf16[8,2,256,1024]{3,2,1,0:T(8,128)(2,1)} copy(bf16[8,2,256,1024]{3,2,0,1:T(8,128)(2,1)} %convert_bitcast_fusion) | data formatting | bytes 16777216 | tf_op jit(solution)/shard_map/convert_element_type | solution.py:221
  412.1 25.1 %all-to-all-done.7 = bf16[16,16,4,16,128]{4,3,2,1,0:T(8,128)(2,1)} async-done(((bf16[16,16,4,16,128]{4,3,2,1,0:T(8,128)(2,1)}), bf16[16,16,4,16,128]{4,3,2,1,0:T(8,128)(2,1)}, u32[]{:S(2)}, u32[]{:S(2)}) %all-to-all-start.7) | async-done | bytes 4194336 | tf_op jit(solution)/shard_map/all_to_all | solution.py:163
  437.2 5.4 all-to-all-start.5
  443.9 7.3 %reshape.142 = bf16[256,8192]{1,0:T(8,128)(2,1)} reshape(bf16[16,16,4,16,128]{4,3,2,1,0:T(8,128)(2,1)} %all-to-all-done.7) | data formatting | bytes 8388608 | tf_op jit(solution)/shard_map/reshape | solution.py:173
  457.9 77.6 %all-to-all-done.5 = bf16[8,512,1024]{2,1,0:T(8,128)(2,1)} async-done(((bf16[8,512,1024]{2,1,0:T(8,128)(2,1)}), bf16[8,512,1024]{2,1,0:T(8,128)(2,1)}, u32[]{:S(2)}, u32[]{:S(2)}) %all-to-all-start.5) | async-done | bytes 8388640 | tf_op jit(solution)/shard_map/all_to_all | solution.py:222
  535.5 5.7 %fusion.26 = f32[256,1024]{1,0:T(8,128)S(1)} fusion(bf16[16,256,1024]{2,1,0:T(8,128)(2,1)} %bitcast.34, f32[16,256]{1,0:T(8,128)S(1)} %broadcast_in_dim.73, s32[16,256]{1,0:T(8,128)S(1)} %eq.64), kind=kOutput, calls=%fused_computation.35 | convolution fusion | flops 2153775104 | bytes 9469952 | tf_op jit(solution)/shard_map/ect,ecd->td/dot_general | solution.py:231
  541.2 6.8 %fusion.32 = bf16[256,1024]{1,0:T(8,128)(2,1)} fusion(f32[256,1024]{1,0:T(8,128)S(1)} %get-tuple-element.9, f32[256,1024]{1,0:T(8,128)S(1)} %fusion.26, bf16[16,256,1024]{2,1,0:T(8,128)(2,1)} %bitcast.34, f32[16,256]{1,0:T(8,128)S(1)} %broadcast_in_dim.73, s32[16,256]{1,0:T(8,128)S(1)} %eq.64), kind=kOutput, calls=%fused_computation.40 | convolution fusion | flops 2150367232 | bytes 11042816 | tf_op jit(solution)/shard_map/ect,ecd->td/dot_general | solution.py:229
  (71 shorter events, 51.8 us)
Async XLA Ops:
  7.2 193.2 %copy-start = (bf16[1024,1024]{1,0:T(8,128)(2,1)S(1)}, bf16[1024,1024]{1,0:T(8,128)(2,1)}, u32[]{:S(2)}) copy-start(bf16[1024,1024]{1,0:T(8,128)(2,1)} %param.18) | copy-start | bytes 6291460
  9.5 11.7 %all-to-all-start = ((bf16[2,128,8,128]{1,3,0,2:T(8,128)(2,1)}), bf16[2,128,8,128]{1,3,0,2:T(8,128)(2,1)S(1)}, u32[]{:S(2)}, u32[]{:S(2)}) async-start(bf16[2,128,8,128]{1,3,0,2:T(8,128)(2,1)} %copy.74), calls=%async_computation | async-start | bytes 1048576 | tf_op jit(solution)/shard_map/all_to_all | solution.py:145
  21.2 10.9 %all-to-all-start.2 = ((bf16[2,128,8,128]{3,1,0,2:T(8,128)(2,1)}), bf16[2,128,8,128]{3,1,0,2:T(8,128)(2,1)S(1)}, u32[]{:S(2)}, u32[]{:S(2)}) async-start(bf16[2,128,8,128]{3,1,0,2:T(8,128)(2,1)} %copy.79), calls=%async_computation.2 | async-start | bytes 1048576 | tf_op jit(solution)/shard_map/all_to_all | solution.py:144
  29.7 8.0 %copy-start.2 = (s32[256,8]{0,1:T(8,128)S(1)}, s32[256,8]{0,1:T(8,128)}, u32[]{:S(2)}) copy-start(s32[256,8]{0,1:T(8,128)} %param.20) | copy-start | bytes 24580
  29.7 9.0 %copy-start.7 = (s32[32]{0:T(128)S(1)}, s32[32]{0:T(128)}, u32[]{:S(2)}) copy-start(s32[32]{0:T(128)} %param.16) | copy-start | bytes 388
  29.7 9.0 %copy-start.5 = (s32[2,128]{1,0:T(2,128)S(1)}, s32[2,128]{1,0:T(2,128)}, u32[]{:S(2)}) copy-start(s32[2,128]{1,0:T(2,128)} %param.23) | copy-start | bytes 3076
  29.7 12.2 %copy-start.8 = (s32[32]{0:T(128)S(1)}, s32[32]{0:T(128)}, u32[]{:S(2)}) copy-start(s32[32]{0:T(128)} %param.17) | copy-start | bytes 388
  32.1 51.5 %all-to-all-start.1 = ((bf16[2,1024,8,128]{3,1,0,2:T(8,128)(2,1)}), bf16[2,1024,8,128]{3,1,0,2:T(8,128)(2,1)}, u32[]{:S(2)}, u32[]{:S(2)}) async-start(bf16[2,1024,8,128]{3,1,0,2:T(8,128)(2,1)} %copy.77), calls=%async_computation.1 | async-start | bytes 8388608 | tf_op jit(solution)/shard_map/all_to_all | solution.py:143
  135.8 10.1 %all-to-all-start.3 = ((bf16[2,256,4,128]{3,2,0,1:T(4,128)(2,1)}), bf16[2,256,4,128]{3,2,0,1:T(4,128)(2,1)S(1)}, u32[]{:S(2)}, u32[]{:S(2)}) async-start(bf16[2,256,4,128]{3,2,0,1:T(4,128)(2,1)} %copy.81), calls=%async_computation.3 | async-start | bytes 1048576 | tf_op jit(solution)/shard_map/all_to_all | solution.py:148
  139.4 63.0 %copy-start.4 = (f32[1024]{0:T(1024)S(1)}, f32[1024]{0:T(1024)}, u32[]{:S(2)}) copy-start(f32[1024]{0:T(1024)} %param.19) | copy-start | bytes 12292
  145.9 61.7 %all-to-all-start.6 = ((s32[16,1,16]{2,1,0:T(1,128)}), s32[16,1,16]{2,1,0:T(1,128)S(1)}, u32[]{:S(2)}, u32[]{:S(2)}) async-start(s32[16,1,16]{2,1,0:T(1,128)} %all_to_all.75), calls=%async_computation.6 | async-start | bytes 16384 | tf_op jit(solution)/shard_map/all_to_all | solution.py:164
  207.6 131.8 %all-to-all-start.4 = ((bf16[8,512,1024]{2,1,0:T(8,128)(2,1)}), bf16[8,512,1024]{2,1,0:T(8,128)(2,1)}, u32[]{:S(2)}, u32[]{:S(2)}) async-start(bf16[8,512,1024]{2,1,0:T(8,128)(2,1)} %bitcast.143), calls=%async_computation.4 | async-start | bytes 16777216 | tf_op jit(solution)/shard_map/all_to_all | solution.py:208
  212.6 80.4 %copy-start.6 = (s32[2]{0:T(128)S(1)}, s32[2]{0:T(128)}, u32[]{:S(2)}) copy-start(s32[2]{0:T(128)} %fusion.39.len_ref) | copy-start | bytes 28
  212.6 80.4 %all-gather.3.cloned.1.call-start = ((), (), s32[]{:S(2)}) async-start(), calls=%async_computation.8 | async-start | bytes 4718592 | tf_op jit(solution)/shard_map/all_gather | solution.py:205
  213.3 162.8 %all-gather.5.cloned.1.call-start = ((), (), s32[]{:S(2)}) async-start(), calls=%async_computation.9 | async-start | bytes 9437184 | tf_op jit(solution)/shard_map/all_gather | solution.py:206
  339.4 97.8 %all-to-all-start.7 = ((bf16[16,16,4,16,128]{4,3,2,1,0:T(8,128)(2,1)}), bf16[16,16,4,16,128]{4,3,2,1,0:T(8,128)(2,1)}, u32[]{:S(2)}, u32[]{:S(2)}) async-start(bf16[16,16,4,16,128]{4,3,2,1,0:T(8,128)(2,1)} %bitcast.145), calls=%async_computation.7 | async-start | bytes 8388608 | tf_op jit(solution)/shard_map/all_to_all | solution.py:163
  437.2 5.4 copy-start.3
  437.2 98.3 %all-to-all-start.5 = ((bf16[8,512,1024]{2,1,0:T(8,128)(2,1)}), bf16[8,512,1024]{2,1,0:T(8,128)(2,1)}, u32[]{:S(2)}, u32[]{:S(2)}) async-start(bf16[8,512,1024]{2,1,0:T(8,128)(2,1)} %bitcast.144), calls=%async_computation.5 | async-start | bytes 16777216 | tf_op jit(solution)/shard_map/all_to_all | solution.py:222
  541.2 6.8 %copy-start.1 = (bf16[1024,1024]{1,0:T(8,128)(2,1)S(1)}, bf16[1024,1024]{1,0:T(8,128)(2,1)}, u32[]{:S(2)}) copy-start(bf16[1024,1024]{1,0:T(8,128)(2,1)} %param.18) | copy-start | bytes 6291460
Sparse Core Ops, SparseCore 0:
  215.0 77.9 all-gather.2
  294.5 81.5 all-gather.4

commit v3 on v2

--- a/solution.py
+++ b/solution.py
@@ -144,10 +144,7 @@
         lax.all_to_all(span_kv, "kv", split_axis=2, concat_axis=1, tiled=True),
         lax.all_to_all(queries_grouped, "kv", split_axis=2, concat_axis=1, tiled=True),
     )
-    attn_heads = attend(query_heads, cache_heads, span_heads, lengths)
-    attn = lax.all_to_all(attn_heads, "kv", split_axis=1, concat_axis=2, tiled=True).reshape(
-        row_count, kv_heads * group_width
-    )
+    full_weights = lax.all_gather(w_experts, ("zhi", "kv"), axis=0, tiled=False)
     page_total = block_map.shape[1]
     visible = jnp.arange(cache_heads.shape[1])[None, :] < lengths[:, None]
     visible_cache = jnp.where(visible[:, :, None, None], cache_heads, jnp.zeros((), jnp.bfloat16))
@@ -164,6 +161,13 @@
         lax.all_to_all(
             local_slot.reshape(req_count, per_owner), REQ, split_axis=0, concat_axis=0, tiled=True
         ),
+    )
+    attn_heads = attend(query_heads, cache_heads, span_heads, lengths)
+    attn_heads, full_weights, arrived, where_to = lax.optimization_barrier(
+        (attn_heads, full_weights, arrived, where_to)
+    )
+    attn = lax.all_to_all(attn_heads, "kv", split_axis=1, concat_axis=2, tiled=True).reshape(
+        row_count, kv_heads * group_width
     )
     placement = (
         where_to.reshape(1, -1) == jnp.arange(slots_dev, dtype=jnp.int32)[:, None]
@@ -202,22 +206,21 @@
     buffer = jnp.einsum(
         "ect,td->ecd", selector.astype(jnp.bfloat16), normed, preferred_element_type=jnp.float32
     ).astype(jnp.bfloat16)
-    pair_weights = lax.all_gather(w_experts, "zhi", axis=0, tiled=True)
-    full_weights = lax.all_gather(pair_weights, "kv", axis=3, tiled=True)
     per_dev = halves * exp_dev
     slot_block = lax.all_to_all(
         buffer.reshape(side, per_dev * capacity, width_model), "rlow", split_axis=0, concat_axis=0, tiled=True
     )
-    grouped = slot_block.reshape(side, per_dev, capacity, width_model)
+    grouped = slot_block.reshape(side, halves, exp_dev, capacity, width_model)
+    weights = full_weights.reshape(halves, kv_count, *w_experts.shape)
     gate_act = jnp.einsum(
-        "sejd,edf->sejf", grouped, full_weights[:, 0], preferred_element_type=jnp.float32
+        "szjcd,zkjdf->szjckf", grouped, weights[:, :, :, 0], preferred_element_type=jnp.float32
     )
     up_act = jnp.einsum(
-        "sejd,edf->sejf", grouped, full_weights[:, 1], preferred_element_type=jnp.float32
+        "szjcd,zkjdf->szjckf", grouped, weights[:, :, :, 1], preferred_element_type=jnp.float32
     )
     activated = (jax.nn.silu(gate_act) * up_act).astype(jnp.bfloat16)
     expert_out = jnp.einsum(
-        "sejf,edf->sejd", activated, full_weights[:, 2], preferred_element_type=jnp.float32
+        "szjckf,zkjdf->szjcd", activated, weights[:, :, :, 2], preferred_element_type=jnp.float32
     ).astype(jnp.bfloat16)
     returned = lax.all_to_all(
         expert_out.reshape(side, per_dev * capacity, width_model), "rlow", split_axis=0, concat_axis=0, tiled=True

time: 558 us -> 522 us (0.935)
  Pallas kernels: 35.5 us -> 85.1 us
  waiting for transfers between devices: 300 us -> 253 us
  starting transfers between devices: 84.4 us -> 39.2 us
  local copies, waits for them, and re-layouts: 59.5 us -> 66.4 us
    all_gather x2 -> x1, waiting for transfers between devices: 111 us -> 0.02 us  [body(): full_weights = lax.all_gather(w_experts, ('zhi', 'kv'), axis=0, tiled=False)]
    pallas_call x1, Pallas kernels: 35.5 us -> 85.1 us  [attend(): pl.pallas_call(functools.partial(attend_kernel, tk=tk, head_dim=head_dim)...]
    all_to_all x1, waiting for transfers between devices: 36.9 us -> 84.5 us  [body(): lax.all_to_all(buffer.reshape(side, per_dev * capacity, width_model), 'rl...]
    all_to_all x1, starting transfers between devices: 52.8 us -> 6.16 us  [body(): lax.all_to_all(local_slot.reshape(req_count, per_owner), REQ, split_axis=...]
    all_to_all x1, waiting for transfers between devices: 36.3 us -> 71.2 us  [body(): lax.all_to_all(cache, 'kv', split_axis=2, concat_axis=1, tiled=True)]
    all_to_all x1, waiting for transfers between devices: 25.1 us -> 2.03 us  [body(): lax.all_to_all(outgoing, REQ, split_axis=0, concat_axis=0, tiled=True)]
    optimization_barrier x0 -> x2, local copies, waits for them, and re-layouts: none -> 9.59 us  [body(): lax.optimization_barrier((attn_heads, full_weights, arrived, where_to))]
  transfers between devices with their start and end apart: 10 -> 9, of which waited for: 9 -> 7; matrix products, arithmetic and copies ran while one was open for 16% -> 12% of each run, Pallas kernels for 0% -> 16%
where the time goes in v3:
time: 522 us; the launch traced here: 519 us
  waiting for transfers between devices  253 us (48%)
  Pallas kernels  85.1 us (16%)
  local copies, waits for them, and re-layouts  66.4 us (13%)
  matrix products  51.6 us (10%)
  starting transfers between devices  39.2 us (8%)
  between operations  14.3 us (3%)
  other arithmetic  9.17 us (2%)
    pallas_call x1, Pallas kernels, attend(): pl.pallas_call(functools.partial(attend_kernel, tk=tk, head_dim=head_dim)...  85.1 us
    all_to_all x1, waiting for transfers between devices, body(): lax.all_to_all(buffer.reshape(side, per_dev * capacity, width_model), 'rl...  84.5 us
    all_to_all x1, waiting for transfers between devices, body(): lax.all_to_all(expert_out.reshape(side, per_dev * capacity, width_model),...  78.8 us
    all_to_all x1, waiting for transfers between devices, body(): lax.all_to_all(cache, 'kv', split_axis=2, concat_axis=1, tiled=True)  71.2 us
    dot_general x1, matrix products, body(): jnp.einsum('szjckf,zkjdf->szjcd', activated, weights[:, :, :, 2], preferr...  16.6 us
    dot_general x1, matrix products, body(): jnp.einsum('szjcd,zkjdf->szjckf', grouped, weights[:, :, :, 1], preferred...  11.8 us
    unnamed x22, local copies, waits for them, and re-layouts  10.5 us
  transfers between devices with their start and end apart: 9, of which 7 were waited for; matrix products, arithmetic and copies ran while one was open for 12% of the time, Pallas kernels for 16%

profile of v3, /device:TPU:16, one launch (start us, length us, event | category | flops | bytes accessed | tf_op | source)
XLA Modules:
  0.0 519.1 jit_solution(6910156217124934860)
XLA Ops:
  13.8 6.2 %all-to-all-start.4 = ((s32[16,1,16]{2,1,0:T(1,128)}), s32[16,1,16]{2,1,0:T(1,128)S(1)}, u32[]{:S(2)}, u32[]{:S(2)}) async-start(s32[16,1,16]{2,1,0:T(1,128)} %all_to_all.74), calls=%async_computation.4 | async-start | bytes 16384 | tf_op jit(solution)/shard_map/all_to_all | solution.py:161
  20.0 5.0 copy.86
  25.0 5.7 %all-to-all-start.1 = ((bf16[2,1024,8,128]{3,1,0,2:T(8,128)(2,1)}), bf16[2,1024,8,128]{3,1,0,2:T(8,128)(2,1)}, u32[]{:S(2)}, u32[]{:S(2)}) async-start(bf16[2,1024,8,128]{3,1,0,2:T(8,128)(2,1)} %copy.86), calls=%async_computation.1 | async-start | bytes 8388608 | tf_op jit(solution)/shard_map/all_to_all | solution.py:143
  32.7 71.2 %all-to-all-done.1 = bf16[2,1024,8,128]{3,1,0,2:T(8,128)(2,1)} async-done(((bf16[2,1024,8,128]{3,1,0,2:T(8,128)(2,1)}), bf16[2,1024,8,128]{3,1,0,2:T(8,128)(2,1)}, u32[]{:S(2)}, u32[]{:S(2)}) %all-to-all-start.1) | async-done | bytes 4194336 | tf_op jit(solution)/shard_map/all_to_all | solution.py:143
  109.7 7.4 %copy.139 = bf16[2,1024,2,4,128]{4,3,1,2,0:T(4,128)(2,1)} copy(bf16[2,1024,2,4,128]{4,1,0,3,2:T(8,128)(2,1)} %bitcast.5) | data formatting | bytes 8388608 | tf_op jit(solution)/shard_map/all_to_all | solution.py:143
  117.1 4.2 all-to-all-done
  128.9 5.3 %gather_fusion = bf16[256,4,16,128]{3,2,1,0:T(8,128)(2,1)} fusion(bf16[256,4,16,128]{3,2,1,0:T(8,128)(2,1)} %bitcast.179, s32[1024]{0:T(1024)S(1)} %pad_clamp_fusion), kind=kCustom, calls=%fused_computation | custom fusion | bytes 8389632 | tf_op jit(solution)/shard_map/gather | solution.py:114
  134.2 4.2 all-to-all-done.2
  138.4 6.1 %all-to-all-start.3 = ((bf16[16,16,4,16,128]{4,3,2,1,0:T(8,128)(2,1)}), bf16[16,16,4,16,128]{4,3,2,1,0:T(8,128)(2,1)}, u32[]{:S(2)}, u32[]{:S(2)}) async-start(bf16[16,16,4,16,128]{4,3,2,1,0:T(8,128)(2,1)} %bitcast.178), calls=%async_computation.3 | async-start | bytes 8388608 | tf_op jit(solution)/shard_map/all_to_all | solution.py:160
  149.7 7.2 %reshape.151.c_ref = bf16[2,2048,512]{2,1,0:T(8,128)(2,1)} reshape(bf16[2,2,1024,4,128]{4,3,2,1,0:T(4,128)(2,1)} %bitcast.175) | data formatting | bytes 8388608 | tf_op jit(solution)/shard_map/reshape | solution.py:86
  156.9 85.1 %shard_map.131 = bf16[2,256,512]{2,1,0:T(8,128)(2,1)} custom-call(s32[2]{0:T(128)} %copy-done.6, bf16[2,256,512]{2,1,0:T(8,128)(2,1)} %reshape.150.q_ref, bf16[2,2048,512]{2,1,0:T(8,128)(2,1)} %reshape.151.c_ref, bf16[2,256,512]{2,1,0:T(8,128)(2,1)} %reshape.152.s_ref), custom_call_target="tpu_custom_call" | custom-call | flops 7247757312 | bytes 5767168 | tf_op jit(solution)/shard_map/pallas_call | solution.py:89
  250.3 7.8 %all-to-all-done.5 = bf16[2,256,4,128]{3,2,0,1:T(4,128)(2,1)S(1)} async-done(((bf16[2,256,4,128]{3,2,0,1:T(4,128)(2,1)}), bf16[2,256,4,128]{3,2,0,1:T(4,128)(2,1)S(1)}, u32[]{:S(2)}, u32[]{:S(2)}) %all-to-all-start.5) | async-done | bytes 524320 | tf_op jit(solution)/shard_map/all_to_all | solution.py:169
  261.8 5.2 %convolution_convert_fusion.1 = bf16[16,256,1024]{2,1,0:T(8,128)(2,1)} fusion(s32[16,256]{1,0:T(8,128)S(1)} %eq.64, f32[256,1024]{1,0:T(8,128)S(1)} %get-tuple-element.17, f32[1024]{0:T(1024)S(1)} %copy-done.5, f32[256]{0:T(256)S(1)} %add_rsqrt_fusion), kind=kOutput, calls=%fused_computation.16 | convolution fusion | flops 2153512960 | bytes 9458688 | tf_op jit(solution)/shard_map/ect,td->ecd/dot_general | solution.py:206
  267.0 4.9 all-to-all-start.6
  272.0 8.6 %copy.98 = bf16[4,1,3,1024,256]{3,4,0,2,1:T(8,128)(2,1)} copy(bf16[4,1,3,1024,256]{4,3,2,0,1:T(8,128)(2,1)} %bitcast.180) | data formatting | bytes 12582912 | tf_op jit(solution)/shard_map/optimization_barrier | solution.py:166
  280.6 84.5 %all-to-all-done.6 = bf16[8,512,1024]{2,1,0:T(8,128)(2,1)} async-done(((bf16[8,512,1024]{2,1,0:T(8,128)(2,1)}), bf16[8,512,1024]{2,1,0:T(8,128)(2,1)}, u32[]{:S(2)}, u32[]{:S(2)}) %all-to-all-start.6) | async-done | bytes 8388640 | tf_op jit(solution)/shard_map/all_to_all | solution.py:210
  365.1 11.8 %fusion.5 = f32[2,2,256,8,256]{4,2,3,1,0:T(8,128)} fusion(bf16[8,2,256,1024,1]{3,2,1,0,4:T(8,128)(2,1)} %bitcast.33, bf16[2,2,1,3,1024,256]{4,5,1,0,3,2:T(8,128)(2,1)} %bitcast.181), kind=kOutput, calls=%fused_computation.12 | convolution fusion | flops 4294967296 | bytes 18874368 | tf_op jit(solution)/shard_map/szjcd,zkjdf->szjckf/dot_general | solution.py:218
  376.9 16.6 %fusion = bf16[8,2,1,256,1024]{4,3,0,1,2:T(8,128)(2,1)} fusion(f32[2,2,256,8,256]{4,2,3,1,0:T(8,128)} %fusion.5, bf16[2,2,1,3,1024,256]{4,5,1,0,3,2:T(8,128)(2,1)} %bitcast.182, bf16[8,2,256,1024,1]{3,2,1,0,4:T(8,128)(2,1)} %bitcast.33), kind=kOutput, calls=%fused_computation.4 | convolution fusion | flops 8606711808 | bytes 29360128 | tf_op jit(solution)/shard_map/szjckf,zkjdf->szjcd/dot_general | solution.py:222
  393.5 7.9 %copy.104 = bf16[8,2,1,256,1024]{4,3,1,0,2:T(8,128)(2,1)} copy(bf16[8,2,1,256,1024]{4,3,0,1,2:T(8,128)(2,1)} %fusion) | data formatting | bytes 16777216 | tf_op jit(solution)/shard_map/convert_element_type | solution.py:224
  401.4 5.4 %all-to-all-start.7 = ((bf16[8,512,1024]{2,1,0:T(8,128)(2,1)}), bf16[8,512,1024]{2,1,0:T(8,128)(2,1)}, u32[]{:S(2)}, u32[]{:S(2)}) async-start(bf16[8,512,1024]{2,1,0:T(8,128)(2,1)} %bitcast.176), calls=%async_computation.7 | async-start | bytes 16777216 | tf_op jit(solution)/shard_map/all_to_all | solution.py:225
  406.9 7.3 %reshape.172 = bf16[256,8192]{1,0:T(8,128)(2,1)} reshape(bf16[16,16,4,16,128]{4,3,2,1,0:T(8,128)(2,1)} %all-to-all-done.3) | data formatting | bytes 8388608 | tf_op jit(solution)/shard_map/reshape | solution.py:177
  420.9 78.8 %all-to-all-done.7 = bf16[8,512,1024]{2,1,0:T(8,128)(2,1)} async-done(((bf16[8,512,1024]{2,1,0:T(8,128)(2,1)}), bf16[8,512,1024]{2,1,0:T(8,128)(2,1)}, u32[]{:S(2)}, u32[]{:S(2)}) %all-to-all-start.7) | async-done | bytes 8388640 | tf_op jit(solution)/shard_map/all_to_all | solution.py:225
  499.7 5.7 %fusion.27 = f32[256,1024]{1,0:T(8,128)S(1)} fusion(bf16[16,256,1024]{2,1,0:T(8,128)(2,1)} %bitcast.49, f32[16,256]{1,0:T(8,128)S(1)} %broadcast_in_dim.76, s32[16,256]{1,0:T(8,128)S(1)} %eq.64), kind=kOutput, calls=%fused_computation.36 | convolution fusion | flops 2153775104 | bytes 9469952 | tf_op jit(solution)/shard_map/ect,ecd->td/dot_general | solution.py:234
  505.4 6.8 %fusion.33 = bf16[256,1024]{1,0:T(8,128)(2,1)} fusion(f32[256,1024]{1,0:T(8,128)S(1)} %get-tuple-element.17, f32[256,1024]{1,0:T(8,128)S(1)} %fusion.27, bf16[16,256,1024]{2,1,0:T(8,128)(2,1)} %bitcast.49, f32[16,256]{1,0:T(8,128)S(1)} %broadcast_in_dim.76, s32[16,256]{1,0:T(8,128)S(1)} %eq.64), kind=kOutput, calls=%fused_computation.41 | convolution fusion | flops 2150367232 | bytes 11042816 | tf_op jit(solution)/shard_map/ect,ecd->td/dot_general | solution.py:232
  (67 shorter events, 45.8 us)
Async XLA Ops:
  7.2 252.6 %copy-start = (bf16[1024,1024]{1,0:T(8,128)(2,1)S(1)}, bf16[1024,1024]{1,0:T(8,128)(2,1)}, u32[]{:S(2)}) copy-start(bf16[1024,1024]{1,0:T(8,128)(2,1)} %param.18) | copy-start | bytes 6291460
  13.8 11.2 %all-to-all-start.4 = ((s32[16,1,16]{2,1,0:T(1,128)}), s32[16,1,16]{2,1,0:T(1,128)S(1)}, u32[]{:S(2)}, u32[]{:S(2)}) async-start(s32[16,1,16]{2,1,0:T(1,128)} %all_to_all.74), calls=%async_computation.4 | async-start | bytes 16384 | tf_op jit(solution)/shard_map/all_to_all | solution.py:161
  25.0 6.5 %copy-start.2 = (bf16[2,128,1024]{2,1,0:T(8,128)(2,1)S(1)}, bf16[2,128,1024]{2,1,0:T(8,128)(2,1)}, u32[]{:S(2)}) copy-start(bf16[2,128,1024]{2,1,0:T(8,128)(2,1)} %param.13) | copy-start | bytes 1572868
  25.0 7.6 %copy-start.7 = (s32[32]{0:T(128)S(1)}, s32[32]{0:T(128)}, u32[]{:S(2)}) copy-start(s32[32]{0:T(128)} %param.16) | copy-start | bytes 388
  25.0 78.9 %all-to-all-start.1 = ((bf16[2,1024,8,128]{3,1,0,2:T(8,128)(2,1)}), bf16[2,1024,8,128]{3,1,0,2:T(8,128)(2,1)}, u32[]{:S(2)}, u32[]{:S(2)}) async-start(bf16[2,1024,8,128]{3,1,0,2:T(8,128)(2,1)} %copy.86), calls=%async_computation.1 | async-start | bytes 8388608 | tf_op jit(solution)/shard_map/all_to_all | solution.py:143
  30.8 76.7 %copy-start.8 = (s32[32]{0:T(128)S(1)}, s32[32]{0:T(128)}, u32[]{:S(2)}) copy-start(s32[32]{0:T(128)} %param.17) | copy-start | bytes 388
  30.8 212.4 %all-gather.3.cloned.1.call-start = ((), (), s32[]{:S(2)}) async-start(), calls=%async_computation.8 | async-start | bytes 7864320 | tf_op jit(solution)/shard_map/all_gather | solution.py:147
  104.0 17.4 %all-to-all-start = ((bf16[2,128,8,128]{1,3,0,2:T(8,128)(2,1)}), bf16[2,128,8,128]{1,3,0,2:T(8,128)(2,1)S(1)}, u32[]{:S(2)}, u32[]{:S(2)}) async-start(bf16[2,128,8,128]{1,3,0,2:T(8,128)(2,1)} %copy.83), calls=%async_computation | async-start | bytes 1048576 | tf_op jit(solution)/shard_map/all_to_all | solution.py:145
  107.6 9.5 %copy-start.6 = (s32[2]{0:T(128)}, s32[2]{0:T(128)S(1)}, u32[]{:S(2)}) copy-start(s32[2]{0:T(128)S(1)} %fusion.40.len_ref) | copy-start | bytes 28
  121.3 17.1 %all-to-all-start.2 = ((bf16[2,128,8,128]{3,1,0,2:T(8,128)(2,1)}), bf16[2,128,8,128]{3,1,0,2:T(8,128)(2,1)S(1)}, u32[]{:S(2)}, u32[]{:S(2)}) async-start(bf16[2,128,8,128]{3,1,0,2:T(8,128)(2,1)} %copy.88), calls=%async_computation.2 | async-start | bytes 1048576 | tf_op jit(solution)/shard_map/all_to_all | solution.py:144
  138.4 6.1 %copy-start.3 = (s32[256,8]{0,1:T(8,128)S(1)}, s32[256,8]{0,1:T(8,128)}, u32[]{:S(2)}) copy-start(s32[256,8]{0,1:T(8,128)} %param.20) | copy-start | bytes 24580
  138.4 106.7 %all-to-all-start.3 = ((bf16[16,16,4,16,128]{4,3,2,1,0:T(8,128)(2,1)}), bf16[16,16,4,16,128]{4,3,2,1,0:T(8,128)(2,1)}, u32[]{:S(2)}, u32[]{:S(2)}) async-start(bf16[16,16,4,16,128]{4,3,2,1,0:T(8,128)(2,1)} %bitcast.178), calls=%async_computation.3 | async-start | bytes 8388608 | tf_op jit(solution)/shard_map/all_to_all | solution.py:160
  246.2 15.6 %copy-start.5 = (f32[1024]{0:T(1024)S(1)}, f32[1024]{0:T(1024)}, u32[]{:S(2)}) copy-start(f32[1024]{0:T(1024)} %param.19) | copy-start | bytes 12292
  246.2 12.0 %all-to-all-start.5 = ((bf16[2,256,4,128]{3,2,0,1:T(4,128)(2,1)}), bf16[2,256,4,128]{3,2,0,1:T(4,128)(2,1)S(1)}, u32[]{:S(2)}, u32[]{:S(2)}) async-start(bf16[2,256,4,128]{3,2,0,1:T(4,128)(2,1)} %copy.91), calls=%async_computation.5 | async-start | bytes 1048576 | tf_op jit(solution)/shard_map/all_to_all | solution.py:169
  267.0 98.1 %all-to-all-start.6 = ((bf16[8,512,1024]{2,1,0:T(8,128)(2,1)}), bf16[8,512,1024]{2,1,0:T(8,128)(2,1)}, u32[]{:S(2)}, u32[]{:S(2)}) async-start(bf16[8,512,1024]{2,1,0:T(8,128)(2,1)} %bitcast.177), calls=%async_computation.6 | async-start | bytes 16777216 | tf_op jit(solution)/shard_map/all_to_all | solution.py:210
  401.4 5.4 %copy-start.4 = (f32[256,8]{0,1:T(8,128)S(1)}, f32[256,8]{0,1:T(8,128)}, u32[]{:S(2)}) copy-start(f32[256,8]{0,1:T(8,128)} %param.21) | copy-start | bytes 24580
  401.4 98.3 %all-to-all-start.7 = ((bf16[8,512,1024]{2,1,0:T(8,128)(2,1)}), bf16[8,512,1024]{2,1,0:T(8,128)(2,1)}, u32[]{:S(2)}, u32[]{:S(2)}) async-start(bf16[8,512,1024]{2,1,0:T(8,128)(2,1)} %bitcast.176), calls=%async_computation.7 | async-start | bytes 16777216 | tf_op jit(solution)/shard_map/all_to_all | solution.py:225
  505.4 6.8 %copy-start.1 = (bf16[1024,1024]{1,0:T(8,128)(2,1)S(1)}, bf16[1024,1024]{1,0:T(8,128)(2,1)}, u32[]{:S(2)}) copy-start(bf16[1024,1024]{1,0:T(8,128)(2,1)} %param.18) | copy-start | bytes 6291460
Sparse Core Ops, SparseCore 0:
  33.5 172.9 all-gather.2

commit v4 on v3

--- a/solution.py
+++ b/solution.py
@@ -29,46 +29,56 @@
     per_group = lanes // head_dim
     scale = 1.0 / math.sqrt(head_dim)
     lane = lax.broadcasted_iota(jnp.int32, (span, lanes), 1)
-    q_all = q_ref[0].astype(jnp.float32)
-    nblk = (length + tk - 1) // tk
+    q_all = q_ref[0].astype(jnp.float32) * scale
+    blocks = c_ref.shape[1] // tk
+    full = length // tk
+    tail = jnp.minimum(full, blocks - 1)
     row = lax.broadcasted_iota(jnp.int32, (span, span), 0)
     col = lax.broadcasted_iota(jnp.int32, (span, span), 1)
     causal = col <= row
+    key_lane = lax.broadcasted_iota(jnp.int32, (tk, lanes), 1) < head_dim
+    span_lane = lax.broadcasted_iota(jnp.int32, (span, lanes), 1) < head_dim
     span_keys = s_ref[0]
+    span_vals = jnp.where(span_lane, jnp.ones_like(span_keys), span_keys)
     dims = (((1,), (1,)), ((), ()))
+    tail_pos = tail * tk + lax.broadcasted_iota(jnp.int32, (span, tk), 1)
+    tail_ok = (tail_pos >= full * tk) & (tail_pos < length)
     outs = []
     for j in range(per_group):
         shifted = q_all if j == 0 else pltpu.roll(q_all, lanes - j * head_dim, 1)
         qj = jnp.where(lane < head_dim, shifted, 0.0).astype(jnp.bfloat16)
 
-        def block_scores(kb):
+        def block(kb):
             start = pl.multiple_of(kb * tk, tk)
             keys = c_ref[0, pl.ds(start, tk), :]
-            s = lax.dot_general(qj, keys, dims, preferred_element_type=jnp.float32) * scale
-            pos = start + lax.broadcasted_iota(jnp.int32, (span, tk), 1)
-            return keys, pos < length, s
+            s = lax.dot_general(qj, keys, dims, preferred_element_type=jnp.float32)
+            return keys, s
 
         def max_body(kb, m):
-            _, ok, s = block_scores(kb)
-            return jnp.maximum(m, jnp.max(jnp.where(ok, s, -1e30), axis=1, keepdims=True))
-
-        s_span = lax.dot_general(qj, span_keys, dims, preferred_element_type=jnp.float32) * scale
-        m0 = jnp.max(jnp.where(causal, s_span, -1e30), axis=1, keepdims=True)
-        m = lax.fori_loop(0, nblk, max_body, m0)
-
-        def sum_body(kb, carry):
-            l, acc = carry
-            keys, ok, s = block_scores(kb)
-            p = jnp.where(ok, jnp.exp(s - m), 0.0)
-            l = l + jnp.sum(p, axis=1, keepdims=True)
-            acc = acc + jnp.dot(p.astype(jnp.bfloat16), keys, preferred_element_type=jnp.float32)
-            return l, acc
+            _, s = block(kb)
+            return jnp.maximum(m, jnp.max(s, axis=1, keepdims=True))
+
+        s_span = lax.dot_general(qj, span_keys, dims, preferred_element_type=jnp.float32)
+        m = jnp.max(jnp.where(causal, s_span, -1e30), axis=1, keepdims=True)
+        m = lax.fori_loop(0, full, max_body, m)
+        _, s_tail = block(tail)
+        m = jnp.maximum(m, jnp.max(jnp.where(tail_ok, s_tail, -1e30), axis=1, keepdims=True))
+
+        def accumulate(acc, p, keys):
+            vals = jnp.where(key_lane, jnp.ones_like(keys), keys)
+            return acc + jnp.dot(p.astype(jnp.bfloat16), vals, preferred_element_type=jnp.float32)
+
+        def sum_body(kb, acc):
+            keys, s = block(kb)
+            return accumulate(acc, jnp.exp(s - m), keys)
 
         p_span = jnp.where(causal, jnp.exp(s_span - m), 0.0)
-        l0 = jnp.sum(p_span, axis=1, keepdims=True)
-        acc0 = jnp.dot(p_span.astype(jnp.bfloat16), span_keys, preferred_element_type=jnp.float32)
-        l, acc = lax.fori_loop(0, nblk, sum_body, (l0, acc0))
-        res = acc / l
+        acc = jnp.dot(p_span.astype(jnp.bfloat16), span_vals, preferred_element_type=jnp.float32)
+        acc = lax.fori_loop(0, full, sum_body, acc)
+        keys_tail, s_tail = block(tail)
+        acc = accumulate(acc, jnp.where(tail_ok, jnp.exp(s_tail - m), 0.0), keys_tail)
+        total = acc[:, 0:1]
+        res = acc / total
         shift = (j * head_dim - head_dim) % lanes
         outs.append(res if shift == 0 else pltpu.roll(res, shift, 1))
     out = outs[0]
@@ -144,7 +154,8 @@
         lax.all_to_all(span_kv, "kv", split_axis=2, concat_axis=1, tiled=True),
         lax.all_to_all(queries_grouped, "kv", split_axis=2, concat_axis=1, tiled=True),
     )
-    full_weights = lax.all_gather(w_experts, ("zhi", "kv"), axis=0, tiled=False)
+    expert_part, cache_heads = lax.optimization_barrier((w_experts, cache_heads))
+    full_weights = lax.all_gather(expert_part, ("zhi", "kv"), axis=0, tiled=False)
     page_total = block_map.shape[1]
     visible = jnp.arange(cache_heads.shape[1])[None, :] < lengths[:, None]
     visible_cache = jnp.where(visible[:, :, None, None], cache_heads, jnp.zeros((), jnp.bfloat16))

time: 522 us -> 560 us (1.073)
  waiting for transfers between devices: 253 us -> 289 us
  other arithmetic: 9.17 us -> 16.7 us
  Pallas kernels: 85.1 us -> 77.6 us
    all_to_all x1, waiting for transfers between devices: 2.03 us -> 49.6 us  [body(): lax.all_to_all(outgoing, REQ, split_axis=0, concat_axis=0, tiled=True)]
    all_to_all x1, waiting for transfers between devices: 71.2 us -> 44.4 us  [body(): lax.all_to_all(cache, 'kv', split_axis=2, concat_axis=1, tiled=True)]
    all_to_all x1, waiting for transfers between devices: 0.01 us -> 16.6 us  [body(): lax.all_to_all(local_slot.reshape(req_count, per_owner), REQ, split_axis=...]
    select_n x1, other arithmetic: 4.12 us -> 12.5 us  [body(): jnp.where(visible[:, :, None, None], cache_heads, jnp.zeros((), jnp.bfloa...]
    pallas_call x1, Pallas kernels: 85.1 us -> 77.6 us  [attend(): pl.pallas_call(functools.partial(attend_kernel, tk=tk, head_dim=head_dim)...]
  transfers between devices with their start and end apart: 9 -> 9, of which waited for: 7 -> 7; matrix products, arithmetic and copies ran while one was open for 12% -> 12% of each run, Pallas kernels for 16% -> 14%
where the time goes in v4:
time: 560 us; the launch traced here: 558 us
  waiting for transfers between devices  289 us (52%)
  Pallas kernels  77.6 us (14%)
  local copies, waits for them, and re-layouts  69.8 us (12%)
  matrix products  51.6 us (9%)
  starting transfers between devices  38.8 us (7%)
  other arithmetic  16.7 us (3%)
  between operations  14.3 us (3%)
    all_to_all x1, waiting for transfers between devices, body(): lax.all_to_all(buffer.reshape(side, per_dev * capacity, width_model), 'rl...  84.5 us
    all_to_all x1, waiting for transfers between devices, body(): lax.all_to_all(expert_out.reshape(side, per_dev * capacity, width_model),...  78.8 us
    pallas_call x1, Pallas kernels, attend(): pl.pallas_call(functools.partial(attend_kernel, tk=tk, head_dim=head_dim)...  77.6 us
    all_to_all x1, waiting for transfers between devices, body(): lax.all_to_all(outgoing, REQ, split_axis=0, concat_axis=0, tiled=True)  49.6 us
    all_to_all x1, waiting for transfers between devices, body(): lax.all_to_all(cache, 'kv', split_axis=2, concat_axis=1, tiled=True)  44.4 us
    dot_general x1, matrix products, body(): jnp.einsum('szjckf,zkjdf->szjcd', activated, weights[:, :, :, 2], preferr...  16.6 us
    all_to_all x1, waiting for transfers between devices, body(): lax.all_to_all(local_slot.reshape(req_count, per_owner), REQ, split_axis=...  16.6 us
    select_n x1, other arithmetic, body(): jnp.where(visible[:, :, None, None], cache_heads, jnp.zeros((), jnp.bfloa...  12.5 us
  transfers between devices with their start and end apart: 9, of which 7 were waited for; matrix products, arithmetic and copies ran while one was open for 12% of the time, Pallas kernels for 14%

profile of v4, /device:TPU:16, one launch (start us, length us, event | category | flops | bytes accessed | tf_op | source)
XLA Modules:
  0.0 558.1 jit_solution(16287888322465720955)
XLA Ops:
  12.3 5.7 %all-to-all-start.1 = ((bf16[2,1024,8,128]{3,1,0,2:T(8,128)(2,1)}), bf16[2,1024,8,128]{3,1,0,2:T(8,128)(2,1)}, u32[]{:S(2)}, u32[]{:S(2)}) async-start(bf16[2,1024,8,128]{3,1,0,2:T(8,128)(2,1)} %copy.86), calls=%async_computation.1 | async-start | bytes 8388608 | tf_op jit(solution)/shard_map/all_to_all | solution.py:153
  21.3 44.4 %all-to-all-done.1 = bf16[2,1024,8,128]{3,1,0,2:T(8,128)(2,1)} async-done(((bf16[2,1024,8,128]{3,1,0,2:T(8,128)(2,1)}), bf16[2,1024,8,128]{3,1,0,2:T(8,128)(2,1)}, u32[]{:S(2)}, u32[]{:S(2)}) %all-to-all-start.1) | async-done | bytes 4194336 | tf_op jit(solution)/shard_map/all_to_all | solution.py:153
  65.8 7.5 %copy.87 = bf16[2,2,1024,4,128]{4,3,2,1,0:T(4,128)(2,1)} copy(bf16[2,2,1024,4,128]{4,2,0,3,1:T(8,128)(2,1)} %bitcast.6) | data formatting | bytes 8388608 | tf_op jit(solution)/shard_map/all_to_all | solution.py:153
  75.9 6.2 %all-to-all-start.4 = ((s32[16,1,16]{2,1,0:T(1,128)}), s32[16,1,16]{2,1,0:T(1,128)S(1)}, u32[]{:S(2)}, u32[]{:S(2)}) async-start(s32[16,1,16]{2,1,0:T(1,128)} %all_to_all.74), calls=%async_computation.4 | async-start | bytes 16384 | tf_op jit(solution)/shard_map/all_to_all | solution.py:172
  85.5 16.6 %all-to-all-done.4 = s32[16,1,16]{2,1,0:T(1,128)S(1)} async-done(((s32[16,1,16]{2,1,0:T(1,128)}), s32[16,1,16]{2,1,0:T(1,128)S(1)}, u32[]{:S(2)}, u32[]{:S(2)}) %all-to-all-start.4) | async-done | bytes 1056 | tf_op jit(solution)/shard_map/all_to_all | solution.py:172
  105.7 7.3 %all-to-all-done = bf16[2,128,8,128]{1,3,0,2:T(8,128)(2,1)S(1)} async-done(((bf16[2,128,8,128]{1,3,0,2:T(8,128)(2,1)}), bf16[2,128,8,128]{1,3,0,2:T(8,128)(2,1)S(1)}, u32[]{:S(2)}, u32[]{:S(2)}) %all-to-all-start) | async-done | bytes 524320 | tf_op jit(solution)/shard_map/all_to_all | solution.py:155
  116.5 12.5 %broadcast_select_fusion = bf16[2,2048,4,128]{3,2,1,0:T(4,128)(2,1)S(1)} fusion(bf16[2,2048,4,128]{3,2,1,0:T(4,128)(2,1)} %bitcast.174, pred[2,2048]{1,0:T(4,128)(4,1)S(1)} %iota_compare_fusion.5), kind=kLoop, calls=%fused_computation.22 | loop fusion | flops 2097152 | bytes 8392704 | tf_op jit(solution)/shard_map/jit(_where)/select_n | solution.py:161
  132.1 5.3 gather_fusion
  137.4 5.8 %all-to-all-start.3 = ((bf16[16,16,4,16,128]{4,3,2,1,0:T(8,128)(2,1)}), bf16[16,16,4,16,128]{4,3,2,1,0:T(8,128)(2,1)}, u32[]{:S(2)}, u32[]{:S(2)}) async-start(bf16[16,16,4,16,128]{4,3,2,1,0:T(8,128)(2,1)} %bitcast.179), calls=%async_computation.3 | async-start | bytes 8388608 | tf_op jit(solution)/shard_map/all_to_all | solution.py:171
  148.3 7.2 %reshape.149.c_ref = bf16[2,2048,512]{2,1,0:T(8,128)(2,1)} reshape(bf16[2,2048,4,128]{3,2,1,0:T(4,128)(2,1)} %bitcast.175) | data formatting | bytes 8388608 | tf_op jit(solution)/shard_map/reshape | solution.py:96
  155.4 77.6 %shard_map.131 = bf16[2,256,512]{2,1,0:T(8,128)(2,1)} custom-call(s32[2]{0:T(128)} %copy-done.7, bf16[2,256,512]{2,1,0:T(8,128)(2,1)} %reshape.148.q_ref, bf16[2,2048,512]{2,1,0:T(8,128)(2,1)} %reshape.149.c_ref, bf16[2,256,512]{2,1,0:T(8,128)(2,1)} %reshape.150.s_ref), custom_call_target="tpu_custom_call" | custom-call | flops 7247757312 | bytes 5767168 | tf_op jit(solution)/shard_map/pallas_call | solution.py:99
  234.2 49.6 %all-to-all-done.3 = bf16[16,16,4,16,128]{4,3,2,1,0:T(8,128)(2,1)} async-done(((bf16[16,16,4,16,128]{4,3,2,1,0:T(8,128)(2,1)}), bf16[16,16,4,16,128]{4,3,2,1,0:T(8,128)(2,1)}, u32[]{:S(2)}, u32[]{:S(2)}) %all-to-all-start.3) | async-done | bytes 4194336 | tf_op jit(solution)/shard_map/all_to_all | solution.py:171
  288.9 8.1 %all-to-all-done.5 = bf16[2,256,4,128]{3,2,0,1:T(4,128)(2,1)S(1)} async-done(((bf16[2,256,4,128]{3,2,0,1:T(4,128)(2,1)}), bf16[2,256,4,128]{3,2,0,1:T(4,128)(2,1)S(1)}, u32[]{:S(2)}, u32[]{:S(2)}) %all-to-all-start.5) | async-done | bytes 524320 | tf_op jit(solution)/shard_map/all_to_all | solution.py:180
  300.7 5.2 convolution_convert_fusion.1
  310.9 8.6 %copy.98 = bf16[4,1,3,1024,256]{3,4,0,2,1:T(8,128)(2,1)} copy(bf16[4,1,3,1024,256]{4,3,2,0,1:T(8,128)(2,1)} %bitcast.181) | data formatting | bytes 12582912 | tf_op jit(solution)/shard_map/optimization_barrier | solution.py:177
  319.6 84.5 %all-to-all-done.6 = bf16[8,512,1024]{2,1,0:T(8,128)(2,1)} async-done(((bf16[8,512,1024]{2,1,0:T(8,128)(2,1)}), bf16[8,512,1024]{2,1,0:T(8,128)(2,1)}, u32[]{:S(2)}, u32[]{:S(2)}) %all-to-all-start.6) | async-done | bytes 8388640 | tf_op jit(solution)/shard_map/all_to_all | solution.py:221
  404.0 11.8 %fusion.5 = f32[2,2,256,8,256]{4,2,3,1,0:T(8,128)} fusion(bf16[8,2,256,1024,1]{3,2,1,0,4:T(8,128)(2,1)} %bitcast.34, bf16[2,2,1,3,1024,256]{4,5,1,0,3,2:T(8,128)(2,1)} %bitcast.182), kind=kOutput, calls=%fused_computation.12 | convolution fusion | flops 4294967296 | bytes 18874368 | tf_op jit(solution)/shard_map/szjcd,zkjdf->szjckf/dot_general | solution.py:229
  415.8 16.6 %fusion = bf16[8,2,1,256,1024]{4,3,0,1,2:T(8,128)(2,1)} fusion(f32[2,2,256,8,256]{4,2,3,1,0:T(8,128)} %fusion.5, bf16[2,2,1,3,1024,256]{4,5,1,0,3,2:T(8,128)(2,1)} %bitcast.183, bf16[8,2,256,1024,1]{3,2,1,0,4:T(8,128)(2,1)} %bitcast.34), kind=kOutput, calls=%fused_computation.4 | convolution fusion | flops 8606711808 | bytes 29360128 | tf_op jit(solution)/shard_map/szjckf,zkjdf->szjcd/dot_general | solution.py:233
  432.4 8.0 %copy.104 = bf16[8,2,1,256,1024]{4,3,1,0,2:T(8,128)(2,1)} copy(bf16[8,2,1,256,1024]{4,3,0,1,2:T(8,128)(2,1)} %fusion) | data formatting | bytes 16777216 | tf_op jit(solution)/shard_map/convert_element_type | solution.py:235
  440.4 5.4 all-to-all-start.7
  445.9 7.3 %reshape.171 = bf16[256,8192]{1,0:T(8,128)(2,1)} reshape(bf16[16,16,4,16,128]{4,3,2,1,0:T(8,128)(2,1)} %all-to-all-done.3) | data formatting | bytes 8388608 | tf_op jit(solution)/shard_map/reshape | solution.py:188
  459.9 78.8 %all-to-all-done.7 = bf16[8,512,1024]{2,1,0:T(8,128)(2,1)} async-done(((bf16[8,512,1024]{2,1,0:T(8,128)(2,1)}), bf16[8,512,1024]{2,1,0:T(8,128)(2,1)}, u32[]{:S(2)}, u32[]{:S(2)}) %all-to-all-start.7) | async-done | bytes 8388640 | tf_op jit(solution)/shard_map/all_to_all | solution.py:236
  538.7 5.7 %fusion.27 = f32[256,1024]{1,0:T(8,128)S(1)} fusion(bf16[16,256,1024]{2,1,0:T(8,128)(2,1)} %bitcast.50, f32[16,256]{1,0:T(8,128)S(1)} %broadcast_in_dim.76, s32[16,256]{1,0:T(8,128)S(1)} %eq.64), kind=kOutput, calls=%fused_computation.36 | convolution fusion | flops 2153775104 | bytes 9469952 | tf_op jit(solution)/shard_map/ect,ecd->td/dot_general | solution.py:245
  544.4 6.8 %fusion.33 = bf16[256,1024]{1,0:T(8,128)(2,1)} fusion(f32[256,1024]{1,0:T(8,128)S(1)} %get-tuple-element.19, f32[256,1024]{1,0:T(8,128)S(1)} %fusion.27, bf16[16,256,1024]{2,1,0:T(8,128)(2,1)} %bitcast.50, f32[16,256]{1,0:T(8,128)S(1)} %broadcast_in_dim.76, s32[16,256]{1,0:T(8,128)S(1)} %eq.64), kind=kOutput, calls=%fused_computation.41 | convolution fusion | flops 2150367232 | bytes 11042816 | tf_op jit(solution)/shard_map/ect,ecd->td/dot_general | solution.py:243
  (69 shorter events, 51.3 us)
Async XLA Ops:
  7.2 291.5 %copy-start = (bf16[1024,1024]{1,0:T(8,128)(2,1)S(1)}, bf16[1024,1024]{1,0:T(8,128)(2,1)}, u32[]{:S(2)}) copy-start(bf16[1024,1024]{1,0:T(8,128)(2,1)} %param.18) | copy-start | bytes 6291460
  12.3 5.8 %copy-start.6 = (s32[2,128]{1,0:T(2,128)S(1)}, s32[2,128]{1,0:T(2,128)}, u32[]{:S(2)}) copy-start(s32[2,128]{1,0:T(2,128)} %param.23) | copy-start | bytes 3076
  12.3 53.4 %all-to-all-start.1 = ((bf16[2,1024,8,128]{3,1,0,2:T(8,128)(2,1)}), bf16[2,1024,8,128]{3,1,0,2:T(8,128)(2,1)}, u32[]{:S(2)}, u32[]{:S(2)}) async-start(bf16[2,1024,8,128]{3,1,0,2:T(8,128)(2,1)} %copy.86), calls=%async_computation.1 | async-start | bytes 8388608 | tf_op jit(solution)/shard_map/all_to_all | solution.py:153
  18.1 265.7 %all-gather.3.cloned.1.call-start = ((), (), s32[]{:S(2)}) async-start(), calls=%async_computation.8 | async-start | bytes 7864320 | tf_op jit(solution)/shard_map/all_gather | solution.py:158
  65.8 16.4 %copy-start.8 = (s32[32]{0:T(128)S(1)}, s32[32]{0:T(128)}, u32[]{:S(2)}) copy-start(s32[32]{0:T(128)} %param.16) | copy-start | bytes 388
  65.8 16.4 %copy-start.9 = (s32[32]{0:T(128)S(1)}, s32[32]{0:T(128)}, u32[]{:S(2)}) copy-start(s32[32]{0:T(128)} %param.17) | copy-start | bytes 388
  65.8 16.6 %copy-start.2 = (bf16[2,128,1024]{2,1,0:T(8,128)(2,1)S(1)}, bf16[2,128,1024]{2,1,0:T(8,128)(2,1)}, u32[]{:S(2)}) copy-start(bf16[2,128,1024]{2,1,0:T(8,128)(2,1)} %param.13) | copy-start | bytes 1572868
  75.9 26.2 %all-to-all-start.4 = ((s32[16,1,16]{2,1,0:T(1,128)}), s32[16,1,16]{2,1,0:T(1,128)S(1)}, u32[]{:S(2)}, u32[]{:S(2)}) async-start(s32[16,1,16]{2,1,0:T(1,128)} %all_to_all.74), calls=%async_computation.4 | async-start | bytes 16384 | tf_op jit(solution)/shard_map/all_to_all | solution.py:172
  82.4 46.7 %copy-start.7 = (s32[2]{0:T(128)}, s32[2]{0:T(128)S(1)}, u32[]{:S(2)}) copy-start(s32[2]{0:T(128)S(1)} %fusion.40.len_ref) | copy-start | bytes 28
  102.1 10.9 %all-to-all-start = ((bf16[2,128,8,128]{1,3,0,2:T(8,128)(2,1)}), bf16[2,128,8,128]{1,3,0,2:T(8,128)(2,1)S(1)}, u32[]{:S(2)}, u32[]{:S(2)}) async-start(bf16[2,128,8,128]{1,3,0,2:T(8,128)(2,1)} %copy.83), calls=%async_computation | async-start | bytes 1048576 | tf_op jit(solution)/shard_map/all_to_all | solution.py:155
  113.0 24.4 %all-to-all-start.2 = ((bf16[2,128,8,128]{3,1,0,2:T(8,128)(2,1)}), bf16[2,128,8,128]{3,1,0,2:T(8,128)(2,1)S(1)}, u32[]{:S(2)}, u32[]{:S(2)}) async-start(bf16[2,128,8,128]{3,1,0,2:T(8,128)(2,1)} %copy.88), calls=%async_computation.2 | async-start | bytes 1048576 | tf_op jit(solution)/shard_map/all_to_all | solution.py:154
  137.4 5.8 %copy-start.3 = (s32[256,8]{0,1:T(8,128)S(1)}, s32[256,8]{0,1:T(8,128)}, u32[]{:S(2)}) copy-start(s32[256,8]{0,1:T(8,128)} %param.20) | copy-start | bytes 24580
  137.4 146.4 %all-to-all-start.3 = ((bf16[16,16,4,16,128]{4,3,2,1,0:T(8,128)(2,1)}), bf16[16,16,4,16,128]{4,3,2,1,0:T(8,128)(2,1)}, u32[]{:S(2)}, u32[]{:S(2)}) async-start(bf16[16,16,4,16,128]{4,3,2,1,0:T(8,128)(2,1)} %bitcast.179), calls=%async_computation.3 | async-start | bytes 8388608 | tf_op jit(solution)/shard_map/all_to_all | solution.py:171
  284.8 16.0 %copy-start.5 = (f32[1024]{0:T(1024)S(1)}, f32[1024]{0:T(1024)}, u32[]{:S(2)}) copy-start(f32[1024]{0:T(1024)} %param.19) | copy-start | bytes 12292
  284.8 12.3 %all-to-all-start.5 = ((bf16[2,256,4,128]{3,2,0,1:T(4,128)(2,1)}), bf16[2,256,4,128]{3,2,0,1:T(4,128)(2,1)S(1)}, u32[]{:S(2)}, u32[]{:S(2)}) async-start(bf16[2,256,4,128]{3,2,0,1:T(4,128)(2,1)} %copy.91), calls=%async_computation.5 | async-start | bytes 1048576 | tf_op jit(solution)/shard_map/all_to_all | solution.py:180
  306.0 98.1 %all-to-all-start.6 = ((bf16[8,512,1024]{2,1,0:T(8,128)(2,1)}), bf16[8,512,1024]{2,1,0:T(8,128)(2,1)}, u32[]{:S(2)}, u32[]{:S(2)}) async-start(bf16[8,512,1024]{2,1,0:T(8,128)(2,1)} %bitcast.177), calls=%async_computation.6 | async-start | bytes 16777216 | tf_op jit(solution)/shard_map/all_to_all | solution.py:221
  440.4 5.4 copy-start.4
  440.4 98.3 %all-to-all-start.7 = ((bf16[8,512,1024]{2,1,0:T(8,128)(2,1)}), bf16[8,512,1024]{2,1,0:T(8,128)(2,1)}, u32[]{:S(2)}, u32[]{:S(2)}) async-start(bf16[8,512,1024]{2,1,0:T(8,128)(2,1)} %bitcast.176), calls=%async_computation.7 | async-start | bytes 16777216 | tf_op jit(solution)/shard_map/all_to_all | solution.py:236
  544.4 6.8 %copy-start.1 = (bf16[1024,1024]{1,0:T(8,128)(2,1)S(1)}, bf16[1024,1024]{1,0:T(8,128)(2,1)}, u32[]{:S(2)}) copy-start(bf16[1024,1024]{1,0:T(8,128)(2,1)} %param.18) | copy-start | bytes 6291460
Sparse Core Ops, SparseCore 0:
  73.4 196.4 all-gather.2

commit v5 on v4

--- a/solution.py
+++ b/solution.py
@@ -154,8 +154,9 @@
         lax.all_to_all(span_kv, "kv", split_axis=2, concat_axis=1, tiled=True),
         lax.all_to_all(queries_grouped, "kv", split_axis=2, concat_axis=1, tiled=True),
     )
-    expert_part, cache_heads = lax.optimization_barrier((w_experts, cache_heads))
-    full_weights = lax.all_gather(expert_part, ("zhi", "kv"), axis=0, tiled=False)
+    pair_weights = lax.all_gather(w_experts, "zhi", axis=0, tiled=False)
+    pair_weights, cache_heads = lax.optimization_barrier((pair_weights, cache_heads))
+    full_weights = lax.all_gather(pair_weights, "kv", axis=1, tiled=False)
     page_total = block_map.shape[1]
     visible = jnp.arange(cache_heads.shape[1])[None, :] < lengths[:, None]
     visible_cache = jnp.where(visible[:, :, None, None], cache_heads, jnp.zeros((), jnp.bfloat16))

time: 560 us -> 520 us (0.929)
  blocking collectives: 0 us -> 97.2 us
  waiting for transfers between devices: 289 us -> 196 us
  Pallas kernels: 77.6 us -> 43.3 us
  matrix products: 51.6 us -> 46 us
    all_to_all x0 -> x1, blocking collectives: none -> 97.2 us  [body(): lax.all_to_all(buffer.reshape(side, per_dev * capacity, width_model), 'rl...]
    all_to_all x1 -> x0, waiting for transfers between devices: 84.5 us -> none  [body(): lax.all_to_all(buffer.reshape(side, per_dev * capacity, width_model), 'rl...]
    all_to_all x1, waiting for transfers between devices: 49.6 us -> 8.44 us  [body(): lax.all_to_all(outgoing, REQ, split_axis=0, concat_axis=0, tiled=True)]
    pallas_call x1, Pallas kernels: 77.6 us -> 43.3 us  [attend(): pl.pallas_call(functools.partial(attend_kernel, tk=tk, head_dim=head_dim)...]
    all_gather x1 -> x2, waiting for transfers between devices: 0.01 us -> 26.5 us  [the longest x1 26.5 us: body(): full_weights = lax.all_gather(pair_weights, 'kv', axis=1, tiled=False)]
    all_to_all x1, waiting for transfers between devices: 16.6 us -> 29 us  [body(): lax.all_to_all(local_slot.reshape(req_count, per_owner), REQ, split_axis=...]
    optimization_barrier x2 -> x1, local copies, waits for them, and re-layouts: 9.62 us -> 0.97 us  [body(): lax.optimization_barrier((attn_heads, full_weights, arrived, where_to))]
    all_to_all x1, waiting for transfers between devices: 7.3 us -> 0.01 us  [body(): lax.all_to_all(queries_grouped, 'kv', split_axis=2, concat_axis=1, tiled=...]
  transfers between devices with their start and end apart: 9 -> 9, of which waited for: 7 -> 6; matrix products, arithmetic and copies ran while one was open for 12% -> 14% of each run, Pallas kernels for 14% -> 8%
where the time goes in v5:
time: 520 us; the launch traced here: 516 us
  waiting for transfers between devices  196 us (38%)
  blocking collectives  97.2 us (19%)
  local copies, waits for them, and re-layouts  67.1 us (13%)
  matrix products  46 us (9%)
  Pallas kernels  43.3 us (8%)
  starting transfers between devices  35.5 us (7%)
  other arithmetic  16.7 us (3%)
  between operations  14.3 us (3%)
    all_to_all x1, blocking collectives, body(): lax.all_to_all(buffer.reshape(side, per_dev * capacity, width_model), 'rl...  97.2 us
    all_to_all x1, waiting for transfers between devices, body(): lax.all_to_all(expert_out.reshape(side, per_dev * capacity, width_model),...  79 us
    all_to_all x1, waiting for transfers between devices, body(): lax.all_to_all(cache, 'kv', split_axis=2, concat_axis=1, tiled=True)  44.3 us
    pallas_call x1, Pallas kernels, attend(): pl.pallas_call(functools.partial(attend_kernel, tk=tk, head_dim=head_dim)...  43.3 us
    all_to_all x1, waiting for transfers between devices, body(): lax.all_to_all(local_slot.reshape(req_count, per_owner), REQ, split_axis=...  29 us
    all_gather x1, waiting for transfers between devices, body(): full_weights = lax.all_gather(pair_weights, 'kv', axis=1, tiled=False)  26.5 us
    unnamed x27, local copies, waits for them, and re-layouts  16.6 us
    dot_general x1, matrix products, body(): jnp.einsum('szjckf,zkjdf->szjcd', activated, weights[:, :, :, 2], preferr...  16.4 us
  transfers between devices with their start and end apart: 9, of which 6 were waited for; matrix products, arithmetic and copies ran while one was open for 14% of the time, Pallas kernels for 8%

profile of v5, /device:TPU:16, one launch (start us, length us, event | category | flops | bytes accessed | tf_op | source)
XLA Modules:
  0.0 515.8 jit_solution(6449695115630853853)
XLA Ops:
  15.8 6.2 %all-to-all-start.4 = ((s32[16,1,16]{2,1,0:T(1,128)}), s32[16,1,16]{2,1,0:T(1,128)S(1)}, u32[]{:S(2)}, u32[]{:S(2)}) async-start(s32[16,1,16]{2,1,0:T(1,128)} %all_to_all.74), calls=%async_computation.4 | async-start | bytes 16384 | tf_op jit(solution)/shard_map/all_to_all | solution.py:173
  22.0 5.2 %copy.87 = bf16[2,1024,8,128]{3,1,0,2:T(8,128)(2,1)} copy(bf16[2,1024,8,128]{3,2,1,0:T(8,128)(2,1)} %param.15) | data formatting | bytes 8388608 | tf_op args[3]
  27.2 29.0 %all-to-all-done.4 = s32[16,1,16]{2,1,0:T(1,128)S(1)} async-done(((s32[16,1,16]{2,1,0:T(1,128)}), s32[16,1,16]{2,1,0:T(1,128)S(1)}, u32[]{:S(2)}, u32[]{:S(2)}) %all-to-all-start.4) | async-done | bytes 1056 | tf_op jit(solution)/shard_map/all_to_all | solution.py:173
  56.2 5.6 %all-to-all-start.1 = ((bf16[2,1024,8,128]{3,1,0,2:T(8,128)(2,1)}), bf16[2,1024,8,128]{3,1,0,2:T(8,128)(2,1)}, u32[]{:S(2)}, u32[]{:S(2)}) async-start(bf16[2,1024,8,128]{3,1,0,2:T(8,128)(2,1)} %copy.87), calls=%async_computation.1 | async-start | bytes 8388608 | tf_op jit(solution)/shard_map/all_to_all | solution.py:153
  65.1 44.3 %all-to-all-done.1 = bf16[2,1024,8,128]{3,1,0,2:T(8,128)(2,1)} async-done(((bf16[2,1024,8,128]{3,1,0,2:T(8,128)(2,1)}), bf16[2,1024,8,128]{3,1,0,2:T(8,128)(2,1)}, u32[]{:S(2)}, u32[]{:S(2)}) %all-to-all-start.1) | async-done | bytes 4194336 | tf_op jit(solution)/shard_map/all_to_all | solution.py:153
  113.0 7.4 %copy.88 = bf16[2,2,1024,4,128]{4,3,2,1,0:T(4,128)(2,1)} copy(bf16[2,2,1024,4,128]{4,2,0,3,1:T(8,128)(2,1)} %bitcast.7) | data formatting | bytes 8388608 | tf_op jit(solution)/shard_map/all_to_all | solution.py:153
  124.0 12.5 %broadcast_select_fusion = bf16[2,2048,4,128]{3,2,1,0:T(4,128)(2,1)S(1)} fusion(bf16[2,2048,4,128]{3,2,1,0:T(4,128)(2,1)} %bitcast.174, pred[2,2048]{1,0:T(4,128)(4,1)S(1)} %iota_compare_fusion.5), kind=kLoop, calls=%fused_computation.22 | loop fusion | flops 2097152 | bytes 8392704 | tf_op jit(solution)/shard_map/jit(_where)/select_n | solution.py:162
  139.6 5.2 %gather_fusion = bf16[256,4,16,128]{3,2,1,0:T(8,128)(2,1)} fusion(bf16[256,4,16,128]{3,2,1,0:T(8,128)(2,1)} %bitcast.180, s32[1024]{0:T(1024)S(1)} %pad_clamp_fusion), kind=kCustom, calls=%fused_computation | custom fusion | bytes 8389632 | tf_op jit(solution)/shard_map/gather | solution.py:124
  144.8 7.8 %all-to-all-start.3 = ((bf16[16,16,4,16,128]{4,3,2,1,0:T(8,128)(2,1)}), bf16[16,16,4,16,128]{4,3,2,1,0:T(8,128)(2,1)}, u32[]{:S(2)}, u32[]{:S(2)}) async-start(bf16[16,16,4,16,128]{4,3,2,1,0:T(8,128)(2,1)} %bitcast.179), calls=%async_computation.3 | async-start | bytes 8388608 | tf_op jit(solution)/shard_map/all_to_all | solution.py:172
  158.5 7.4 %reshape.146.c_ref = bf16[2,2048,512]{2,1,0:T(8,128)(2,1)} reshape(bf16[2,2048,4,128]{3,2,1,0:T(4,128)(2,1)} %bitcast.175) | data formatting | bytes 8388608 | tf_op jit(solution)/shard_map/reshape | solution.py:96
  165.9 43.3 %shard_map.131 = bf16[2,256,512]{2,1,0:T(8,128)(2,1)} custom-call(s32[2]{0:T(128)} %copy-done.8, bf16[2,256,512]{2,1,0:T(8,128)(2,1)} %reshape.145.q_ref, bf16[2,2048,512]{2,1,0:T(8,128)(2,1)} %reshape.146.c_ref, bf16[2,256,512]{2,1,0:T(8,128)(2,1)} %reshape.147.s_ref), custom_call_target="tpu_custom_call" | custom-call | flops 7247757312 | bytes 5767168 | tf_op jit(solution)/shard_map/pallas_call | solution.py:99
  210.3 26.5 %all-gather.7.cloned.1.call-done = bf16[2,2,3,1024,256]{3,4,1,0,2:T(8,128)(2,1)} async-done(((bf16[2,1,3,1024,256]{3,4,1,0,2:T(8,128)(2,1)}), bf16[2,2,3,1024,256]{3,4,1,0,2:T(8,128)(2,1)}) %all-gather.7.cloned.1.call-update) | async-done | bytes 6291472 | tf_op jit(solution)/shard_map/all_gather | solution.py:159
  236.8 8.4 %all-to-all-done.3 = bf16[16,16,4,16,128]{4,3,2,1,0:T(8,128)(2,1)} async-done(((bf16[16,16,4,16,128]{4,3,2,1,0:T(8,128)(2,1)}), bf16[16,16,4,16,128]{4,3,2,1,0:T(8,128)(2,1)}, u32[]{:S(2)}, u32[]{:S(2)}) %all-to-all-start.3) | async-done | bytes 4194336 | tf_op jit(solution)/shard_map/all_to_all | solution.py:172
  246.2 3.6 all-to-all-start.5
  250.2 8.0 %all-to-all-done.5 = bf16[2,256,4,128]{3,2,0,1:T(4,128)(2,1)S(1)} async-done(((bf16[2,256,4,128]{3,2,0,1:T(4,128)(2,1)}), bf16[2,256,4,128]{3,2,0,1:T(4,128)(2,1)S(1)}, u32[]{:S(2)}, u32[]{:S(2)}) %all-to-all-start.5) | async-done | bytes 524320 | tf_op jit(solution)/shard_map/all_to_all | solution.py:181
  265.1 97.2 %all_to_all.90 = bf16[8,512,1024]{2,1,0:T(8,128)(2,1)S(1)} all-to-all(bf16[8,512,1024]{2,1,0:T(8,128)(2,1)S(1)} %bitcast.177), channel_id=1, replica_groups=mesh['zhi'=2,'rlow'=8,'kv'=2] {'rlow'}, dimensions={0} | all-to-all | bytes 16777216 | tf_op jit(solution)/shard_map/all_to_all | solution.py:222
  365.6 8.3 %fusion.7 = f32[2,2,256,8,256]{4,2,3,1,0:T(8,128)} fusion(bf16[8,2,256,1024,1]{3,2,1,0,4:T(8,128)(2,1)S(1)} %bitcast.181, bf16[2,2,1,3,1024,256]{4,5,1,0,3,2:T(8,128)(2,1)} %bitcast.193), kind=kOutput, calls=%fused_computation.14 | convolution fusion | flops 4294967296 | bytes 18874368 | tf_op jit(solution)/shard_map/szjcd,zkjdf->szjckf/dot_general | solution.py:227
  373.9 16.4 %fusion = bf16[8,2,1,256,1024]{4,3,0,1,2:T(8,128)(2,1)} fusion(f32[2,2,256,8,256]{4,2,3,1,0:T(8,128)} %fusion.7, bf16[8,2,256,1024,1]{3,2,1,0,4:T(8,128)(2,1)} %bitcast.182, bf16[2,2,1,3,1024,256]{4,5,1,0,3,2:T(8,128)(2,1)} %bitcast.194), kind=kOutput, calls=%fused_computation.4 | convolution fusion | flops 8606711808 | bytes 29360128 | tf_op jit(solution)/shard_map/szjckf,zkjdf->szjcd/dot_general | solution.py:234
  390.3 7.9 %copy.104 = bf16[8,2,1,256,1024]{4,3,1,0,2:T(8,128)(2,1)} copy(bf16[8,2,1,256,1024]{4,3,0,1,2:T(8,128)(2,1)} %fusion) | data formatting | bytes 16777216 | tf_op jit(solution)/shard_map/convert_element_type | solution.py:236
  398.2 5.1 all-to-all-start.7
  403.4 7.3 %reshape.167 = bf16[256,8192]{1,0:T(8,128)(2,1)} reshape(bf16[16,16,4,16,128]{4,3,2,1,0:T(8,128)(2,1)} %all-to-all-done.3) | data formatting | bytes 8388608 | tf_op jit(solution)/shard_map/reshape | solution.py:189
  417.4 79.0 %all-to-all-done.7 = bf16[8,512,1024]{2,1,0:T(8,128)(2,1)} async-done(((bf16[8,512,1024]{2,1,0:T(8,128)(2,1)}), bf16[8,512,1024]{2,1,0:T(8,128)(2,1)}, u32[]{:S(2)}, u32[]{:S(2)}) %all-to-all-start.7) | async-done | bytes 8388640 | tf_op jit(solution)/shard_map/all_to_all | solution.py:237
  496.4 5.7 %fusion.38 = f32[256,1024]{1,0:T(8,128)S(1)} fusion(bf16[16,256,1024]{2,1,0:T(8,128)(2,1)} %bitcast.50, f32[16,256]{1,0:T(8,128)S(1)} %broadcast_in_dim.76, s32[16,256]{1,0:T(8,128)S(1)} %eq.64), kind=kOutput, calls=%fused_computation.39 | convolution fusion | flops 2153775104 | bytes 9469952 | tf_op jit(solution)/shard_map/ect,ecd->td/dot_general | solution.py:246
  502.1 6.8 %fusion.44 = bf16[256,1024]{1,0:T(8,128)(2,1)} fusion(f32[256,1024]{1,0:T(8,128)S(1)} %get-tuple-element.19, f32[256,1024]{1,0:T(8,128)S(1)} %fusion.38, bf16[16,256,1024]{2,1,0:T(8,128)(2,1)} %bitcast.50, f32[16,256]{1,0:T(8,128)S(1)} %broadcast_in_dim.76, s32[16,256]{1,0:T(8,128)S(1)} %eq.64), kind=kOutput, calls=%fused_computation.44 | convolution fusion | flops 2150367232 | bytes 11042816 | tf_op jit(solution)/shard_map/ect,ecd->td/dot_general | solution.py:244
  (73 shorter events, 47.3 us)
Async XLA Ops:
  7.2 252.7 %copy-start = (bf16[1024,1024]{1,0:T(8,128)(2,1)S(1)}, bf16[1024,1024]{1,0:T(8,128)(2,1)}, u32[]{:S(2)}) copy-start(bf16[1024,1024]{1,0:T(8,128)(2,1)} %param.18) | copy-start | bytes 6291460
  7.2 2.8 copy-start.7
  7.2 113.3 %all-gather.5.cloned.1.call-start = ((), (), s32[]{:S(2)}) async-start(), calls=%async_computation.8 | async-start | bytes 4718592 | tf_op jit(solution)/shard_map/all_gather | solution.py:157
  15.8 40.3 %all-to-all-start.4 = ((s32[16,1,16]{2,1,0:T(1,128)}), s32[16,1,16]{2,1,0:T(1,128)S(1)}, u32[]{:S(2)}, u32[]{:S(2)}) async-start(s32[16,1,16]{2,1,0:T(1,128)} %all_to_all.74), calls=%async_computation.4 | async-start | bytes 16384 | tf_op jit(solution)/shard_map/all_to_all | solution.py:173
  27.2 34.6 %copy-start.3 = (bf16[2,128,1024]{2,1,0:T(8,128)(2,1)S(1)}, bf16[2,128,1024]{2,1,0:T(8,128)(2,1)}, u32[]{:S(2)}) copy-start(bf16[2,128,1024]{2,1,0:T(8,128)(2,1)} %param.13) | copy-start | bytes 1572868
  27.2 37.7 %copy-start.9 = (s32[32]{0:T(128)S(1)}, s32[32]{0:T(128)}, u32[]{:S(2)}) copy-start(s32[32]{0:T(128)} %param.16) | copy-start | bytes 388
  27.2 37.7 %copy-start.10 = (s32[32]{0:T(128)S(1)}, s32[32]{0:T(128)}, u32[]{:S(2)}) copy-start(s32[32]{0:T(128)} %param.17) | copy-start | bytes 388
  56.2 53.3 %all-to-all-start.1 = ((bf16[2,1024,8,128]{3,1,0,2:T(8,128)(2,1)}), bf16[2,1024,8,128]{3,1,0,2:T(8,128)(2,1)}, u32[]{:S(2)}, u32[]{:S(2)}) async-start(bf16[2,1024,8,128]{3,1,0,2:T(8,128)(2,1)} %copy.87), calls=%async_computation.1 | async-start | bytes 8388608 | tf_op jit(solution)/shard_map/all_to_all | solution.py:153
  65.1 55.4 %copy-start.8 = (s32[2]{0:T(128)}, s32[2]{0:T(128)S(1)}, u32[]{:S(2)}) copy-start(s32[2]{0:T(128)S(1)} %fusion.51.len_ref) | copy-start | bytes 28
  109.4 11.0 %all-to-all-start = ((bf16[2,128,8,128]{1,3,0,2:T(8,128)(2,1)}), bf16[2,128,8,128]{1,3,0,2:T(8,128)(2,1)S(1)}, u32[]{:S(2)}, u32[]{:S(2)}) async-start(bf16[2,128,8,128]{1,3,0,2:T(8,128)(2,1)} %copy.83), calls=%async_computation | async-start | bytes 1048576 | tf_op jit(solution)/shard_map/all_to_all | solution.py:155
  120.5 24.3 %all-to-all-start.2 = ((bf16[2,128,8,128]{3,1,0,2:T(8,128)(2,1)}), bf16[2,128,8,128]{3,1,0,2:T(8,128)(2,1)S(1)}, u32[]{:S(2)}, u32[]{:S(2)}) async-start(bf16[2,128,8,128]{3,1,0,2:T(8,128)(2,1)} %copy.89), calls=%async_computation.2 | async-start | bytes 1048576 | tf_op jit(solution)/shard_map/all_to_all | solution.py:154
  144.8 8.5 %copy-start.4 = (s32[256,8]{0,1:T(8,128)S(1)}, s32[256,8]{0,1:T(8,128)}, u32[]{:S(2)}) copy-start(s32[256,8]{0,1:T(8,128)} %param.20) | copy-start | bytes 24580
  144.8 100.5 %all-to-all-start.3 = ((bf16[16,16,4,16,128]{4,3,2,1,0:T(8,128)(2,1)}), bf16[16,16,4,16,128]{4,3,2,1,0:T(8,128)(2,1)}, u32[]{:S(2)}, u32[]{:S(2)}) async-start(bf16[16,16,4,16,128]{4,3,2,1,0:T(8,128)(2,1)} %bitcast.179), calls=%async_computation.3 | async-start | bytes 8388608 | tf_op jit(solution)/shard_map/all_to_all | solution.py:172
  152.6 84.2 %all-gather.7.cloned.1.call-start = ((), (), s32[]{:S(2)}) async-start(), calls=%async_computation.9 | async-start | bytes 9437184 | tf_op jit(solution)/shard_map/all_gather | solution.py:159
  246.2 15.6 %copy-start.6 = (f32[1024]{0:T(1024)S(1)}, f32[1024]{0:T(1024)}, u32[]{:S(2)}) copy-start(f32[1024]{0:T(1024)} %param.19) | copy-start | bytes 12292
  246.2 11.9 %all-to-all-start.5 = ((bf16[2,256,4,128]{3,2,0,1:T(4,128)(2,1)}), bf16[2,256,4,128]{3,2,0,1:T(4,128)(2,1)S(1)}, u32[]{:S(2)}, u32[]{:S(2)}) async-start(bf16[2,256,4,128]{3,2,0,1:T(4,128)(2,1)} %copy.92), calls=%async_computation.5 | async-start | bytes 1048576 | tf_op jit(solution)/shard_map/all_to_all | solution.py:181
  362.3 3.2 copy-start.2
  398.2 5.1 copy-start.5
  398.2 98.2 %all-to-all-start.7 = ((bf16[8,512,1024]{2,1,0:T(8,128)(2,1)}), bf16[8,512,1024]{2,1,0:T(8,128)(2,1)}, u32[]{:S(2)}, u32[]{:S(2)}) async-start(bf16[8,512,1024]{2,1,0:T(8,128)(2,1)} %bitcast.176), calls=%async_computation.7 | async-start | bytes 16777216 | tf_op jit(solution)/shard_map/all_to_all | solution.py:237
  502.1 6.8 %copy-start.1 = (bf16[1024,1024]{1,0:T(8,128)(2,1)S(1)}, bf16[1024,1024]{1,0:T(8,128)(2,1)}, u32[]{:S(2)}) copy-start(bf16[1024,1024]{1,0:T(8,128)(2,1)} %param.18) | copy-start | bytes 6291460
Sparse Core Ops, SparseCore 0:
  10.1 77.8 all-gather.4
  155.0 81.8 all-gather.6

commit v6 on v4

--- a/solution.py
+++ b/solution.py
@@ -21,29 +21,33 @@
     return jnp.sum(jnp.where(match, cached_len[None, :], 0), axis=1)
 
 
-def attend_kernel(len_ref, q_ref, c_ref, s_ref, o_ref, *, tk, head_dim):
+def attend_kernel(meta_ref, q_ref, c_ref, s_ref, o_ref, st_ref, *, tk, head_dim):
     b = pl.program_id(0)
-    length = len_ref[b]
+    reqs = pl.num_programs(0)
+    cached = c_ref.shape[1]
+    length = jnp.clip(meta_ref[b], 0, cached)
+    offset = meta_ref[reqs]
     span = q_ref.shape[1]
+    span_here = s_ref.shape[1]
     lanes = q_ref.shape[2]
     per_group = lanes // head_dim
     scale = 1.0 / math.sqrt(head_dim)
     lane = lax.broadcasted_iota(jnp.int32, (span, lanes), 1)
     q_all = q_ref[0].astype(jnp.float32) * scale
-    blocks = c_ref.shape[1] // tk
+    blocks = cached // tk
     full = length // tk
     tail = jnp.minimum(full, blocks - 1)
-    row = lax.broadcasted_iota(jnp.int32, (span, span), 0)
-    col = lax.broadcasted_iota(jnp.int32, (span, span), 1)
-    causal = col <= row
+    row = lax.broadcasted_iota(jnp.int32, (span, span_here), 0)
+    col = lax.broadcasted_iota(jnp.int32, (span, span_here), 1)
+    causal = col + offset <= row
     key_lane = lax.broadcasted_iota(jnp.int32, (tk, lanes), 1) < head_dim
-    span_lane = lax.broadcasted_iota(jnp.int32, (span, lanes), 1) < head_dim
+    span_lane = lax.broadcasted_iota(jnp.int32, (span_here, lanes), 1) < head_dim
     span_keys = s_ref[0]
     span_vals = jnp.where(span_lane, jnp.ones_like(span_keys), span_keys)
     dims = (((1,), (1,)), ((), ()))
     tail_pos = tail * tk + lax.broadcasted_iota(jnp.int32, (span, tk), 1)
     tail_ok = (tail_pos >= full * tk) & (tail_pos < length)
-    outs = []
+    outs, stats = [], []
     for j in range(per_group):
         shifted = q_all if j == 0 else pltpu.roll(q_all, lanes - j * head_dim, 1)
         qj = jnp.where(lane < head_dim, shifted, 0.0).astype(jnp.bfloat16)
@@ -78,44 +82,58 @@
         keys_tail, s_tail = block(tail)
         acc = accumulate(acc, jnp.where(tail_ok, jnp.exp(s_tail - m), 0.0), keys_tail)
         total = acc[:, 0:1]
-        res = acc / total
+        res = acc / jnp.where(total > 0.0, total, 1.0)
         shift = (j * head_dim - head_dim) % lanes
         outs.append(res if shift == 0 else pltpu.roll(res, shift, 1))
+        stats.append((m, total))
     out = outs[0]
-    for j in range(1, per_group):
-        out = jnp.where(lane >= j * head_dim, outs[j], out)
+    stat = jnp.zeros((span, lanes), jnp.float32)
+    for j in range(per_group):
+        if j > 0:
+            out = jnp.where(lane >= j * head_dim, outs[j], out)
+        m, total = stats[j]
+        here = (lane >= j * head_dim) & (lane < (j + 1) * head_dim)
+        first = lane < j * head_dim + head_dim // 2
+        stat = jnp.where(here, jnp.where(first, m, total), stat)
     o_ref[0] = out.astype(o_ref.dtype)
-
-
-def attend(query_heads, cache_heads, span_heads, lengths):
-    local_reqs, span, groups, lanes = query_heads.shape
-    cached = cache_heads.shape[1]
-    head_dim = cache_heads.shape[-1] // 2
+    st_ref[0] = stat
+
+
+def attend(q_all, cache, span_kv, meta):
+    local_reqs, span, width = q_all.shape
+    cached, kv_heads, lanes = cache.shape[1:]
+    span_here = span_kv.shape[1]
+    head_dim = lanes // 2
     tk = 256 if cached % 256 == 0 else cached
-    q2 = query_heads.reshape(local_reqs, span, groups * lanes)
-    c2 = cache_heads.reshape(local_reqs, cached, groups * lanes)
-    s2 = span_heads.reshape(local_reqs, span, groups * lanes)
-    flops = 2 * local_reqs * groups * (lanes // head_dim) * span * (cached + span) * lanes * 3
-    out = pl.pallas_call(
+    c2 = cache.reshape(local_reqs, cached, kv_heads * lanes)
+    s2 = span_kv.reshape(local_reqs, span_here, kv_heads * lanes)
+    flops = 2 * local_reqs * kv_heads * (lanes // head_dim) * span * (cached + span_here) * lanes * 3
+    out, stat = pl.pallas_call(
         functools.partial(attend_kernel, tk=tk, head_dim=head_dim),
-        out_shape=jax.ShapeDtypeStruct(q2.shape, jnp.bfloat16),
+        out_shape=(
+            jax.ShapeDtypeStruct(q_all.shape, jnp.bfloat16),
+            jax.ShapeDtypeStruct(q_all.shape, jnp.float32),
+        ),
         grid_spec=pltpu.PrefetchScalarGridSpec(
             num_scalar_prefetch=1,
-            grid=(local_reqs, groups),
+            grid=(local_reqs, kv_heads),
             in_specs=[
                 pl.BlockSpec((1, span, lanes), lambda b, g, n: (b, 0, g)),
                 pl.BlockSpec((1, cached, lanes), lambda b, g, n: (b, 0, g)),
+                pl.BlockSpec((1, span_here, lanes), lambda b, g, n: (b, 0, g)),
+            ],
+            out_specs=(
                 pl.BlockSpec((1, span, lanes), lambda b, g, n: (b, 0, g)),
-            ],
-            out_specs=pl.BlockSpec((1, span, lanes), lambda b, g, n: (b, 0, g)),
+                pl.BlockSpec((1, span, lanes), lambda b, g, n: (b, 0, g)),
+            ),
         ),
         cost_estimate=pl.CostEstimate(
             flops=flops,
-            transcendentals=local_reqs * groups * 2 * span * (cached + span),
-            bytes_accessed=2 * (2 * q2.size + c2.size + s2.size),
+            transcendentals=local_reqs * kv_heads * 2 * span * (cached + span_here),
+            bytes_accessed=2 * (3 * q_all.size + c2.size + s2.size) + 4 * q_all.size,
         ),
-    )(lengths.astype(jnp.int32), q2, c2, s2)
-    return out.reshape(local_reqs, span, groups, lanes)
+    )(meta, q_all, c2, s2)
+    return out, stat
 
 
 def place_pages(page_rows, slot_numbers, slots_dev):
@@ -148,38 +166,63 @@
     group_count = kv_heads // kv_count
     slots_dev = local_reqs * block_map.shape[1]
     lengths = lookup_lengths(req_order, cached_len, local_reqs)
-    queries_grouped = queries.reshape(local_reqs, local_tokens, kv_heads, group_width)
-    cache_heads, span_heads, query_heads = (
-        lax.all_to_all(cache, "kv", split_axis=2, concat_axis=1, tiled=True),
-        lax.all_to_all(span_kv, "kv", split_axis=2, concat_axis=1, tiled=True),
-        lax.all_to_all(queries_grouped, "kv", split_axis=2, concat_axis=1, tiled=True),
-    )
-    expert_part, cache_heads = lax.optimization_barrier((w_experts, cache_heads))
-    full_weights = lax.all_gather(expert_part, ("zhi", "kv"), axis=0, tiled=False)
-    page_total = block_map.shape[1]
-    visible = jnp.arange(cache_heads.shape[1])[None, :] < lengths[:, None]
-    visible_cache = jnp.where(visible[:, :, None, None], cache_heads, jnp.zeros((), jnp.bfloat16))
+    kv_index = lax.axis_index("kv")
+    cached_local = cache.shape[1]
+    head_dim = head_pair // 2
+    heads = kv_heads * (group_width // head_dim)
+    full_weights = lax.all_gather(w_experts, ("zhi", "kv"), axis=0, tiled=False)
+    pages_local = cached_local // BLOCK
+    position = kv_index * cached_local + jnp.arange(cached_local)
+    visible = position[None, :] < lengths[:, None]
+    visible_cache = jnp.where(visible[:, :, None, None], cache, jnp.zeros((), jnp.bfloat16))
     page_rows = (
-        visible_cache.reshape(local_reqs, page_total, BLOCK, group_count, head_pair)
+        visible_cache.reshape(local_reqs, pages_local, BLOCK, kv_heads, head_pair)
         .transpose(0, 1, 3, 2, 4)
-        .reshape(local_reqs * page_total, group_count, BLOCK, head_pair)
-    )
-    sorted_pages, local_slot = place_pages(page_rows, block_map.reshape(-1), slots_dev)
+        .reshape(local_reqs * pages_local, kv_heads, BLOCK, head_pair)
+    )
+    my_map = lax.dynamic_slice_in_dim(block_map, kv_index * pages_local, pages_local, axis=1)
+    sorted_pages, local_slot = place_pages(page_rows, my_map.reshape(-1), slots_dev)
     per_owner = sorted_pages.shape[0] // req_count
-    outgoing = sorted_pages.reshape(req_count, per_owner, group_count, BLOCK, head_pair)
+    outgoing = (
+        sorted_pages.reshape(req_count, per_owner, kv_count, group_count, BLOCK, head_pair)
+        .transpose(0, 2, 1, 3, 4, 5)
+        .reshape(req_count * kv_count, per_owner, group_count, BLOCK, head_pair)
+    )
+    slots_out = jnp.broadcast_to(
+        local_slot.reshape(req_count, 1, per_owner), (req_count, kv_count, per_owner)
+    ).reshape(req_count * kv_count, per_owner)
+    everyone = (*REQ, "kv")
     arrived, where_to = (
-        lax.all_to_all(outgoing, REQ, split_axis=0, concat_axis=0, tiled=True),
-        lax.all_to_all(
-            local_slot.reshape(req_count, per_owner), REQ, split_axis=0, concat_axis=0, tiled=True
-        ),
-    )
-    attn_heads = attend(query_heads, cache_heads, span_heads, lengths)
-    attn_heads, full_weights, arrived, where_to = lax.optimization_barrier(
-        (attn_heads, full_weights, arrived, where_to)
-    )
-    attn = lax.all_to_all(attn_heads, "kv", split_axis=1, concat_axis=2, tiled=True).reshape(
-        row_count, kv_heads * group_width
-    )
+        lax.all_to_all(outgoing, everyone, split_axis=0, concat_axis=0, tiled=True),
+        lax.all_to_all(slots_out, everyone, split_axis=0, concat_axis=0, tiled=True),
+    )
+    q_all = lax.all_gather(queries, "kv", axis=1, tiled=True)
+    meta = jnp.concatenate(
+        [lengths - kv_index * cached_local, (kv_index * local_tokens)[None]]
+    ).astype(jnp.int32)
+    part_out, part_stat = attend(q_all, cache, span_kv, meta)
+    part_out, part_stat, full_weights, arrived, where_to = lax.optimization_barrier(
+        (part_out, part_stat, full_weights, arrived, where_to)
+    )
+    span_total = q_all.shape[1]
+    stat = part_stat.reshape(local_reqs, span_total, heads, 2, head_dim // 2)[..., 0]
+    got_out = lax.all_to_all(
+        part_out.reshape(local_reqs, kv_count, local_tokens, width_model),
+        "kv", split_axis=1, concat_axis=1, tiled=True,
+    )
+    got_stat = lax.all_to_all(
+        stat.reshape(local_reqs, kv_count, local_tokens, heads, 2),
+        "kv", split_axis=1, concat_axis=1, tiled=True,
+    )
+    part_max = got_stat[..., 0]
+    top = jnp.max(part_max, axis=1, keepdims=True)
+    part_weight = got_stat[..., 1] * jnp.exp(part_max - top)
+    merged = jnp.sum(
+        got_out.reshape(local_reqs, kv_count, local_tokens, heads, head_dim).astype(jnp.float32)
+        * part_weight[..., None],
+        axis=1,
+    ) / jnp.sum(part_weight, axis=1)[..., None]
+    attn = merged.astype(jnp.bfloat16).reshape(row_count, width_model)
     placement = (
         where_to.reshape(1, -1) == jnp.arange(slots_dev, dtype=jnp.int32)[:, None]
     ).astype(jnp.bfloat16)

time: 560 us -> 533 us (0.952)
  waiting for transfers between devices: 289 us -> 267 us
  starting transfers between devices: 38.8 us -> 29.3 us
    all_to_all x6 -> x4, waiting for transfers between devices: 126 us -> 89.4 us  [the longest x1 77.8 us: body(): lax.all_to_all(outgoing, everyone, split_axis=0, concat_axis=0, tiled=True)]
    all_gather x1 -> x2, waiting for transfers between devices: 0.01 us -> 13.4 us  [the longest x1 13.4 us: body(): full_weights = lax.all_gather(w_experts, ('zhi', 'kv'), axis=0, tiled=False)]
    all_to_all x6 -> x0, local copies, waits for them, and re-layouts: 10.1 us -> none  [the longest x1 7.5 us: body(): lax.all_to_all(cache, 'kv', split_axis=2, concat_axis=1, tiled=True)]
    all_to_all x6 -> x4, starting transfers between devices: 28.4 us -> 18.7 us  [the longest x1 5.93 us: body(): lax.all_to_all(slots_out, everyone, split_axis=0, concat_axis=0, tiled=True)]
    unnamed x24 -> x18, local copies, waits for them, and re-layouts: 10.7 us -> 4.3 us
    transpose x0 -> x1, local copies, waits for them, and re-layouts: none -> 6.03 us  [body(): outgoing = sorted_pages.reshape(req_count, per_owner, kv_count, group_cou...]
    reshape x8 -> x6, local copies, waits for them, and re-layouts: 16.4 us -> 13.2 us  [the longest x1 7.33 us: attend(): c2 = cache.reshape(local_reqs, cached, kv_heads * lanes)]
  transfers between devices with their start and end apart: 9 -> 8, of which waited for: 7 -> 6; matrix products, arithmetic and copies ran while one was open for 12% -> 13% of each run, Pallas kernels for 14% -> 16%
where the time goes in v6:
time: 533 us; the launch traced here: 527 us
  waiting for transfers between devices  267 us (50%)
  Pallas kernels  82.5 us (15%)
  local copies, waits for them, and re-layouts  65.3 us (12%)
  matrix products  51.5 us (10%)
  starting transfers between devices  29.3 us (5%)
  other arithmetic  16.6 us (3%)
  between operations  14.3 us (3%)
    all_to_all x1, waiting for transfers between devices, body(): lax.all_to_all(buffer.reshape(side, per_dev * capacity, width_model), 'rl...  84.4 us
    pallas_call x1, Pallas kernels, attend(): pl.pallas_call(functools.partial(attend_kernel, tk=tk, head_dim=head_dim)...  82.5 us
    all_to_all x1, waiting for transfers between devices, body(): lax.all_to_all(expert_out.reshape(side, per_dev * capacity, width_model),...  78.8 us
    all_to_all x1, waiting for transfers between devices, body(): lax.all_to_all(outgoing, everyone, split_axis=0, concat_axis=0, tiled=True)  77.8 us
    dot_general x1, matrix products, body(): jnp.einsum('szjckf,zkjdf->szjcd', activated, weights[:, :, :, 2], preferr...  16.6 us
    all_gather x1, waiting for transfers between devices, body(): full_weights = lax.all_gather(w_experts, ('zhi', 'kv'), axis=0, tiled=False)  13.4 us
    dot_general x1, matrix products, body(): jnp.einsum('szjcd,zkjdf->szjckf', grouped, weights[:, :, :, 1], preferred...  11.8 us
    optimization_barrier x2, local copies, waits for them, and re-layouts, body(): lax.optimization_barrier((part_out, part_stat, full_weights, arrived, whe...  11.5 us
  transfers between devices with their start and end apart: 8, of which 6 were waited for; matrix products, arithmetic and copies ran while one was open for 13% of the time, Pallas kernels for 16%

profile of v6, /device:TPU:16, one launch (start us, length us, event | category | flops | bytes accessed | tf_op | source)
XLA Modules:
  0.0 526.9 jit_solution(4266545632590643465)
XLA Ops:
  14.0 5.9 %all-to-all-start.1 = ((s32[32,1,8]{2,1,0:T(1,128)}), s32[32,1,8]{2,1,0:T(1,128)S(1)}, u32[]{:S(2)}, u32[]{:S(2)}) async-start(s32[32,1,8]{2,1,0:T(1,128)} %bitcast.9), calls=%async_computation.1 | async-start | bytes 32768 | tf_op jit(solution)/shard_map/all_to_all | solution.py:197
  21.6 9.2 %broadcast_select_fusion = bf16[2,1024,8,128]{3,2,1,0:T(8,128)(2,1)S(1)} fusion(bf16[2,1024,8,128]{3,2,1,0:T(8,128)(2,1)} %param.15, pred[2,1024]{1,0:T(4,128)(4,1)S(1)} %broadcast_compare_fusion), kind=kLoop, calls=%fused_computation.22 | loop fusion | flops 2097152 | bytes 8390656 | tf_op jit(solution)/shard_map/jit(_where)/select_n | solution.py:177
  34.2 5.2 gather_fusion
  39.4 6.0 %copy.131 = bf16[16,2,8,4,16,128]{5,4,3,2,1,0:T(8,128)(2,1)} copy(bf16[16,2,8,4,16,128]{5,4,3,1,2,0:T(8,128)(2,1)} %bitcast.182) | data formatting | bytes 8388608 | tf_op jit(solution)/shard_map/transpose | solution.py:188
  45.4 5.9 %all-to-all-start = ((bf16[32,8,4,16,128]{4,3,2,1,0:T(8,128)(2,1)}), bf16[32,8,4,16,128]{4,3,2,1,0:T(8,128)(2,1)}, u32[]{:S(2)}, u32[]{:S(2)}) async-start(bf16[32,8,4,16,128]{4,3,2,1,0:T(8,128)(2,1)} %bitcast.180), calls=%async_computation | async-start | bytes 8388608 | tf_op jit(solution)/shard_map/all_to_all | solution.py:196
  51.4 7.3 %reshape.163.c_ref = bf16[2,1024,1024]{2,1,0:T(8,128)(2,1)} reshape(bf16[2,1024,8,128]{3,2,1,0:T(8,128)(2,1)} %param.15) | data formatting | bytes 8388608 | tf_op jit(solution)/shard_map/reshape | solution.py:108
  61.2 82.5 %shard_map.131 = (bf16[2,256,1024]{2,1,0:T(8,128)(2,1)}, f32[2,256,1024]{2,1,0:T(8,128)}) custom-call(s32[3]{0:T(128)} %pad_add_fusion.meta_ref, bf16[2,256,1024]{2,1,0:T(8,128)(2,1)} %all-gather.4.cloned.1.call-done.q_ref, bf16[2,1024,1024]{2,1,0:T(8,128)(2,1)} %reshape.163.c_ref, bf16[2,128,1024]{2,1,0:T(8,128)(2,1)} %reshape.164.s_ref), custom_call_target="tpu_custom_call" | custom-call | flops 7247757312 | bytes 9961472 | tf_op jit(solution)/shard_map/pallas_call | solution.py:111
  143.7 77.8 %all-to-all-done = bf16[32,8,4,16,128]{4,3,2,1,0:T(8,128)(2,1)} async-done(((bf16[32,8,4,16,128]{4,3,2,1,0:T(8,128)(2,1)}), bf16[32,8,4,16,128]{4,3,2,1,0:T(8,128)(2,1)}, u32[]{:S(2)}, u32[]{:S(2)}) %all-to-all-start) | async-done | bytes 4194336 | tf_op jit(solution)/shard_map/all_to_all | solution.py:196
  221.5 13.4 %all-gather.6.cloned.1.call-done = bf16[4,3,1024,256]{3,2,1,0:T(8,128)(2,1)} async-done(((bf16[1,3,1024,256]{3,2,1,0:T(8,128)(2,1)}), bf16[4,3,1024,256]{3,2,1,0:T(8,128)(2,1)}) %all-gather.6.cloned.1.call-update) | async-done | bytes 6291472 | tf_op jit(solution)/shard_map/all_gather | solution.py:173
  246.9 3.6 all-to-all-start.2
  254.4 9.0 %all-to-all-done.2 = bf16[2,2,128,1024]{2,3,0,1:T(8,128)(2,1)S(1)} async-done(((bf16[2,2,128,1024]{2,3,0,1:T(8,128)(2,1)}), bf16[2,2,128,1024]{2,3,0,1:T(8,128)(2,1)S(1)}, u32[]{:S(2)}, u32[]{:S(2)}) %all-to-all-start.2) | async-done | bytes 1048608 | tf_op jit(solution)/shard_map/all_to_all | solution.py:209
  269.5 5.2 convolution_convert_fusion.1
  274.7 5.1 all-to-all-start.4
  279.9 8.6 %copy.147 = bf16[4,1,3,1024,256]{3,4,0,2,1:T(8,128)(2,1)} copy(bf16[4,1,3,1024,256]{4,3,2,0,1:T(8,128)(2,1)} %bitcast.184) | data formatting | bytes 12582912 | tf_op jit(solution)/shard_map/optimization_barrier | solution.py:204
  288.5 84.4 %all-to-all-done.4 = bf16[8,512,1024]{2,1,0:T(8,128)(2,1)} async-done(((bf16[8,512,1024]{2,1,0:T(8,128)(2,1)}), bf16[8,512,1024]{2,1,0:T(8,128)(2,1)}, u32[]{:S(2)}, u32[]{:S(2)}) %all-to-all-start.4) | async-done | bytes 8388640 | tf_op jit(solution)/shard_map/all_to_all | solution.py:264
  372.8 11.8 %fusion.5 = f32[2,2,256,8,256]{4,2,3,1,0:T(8,128)} fusion(bf16[8,2,256,1024,1]{3,2,1,0,4:T(8,128)(2,1)} %bitcast.34, bf16[2,2,1,3,1024,256]{4,5,1,0,3,2:T(8,128)(2,1)} %bitcast.185), kind=kOutput, calls=%fused_computation.12 | convolution fusion | flops 4294967296 | bytes 18874368 | tf_op jit(solution)/shard_map/szjcd,zkjdf->szjckf/dot_general | solution.py:272
  384.6 16.6 %fusion = bf16[8,2,1,256,1024]{4,3,0,1,2:T(8,128)(2,1)} fusion(f32[2,2,256,8,256]{4,2,3,1,0:T(8,128)} %fusion.5, bf16[2,2,1,3,1024,256]{4,5,1,0,3,2:T(8,128)(2,1)} %bitcast.186, bf16[8,2,256,1024,1]{3,2,1,0,4:T(8,128)(2,1)} %bitcast.34), kind=kOutput, calls=%fused_computation.4 | convolution fusion | flops 8606711808 | bytes 29360128 | tf_op jit(solution)/shard_map/szjckf,zkjdf->szjcd/dot_general | solution.py:276
  401.3 7.9 %copy.153 = bf16[8,2,1,256,1024]{4,3,1,0,2:T(8,128)(2,1)} copy(bf16[8,2,1,256,1024]{4,3,0,1,2:T(8,128)(2,1)} %fusion) | data formatting | bytes 16777216 | tf_op jit(solution)/shard_map/convert_element_type | solution.py:278
  409.2 5.4 %all-to-all-start.5 = ((bf16[8,512,1024]{2,1,0:T(8,128)(2,1)}), bf16[8,512,1024]{2,1,0:T(8,128)(2,1)}, u32[]{:S(2)}, u32[]{:S(2)}) async-start(bf16[8,512,1024]{2,1,0:T(8,128)(2,1)} %bitcast.178), calls=%async_computation.5 | async-start | bytes 16777216 | tf_op jit(solution)/shard_map/all_to_all | solution.py:279
  414.8 7.3 %reshape.186 = bf16[256,8192]{1,0:T(8,128)(2,1)} reshape(bf16[32,8,4,16,128]{4,3,2,1,0:T(8,128)(2,1)} %all-to-all-done) | data formatting | bytes 8388608 | tf_op jit(solution)/shard_map/reshape | solution.py:231
  422.0 3.4 fusion.13
  428.7 78.8 %all-to-all-done.5 = bf16[8,512,1024]{2,1,0:T(8,128)(2,1)} async-done(((bf16[8,512,1024]{2,1,0:T(8,128)(2,1)}), bf16[8,512,1024]{2,1,0:T(8,128)(2,1)}, u32[]{:S(2)}, u32[]{:S(2)}) %all-to-all-start.5) | async-done | bytes 8388640 | tf_op jit(solution)/shard_map/all_to_all | solution.py:279
  507.5 5.7 %fusion.28 = f32[256,1024]{1,0:T(8,128)S(1)} fusion(bf16[16,256,1024]{2,1,0:T(8,128)(2,1)} %bitcast.50, f32[16,256]{1,0:T(8,128)S(1)} %broadcast_in_dim.92, s32[16,256]{1,0:T(8,128)S(1)} %eq.64), kind=kOutput, calls=%fused_computation.38 | convolution fusion | flops 2153775104 | bytes 9469952 | tf_op jit(solution)/shard_map/ect,ecd->td/dot_general | solution.py:288
  513.2 6.8 %fusion.34 = bf16[256,1024]{1,0:T(8,128)(2,1)} fusion(f32[256,1024]{1,0:T(8,128)S(1)} %get-tuple-element.24, f32[256,1024]{1,0:T(8,128)S(1)} %fusion.28, bf16[16,256,1024]{2,1,0:T(8,128)(2,1)} %bitcast.50, f32[16,256]{1,0:T(8,128)S(1)} %broadcast_in_dim.92, s32[16,256]{1,0:T(8,128)S(1)} %eq.64), kind=kOutput, calls=%fused_computation.43 | convolution fusion | flops 2150367232 | bytes 11042816 | tf_op jit(solution)/shard_map/ect,ecd->td/dot_general | solution.py:286
  (73 shorter events, 39.6 us)
Async XLA Ops:
  7.2 260.4 %copy-start = (bf16[1024,1024]{1,0:T(8,128)(2,1)S(1)}, bf16[1024,1024]{1,0:T(8,128)(2,1)}, u32[]{:S(2)}) copy-start(bf16[1024,1024]{1,0:T(8,128)(2,1)} %param.18) | copy-start | bytes 6291460
  7.2 54.0 %all-gather.4.cloned.1.call-start = ((), (), s32[]{:S(2)}) async-start(), calls=%async_computation.6 | async-start | bytes 1572864 | tf_op jit(solution)/shard_map/all_gather | solution.py:199
  7.9 227.0 %all-gather.6.cloned.1.call-start = ((), (), s32[]{:S(2)}) async-start(), calls=%async_computation.7 | async-start | bytes 7864320 | tf_op jit(solution)/shard_map/all_gather | solution.py:173
  14.0 31.4 %all-to-all-start.1 = ((s32[32,1,8]{2,1,0:T(1,128)}), s32[32,1,8]{2,1,0:T(1,128)S(1)}, u32[]{:S(2)}, u32[]{:S(2)}) async-start(s32[32,1,8]{2,1,0:T(1,128)} %bitcast.9), calls=%async_computation.1 | async-start | bytes 32768 | tf_op jit(solution)/shard_map/all_to_all | solution.py:197
  45.4 176.1 %all-to-all-start = ((bf16[32,8,4,16,128]{4,3,2,1,0:T(8,128)(2,1)}), bf16[32,8,4,16,128]{4,3,2,1,0:T(8,128)(2,1)}, u32[]{:S(2)}, u32[]{:S(2)}) async-start(bf16[32,8,4,16,128]{4,3,2,1,0:T(8,128)(2,1)} %bitcast.180), calls=%async_computation | async-start | bytes 8388608 | tf_op jit(solution)/shard_map/all_to_all | solution.py:196
  51.4 7.4 %copy-start.4 = (s32[256,8]{0,1:T(8,128)S(1)}, s32[256,8]{0,1:T(8,128)}, u32[]{:S(2)}) copy-start(s32[256,8]{0,1:T(8,128)} %param.20) | copy-start | bytes 24580
  51.4 8.2 %copy-start.3 = (bf16[2,128,8,128]{3,2,1,0:T(8,128)(2,1)S(1)}, bf16[2,128,8,128]{3,2,1,0:T(8,128)(2,1)}, u32[]{:S(2)}) copy-start(bf16[2,128,8,128]{3,2,1,0:T(8,128)(2,1)} %param.14) | copy-start | bytes 1572868
  59.6 84.2 %copy-start.6 = (s32[16,3]{0,1:T(4,128)}, s32[16,3]{0,1:T(4,128)S(1)}, u32[]{:S(2)}) copy-start(s32[16,3]{0,1:T(4,128)S(1)} %reduce-window.9) | copy-start | bytes 580
  143.7 99.2 %copy-start.2 = (bf16[2,256,1024]{2,1,0:T(8,128)(2,1)S(1)}, bf16[2,256,1024]{2,1,0:T(8,128)(2,1)}, u32[]{:S(2)}) copy-start(bf16[2,256,1024]{2,1,0:T(8,128)(2,1)} %get-tuple-element.13) | copy-start | bytes 3145732
  221.5 21.3 %slice-start = ((s32[16,3]{0,1:T(4,128)}), s32[16,2]{0,1:T(2,128)S(1)}, s32[]{:S(2)}) async-start(s32[16,3]{0,1:T(4,128)} %copy-done.6), calls=%async_computation.8 | async-start | bytes 2048 | tf_op jit(solution)/shard_map/slice.1
  239.5 7.4 %all-to-all-start.3 = ((f32[2,2,128,16,2]{2,3,4,0,1:T(8,128)}), f32[2,2,128,16,2]{2,3,4,0,1:T(8,128)S(1)}, u32[]{:S(2)}, u32[]{:S(2)}) async-start(f32[2,2,128,16,2]{2,3,4,0,1:T(8,128)} %copy.136), calls=%async_computation.3 | async-start | bytes 131072 | tf_op jit(solution)/shard_map/all_to_all | solution.py:213
  246.9 16.5 %all-to-all-start.2 = ((bf16[2,2,128,1024]{2,3,0,1:T(8,128)(2,1)}), bf16[2,2,128,1024]{2,3,0,1:T(8,128)(2,1)S(1)}, u32[]{:S(2)}, u32[]{:S(2)}) async-start(bf16[2,2,128,1024]{2,3,0,1:T(8,128)(2,1)} %copy.132), calls=%async_computation.2 | async-start | bytes 2097152 | tf_op jit(solution)/shard_map/all_to_all | solution.py:209
  264.6 4.8 copy-start.7
  274.7 98.1 %all-to-all-start.4 = ((bf16[8,512,1024]{2,1,0:T(8,128)(2,1)}), bf16[8,512,1024]{2,1,0:T(8,128)(2,1)}, u32[]{:S(2)}, u32[]{:S(2)}) async-start(bf16[8,512,1024]{2,1,0:T(8,128)(2,1)} %bitcast.179), calls=%async_computation.4 | async-start | bytes 16777216 | tf_op jit(solution)/shard_map/all_to_all | solution.py:264
  409.2 5.4 %copy-start.5 = (f32[256,8]{0,1:T(8,128)S(1)}, f32[256,8]{0,1:T(8,128)}, u32[]{:S(2)}) copy-start(f32[256,8]{0,1:T(8,128)} %param.21) | copy-start | bytes 24580
  409.2 98.3 %all-to-all-start.5 = ((bf16[8,512,1024]{2,1,0:T(8,128)(2,1)}), bf16[8,512,1024]{2,1,0:T(8,128)(2,1)}, u32[]{:S(2)}, u32[]{:S(2)}) async-start(bf16[8,512,1024]{2,1,0:T(8,128)(2,1)} %bitcast.178), calls=%async_computation.5 | async-start | bytes 16777216 | tf_op jit(solution)/shard_map/all_to_all | solution.py:279
  513.2 6.8 %copy-start.1 = (bf16[1024,1024]{1,0:T(8,128)(2,1)S(1)}, bf16[1024,1024]{1,0:T(8,128)(2,1)}, u32[]{:S(2)}) copy-start(bf16[1024,1024]{1,0:T(8,128)(2,1)} %param.18) | copy-start | bytes 6291460
Sparse Core Ops, SparseCore 0:
  9.6 22.5 all-gather.3
  34.0 200.8 all-gather.5

commit v7 on v6

--- a/solution.py
+++ b/solution.py
@@ -21,66 +21,84 @@
     return jnp.sum(jnp.where(match, cached_len[None, :], 0), axis=1)
 
 
-def attend_kernel(meta_ref, q_ref, c_ref, s_ref, o_ref, st_ref, *, tk, head_dim):
+def attend_kernel(meta_ref, q_ref, c_ref, *rest, piece, kv_count, head_dim, received):
+    if received:
+        o_ref, st_ref = rest
+    else:
+        s_ref, o_ref, st_ref = rest
     b = pl.program_id(0)
     reqs = pl.num_programs(0)
-    cached = c_ref.shape[1]
-    length = jnp.clip(meta_ref[b], 0, cached)
-    offset = meta_ref[reqs]
+    length = meta_ref[b]
+    me = meta_ref[reqs]
+    cached = meta_ref[reqs + 1]
     span = q_ref.shape[1]
-    span_here = s_ref.shape[1]
     lanes = q_ref.shape[2]
     per_group = lanes // head_dim
+    step = kv_count * piece
+    rounds = (c_ref.shape[1] if received else c_ref.shape[1] // step)
     scale = 1.0 / math.sqrt(head_dim)
     lane = lax.broadcasted_iota(jnp.int32, (span, lanes), 1)
     q_all = q_ref[0].astype(jnp.float32) * scale
-    blocks = cached // tk
-    full = length // tk
-    tail = jnp.minimum(full, blocks - 1)
-    row = lax.broadcasted_iota(jnp.int32, (span, span_here), 0)
-    col = lax.broadcasted_iota(jnp.int32, (span, span_here), 1)
-    causal = col + offset <= row
-    key_lane = lax.broadcasted_iota(jnp.int32, (tk, lanes), 1) < head_dim
-    span_lane = lax.broadcasted_iota(jnp.int32, (span_here, lanes), 1) < head_dim
-    span_keys = s_ref[0]
-    span_vals = jnp.where(span_lane, jnp.ones_like(span_keys), span_keys)
+    key_lane = lax.broadcasted_iota(jnp.int32, (piece, lanes), 1) < head_dim
+    key_col = lax.broadcasted_iota(jnp.int32, (span, piece), 1)
     dims = (((1,), (1,)), ((), ()))
-    tail_pos = tail * tk + lax.broadcasted_iota(jnp.int32, (span, tk), 1)
-    tail_ok = (tail_pos >= full * tk) & (tail_pos < length)
+
+    def count(base):
+        return jnp.minimum((jnp.maximum(length - base, 0) + step - 1) // step, rounds)
+
+    runs = []
+    if received:
+        for t in range(1, kv_count):
+            src = lax.rem(me + t, kv_count)
+            base = src * cached + me * piece
+            runs.append((count(base), functools.partial(
+                lambda i, src, base: (c_ref[0, i, src], base + i * step), src=src, base=base)))
+    else:
+        base = me * cached + me * piece
+
+        def local_piece(i):
+            start = pl.multiple_of((i * kv_count + me) * piece, piece)
+            return c_ref[0, pl.ds(start, piece), :], base + i * step
+
+        runs.append((count(base), local_piece))
+    if not received:
+        span_keys = s_ref[0]
+        span_here = span_keys.shape[0]
+        row = lax.broadcasted_iota(jnp.int32, (span, span_here), 0)
+        col = lax.broadcasted_iota(jnp.int32, (span, span_here), 1)
+        causal = col + me * span_here <= row
+        span_lane = lax.broadcasted_iota(jnp.int32, (span_here, lanes), 1) < head_dim
+        span_vals = jnp.where(span_lane, jnp.ones_like(span_keys), span_keys)
     outs, stats = [], []
     for j in range(per_group):
         shifted = q_all if j == 0 else pltpu.roll(q_all, lanes - j * head_dim, 1)
         qj = jnp.where(lane < head_dim, shifted, 0.0).astype(jnp.bfloat16)
 
-        def block(kb):
-            start = pl.multiple_of(kb * tk, tk)
-            keys = c_ref[0, pl.ds(start, tk), :]
+        def scores(get, i):
+            keys, first = get(i)
             s = lax.dot_general(qj, keys, dims, preferred_element_type=jnp.float32)
-            return keys, s
-
-        def max_body(kb, m):
-            _, s = block(kb)
-            return jnp.maximum(m, jnp.max(s, axis=1, keepdims=True))
-
-        s_span = lax.dot_general(qj, span_keys, dims, preferred_element_type=jnp.float32)
-        m = jnp.max(jnp.where(causal, s_span, -1e30), axis=1, keepdims=True)
-        m = lax.fori_loop(0, full, max_body, m)
-        _, s_tail = block(tail)
-        m = jnp.maximum(m, jnp.max(jnp.where(tail_ok, s_tail, -1e30), axis=1, keepdims=True))
-
-        def accumulate(acc, p, keys):
-            vals = jnp.where(key_lane, jnp.ones_like(keys), keys)
-            return acc + jnp.dot(p.astype(jnp.bfloat16), vals, preferred_element_type=jnp.float32)
-
-        def sum_body(kb, acc):
-            keys, s = block(kb)
-            return accumulate(acc, jnp.exp(s - m), keys)
-
-        p_span = jnp.where(causal, jnp.exp(s_span - m), 0.0)
-        acc = jnp.dot(p_span.astype(jnp.bfloat16), span_vals, preferred_element_type=jnp.float32)
-        acc = lax.fori_loop(0, full, sum_body, acc)
-        keys_tail, s_tail = block(tail)
-        acc = accumulate(acc, jnp.where(tail_ok, jnp.exp(s_tail - m), 0.0), keys_tail)
+            return keys, first + key_col < length, s
+
+        m = jnp.full((span, 1), -1e30, jnp.float32)
+        if not received:
+            s_span = lax.dot_general(qj, span_keys, dims, preferred_element_type=jnp.float32)
+            m = jnp.maximum(m, jnp.max(jnp.where(causal, s_span, -1e30), axis=1, keepdims=True))
+        for n, get in runs:
+            def max_body(i, m, get=get):
+                _, ok, s = scores(get, i)
+                return jnp.maximum(m, jnp.max(jnp.where(ok, s, -1e30), axis=1, keepdims=True))
+            m = lax.fori_loop(0, n, max_body, m)
+        acc = jnp.zeros((span, lanes), jnp.float32)
+        if not received:
+            p_span = jnp.where(causal, jnp.exp(s_span - m), 0.0)
+            acc = acc + jnp.dot(p_span.astype(jnp.bfloat16), span_vals, preferred_element_type=jnp.float32)
+        for n, get in runs:
+            def sum_body(i, acc, get=get):
+                keys, ok, s = scores(get, i)
+                p = jnp.where(ok, jnp.exp(s - m), 0.0)
+                vals = jnp.where(key_lane, jnp.ones_like(keys), keys)
+                return acc + jnp.dot(p.astype(jnp.bfloat16), vals, preferred_element_type=jnp.float32)
+            acc = lax.fori_loop(0, n, sum_body, acc)
         total = acc[:, 0:1]
         res = acc / jnp.where(total > 0.0, total, 1.0)
         shift = (j * head_dim - head_dim) % lanes
@@ -95,33 +113,44 @@
         here = (lane >= j * head_dim) & (lane < (j + 1) * head_dim)
         first = lane < j * head_dim + head_dim // 2
         stat = jnp.where(here, jnp.where(first, m, total), stat)
-    o_ref[0] = out.astype(o_ref.dtype)
+    o_ref[0] = out
     st_ref[0] = stat
 
 
-def attend(q_all, cache, span_kv, meta):
+def attend(q_all, keys, span_kv, meta, piece, kv_count):
     local_reqs, span, width = q_all.shape
-    cached, kv_heads, lanes = cache.shape[1:]
-    span_here = span_kv.shape[1]
+    received = span_kv is None
+    if received:
+        _, rounds, _, _, kv_heads, lanes = keys.shape
+        k2 = keys.reshape(local_reqs, rounds, kv_count, piece, kv_heads * lanes)
+        key_spec = pl.BlockSpec((1, rounds, kv_count, piece, lanes), lambda b, g, n: (b, 0, 0, 0, g))
+        key_count = rounds * (kv_count - 1) * piece
+        operands = (k2,)
+        specs = [key_spec]
+    else:
+        cached, kv_heads, lanes = keys.shape[1:]
+        k2 = keys.reshape(local_reqs, cached, kv_heads * lanes)
+        s2 = span_kv.reshape(local_reqs, span_kv.shape[1], kv_heads * lanes)
+        key_count = cached // kv_count + s2.shape[1]
+        operands = (k2, s2)
+        specs = [
+            pl.BlockSpec((1, cached, lanes), lambda b, g, n: (b, 0, g)),
+            pl.BlockSpec((1, s2.shape[1], lanes), lambda b, g, n: (b, 0, g)),
+        ]
     head_dim = lanes // 2
-    tk = 256 if cached % 256 == 0 else cached
-    c2 = cache.reshape(local_reqs, cached, kv_heads * lanes)
-    s2 = span_kv.reshape(local_reqs, span_here, kv_heads * lanes)
-    flops = 2 * local_reqs * kv_heads * (lanes // head_dim) * span * (cached + span_here) * lanes * 3
-    out, stat = pl.pallas_call(
-        functools.partial(attend_kernel, tk=tk, head_dim=head_dim),
+    flops = 2 * local_reqs * kv_heads * (lanes // head_dim) * span * key_count * lanes * 3
+    return pl.pallas_call(
+        functools.partial(
+            attend_kernel, piece=piece, kv_count=kv_count, head_dim=head_dim, received=received
+        ),
         out_shape=(
-            jax.ShapeDtypeStruct(q_all.shape, jnp.bfloat16),
+            jax.ShapeDtypeStruct(q_all.shape, jnp.float32),
             jax.ShapeDtypeStruct(q_all.shape, jnp.float32),
         ),
         grid_spec=pltpu.PrefetchScalarGridSpec(
             num_scalar_prefetch=1,
             grid=(local_reqs, kv_heads),
-            in_specs=[
-                pl.BlockSpec((1, span, lanes), lambda b, g, n: (b, 0, g)),
-                pl.BlockSpec((1, cached, lanes), lambda b, g, n: (b, 0, g)),
-                pl.BlockSpec((1, span_here, lanes), lambda b, g, n: (b, 0, g)),
-            ],
+            in_specs=[pl.BlockSpec((1, span, lanes), lambda b, g, n: (b, 0, g))] + specs,
             out_specs=(
                 pl.BlockSpec((1, span, lanes), lambda b, g, n: (b, 0, g)),
                 pl.BlockSpec((1, span, lanes), lambda b, g, n: (b, 0, g)),
@@ -129,11 +158,10 @@
         ),
         cost_estimate=pl.CostEstimate(
             flops=flops,
-            transcendentals=local_reqs * kv_heads * 2 * span * (cached + span_here),
-            bytes_accessed=2 * (3 * q_all.size + c2.size + s2.size) + 4 * q_all.size,
-        ),
-    )(meta, q_all, c2, s2)
-    return out, stat
+            transcendentals=local_reqs * kv_heads * 2 * span * key_count,
+            bytes_accessed=2 * (q_all.size + sum(x.size for x in operands)) + 8 * q_all.size,
+        ),
+    )(meta, q_all, *operands)
 
 
 def place_pages(page_rows, slot_numbers, slots_dev):
@@ -196,16 +224,37 @@
         lax.all_to_all(outgoing, everyone, split_axis=0, concat_axis=0, tiled=True),
         lax.all_to_all(slots_out, everyone, split_axis=0, concat_axis=0, tiled=True),
     )
+    piece = min(256, cached_local // kv_count)
+    rounds = cached_local // (kv_count * piece)
+    dealt = lax.all_to_all(
+        cache.reshape(local_reqs, rounds, kv_count, piece, kv_heads, head_pair),
+        "kv", split_axis=2, concat_axis=2, tiled=True,
+    )
     q_all = lax.all_gather(queries, "kv", axis=1, tiled=True)
     meta = jnp.concatenate(
-        [lengths - kv_index * cached_local, (kv_index * local_tokens)[None]]
+        [lengths, kv_index[None], jnp.full((1,), cached_local)]
     ).astype(jnp.int32)
-    part_out, part_stat = attend(q_all, cache, span_kv, meta)
-    part_out, part_stat, full_weights, arrived, where_to = lax.optimization_barrier(
-        (part_out, part_stat, full_weights, arrived, where_to)
-    )
+    own_out, own_stat = attend(q_all, cache, span_kv, meta, piece, kv_count)
+    got_out, got_stat = attend(q_all, dealt, None, meta, piece, kv_count)
     span_total = q_all.shape[1]
-    stat = part_stat.reshape(local_reqs, span_total, heads, 2, head_dim // 2)[..., 0]
+
+    def split_stat(table):
+        table = table.reshape(local_reqs, span_total, heads, 2, head_dim // 2)[..., 0]
+        return table[..., 0], table[..., 1]
+
+    own_max, own_sum = split_stat(own_stat)
+    got_max, got_sum = split_stat(got_stat)
+    top = jnp.maximum(own_max, got_max)
+    own_w = own_sum * jnp.exp(own_max - top)
+    got_w = got_sum * jnp.exp(got_max - top)
+    both_w = own_w + got_w
+    part_out = (
+        (own_out.reshape(local_reqs, span_total, heads, head_dim) * own_w[..., None]
+         + got_out.reshape(local_reqs, span_total, heads, head_dim) * got_w[..., None])
+        / jnp.where(both_w > 0.0, both_w, 1.0)[..., None]
+    ).astype(jnp.bfloat16).reshape(local_reqs, span_total, width_model)
+    stat = jnp.stack([top, both_w], axis=-1)
+    part_out, stat, full_weights = lax.optimization_barrier((part_out, stat, full_weights))
     got_out = lax.all_to_all(
         part_out.reshape(local_reqs, kv_count, local_tokens, width_model),
         "kv", split_axis=1, concat_axis=1, tiled=True,

time: 533 us -> 539 us (1.011)
  waiting for transfers between devices: 267 us -> 212 us
  local copies, waits for them, and re-layouts: 65.3 us -> 98 us
  Pallas kernels: 82.5 us -> 108 us
  other arithmetic: 16.6 us -> 22.1 us
    all_to_all x1, waiting for transfers between devices: 77.8 us -> 46.4 us  [body(): lax.all_to_all(outgoing, everyone, split_axis=0, concat_axis=0, tiled=True)]
    pallas_call x1 -> x2, Pallas kernels: 82.5 us -> 108 us  [attend(): pl.pallas_call(functools.partial(attend_kernel, piece=piece, kv_count=kv_...]
    reshape x3 -> x8, local copies, waits for them, and re-layouts: 8.36 us -> 25.5 us  [the longest x2 11.8 us: attend(): k2 = keys.reshape(local_reqs, rounds, kv_count, piece, kv_heads * lanes)]
    all_to_all x1, waiting for transfers between devices: 84.4 us -> 69.5 us  [body(): lax.all_to_all(buffer.reshape(side, per_dev * capacity, width_model), 'rl...]
    all_gather x1, waiting for transfers between devices: 13.4 us -> 0.02 us  [body(): full_weights = lax.all_gather(w_experts, ('zhi', 'kv'), axis=0, tiled=False)]
    all_gather x1, waiting for transfers between devices: 0.01 us -> 10.6 us  [body(): q_all = lax.all_gather(queries, 'kv', axis=1, tiled=True)]
    mul x0 -> x4, local copies, waits for them, and re-layouts: none -> 8.83 us  [the longest x2 4.42 us: body(): own_out.reshape(local_reqs, span_total, heads, head_dim) * own_w[..., None]]
    pallas_call x0 -> x2, local copies, waits for them, and re-layouts: none -> 5.83 us  [attend(): pl.pallas_call(functools.partial(attend_kernel, piece=piece, kv_count=kv_...]
  transfers between devices with their start and end apart: 8 -> 9, of which waited for: 6 -> 6; matrix products, arithmetic and copies ran while one was open for 13% -> 29% of each run, Pallas kernels for 16% -> 20%
where the time goes in v7:
time: 539 us; the launch traced here: 538 us
  waiting for transfers between devices  212 us (39%)
  Pallas kernels  108 us (20%)
  local copies, waits for them, and re-layouts  98 us (18%)
  matrix products  51.5 us (10%)
  starting transfers between devices  31.4 us (6%)
  other arithmetic  22.1 us (4%)
  between operations  14.5 us (3%)
    pallas_call x2, Pallas kernels, attend(): pl.pallas_call(functools.partial(attend_kernel, piece=piece, kv_count=kv_...  108 us
    all_to_all x1, waiting for transfers between devices, body(): lax.all_to_all(expert_out.reshape(side, per_dev * capacity, width_model),...  77.5 us
    all_to_all x1, waiting for transfers between devices, body(): lax.all_to_all(buffer.reshape(side, per_dev * capacity, width_model), 'rl...  69.5 us
    all_to_all x1, waiting for transfers between devices, body(): lax.all_to_all(outgoing, everyone, split_axis=0, concat_axis=0, tiled=True)  46.4 us
    dot_general x1, matrix products, body(): jnp.einsum('szjckf,zkjdf->szjcd', activated, weights[:, :, :, 2], preferr...  16.6 us
    reshape x2, local copies, waits for them, and re-layouts, attend(): k2 = keys.reshape(local_reqs, rounds, kv_count, piece, kv_heads * lanes)  11.8 us
    dot_general x1, matrix products, body(): jnp.einsum('szjcd,zkjdf->szjckf', grouped, weights[:, :, :, 1], preferred...  11.8 us
  transfers between devices with their start and end apart: 9, of which 6 were waited for; matrix products, arithmetic and copies ran while one was open for 29% of the time, Pallas kernels for 20%

profile of v7, /device:TPU:16, one launch (start us, length us, event | category | flops | bytes accessed | tf_op | source)
XLA Modules:
  0.0 538.0 jit_solution(9474122089602675517)
XLA Ops:
  13.2 5.6 %all-to-all-start = ((bf16[2,2,2,256,8,128]{5,4,3,1,0,2:T(8,128)(2,1)}), bf16[2,2,2,256,8,128]{5,4,3,1,0,2:T(8,128)(2,1)}, u32[]{:S(2)}, u32[]{:S(2)}) async-start(bf16[2,2,2,256,8,128]{5,4,3,1,0,2:T(8,128)(2,1)} %copy.157), calls=%async_computation | async-start | bytes 8388608 | tf_op jit(solution)/shard_map/all_to_all | solution.py:229
  18.9 7.4 %reshape.182.c_ref = bf16[2,1024,1024]{2,1,0:T(8,128)(2,1)} reshape(bf16[2,1024,8,128]{3,2,1,0:T(8,128)(2,1)} %param.15) | data formatting | bytes 8388608 | tf_op jit(solution)/shard_map/reshape | solution.py:132
  31.8 10.6 %all-gather.4.cloned.1.call-done.q_ref = bf16[2,256,1024]{2,1,0:T(8,128)(2,1)} async-done(((bf16[2,128,1024]{2,1,0:T(8,128)(2,1)}), bf16[2,256,1024]{2,1,0:T(8,128)(2,1)}) %all-gather.4.cloned.1.call-update) | async-done | bytes 1048592 | tf_op jit(solution)/shard_map/all_gather | solution.py:233
  42.3 59.4 %shard_map.131 = (f32[2,256,1024]{2,1,0:T(8,128)}, f32[2,256,1024]{2,1,0:T(8,128)}) custom-call(s32[4]{0:T(128)} %pad_add_fusion.meta_ref, bf16[2,256,1024]{2,1,0:T(8,128)(2,1)} %all-gather.4.cloned.1.call-done.q_ref, bf16[2,1024,1024]{2,1,0:T(8,128)(2,1)} %reshape.182.c_ref, bf16[2,128,1024]{2,1,0:T(8,128)(2,1)} %reshape.183.rest_0_), custom_call_target="tpu_custom_call" | custom-call | flops 4026531840 | bytes 9961472 | tf_op jit(solution)/shard_map/pallas_call | solution.py:142
  105.8 7.3 %reshape.240 = bf16[2,2,2,256,1024]{4,3,1,0,2:T(8,128)(2,1)} reshape(bf16[2,2,2,256,8,128]{5,4,3,1,0,2:T(8,128)(2,1)} %all-to-all-done) | data formatting | bytes 8388608 | tf_op jit(solution)/shard_map/reshape | solution.py:125
  117.6 49.0 %shard_map.132 = (f32[2,256,1024]{2,1,0:T(8,128)}, f32[2,256,1024]{2,1,0:T(8,128)}) custom-call(s32[4]{0:T(128)} %pad_add_fusion.meta_ref, bf16[2,256,1024]{2,1,0:T(8,128)(2,1)} %all-gather.4.cloned.1.call-done.q_ref, bf16[2,2,2,256,1024]{4,3,2,1,0:T(8,128)(2,1)} %copy.195.c_ref), custom_call_target="tpu_custom_call" | custom-call | flops 3221225472 | bytes 9437184 | tf_op jit(solution)/shard_map/pallas_call | solution.py:142
  184.1 5.2 divide_convert_fusion
  205.1 5.4 %all-to-all-done.1 = bf16[2,2,128,1024]{2,3,0,1:T(8,128)(2,1)S(1)} async-done(((bf16[2,2,128,1024]{2,3,0,1:T(8,128)(2,1)}), bf16[2,2,128,1024]{2,3,0,1:T(8,128)(2,1)S(1)}, u32[]{:S(2)}, u32[]{:S(2)}) %all-to-all-start.1) | async-done | bytes 1048608 | tf_op jit(solution)/shard_map/all_to_all | solution.py:258
  220.7 5.2 convolution_convert_fusion.1
  225.9 5.0 all-to-all-start.3
  231.0 9.2 %broadcast_select_fusion = bf16[2,1024,8,128]{3,2,1,0:T(8,128)(2,1)S(1)} fusion(bf16[2,1024,8,128]{3,2,1,0:T(8,128)(2,1)} %param.15, pred[2,1024]{1,0:T(4,128)(4,1)S(1)} %broadcast_compare_fusion), kind=kLoop, calls=%fused_computation.22 | loop fusion | flops 2097152 | bytes 8390656 | tf_op jit(solution)/shard_map/jit(_where)/select_n | solution.py:205
  243.6 5.3 gather_fusion.1
  248.9 5.6 %copy.186 = bf16[16,2,8,4,16,128]{5,4,3,2,1,0:T(8,128)(2,1)} copy(bf16[16,2,8,4,16,128]{5,4,3,1,2,0:T(8,128)(2,1)} %bitcast.205) | data formatting | bytes 8388608 | tf_op jit(solution)/shard_map/transpose | solution.py:216
  254.5 69.5 %all-to-all-done.3 = bf16[8,512,1024]{2,1,0:T(8,128)(2,1)} async-done(((bf16[8,512,1024]{2,1,0:T(8,128)(2,1)}), bf16[8,512,1024]{2,1,0:T(8,128)(2,1)}, u32[]{:S(2)}, u32[]{:S(2)}) %all-to-all-start.3) | async-done | bytes 8388640 | tf_op jit(solution)/shard_map/all_to_all | solution.py:313
  329.0 8.6 %copy.178 = bf16[4,1,3,1024,256]{3,4,0,2,1:T(8,128)(2,1)} copy(bf16[4,1,3,1024,256]{4,3,2,0,1:T(8,128)(2,1)} %bitcast.210) | data formatting | bytes 12582912 | tf_op jit(solution)/shard_map/optimization_barrier | solution.py:257
  337.6 11.8 %fusion.5 = f32[2,2,256,8,256]{4,2,3,1,0:T(8,128)} fusion(bf16[8,2,256,1024,1]{3,2,1,0,4:T(8,128)(2,1)} %bitcast.31, bf16[2,2,1,3,1024,256]{4,5,1,0,3,2:T(8,128)(2,1)} %bitcast.211), kind=kOutput, calls=%fused_computation.12 | convolution fusion | flops 4294967296 | bytes 18874368 | tf_op jit(solution)/shard_map/szjcd,zkjdf->szjckf/dot_general | solution.py:321
  349.3 16.6 %fusion = bf16[8,2,1,256,1024]{4,3,0,1,2:T(8,128)(2,1)} fusion(f32[2,2,256,8,256]{4,2,3,1,0:T(8,128)} %fusion.5, bf16[2,2,1,3,1024,256]{4,5,1,0,3,2:T(8,128)(2,1)} %bitcast.212, bf16[8,2,256,1024,1]{3,2,1,0,4:T(8,128)(2,1)} %bitcast.31), kind=kOutput, calls=%fused_computation.4 | convolution fusion | flops 8606711808 | bytes 29360128 | tf_op jit(solution)/shard_map/szjckf,zkjdf->szjcd/dot_general | solution.py:325
  366.0 7.9 %copy.184 = bf16[8,2,1,256,1024]{4,3,1,0,2:T(8,128)(2,1)} copy(bf16[8,2,1,256,1024]{4,3,0,1,2:T(8,128)(2,1)} %fusion) | data formatting | bytes 16777216 | tf_op jit(solution)/shard_map/convert_element_type | solution.py:327
  373.9 46.4 %all-to-all-done.6 = bf16[32,8,4,16,128]{4,3,2,1,0:T(8,128)(2,1)} async-done(((bf16[32,8,4,16,128]{4,3,2,1,0:T(8,128)(2,1)}), bf16[32,8,4,16,128]{4,3,2,1,0:T(8,128)(2,1)}, u32[]{:S(2)}, u32[]{:S(2)}) %all-to-all-start.6) | async-done | bytes 4194336 | tf_op jit(solution)/shard_map/all_to_all | solution.py:224
  420.3 5.4 %all-to-all-start.4 = ((bf16[8,512,1024]{2,1,0:T(8,128)(2,1)}), bf16[8,512,1024]{2,1,0:T(8,128)(2,1)}, u32[]{:S(2)}, u32[]{:S(2)}) async-start(bf16[8,512,1024]{2,1,0:T(8,128)(2,1)} %bitcast.201), calls=%async_computation.4 | async-start | bytes 16777216 | tf_op jit(solution)/shard_map/all_to_all | solution.py:328
  427.2 7.3 %reshape.209 = bf16[256,8192]{1,0:T(8,128)(2,1)} reshape(bf16[32,8,4,16,128]{4,3,2,1,0:T(8,128)(2,1)} %all-to-all-done.6) | data formatting | bytes 8388608 | tf_op jit(solution)/shard_map/reshape | solution.py:280
  441.1 77.5 %all-to-all-done.4 = bf16[8,512,1024]{2,1,0:T(8,128)(2,1)} async-done(((bf16[8,512,1024]{2,1,0:T(8,128)(2,1)}), bf16[8,512,1024]{2,1,0:T(8,128)(2,1)}, u32[]{:S(2)}, u32[]{:S(2)}) %all-to-all-start.4) | async-done | bytes 8388640 | tf_op jit(solution)/shard_map/all_to_all | solution.py:328
  518.6 5.7 %fusion.28 = f32[256,1024]{1,0:T(8,128)S(1)} fusion(bf16[16,256,1024]{2,1,0:T(8,128)(2,1)} %bitcast.47, f32[16,256]{1,0:T(8,128)S(1)} %broadcast_in_dim.95, s32[16,256]{1,0:T(8,128)S(1)} %eq.64), kind=kOutput, calls=%fused_computation.39 | convolution fusion | flops 2153775104 | bytes 9469952 | tf_op jit(solution)/shard_map/ect,ecd->td/dot_general | solution.py:337
  524.4 6.8 %fusion.34 = bf16[256,1024]{1,0:T(8,128)(2,1)} fusion(f32[256,1024]{1,0:T(8,128)S(1)} %get-tuple-element.31, f32[256,1024]{1,0:T(8,128)S(1)} %fusion.28, bf16[16,256,1024]{2,1,0:T(8,128)(2,1)} %bitcast.47, f32[16,256]{1,0:T(8,128)S(1)} %broadcast_in_dim.95, s32[16,256]{1,0:T(8,128)S(1)} %eq.64), kind=kOutput, calls=%fused_computation.44 | convolution fusion | flops 2150367232 | bytes 11042816 | tf_op jit(solution)/shard_map/ect,ecd->td/dot_general | solution.py:335
  (98 shorter events, 79.7 us)
Async XLA Ops:
  7.2 211.7 %copy-start = (bf16[1024,1024]{1,0:T(8,128)(2,1)S(1)}, bf16[1024,1024]{1,0:T(8,128)(2,1)}, u32[]{:S(2)}) copy-start(bf16[1024,1024]{1,0:T(8,128)(2,1)} %param.18) | copy-start | bytes 6291460
  7.2 35.2 %all-gather.4.cloned.1.call-start = ((), (), s32[]{:S(2)}) async-start(), calls=%async_computation.7 | async-start | bytes 1572864 | tf_op jit(solution)/shard_map/all_gather | solution.py:233
  7.9 181.5 %all-gather.6.cloned.1.call-start = ((), (), s32[]{:S(2)}) async-start(), calls=%async_computation.8 | async-start | bytes 7864320 | tf_op jit(solution)/shard_map/all_gather | solution.py:201
  13.2 92.6 %all-to-all-start = ((bf16[2,2,2,256,8,128]{5,4,3,1,0,2:T(8,128)(2,1)}), bf16[2,2,2,256,8,128]{5,4,3,1,0,2:T(8,128)(2,1)}, u32[]{:S(2)}, u32[]{:S(2)}) async-start(bf16[2,2,2,256,8,128]{5,4,3,1,0,2:T(8,128)(2,1)} %copy.157), calls=%async_computation | async-start | bytes 8388608 | tf_op jit(solution)/shard_map/all_to_all | solution.py:229
  18.8 7.5 %copy-start.2 = (bf16[2,128,8,128]{3,2,1,0:T(8,128)(2,1)S(1)}, bf16[2,128,8,128]{3,2,1,0:T(8,128)(2,1)}, u32[]{:S(2)}) copy-start(bf16[2,128,8,128]{3,2,1,0:T(8,128)(2,1)} %param.14) | copy-start | bytes 1572868
  18.8 8.5 %copy-start.3 = (s32[256,8]{0,1:T(8,128)S(1)}, s32[256,8]{0,1:T(8,128)}, u32[]{:S(2)}) copy-start(s32[256,8]{0,1:T(8,128)} %param.20) | copy-start | bytes 24580
  18.8 9.3 %copy-start.6 = (s32[2,128]{1,0:T(2,128)S(1)}, s32[2,128]{1,0:T(2,128)}, u32[]{:S(2)}) copy-start(s32[2,128]{1,0:T(2,128)} %param.23) | copy-start | bytes 3076
  18.8 9.4 %copy-start.7 = (s32[32]{0:T(128)S(1)}, s32[32]{0:T(128)}, u32[]{:S(2)}) copy-start(s32[32]{0:T(128)} %param.16) | copy-start | bytes 388
  18.9 12.1 %copy-start.8 = (s32[32]{0:T(128)S(1)}, s32[32]{0:T(128)}, u32[]{:S(2)}) copy-start(s32[32]{0:T(128)} %param.17) | copy-start | bytes 388
  190.1 7.4 %all-to-all-start.2 = ((f32[2,2,128,16,2]{2,3,0,4,1:T(8,128)}), f32[2,2,128,16,2]{2,3,0,4,1:T(8,128)S(1)}, u32[]{:S(2)}, u32[]{:S(2)}) async-start(f32[2,2,128,16,2]{2,3,0,4,1:T(8,128)} %copy.168), calls=%async_computation.2 | async-start | bytes 131072 | tf_op jit(solution)/shard_map/all_to_all | solution.py:262
  197.5 13.0 %all-to-all-start.1 = ((bf16[2,2,128,1024]{2,3,0,1:T(8,128)(2,1)}), bf16[2,2,128,1024]{2,3,0,1:T(8,128)(2,1)S(1)}, u32[]{:S(2)}, u32[]{:S(2)}) async-start(bf16[2,2,128,1024]{2,3,0,1:T(8,128)(2,1)} %copy.166), calls=%async_computation.1 | async-start | bytes 2097152 | tf_op jit(solution)/shard_map/all_to_all | solution.py:258
  211.1 14.8 %all-to-all-start.5 = ((s32[32,1,8]{2,1,0:T(1,128)}), s32[32,1,8]{2,1,0:T(1,128)S(1)}, u32[]{:S(2)}, u32[]{:S(2)}) async-start(s32[32,1,8]{2,1,0:T(1,128)} %bitcast.51), calls=%async_computation.5 | async-start | bytes 32768 | tf_op jit(solution)/shard_map/all_to_all | solution.py:225
  215.9 4.8 copy-start.5
  225.9 98.1 %all-to-all-start.3 = ((bf16[8,512,1024]{2,1,0:T(8,128)(2,1)}), bf16[8,512,1024]{2,1,0:T(8,128)(2,1)}, u32[]{:S(2)}, u32[]{:S(2)}) async-start(bf16[8,512,1024]{2,1,0:T(8,128)(2,1)} %bitcast.202), calls=%async_computation.3 | async-start | bytes 16777216 | tf_op jit(solution)/shard_map/all_to_all | solution.py:313
  324.0 96.3 %all-to-all-start.6 = ((bf16[32,8,4,16,128]{4,3,2,1,0:T(8,128)(2,1)}), bf16[32,8,4,16,128]{4,3,2,1,0:T(8,128)(2,1)}, u32[]{:S(2)}, u32[]{:S(2)}) async-start(bf16[32,8,4,16,128]{4,3,2,1,0:T(8,128)(2,1)} %bitcast.203), calls=%async_computation.6 | async-start | bytes 8388608 | tf_op jit(solution)/shard_map/all_to_all | solution.py:224
  420.3 5.4 %copy-start.4 = (f32[256,8]{0,1:T(8,128)S(1)}, f32[256,8]{0,1:T(8,128)}, u32[]{:S(2)}) copy-start(f32[256,8]{0,1:T(8,128)} %param.21) | copy-start | bytes 24580
  420.3 98.3 %all-to-all-start.4 = ((bf16[8,512,1024]{2,1,0:T(8,128)(2,1)}), bf16[8,512,1024]{2,1,0:T(8,128)(2,1)}, u32[]{:S(2)}, u32[]{:S(2)}) async-start(bf16[8,512,1024]{2,1,0:T(8,128)(2,1)} %bitcast.201), calls=%async_computation.4 | async-start | bytes 16777216 | tf_op jit(solution)/shard_map/all_to_all | solution.py:328
  524.4 6.8 %copy-start.1 = (bf16[1024,1024]{1,0:T(8,128)(2,1)S(1)}, bf16[1024,1024]{1,0:T(8,128)(2,1)}, u32[]{:S(2)}) copy-start(bf16[1024,1024]{1,0:T(8,128)(2,1)} %param.18) | copy-start | bytes 6291460
Sparse Core Ops, SparseCore 0:
  9.6 32.7 all-gather.3
  44.2 118.8 all-gather.5

commit v8 on v7

--- a/solution.py
+++ b/solution.py
@@ -80,25 +80,25 @@
             return keys, first + key_col < length, s
 
         m = jnp.full((span, 1), -1e30, jnp.float32)
+        acc = jnp.zeros((span, lanes), jnp.float32)
+
+        def update(m, acc, ok, s, vals):
+            m_new = jnp.maximum(m, jnp.max(jnp.where(ok, s, -1e30), axis=1, keepdims=True))
+            p = jnp.where(ok, jnp.exp(s - m_new), 0.0)
+            acc = acc * jnp.exp(m - m_new) + jnp.dot(
+                p.astype(jnp.bfloat16), vals, preferred_element_type=jnp.float32
+            )
+            return m_new, acc
+
         if not received:
             s_span = lax.dot_general(qj, span_keys, dims, preferred_element_type=jnp.float32)
-            m = jnp.maximum(m, jnp.max(jnp.where(causal, s_span, -1e30), axis=1, keepdims=True))
+            m, acc = update(m, acc, causal, s_span, span_vals)
         for n, get in runs:
-            def max_body(i, m, get=get):
-                _, ok, s = scores(get, i)
-                return jnp.maximum(m, jnp.max(jnp.where(ok, s, -1e30), axis=1, keepdims=True))
-            m = lax.fori_loop(0, n, max_body, m)
-        acc = jnp.zeros((span, lanes), jnp.float32)
-        if not received:
-            p_span = jnp.where(causal, jnp.exp(s_span - m), 0.0)
-            acc = acc + jnp.dot(p_span.astype(jnp.bfloat16), span_vals, preferred_element_type=jnp.float32)
-        for n, get in runs:
-            def sum_body(i, acc, get=get):
+            def body_fn(i, carry, get=get):
                 keys, ok, s = scores(get, i)
-                p = jnp.where(ok, jnp.exp(s - m), 0.0)
                 vals = jnp.where(key_lane, jnp.ones_like(keys), keys)
-                return acc + jnp.dot(p.astype(jnp.bfloat16), vals, preferred_element_type=jnp.float32)
-            acc = lax.fori_loop(0, n, sum_body, acc)
+                return update(*carry, ok, s, vals)
+            m, acc = lax.fori_loop(0, n, body_fn, (m, acc))
         total = acc[:, 0:1]
         res = acc / jnp.where(total > 0.0, total, 1.0)
         shift = (j * head_dim - head_dim) % lanes
@@ -236,6 +236,9 @@
     ).astype(jnp.int32)
     own_out, own_stat = attend(q_all, cache, span_kv, meta, piece, kv_count)
     got_out, got_stat = attend(q_all, dealt, None, meta, piece, kv_count)
+    got_out, got_stat, arrived, where_to = lax.optimization_barrier(
+        (got_out, got_stat, arrived, where_to)
+    )
     span_total = q_all.shape[1]
 
     def split_stat(table):
@@ -272,14 +275,6 @@
         axis=1,
     ) / jnp.sum(part_weight, axis=1)[..., None]
     attn = merged.astype(jnp.bfloat16).reshape(row_count, width_model)
-    placement = (
-        where_to.reshape(1, -1) == jnp.arange(slots_dev, dtype=jnp.int32)[:, None]
-    ).astype(jnp.bfloat16)
-    decode_pool = jnp.dot(
-        placement,
-        arrived.reshape(slots_dev, group_count * BLOCK * head_pair),
-        preferred_element_type=jnp.float32,
-    ).astype(jnp.bfloat16).reshape(slots_dev, group_count, BLOCK, head_pair)
     residual = hidden.reshape(row_count, width_model).astype(jnp.float32) + jnp.dot(
         attn, out_weight, preferred_element_type=jnp.float32
     )
@@ -335,6 +330,14 @@
     expert_sum = jnp.einsum(
         "ect,ecd->td", combine_hi, returned, preferred_element_type=jnp.float32
     ) + jnp.einsum("ect,ecd->td", combine_lo, returned, preferred_element_type=jnp.float32)
+    placement = (
+        where_to.reshape(1, -1) == jnp.arange(slots_dev, dtype=jnp.int32)[:, None]
+    ).astype(jnp.bfloat16)
+    decode_pool = jnp.dot(
+        placement,
+        arrived.reshape(slots_dev, group_count * BLOCK * head_pair),
+        preferred_element_type=jnp.float32,
+    ).astype(jnp.bfloat16).reshape(slots_dev, group_count, BLOCK, head_pair)
     layer_out = (
         (residual + expert_sum).astype(jnp.bfloat16).reshape(local_reqs, local_tokens, width_model)
     )

time: 539 us -> 584 us (1.083); the launches traced: 538 us -> 577 us
  waiting for transfers between devices: 212 us -> 286 us
  Pallas kernels: 108 us -> 70.5 us
    pallas_call x2, Pallas kernels: 108 us -> 70.5 us  [attend(): pl.pallas_call(functools.partial(attend_kernel, piece=piece, kv_count=kv_...]
    all_to_all x1, waiting for transfers between devices: 0.01 us -> 34.5 us  [body(): lax.all_to_all(cache.reshape(local_reqs, rounds, kv_count, piece, kv_head...]
    all_to_all x1, waiting for transfers between devices: 46.4 us -> 76.6 us  [body(): lax.all_to_all(outgoing, everyone, split_axis=0, concat_axis=0, tiled=True)]
    all_to_all x1, waiting for transfers between devices: 69.5 us -> 84.3 us  [body(): lax.all_to_all(buffer.reshape(side, per_dev * capacity, width_model), 'rl...]
    all_gather x1, waiting for transfers between devices: 10.6 us -> 0.01 us  [body(): q_all = lax.all_gather(queries, 'kv', axis=1, tiled=True)]
  transfers between devices with their start and end apart: 9 -> 9, of which waited for: 6 -> 7; matrix products, arithmetic and copies ran while one was open for 29% -> 18% of each run, Pallas kernels for 20% -> 12%
where the time goes in v8:
time: 584 us; the launch traced here: 577 us
  waiting for transfers between devices  286 us (49%)
  local copies, waits for them, and re-layouts  98.1 us (17%)
  Pallas kernels  70.5 us (12%)
  matrix products  51.5 us (9%)
  starting transfers between devices  34.8 us (6%)
  other arithmetic  21.4 us (4%)
  between operations  14.4 us (2%)
    all_to_all x1, waiting for transfers between devices, body(): lax.all_to_all(buffer.reshape(side, per_dev * capacity, width_model), 'rl...  84.3 us
    all_to_all x1, waiting for transfers between devices, body(): lax.all_to_all(expert_out.reshape(side, per_dev * capacity, width_model),...  78.7 us
    all_to_all x1, waiting for transfers between devices, body(): lax.all_to_all(outgoing, everyone, split_axis=0, concat_axis=0, tiled=True)  76.6 us
    pallas_call x2, Pallas kernels, attend(): pl.pallas_call(functools.partial(attend_kernel, piece=piece, kv_count=kv_...  70.5 us
    all_to_all x1, waiting for transfers between devices, body(): lax.all_to_all(cache.reshape(local_reqs, rounds, kv_count, piece, kv_head...  34.5 us
    dot_general x1, matrix products, body(): jnp.einsum('szjckf,zkjdf->szjcd', activated, weights[:, :, :, 2], preferr...  16.6 us
    reshape x2, local copies, waits for them, and re-layouts, attend(): k2 = keys.reshape(local_reqs, rounds, kv_count, piece, kv_heads * lanes)  12 us
    dot_general x1, matrix products, body(): jnp.einsum('szjcd,zkjdf->szjckf', grouped, weights[:, :, :, 1], preferred...  11.8 us
  transfers between devices with their start and end apart: 9, of which 7 were waited for; matrix products, arithmetic and copies ran while one was open for 18% of the time, Pallas kernels for 12%

profile of v8, /device:TPU:16, one launch (start us, length us, event | category | flops | bytes accessed | tf_op | source)
XLA Modules:
  0.0 576.7 jit_solution(2322739846726026314)
XLA Ops:
  12.7 5.9 %all-to-all-start.2 = ((s32[32,1,8]{2,1,0:T(1,128)}), s32[32,1,8]{2,1,0:T(1,128)S(1)}, u32[]{:S(2)}, u32[]{:S(2)}) async-start(s32[32,1,8]{2,1,0:T(1,128)} %bitcast.10), calls=%async_computation.2 | async-start | bytes 32768 | tf_op jit(solution)/shard_map/all_to_all | solution.py:225
  23.5 5.6 all-to-all-start
  30.2 9.2 %broadcast_select_fusion = bf16[2,1024,8,128]{3,2,1,0:T(8,128)(2,1)S(1)} fusion(bf16[2,1024,8,128]{3,2,1,0:T(8,128)(2,1)} %param.15, pred[2,1024]{1,0:T(4,128)(4,1)S(1)} %broadcast_compare_fusion), kind=kLoop, calls=%fused_computation.22 | loop fusion | flops 2097152 | bytes 8390656 | tf_op jit(solution)/shard_map/jit(_where)/select_n | solution.py:205
  48.0 5.6 copy.160
  53.6 34.5 %all-to-all-done = bf16[2,2,2,256,8,128]{5,4,3,1,0,2:T(8,128)(2,1)} async-done(((bf16[2,2,2,256,8,128]{5,4,3,1,0,2:T(8,128)(2,1)}), bf16[2,2,2,256,8,128]{5,4,3,1,0,2:T(8,128)(2,1)}, u32[]{:S(2)}, u32[]{:S(2)}) %all-to-all-start) | async-done | bytes 4194336 | tf_op jit(solution)/shard_map/all_to_all | solution.py:229
  88.1 5.6 all-to-all-start.1
  94.4 7.3 %reshape.181.c_ref = bf16[2,1024,1024]{2,1,0:T(8,128)(2,1)} reshape(bf16[2,1024,8,128]{3,2,1,0:T(8,128)(2,1)} %param.15) | data formatting | bytes 8388608 | tf_op jit(solution)/shard_map/reshape | solution.py:132
  104.2 47.3 %shard_map.131 = (f32[2,256,1024]{2,1,0:T(8,128)}, f32[2,256,1024]{2,1,0:T(8,128)}) custom-call(s32[4]{0:T(128)} %pad_add_fusion.meta_ref, bf16[2,256,1024]{2,1,0:T(8,128)(2,1)} %all-gather.4.cloned.1.call-done.q_ref, bf16[2,1024,1024]{2,1,0:T(8,128)(2,1)} %reshape.181.c_ref, bf16[2,128,1024]{2,1,0:T(8,128)(2,1)} %reshape.182.rest_0_), custom_call_target="tpu_custom_call" | custom-call | flops 4026531840 | bytes 9961472 | tf_op jit(solution)/shard_map/pallas_call | solution.py:142
  155.5 7.3 %reshape.239 = bf16[2,2,2,256,1024]{4,3,1,0,2:T(8,128)(2,1)} reshape(bf16[2,2,2,256,8,128]{5,4,3,1,0,2:T(8,128)(2,1)} %all-to-all-done) | data formatting | bytes 8388608 | tf_op jit(solution)/shard_map/reshape | solution.py:125
  167.5 23.3 %shard_map.132 = (f32[2,256,1024]{2,1,0:T(8,128)}, f32[2,256,1024]{2,1,0:T(8,128)}) custom-call(s32[4]{0:T(128)} %pad_add_fusion.meta_ref, bf16[2,256,1024]{2,1,0:T(8,128)(2,1)} %all-gather.4.cloned.1.call-done.q_ref, bf16[2,2,2,256,1024]{4,3,2,1,0:T(8,128)(2,1)} %copy.195.c_ref), custom_call_target="tpu_custom_call" | custom-call | flops 3221225472 | bytes 9437184 | tf_op jit(solution)/shard_map/pallas_call | solution.py:142
  190.7 76.6 %all-to-all-done.1 = bf16[32,8,4,16,128]{4,3,2,1,0:T(8,128)(2,1)} async-done(((bf16[32,8,4,16,128]{4,3,2,1,0:T(8,128)(2,1)}), bf16[32,8,4,16,128]{4,3,2,1,0:T(8,128)(2,1)}, u32[]{:S(2)}, u32[]{:S(2)}) %all-to-all-start.1) | async-done | bytes 4194336 | tf_op jit(solution)/shard_map/all_to_all | solution.py:224
  284.8 5.2 divide_convert_fusion
  305.8 7.6 %all-to-all-done.3 = bf16[2,2,128,1024]{2,3,0,1:T(8,128)(2,1)S(1)} async-done(((bf16[2,2,128,1024]{2,3,0,1:T(8,128)(2,1)}), bf16[2,2,128,1024]{2,3,0,1:T(8,128)(2,1)S(1)}, u32[]{:S(2)}, u32[]{:S(2)}) %all-to-all-start.3) | async-done | bytes 1048608 | tf_op jit(solution)/shard_map/all_to_all | solution.py:261
  319.4 5.2 convolution_convert_fusion.1
  329.8 8.6 %copy.180 = bf16[4,1,3,1024,256]{3,4,0,2,1:T(8,128)(2,1)} copy(bf16[4,1,3,1024,256]{4,3,2,0,1:T(8,128)(2,1)} %bitcast.211) | data formatting | bytes 12582912 | tf_op jit(solution)/shard_map/optimization_barrier | solution.py:260
  338.4 84.3 %all-to-all-done.5 = bf16[8,512,1024]{2,1,0:T(8,128)(2,1)} async-done(((bf16[8,512,1024]{2,1,0:T(8,128)(2,1)}), bf16[8,512,1024]{2,1,0:T(8,128)(2,1)}, u32[]{:S(2)}, u32[]{:S(2)}) %all-to-all-start.5) | async-done | bytes 8388640 | tf_op jit(solution)/shard_map/all_to_all | solution.py:308
  422.7 11.8 %fusion.5 = f32[2,2,256,8,256]{4,2,3,1,0:T(8,128)} fusion(bf16[8,2,256,1024,1]{3,2,1,0,4:T(8,128)(2,1)} %bitcast.39, bf16[2,2,1,3,1024,256]{4,5,1,0,3,2:T(8,128)(2,1)} %bitcast.212), kind=kOutput, calls=%fused_computation.12 | convolution fusion | flops 4294967296 | bytes 18874368 | tf_op jit(solution)/shard_map/szjcd,zkjdf->szjckf/dot_general | solution.py:316
  434.5 16.6 %fusion = bf16[8,2,1,256,1024]{4,3,0,1,2:T(8,128)(2,1)} fusion(f32[2,2,256,8,256]{4,2,3,1,0:T(8,128)} %fusion.5, bf16[2,2,1,3,1024,256]{4,5,1,0,3,2:T(8,128)(2,1)} %bitcast.213, bf16[8,2,256,1024,1]{3,2,1,0,4:T(8,128)(2,1)} %bitcast.39), kind=kOutput, calls=%fused_computation.4 | convolution fusion | flops 8606711808 | bytes 29360128 | tf_op jit(solution)/shard_map/szjckf,zkjdf->szjcd/dot_general | solution.py:320
  451.1 7.9 %copy.186 = bf16[8,2,1,256,1024]{4,3,1,0,2:T(8,128)(2,1)} copy(bf16[8,2,1,256,1024]{4,3,0,1,2:T(8,128)(2,1)} %fusion) | data formatting | bytes 16777216 | tf_op jit(solution)/shard_map/convert_element_type | solution.py:322
  459.1 5.4 all-to-all-start.6
  464.7 7.3 %reshape.208 = bf16[256,8192]{1,0:T(8,128)(2,1)} reshape(bf16[32,8,4,16,128]{4,3,2,1,0:T(8,128)(2,1)} %all-to-all-done.1) | data formatting | bytes 8388608 | tf_op jit(solution)/shard_map/reshape | solution.py:338
  478.6 78.7 %all-to-all-done.6 = bf16[8,512,1024]{2,1,0:T(8,128)(2,1)} async-done(((bf16[8,512,1024]{2,1,0:T(8,128)(2,1)}), bf16[8,512,1024]{2,1,0:T(8,128)(2,1)}, u32[]{:S(2)}, u32[]{:S(2)}) %all-to-all-start.6) | async-done | bytes 8388640 | tf_op jit(solution)/shard_map/all_to_all | solution.py:323
  557.3 5.7 fusion.28
  563.1 6.8 %fusion.34 = bf16[256,1024]{1,0:T(8,128)(2,1)} fusion(f32[256,1024]{1,0:T(8,128)S(1)} %get-tuple-element.39, f32[256,1024]{1,0:T(8,128)S(1)} %fusion.28, bf16[16,256,1024]{2,1,0:T(8,128)(2,1)} %bitcast.55, f32[16,256]{1,0:T(8,128)S(1)} %broadcast_in_dim.100, s32[16,256]{1,0:T(8,128)S(1)} %eq.64), kind=kOutput, calls=%fused_computation.44 | convolution fusion | flops 2150367232 | bytes 11042816 | tf_op jit(solution)/shard_map/ect,ecd->td/dot_general | solution.py:330
  (97 shorter events, 82.9 us)
Async XLA Ops:
  7.2 310.4 %copy-start = (bf16[1024,1024]{1,0:T(8,128)(2,1)S(1)}, bf16[1024,1024]{1,0:T(8,128)(2,1)}, u32[]{:S(2)}) copy-start(bf16[1024,1024]{1,0:T(8,128)(2,1)} %param.18) | copy-start | bytes 6291460
  12.7 10.9 %all-to-all-start.2 = ((s32[32,1,8]{2,1,0:T(1,128)}), s32[32,1,8]{2,1,0:T(1,128)S(1)}, u32[]{:S(2)}, u32[]{:S(2)}) async-start(s32[32,1,8]{2,1,0:T(1,128)} %bitcast.10), calls=%async_computation.2 | async-start | bytes 32768 | tf_op jit(solution)/shard_map/all_to_all | solution.py:225
  23.1 6.7 %copy-start.7 = (s32[32]{0:T(128)S(1)}, s32[32]{0:T(128)}, u32[]{:S(2)}) copy-start(s32[32]{0:T(128)} %param.16) | copy-start | bytes 388
  23.1 6.8 %copy-start.8 = (s32[32]{0:T(128)S(1)}, s32[32]{0:T(128)}, u32[]{:S(2)}) copy-start(s32[32]{0:T(128)} %param.17) | copy-start | bytes 388
  23.5 64.6 %all-to-all-start = ((bf16[2,2,2,256,8,128]{5,4,3,1,0,2:T(8,128)(2,1)}), bf16[2,2,2,256,8,128]{5,4,3,1,0,2:T(8,128)(2,1)}, u32[]{:S(2)}, u32[]{:S(2)}) async-start(bf16[2,2,2,256,8,128]{5,4,3,1,0,2:T(8,128)(2,1)} %copy.157), calls=%async_computation | async-start | bytes 8388608 | tf_op jit(solution)/shard_map/all_to_all | solution.py:229
  29.1 75.1 %all-gather.4.cloned.1.call-start = ((), (), s32[]{:S(2)}) async-start(), calls=%async_computation.7 | async-start | bytes 1572864 | tf_op jit(solution)/shard_map/all_gather | solution.py:233
  88.1 179.2 %all-to-all-start.1 = ((bf16[32,8,4,16,128]{4,3,2,1,0:T(8,128)(2,1)}), bf16[32,8,4,16,128]{4,3,2,1,0:T(8,128)(2,1)}, u32[]{:S(2)}, u32[]{:S(2)}) async-start(bf16[32,8,4,16,128]{4,3,2,1,0:T(8,128)(2,1)} %bitcast.204), calls=%async_computation.1 | async-start | bytes 8388608 | tf_op jit(solution)/shard_map/all_to_all | solution.py:224
  93.7 196.4 %all-gather.6.cloned.1.call-start = ((), (), s32[]{:S(2)}) async-start(), calls=%async_computation.8 | async-start | bytes 7864320 | tf_op jit(solution)/shard_map/all_gather | solution.py:201
  94.4 7.4 %copy-start.3 = (s32[256,8]{0,1:T(8,128)S(1)}, s32[256,8]{0,1:T(8,128)}, u32[]{:S(2)}) copy-start(s32[256,8]{0,1:T(8,128)} %param.20) | copy-start | bytes 24580
  94.4 8.2 %copy-start.2 = (bf16[2,128,8,128]{3,2,1,0:T(8,128)(2,1)S(1)}, bf16[2,128,8,128]{3,2,1,0:T(8,128)(2,1)}, u32[]{:S(2)}) copy-start(bf16[2,128,8,128]{3,2,1,0:T(8,128)(2,1)} %param.14) | copy-start | bytes 1572868
  102.6 48.9 %copy-start.5 = (s32[16,3]{0,1:T(4,128)}, s32[16,3]{0,1:T(4,128)S(1)}, u32[]{:S(2)}) copy-start(s32[16,3]{0,1:T(4,128)S(1)} %reduce-window.9) | copy-start | bytes 580
  284.8 9.3 %slice-start = ((s32[16,3]{0,1:T(4,128)}), s32[16,2]{0,1:T(2,128)S(1)}, s32[]{:S(2)}) async-start(s32[16,3]{0,1:T(4,128)} %copy-done.5), calls=%async_computation.9 | async-start | bytes 2048 | tf_op jit(solution)/shard_map/slice.1
  290.8 7.4 %all-to-all-start.4 = ((f32[2,2,128,16,2]{2,3,0,4,1:T(8,128)}), f32[2,2,128,16,2]{2,3,0,4,1:T(8,128)S(1)}, u32[]{:S(2)}, u32[]{:S(2)}) async-start(f32[2,2,128,16,2]{2,3,0,4,1:T(8,128)} %copy.170), calls=%async_computation.4 | async-start | bytes 131072 | tf_op jit(solution)/shard_map/all_to_all | solution.py:265
  298.2 15.2 %all-to-all-start.3 = ((bf16[2,2,128,1024]{2,3,0,1:T(8,128)(2,1)}), bf16[2,2,128,1024]{2,3,0,1:T(8,128)(2,1)S(1)}, u32[]{:S(2)}, u32[]{:S(2)}) async-start(bf16[2,2,128,1024]{2,3,0,1:T(8,128)(2,1)} %copy.168), calls=%async_computation.3 | async-start | bytes 2097152 | tf_op jit(solution)/shard_map/all_to_all | solution.py:261
  314.6 4.8 copy-start.6
  324.7 98.1 %all-to-all-start.5 = ((bf16[8,512,1024]{2,1,0:T(8,128)(2,1)}), bf16[8,512,1024]{2,1,0:T(8,128)(2,1)}, u32[]{:S(2)}, u32[]{:S(2)}) async-start(bf16[8,512,1024]{2,1,0:T(8,128)(2,1)} %bitcast.203), calls=%async_computation.5 | async-start | bytes 16777216 | tf_op jit(solution)/shard_map/all_to_all | solution.py:308
  459.1 5.4 copy-start.4
  459.1 98.3 %all-to-all-start.6 = ((bf16[8,512,1024]{2,1,0:T(8,128)(2,1)}), bf16[8,512,1024]{2,1,0:T(8,128)(2,1)}, u32[]{:S(2)}, u32[]{:S(2)}) async-start(bf16[8,512,1024]{2,1,0:T(8,128)(2,1)} %bitcast.202), calls=%async_computation.6 | async-start | bytes 16777216 | tf_op jit(solution)/shard_map/all_to_all | solution.py:323
  563.1 6.8 %copy-start.1 = (bf16[1024,1024]{1,0:T(8,128)(2,1)S(1)}, bf16[1024,1024]{1,0:T(8,128)(2,1)}, u32[]{:S(2)}) copy-start(bf16[1024,1024]{1,0:T(8,128)(2,1)} %param.18) | copy-start | bytes 6291460
Sparse Core Ops, SparseCore 0:
  31.5 33.8 all-gather.3
  96.3 189.3 all-gather.5

commit v9 on v5

--- a/solution.py
+++ b/solution.py
@@ -54,29 +54,33 @@
             s = lax.dot_general(qj, keys, dims, preferred_element_type=jnp.float32)
             return keys, s
 
-        def max_body(kb, m):
-            _, s = block(kb)
-            return jnp.maximum(m, jnp.max(s, axis=1, keepdims=True))
+        def update(m, acc, ok, s, vals):
+            if ok is None:
+                m_new = jnp.maximum(m, jnp.max(s, axis=1, keepdims=True))
+                p = jnp.exp(s - m_new)
+            else:
+                m_new = jnp.maximum(m, jnp.max(jnp.where(ok, s, -1e30), axis=1, keepdims=True))
+                p = jnp.where(ok, jnp.exp(s - m_new), 0.0)
+            acc = acc * jnp.exp(m - m_new) + jnp.dot(
+                p.astype(jnp.bfloat16), vals, preferred_element_type=jnp.float32
+            )
+            return m_new, acc
+
+        def values(keys):
+            return jnp.where(key_lane, jnp.ones_like(keys), keys)
 
         s_span = lax.dot_general(qj, span_keys, dims, preferred_element_type=jnp.float32)
-        m = jnp.max(jnp.where(causal, s_span, -1e30), axis=1, keepdims=True)
-        m = lax.fori_loop(0, full, max_body, m)
-        _, s_tail = block(tail)
-        m = jnp.maximum(m, jnp.max(jnp.where(tail_ok, s_tail, -1e30), axis=1, keepdims=True))
-
-        def accumulate(acc, p, keys):
-            vals = jnp.where(key_lane, jnp.ones_like(keys), keys)
-            return acc + jnp.dot(p.astype(jnp.bfloat16), vals, preferred_element_type=jnp.float32)
-
-        def sum_body(kb, acc):
+        m = jnp.full((span, 1), -1e30, jnp.float32)
+        acc = jnp.zeros((span, lanes), jnp.float32)
+        m, acc = update(m, acc, causal, s_span, span_vals)
+
+        def full_body(kb, carry):
             keys, s = block(kb)
-            return accumulate(acc, jnp.exp(s - m), keys)
-
-        p_span = jnp.where(causal, jnp.exp(s_span - m), 0.0)
-        acc = jnp.dot(p_span.astype(jnp.bfloat16), span_vals, preferred_element_type=jnp.float32)
-        acc = lax.fori_loop(0, full, sum_body, acc)
+            return update(*carry, None, s, values(keys))
+
+        m, acc = lax.fori_loop(0, full, full_body, (m, acc))
         keys_tail, s_tail = block(tail)
-        acc = accumulate(acc, jnp.where(tail_ok, jnp.exp(s_tail - m), 0.0), keys_tail)
+        m, acc = update(m, acc, tail_ok, s_tail, values(keys_tail))
         total = acc[:, 0:1]
         res = acc / total
         shift = (j * head_dim - head_dim) % lanes
@@ -155,7 +159,9 @@
         lax.all_to_all(queries_grouped, "kv", split_axis=2, concat_axis=1, tiled=True),
     )
     pair_weights = lax.all_gather(w_experts, "zhi", axis=0, tiled=False)
-    pair_weights, cache_heads = lax.optimization_barrier((pair_weights, cache_heads))
+    pair_weights, cache_heads, block_map = lax.optimization_barrier(
+        (pair_weights, cache_heads, block_map)
+    )
     full_weights = lax.all_gather(pair_weights, "kv", axis=1, tiled=False)
     page_total = block_map.shape[1]
     visible = jnp.arange(cache_heads.shape[1])[None, :] < lengths[:, None]

time: 520 us -> 504 us (0.969)
  waiting for transfers between devices: 196 us -> 180 us
    all_to_all x1, waiting for transfers between devices: 29 us -> 0.01 us  [body(): lax.all_to_all(local_slot.reshape(req_count, per_owner), REQ, split_axis=...]
    all_gather x1, waiting for transfers between devices: 0.01 us -> 6.18 us  [body(): pair_weights = lax.all_gather(w_experts, 'zhi', axis=0, tiled=False)]
    all_to_all x1, waiting for transfers between devices: 0.01 us -> 5.59 us  [body(): lax.all_to_all(span_kv, 'kv', split_axis=2, concat_axis=1, tiled=True)]
  transfers between devices with their start and end apart: 9 -> 9, of which waited for: 6 -> 7; matrix products, arithmetic and copies ran while one was open for 14% -> 14% of each run, Pallas kernels for 8% -> 9%
where the time goes in v9:
time: 504 us; the launch traced here: 500 us
  waiting for transfers between devices  180 us (36%)
  blocking collectives  97.2 us (19%)
  local copies, waits for them, and re-layouts  67 us (13%)
  matrix products  46 us (9%)
  Pallas kernels  43.4 us (9%)
  starting transfers between devices  35.4 us (7%)
  other arithmetic  16.8 us (3%)
  between operations  14.3 us (3%)
    all_to_all x1, blocking collectives, body(): lax.all_to_all(buffer.reshape(side, per_dev * capacity, width_model), 'rl...  97.2 us
    all_to_all x1, waiting for transfers between devices, body(): lax.all_to_all(expert_out.reshape(side, per_dev * capacity, width_model),...  79 us
    all_to_all x1, waiting for transfers between devices, body(): lax.all_to_all(cache, 'kv', split_axis=2, concat_axis=1, tiled=True)  46.3 us
    pallas_call x1, Pallas kernels, attend(): pl.pallas_call(functools.partial(attend_kernel, tk=tk, head_dim=head_dim)...  43.4 us
    all_gather x1, waiting for transfers between devices, body(): full_weights = lax.all_gather(pair_weights, 'kv', axis=1, tiled=False)  24.8 us
    unnamed x27, local copies, waits for them, and re-layouts  16.4 us
    dot_general x1, matrix products, body(): jnp.einsum('szjckf,zkjdf->szjcd', activated, weights[:, :, :, 2], preferr...  16.4 us
    select_n x1, other arithmetic, body(): jnp.where(visible[:, :, None, None], cache_heads, jnp.zeros((), jnp.bfloa...  12.5 us
  transfers between devices with their start and end apart: 9, of which 7 were waited for; matrix products, arithmetic and copies ran while one was open for 14% of the time, Pallas kernels for 9%

profile of v9, /device:TPU:16, one launch (start us, length us, event | category | flops | bytes accessed | tf_op | source)
XLA Modules:
  0.0 500.0 jit_solution(4655790925219717837)
XLA Ops:
  10.0 5.0 %copy.87 = bf16[2,1024,8,128]{3,1,0,2:T(8,128)(2,1)} copy(bf16[2,1024,8,128]{3,2,1,0:T(8,128)(2,1)} %param.15) | data formatting | bytes 8388608 | tf_op args[3]
  15.0 6.0 %all-to-all-start.1 = ((bf16[2,1024,8,128]{3,1,0,2:T(8,128)(2,1)}), bf16[2,1024,8,128]{3,1,0,2:T(8,128)(2,1)}, u32[]{:S(2)}, u32[]{:S(2)}) async-start(bf16[2,1024,8,128]{3,1,0,2:T(8,128)(2,1)} %copy.87), calls=%async_computation.1 | async-start | bytes 8388608 | tf_op jit(solution)/shard_map/all_to_all | solution.py:157
  22.4 46.3 %all-to-all-done.1 = bf16[2,1024,8,128]{3,1,0,2:T(8,128)(2,1)} async-done(((bf16[2,1024,8,128]{3,1,0,2:T(8,128)(2,1)}), bf16[2,1024,8,128]{3,1,0,2:T(8,128)(2,1)}, u32[]{:S(2)}, u32[]{:S(2)}) %all-to-all-start.1) | async-done | bytes 4194336 | tf_op jit(solution)/shard_map/all_to_all | solution.py:157
  74.2 7.5 %copy.88 = bf16[2,2,1024,4,128]{4,3,2,1,0:T(4,128)(2,1)} copy(bf16[2,2,1024,4,128]{4,2,0,3,1:T(8,128)(2,1)} %bitcast.7) | data formatting | bytes 8388608 | tf_op jit(solution)/shard_map/all_to_all | solution.py:157
  81.6 6.2 %all-gather.5.cloned.1.call-done = bf16[2,3,1024,256]{2,3,0,1:T(8,128)(2,1)} async-done(((bf16[1,3,1024,256]{2,3,0,1:T(8,128)(2,1)}), bf16[2,3,1024,256]{2,3,0,1:T(8,128)(2,1)}) %all-gather.5.cloned.1.call-update) | async-done | bytes 3145744 | tf_op jit(solution)/shard_map/all_gather | solution.py:161
  97.2 5.6 %all-to-all-done.2 = bf16[2,128,8,128]{3,1,0,2:T(8,128)(2,1)S(1)} async-done(((bf16[2,128,8,128]{3,1,0,2:T(8,128)(2,1)}), bf16[2,128,8,128]{3,1,0,2:T(8,128)(2,1)S(1)}, u32[]{:S(2)}, u32[]{:S(2)}) %all-to-all-start.2) | async-done | bytes 524320 | tf_op jit(solution)/shard_map/all_to_all | solution.py:158
  102.8 7.3 %all-to-all-start.4 = ((s32[16,1,16]{2,1,0:T(1,128)}), s32[16,1,16]{2,1,0:T(1,128)S(1)}, u32[]{:S(2)}, u32[]{:S(2)}) async-start(s32[16,1,16]{2,1,0:T(1,128)} %all_to_all.74), calls=%async_computation.4 | async-start | bytes 16384 | tf_op jit(solution)/shard_map/all_to_all | solution.py:179
  110.1 12.5 %broadcast_select_fusion = bf16[2,2048,4,128]{3,2,1,0:T(4,128)(2,1)S(1)} fusion(bf16[2,2048,4,128]{3,2,1,0:T(4,128)(2,1)} %bitcast.174, pred[2,2048]{1,0:T(4,128)(4,1)S(1)} %iota_compare_fusion.5), kind=kLoop, calls=%fused_computation.22 | loop fusion | flops 2097152 | bytes 8392704 | tf_op jit(solution)/shard_map/jit(_where)/select_n | solution.py:168
  125.7 5.2 %gather_fusion = bf16[256,4,16,128]{3,2,1,0:T(8,128)(2,1)} fusion(bf16[256,4,16,128]{3,2,1,0:T(8,128)(2,1)} %bitcast.180, s32[1024]{0:T(1024)S(1)} %pad_clamp_fusion), kind=kCustom, calls=%fused_computation | custom fusion | bytes 8389632 | tf_op jit(solution)/shard_map/gather | solution.py:128
  130.9 6.2 %all-to-all-start.3 = ((bf16[16,16,4,16,128]{4,3,2,1,0:T(8,128)(2,1)}), bf16[16,16,4,16,128]{4,3,2,1,0:T(8,128)(2,1)}, u32[]{:S(2)}, u32[]{:S(2)}) async-start(bf16[16,16,4,16,128]{4,3,2,1,0:T(8,128)(2,1)} %bitcast.179), calls=%async_computation.3 | async-start | bytes 8388608 | tf_op jit(solution)/shard_map/all_to_all | solution.py:178
  142.9 7.5 %reshape.146.c_ref = bf16[2,2048,512]{2,1,0:T(8,128)(2,1)} reshape(bf16[2,2048,4,128]{3,2,1,0:T(4,128)(2,1)} %bitcast.175) | data formatting | bytes 8388608 | tf_op jit(solution)/shard_map/reshape | solution.py:100
  150.4 43.4 %shard_map.131 = bf16[2,256,512]{2,1,0:T(8,128)(2,1)} custom-call(s32[2]{0:T(128)} %copy-done.8, bf16[2,256,512]{2,1,0:T(8,128)(2,1)} %reshape.145.q_ref, bf16[2,2048,512]{2,1,0:T(8,128)(2,1)} %reshape.146.c_ref, bf16[2,256,512]{2,1,0:T(8,128)(2,1)} %reshape.147.s_ref), custom_call_target="tpu_custom_call" | custom-call | flops 7247757312 | bytes 5767168 | tf_op jit(solution)/shard_map/pallas_call | solution.py:103
  195.0 24.8 %all-gather.7.cloned.1.call-done = bf16[2,2,3,1024,256]{3,4,1,0,2:T(8,128)(2,1)} async-done(((bf16[2,1,3,1024,256]{3,4,1,0,2:T(8,128)(2,1)}), bf16[2,2,3,1024,256]{3,4,1,0,2:T(8,128)(2,1)}) %all-gather.7.cloned.1.call-update) | async-done | bytes 6291472 | tf_op jit(solution)/shard_map/all_gather | solution.py:165
  219.8 9.9 %all-to-all-done.3 = bf16[16,16,4,16,128]{4,3,2,1,0:T(8,128)(2,1)} async-done(((bf16[16,16,4,16,128]{4,3,2,1,0:T(8,128)(2,1)}), bf16[16,16,4,16,128]{4,3,2,1,0:T(8,128)(2,1)}, u32[]{:S(2)}, u32[]{:S(2)}) %all-to-all-start.3) | async-done | bytes 4194336 | tf_op jit(solution)/shard_map/all_to_all | solution.py:178
  234.7 7.7 %all-to-all-done.5 = bf16[2,256,4,128]{3,2,0,1:T(4,128)(2,1)S(1)} async-done(((bf16[2,256,4,128]{3,2,0,1:T(4,128)(2,1)}), bf16[2,256,4,128]{3,2,0,1:T(4,128)(2,1)S(1)}, u32[]{:S(2)}, u32[]{:S(2)}) %all-to-all-start.5) | async-done | bytes 524320 | tf_op jit(solution)/shard_map/all_to_all | solution.py:187
  249.4 97.2 %all_to_all.90 = bf16[8,512,1024]{2,1,0:T(8,128)(2,1)S(1)} all-to-all(bf16[8,512,1024]{2,1,0:T(8,128)(2,1)S(1)} %bitcast.177), channel_id=1, replica_groups=mesh['zhi'=2,'rlow'=8,'kv'=2] {'rlow'}, dimensions={0} | all-to-all | bytes 16777216 | tf_op jit(solution)/shard_map/all_to_all | solution.py:228
  349.8 8.3 %fusion.7 = f32[2,2,256,8,256]{4,2,3,1,0:T(8,128)} fusion(bf16[8,2,256,1024,1]{3,2,1,0,4:T(8,128)(2,1)S(1)} %bitcast.181, bf16[2,2,1,3,1024,256]{4,5,1,0,3,2:T(8,128)(2,1)} %bitcast.193), kind=kOutput, calls=%fused_computation.14 | convolution fusion | flops 4294967296 | bytes 18874368 | tf_op jit(solution)/shard_map/szjcd,zkjdf->szjckf/dot_general | solution.py:233
  358.1 16.4 %fusion = bf16[8,2,1,256,1024]{4,3,0,1,2:T(8,128)(2,1)} fusion(f32[2,2,256,8,256]{4,2,3,1,0:T(8,128)} %fusion.7, bf16[8,2,256,1024,1]{3,2,1,0,4:T(8,128)(2,1)} %bitcast.182, bf16[2,2,1,3,1024,256]{4,5,1,0,3,2:T(8,128)(2,1)} %bitcast.194), kind=kOutput, calls=%fused_computation.4 | convolution fusion | flops 8606711808 | bytes 29360128 | tf_op jit(solution)/shard_map/szjckf,zkjdf->szjcd/dot_general | solution.py:240
  374.5 7.9 %copy.104 = bf16[8,2,1,256,1024]{4,3,1,0,2:T(8,128)(2,1)} copy(bf16[8,2,1,256,1024]{4,3,0,1,2:T(8,128)(2,1)} %fusion) | data formatting | bytes 16777216 | tf_op jit(solution)/shard_map/convert_element_type | solution.py:242
  382.4 5.1 %all-to-all-start.7 = ((bf16[8,512,1024]{2,1,0:T(8,128)(2,1)}), bf16[8,512,1024]{2,1,0:T(8,128)(2,1)}, u32[]{:S(2)}, u32[]{:S(2)}) async-start(bf16[8,512,1024]{2,1,0:T(8,128)(2,1)} %bitcast.176), calls=%async_computation.7 | async-start | bytes 16777216 | tf_op jit(solution)/shard_map/all_to_all | solution.py:243
  387.6 7.3 %reshape.167 = bf16[256,8192]{1,0:T(8,128)(2,1)} reshape(bf16[16,16,4,16,128]{4,3,2,1,0:T(8,128)(2,1)} %all-to-all-done.3) | data formatting | bytes 8388608 | tf_op jit(solution)/shard_map/reshape | solution.py:195
  401.6 79.0 %all-to-all-done.7 = bf16[8,512,1024]{2,1,0:T(8,128)(2,1)} async-done(((bf16[8,512,1024]{2,1,0:T(8,128)(2,1)}), bf16[8,512,1024]{2,1,0:T(8,128)(2,1)}, u32[]{:S(2)}, u32[]{:S(2)}) %all-to-all-start.7) | async-done | bytes 8388640 | tf_op jit(solution)/shard_map/all_to_all | solution.py:243
  480.6 5.7 %fusion.38 = f32[256,1024]{1,0:T(8,128)S(1)} fusion(bf16[16,256,1024]{2,1,0:T(8,128)(2,1)} %bitcast.50, f32[16,256]{1,0:T(8,128)S(1)} %broadcast_in_dim.76, s32[16,256]{1,0:T(8,128)S(1)} %eq.64), kind=kOutput, calls=%fused_computation.39 | convolution fusion | flops 2153775104 | bytes 9469952 | tf_op jit(solution)/shard_map/ect,ecd->td/dot_general | solution.py:252
  486.4 6.8 %fusion.44 = bf16[256,1024]{1,0:T(8,128)(2,1)} fusion(f32[256,1024]{1,0:T(8,128)S(1)} %get-tuple-element.21, f32[256,1024]{1,0:T(8,128)S(1)} %fusion.38, bf16[16,256,1024]{2,1,0:T(8,128)(2,1)} %bitcast.50, f32[16,256]{1,0:T(8,128)S(1)} %broadcast_in_dim.76, s32[16,256]{1,0:T(8,128)S(1)} %eq.64), kind=kOutput, calls=%fused_computation.44 | convolution fusion | flops 2150367232 | bytes 11042816 | tf_op jit(solution)/shard_map/ect,ecd->td/dot_general | solution.py:250
  (73 shorter events, 51.0 us)
Async XLA Ops:
  7.2 236.9 %copy-start = (bf16[1024,1024]{1,0:T(8,128)(2,1)S(1)}, bf16[1024,1024]{1,0:T(8,128)(2,1)}, u32[]{:S(2)}) copy-start(bf16[1024,1024]{1,0:T(8,128)(2,1)} %param.18) | copy-start | bytes 6291460
  7.2 80.6 %all-gather.5.cloned.1.call-start = ((), (), s32[]{:S(2)}) async-start(), calls=%async_computation.8 | async-start | bytes 4718592 | tf_op jit(solution)/shard_map/all_gather | solution.py:161
  15.0 6.0 %copy-start.3 = (bf16[2,128,1024]{2,1,0:T(8,128)(2,1)S(1)}, bf16[2,128,1024]{2,1,0:T(8,128)(2,1)}, u32[]{:S(2)}) copy-start(bf16[2,128,1024]{2,1,0:T(8,128)(2,1)} %param.13) | copy-start | bytes 1572868
  15.0 7.1 %copy-start.9 = (s32[32]{0:T(128)S(1)}, s32[32]{0:T(128)}, u32[]{:S(2)}) copy-start(s32[32]{0:T(128)} %param.16) | copy-start | bytes 388
  15.0 7.2 %copy-start.10 = (s32[32]{0:T(128)S(1)}, s32[32]{0:T(128)}, u32[]{:S(2)}) copy-start(s32[32]{0:T(128)} %param.17) | copy-start | bytes 388
  15.0 53.6 %all-to-all-start.1 = ((bf16[2,1024,8,128]{3,1,0,2:T(8,128)(2,1)}), bf16[2,1024,8,128]{3,1,0,2:T(8,128)(2,1)}, u32[]{:S(2)}, u32[]{:S(2)}) async-start(bf16[2,1024,8,128]{3,1,0,2:T(8,128)(2,1)} %copy.87), calls=%async_computation.1 | async-start | bytes 8388608 | tf_op jit(solution)/shard_map/all_to_all | solution.py:157
  22.4 59.3 %copy-start.8 = (s32[2]{0:T(128)}, s32[2]{0:T(128)S(1)}, u32[]{:S(2)}) copy-start(s32[2]{0:T(128)S(1)} %fusion.51.len_ref) | copy-start | bytes 28
  68.6 22.4 %all-to-all-start = ((bf16[2,128,8,128]{1,3,0,2:T(8,128)(2,1)}), bf16[2,128,8,128]{1,3,0,2:T(8,128)(2,1)S(1)}, u32[]{:S(2)}, u32[]{:S(2)}) async-start(bf16[2,128,8,128]{1,3,0,2:T(8,128)(2,1)} %copy.83), calls=%async_computation | async-start | bytes 1048576 | tf_op jit(solution)/shard_map/all_to_all | solution.py:159
  74.2 13.6 %copy-start.7 = (s32[2,128]{1,0:T(2,128)S(1)}, s32[2,128]{1,0:T(2,128)}, u32[]{:S(2)}) copy-start(s32[2,128]{1,0:T(2,128)} %param.23) | copy-start | bytes 3076
  91.0 11.8 %all-to-all-start.2 = ((bf16[2,128,8,128]{3,1,0,2:T(8,128)(2,1)}), bf16[2,128,8,128]{3,1,0,2:T(8,128)(2,1)S(1)}, u32[]{:S(2)}, u32[]{:S(2)}) async-start(bf16[2,128,8,128]{3,1,0,2:T(8,128)(2,1)} %copy.89), calls=%async_computation.2 | async-start | bytes 1048576 | tf_op jit(solution)/shard_map/all_to_all | solution.py:158
  102.8 28.1 %all-to-all-start.4 = ((s32[16,1,16]{2,1,0:T(1,128)}), s32[16,1,16]{2,1,0:T(1,128)S(1)}, u32[]{:S(2)}, u32[]{:S(2)}) async-start(s32[16,1,16]{2,1,0:T(1,128)} %all_to_all.74), calls=%async_computation.4 | async-start | bytes 16384 | tf_op jit(solution)/shard_map/all_to_all | solution.py:179
  130.9 6.9 %copy-start.4 = (s32[256,8]{0,1:T(8,128)S(1)}, s32[256,8]{0,1:T(8,128)}, u32[]{:S(2)}) copy-start(s32[256,8]{0,1:T(8,128)} %param.20) | copy-start | bytes 24580
  130.9 98.8 %all-to-all-start.3 = ((bf16[16,16,4,16,128]{4,3,2,1,0:T(8,128)(2,1)}), bf16[16,16,4,16,128]{4,3,2,1,0:T(8,128)(2,1)}, u32[]{:S(2)}, u32[]{:S(2)}) async-start(bf16[16,16,4,16,128]{4,3,2,1,0:T(8,128)(2,1)} %bitcast.179), calls=%async_computation.3 | async-start | bytes 8388608 | tf_op jit(solution)/shard_map/all_to_all | solution.py:178
  137.0 82.8 %all-gather.7.cloned.1.call-start = ((), (), s32[]{:S(2)}) async-start(), calls=%async_computation.9 | async-start | bytes 9437184 | tf_op jit(solution)/shard_map/all_gather | solution.py:165
  230.7 15.3 %copy-start.6 = (f32[1024]{0:T(1024)S(1)}, f32[1024]{0:T(1024)}, u32[]{:S(2)}) copy-start(f32[1024]{0:T(1024)} %param.19) | copy-start | bytes 12292
  230.7 11.7 %all-to-all-start.5 = ((bf16[2,256,4,128]{3,2,0,1:T(4,128)(2,1)}), bf16[2,256,4,128]{3,2,0,1:T(4,128)(2,1)S(1)}, u32[]{:S(2)}, u32[]{:S(2)}) async-start(bf16[2,256,4,128]{3,2,0,1:T(4,128)(2,1)} %copy.92), calls=%async_computation.5 | async-start | bytes 1048576 | tf_op jit(solution)/shard_map/all_to_all | solution.py:187
  346.6 3.2 copy-start.2
  382.4 5.1 %copy-start.5 = (f32[256,8]{0,1:T(8,128)S(1)}, f32[256,8]{0,1:T(8,128)}, u32[]{:S(2)}) copy-start(f32[256,8]{0,1:T(8,128)} %param.21) | copy-start | bytes 24580
  382.4 98.2 %all-to-all-start.7 = ((bf16[8,512,1024]{2,1,0:T(8,128)(2,1)}), bf16[8,512,1024]{2,1,0:T(8,128)(2,1)}, u32[]{:S(2)}, u32[]{:S(2)}) async-start(bf16[8,512,1024]{2,1,0:T(8,128)(2,1)} %bitcast.176), calls=%async_computation.7 | async-start | bytes 16777216 | tf_op jit(solution)/shard_map/all_to_all | solution.py:243
  486.4 6.8 %copy-start.1 = (bf16[1024,1024]{1,0:T(8,128)(2,1)S(1)}, bf16[1024,1024]{1,0:T(8,128)(2,1)}, u32[]{:S(2)}) copy-start(bf16[1024,1024]{1,0:T(8,128)(2,1)} %param.18) | copy-start | bytes 6291460
Sparse Core Ops, SparseCore 0:
  10.1 77.6 all-gather.4
  139.4 80.3 all-gather.6

commit v10 on v9

--- a/solution.py
+++ b/solution.py
@@ -181,9 +181,7 @@
         ),
     )
     attn_heads = attend(query_heads, cache_heads, span_heads, lengths)
-    attn_heads, full_weights, arrived, where_to = lax.optimization_barrier(
-        (attn_heads, full_weights, arrived, where_to)
-    )
+    attn_heads, arrived, where_to = lax.optimization_barrier((attn_heads, arrived, where_to))
     attn = lax.all_to_all(attn_heads, "kv", split_axis=1, concat_axis=2, tiled=True).reshape(
         row_count, kv_heads * group_width
     )

time: 504 us -> 506 us (level)
  blocking collectives: 97.2 us -> 0 us
  waiting for transfers between devices: 180 us -> 252 us
  Pallas kernels: 43.4 us -> 64.1 us
  matrix products: 46 us -> 51.7 us
  starting transfers between devices: 35.4 us -> 40.7 us
    all_to_all x1 -> x0, blocking collectives: 97.2 us -> none  [body(): lax.all_to_all(buffer.reshape(side, per_dev * capacity, width_model), 'rl...]
    all_gather x1, waiting for transfers between devices: 24.8 us -> 82.5 us  [body(): full_weights = lax.all_gather(pair_weights, 'kv', axis=1, tiled=False)]
    pallas_call x1, Pallas kernels: 43.4 us -> 64.1 us  [attend(): pl.pallas_call(functools.partial(attend_kernel, tk=tk, head_dim=head_dim)...]
    all_to_all x0 -> x1, waiting for transfers between devices: none -> 9.88 us  [body(): lax.all_to_all(buffer.reshape(side, per_dev * capacity, width_model), 'rl...]
    all_to_all x1, waiting for transfers between devices: 9.92 us -> 15 us  [body(): lax.all_to_all(outgoing, REQ, split_axis=0, concat_axis=0, tiled=True)]
    unnamed x27 -> x25, local copies, waits for them, and re-layouts: 16.4 us -> 13.2 us
  transfers between devices with their start and end apart: 9 -> 10, of which waited for: 7 -> 8; matrix products, arithmetic and copies ran while one was open for 14% -> 14% of each run, Pallas kernels for 9% -> 13%
where the time goes in v10:
time: 506 us; the launch traced here: 503 us
  waiting for transfers between devices  252 us (50%)
  Pallas kernels  64.1 us (13%)
  local copies, waits for them, and re-layouts  63.6 us (13%)
  matrix products  51.7 us (10%)
  starting transfers between devices  40.7 us (8%)
  other arithmetic  16.7 us (3%)
  between operations  14.3 us (3%)
    all_gather x1, waiting for transfers between devices, body(): full_weights = lax.all_gather(pair_weights, 'kv', axis=1, tiled=False)  82.5 us
    all_to_all x1, waiting for transfers between devices, body(): lax.all_to_all(expert_out.reshape(side, per_dev * capacity, width_model),...  78.7 us
    pallas_call x1, Pallas kernels, attend(): pl.pallas_call(functools.partial(attend_kernel, tk=tk, head_dim=head_dim)...  64.1 us
    all_to_all x1, waiting for transfers between devices, body(): lax.all_to_all(cache, 'kv', split_axis=2, concat_axis=1, tiled=True)  46.3 us
    dot_general x1, matrix products, body(): jnp.einsum('szjckf,zkjdf->szjcd', activated, weights[:, :, :, 2], preferr...  16.6 us
    all_to_all x1, waiting for transfers between devices, body(): lax.all_to_all(outgoing, REQ, split_axis=0, concat_axis=0, tiled=True)  15 us
    unnamed x25, local copies, waits for them, and re-layouts  13.2 us
    select_n x1, other arithmetic, body(): jnp.where(visible[:, :, None, None], cache_heads, jnp.zeros((), jnp.bfloa...  12.5 us
  transfers between devices with their start and end apart: 10, of which 8 were waited for; matrix products, arithmetic and copies ran while one was open for 14% of the time, Pallas kernels for 13%

profile of v10, /device:TPU:16, one launch (start us, length us, event | category | flops | bytes accessed | tf_op | source)
XLA Modules:
  0.0 503.4 jit_solution(4277692114501313009)
XLA Ops:
  15.0 6.0 %all-to-all-start.1 = ((bf16[2,1024,8,128]{3,1,0,2:T(8,128)(2,1)}), bf16[2,1024,8,128]{3,1,0,2:T(8,128)(2,1)}, u32[]{:S(2)}, u32[]{:S(2)}) async-start(bf16[2,1024,8,128]{3,1,0,2:T(8,128)(2,1)} %copy.87), calls=%async_computation.1 | async-start | bytes 8388608 | tf_op jit(solution)/shard_map/all_to_all | solution.py:157
  22.4 46.3 %all-to-all-done.1 = bf16[2,1024,8,128]{3,1,0,2:T(8,128)(2,1)} async-done(((bf16[2,1024,8,128]{3,1,0,2:T(8,128)(2,1)}), bf16[2,1024,8,128]{3,1,0,2:T(8,128)(2,1)}, u32[]{:S(2)}, u32[]{:S(2)}) %all-to-all-start.1) | async-done | bytes 4194336 | tf_op jit(solution)/shard_map/all_to_all | solution.py:157
  74.1 7.5 %copy.88 = bf16[2,2,1024,4,128]{4,3,2,1,0:T(4,128)(2,1)} copy(bf16[2,2,1024,4,128]{4,2,0,3,1:T(8,128)(2,1)} %bitcast.7) | data formatting | bytes 8388608 | tf_op jit(solution)/shard_map/all_to_all | solution.py:157
  81.6 6.2 %all-gather.5.cloned.1.call-done = bf16[2,3,1024,256]{2,3,0,1:T(8,128)(2,1)} async-done(((bf16[1,3,1024,256]{2,3,0,1:T(8,128)(2,1)}), bf16[2,3,1024,256]{2,3,0,1:T(8,128)(2,1)}) %all-gather.5.cloned.1.call-update) | async-done | bytes 3145744 | tf_op jit(solution)/shard_map/all_gather | solution.py:161
  97.2 5.6 %all-to-all-done.2 = bf16[2,128,8,128]{3,1,0,2:T(8,128)(2,1)S(1)} async-done(((bf16[2,128,8,128]{3,1,0,2:T(8,128)(2,1)}), bf16[2,128,8,128]{3,1,0,2:T(8,128)(2,1)S(1)}, u32[]{:S(2)}, u32[]{:S(2)}) %all-to-all-start.2) | async-done | bytes 524320 | tf_op jit(solution)/shard_map/all_to_all | solution.py:158
  102.7 7.3 %all-to-all-start.4 = ((s32[16,1,16]{2,1,0:T(1,128)}), s32[16,1,16]{2,1,0:T(1,128)S(1)}, u32[]{:S(2)}, u32[]{:S(2)}) async-start(s32[16,1,16]{2,1,0:T(1,128)} %all_to_all.74), calls=%async_computation.4 | async-start | bytes 16384 | tf_op jit(solution)/shard_map/all_to_all | solution.py:179
  110.1 12.5 %broadcast_select_fusion = bf16[2,2048,4,128]{3,2,1,0:T(4,128)(2,1)S(1)} fusion(bf16[2,2048,4,128]{3,2,1,0:T(4,128)(2,1)} %bitcast.174, pred[2,2048]{1,0:T(4,128)(4,1)S(1)} %iota_compare_fusion.5), kind=kLoop, calls=%fused_computation.22 | loop fusion | flops 2097152 | bytes 8392704 | tf_op jit(solution)/shard_map/jit(_where)/select_n | solution.py:168
  125.7 5.2 %gather_fusion = bf16[256,4,16,128]{3,2,1,0:T(8,128)(2,1)} fusion(bf16[256,4,16,128]{3,2,1,0:T(8,128)(2,1)} %bitcast.180, s32[1024]{0:T(1024)S(1)} %pad_clamp_fusion), kind=kCustom, calls=%fused_computation | custom fusion | bytes 8389632 | tf_op jit(solution)/shard_map/gather | solution.py:128
  130.9 6.2 %all-to-all-start.3 = ((bf16[16,16,4,16,128]{4,3,2,1,0:T(8,128)(2,1)}), bf16[16,16,4,16,128]{4,3,2,1,0:T(8,128)(2,1)}, u32[]{:S(2)}, u32[]{:S(2)}) async-start(bf16[16,16,4,16,128]{4,3,2,1,0:T(8,128)(2,1)} %bitcast.179), calls=%async_computation.3 | async-start | bytes 8388608 | tf_op jit(solution)/shard_map/all_to_all | solution.py:178
  142.2 7.2 %reshape.146.c_ref = bf16[2,2048,512]{2,1,0:T(8,128)(2,1)} reshape(bf16[2,2048,4,128]{3,2,1,0:T(4,128)(2,1)} %bitcast.175) | data formatting | bytes 8388608 | tf_op jit(solution)/shard_map/reshape | solution.py:100
  149.5 64.1 %shard_map.131 = bf16[2,256,512]{2,1,0:T(8,128)(2,1)} custom-call(s32[2]{0:T(128)} %copy-done.7, bf16[2,256,512]{2,1,0:T(8,128)(2,1)} %reshape.145.q_ref, bf16[2,2048,512]{2,1,0:T(8,128)(2,1)} %reshape.146.c_ref, bf16[2,256,512]{2,1,0:T(8,128)(2,1)} %reshape.147.s_ref), custom_call_target="tpu_custom_call" | custom-call | flops 7247757312 | bytes 5767168 | tf_op jit(solution)/shard_map/pallas_call | solution.py:103
  214.7 15.0 %all-to-all-done.3 = bf16[16,16,4,16,128]{4,3,2,1,0:T(8,128)(2,1)} async-done(((bf16[16,16,4,16,128]{4,3,2,1,0:T(8,128)(2,1)}), bf16[16,16,4,16,128]{4,3,2,1,0:T(8,128)(2,1)}, u32[]{:S(2)}, u32[]{:S(2)}) %all-to-all-start.3) | async-done | bytes 4194336 | tf_op jit(solution)/shard_map/all_to_all | solution.py:178
  234.7 7.7 %all-to-all-done.5 = bf16[2,256,4,128]{3,2,0,1:T(4,128)(2,1)S(1)} async-done(((bf16[2,256,4,128]{3,2,0,1:T(4,128)(2,1)}), bf16[2,256,4,128]{3,2,0,1:T(4,128)(2,1)S(1)}, u32[]{:S(2)}, u32[]{:S(2)}) %all-to-all-start.5) | async-done | bytes 524320 | tf_op jit(solution)/shard_map/all_to_all | solution.py:185
  246.1 5.2 %convolution_convert_fusion.1 = bf16[16,256,1024]{2,1,0:T(8,128)(2,1)} fusion(s32[16,256]{1,0:T(8,128)S(1)} %eq.64, f32[256,1024]{1,0:T(8,128)S(1)} %get-tuple-element.19, f32[1024]{0:T(1024)S(1)} %copy-done.5, f32[256]{0:T(256)S(1)} %add_rsqrt_fusion), kind=kOutput, calls=%fused_computation.16 | convolution fusion | flops 2153512960 | bytes 9458688 | tf_op jit(solution)/shard_map/ect,td->ecd/dot_general | solution.py:222
  257.0 82.5 %all-gather.7.cloned.1.call-done = bf16[2,2,3,1024,256]{3,4,1,0,2:T(8,128)(2,1)} async-done(((bf16[2,1,3,1024,256]{3,4,1,0,2:T(8,128)(2,1)}), bf16[2,2,3,1024,256]{3,4,1,0,2:T(8,128)(2,1)}) %all-gather.7.cloned.1.call-update) | async-done | bytes 6291472 | tf_op jit(solution)/shard_map/all_gather | solution.py:165
  339.5 9.9 %all-to-all-done.6 = bf16[8,512,1024]{2,1,0:T(8,128)(2,1)} async-done(((bf16[8,512,1024]{2,1,0:T(8,128)(2,1)}), bf16[8,512,1024]{2,1,0:T(8,128)(2,1)}, u32[]{:S(2)}, u32[]{:S(2)}) %all-to-all-start.6) | async-done | bytes 8388640 | tf_op jit(solution)/shard_map/all_to_all | solution.py:226
  349.3 11.8 %fusion.5 = f32[2,2,256,8,256]{4,2,3,1,0:T(8,128)} fusion(bf16[8,2,256,1024,1]{3,2,1,0,4:T(8,128)(2,1)} %bitcast.34, bf16[2,2,1,3,1024,256]{4,5,1,0,3,2:T(8,128)(2,1)} %bitcast.191), kind=kOutput, calls=%fused_computation.12 | convolution fusion | flops 4294967296 | bytes 18874368 | tf_op jit(solution)/shard_map/szjcd,zkjdf->szjckf/dot_general | solution.py:234
  361.1 16.6 %fusion = bf16[8,2,1,256,1024]{4,3,0,1,2:T(8,128)(2,1)} fusion(f32[2,2,256,8,256]{4,2,3,1,0:T(8,128)} %fusion.5, bf16[2,2,1,3,1024,256]{4,5,1,0,3,2:T(8,128)(2,1)} %bitcast.192, bf16[8,2,256,1024,1]{3,2,1,0,4:T(8,128)(2,1)} %bitcast.34), kind=kOutput, calls=%fused_computation.4 | convolution fusion | flops 8606711808 | bytes 29360128 | tf_op jit(solution)/shard_map/szjckf,zkjdf->szjcd/dot_general | solution.py:238
  377.8 8.0 %copy.104 = bf16[8,2,1,256,1024]{4,3,1,0,2:T(8,128)(2,1)} copy(bf16[8,2,1,256,1024]{4,3,0,1,2:T(8,128)(2,1)} %fusion) | data formatting | bytes 16777216 | tf_op jit(solution)/shard_map/convert_element_type | solution.py:240
  385.7 5.4 %all-to-all-start.7 = ((bf16[8,512,1024]{2,1,0:T(8,128)(2,1)}), bf16[8,512,1024]{2,1,0:T(8,128)(2,1)}, u32[]{:S(2)}, u32[]{:S(2)}) async-start(bf16[8,512,1024]{2,1,0:T(8,128)(2,1)} %bitcast.176), calls=%async_computation.7 | async-start | bytes 16777216 | tf_op jit(solution)/shard_map/all_to_all | solution.py:241
  391.2 7.3 %reshape.167 = bf16[256,8192]{1,0:T(8,128)(2,1)} reshape(bf16[16,16,4,16,128]{4,3,2,1,0:T(8,128)(2,1)} %all-to-all-done.3) | data formatting | bytes 8388608 | tf_op jit(solution)/shard_map/reshape | solution.py:193
  405.2 78.7 %all-to-all-done.7 = bf16[8,512,1024]{2,1,0:T(8,128)(2,1)} async-done(((bf16[8,512,1024]{2,1,0:T(8,128)(2,1)}), bf16[8,512,1024]{2,1,0:T(8,128)(2,1)}, u32[]{:S(2)}, u32[]{:S(2)}) %all-to-all-start.7) | async-done | bytes 8388640 | tf_op jit(solution)/shard_map/all_to_all | solution.py:241
  484.0 5.7 %fusion.27 = f32[256,1024]{1,0:T(8,128)S(1)} fusion(bf16[16,256,1024]{2,1,0:T(8,128)(2,1)} %bitcast.50, f32[16,256]{1,0:T(8,128)S(1)} %broadcast_in_dim.76, s32[16,256]{1,0:T(8,128)S(1)} %eq.64), kind=kOutput, calls=%fused_computation.36 | convolution fusion | flops 2153775104 | bytes 9469952 | tf_op jit(solution)/shard_map/ect,ecd->td/dot_general | solution.py:250
  489.7 6.8 %fusion.33 = bf16[256,1024]{1,0:T(8,128)(2,1)} fusion(f32[256,1024]{1,0:T(8,128)S(1)} %get-tuple-element.19, f32[256,1024]{1,0:T(8,128)S(1)} %fusion.27, bf16[16,256,1024]{2,1,0:T(8,128)(2,1)} %bitcast.50, f32[16,256]{1,0:T(8,128)S(1)} %broadcast_in_dim.76, s32[16,256]{1,0:T(8,128)S(1)} %eq.64), kind=kOutput, calls=%fused_computation.41 | convolution fusion | flops 2150367232 | bytes 11042816 | tf_op jit(solution)/shard_map/ect,ecd->td/dot_general | solution.py:248
  (72 shorter events, 54.5 us)
Async XLA Ops:
  7.2 236.9 %copy-start = (bf16[1024,1024]{1,0:T(8,128)(2,1)S(1)}, bf16[1024,1024]{1,0:T(8,128)(2,1)}, u32[]{:S(2)}) copy-start(bf16[1024,1024]{1,0:T(8,128)(2,1)} %param.18) | copy-start | bytes 6291460
  7.2 80.6 %all-gather.5.cloned.1.call-start = ((), (), s32[]{:S(2)}) async-start(), calls=%async_computation.8 | async-start | bytes 4718592 | tf_op jit(solution)/shard_map/all_gather | solution.py:161
  15.0 6.0 %copy-start.2 = (bf16[2,128,1024]{2,1,0:T(8,128)(2,1)S(1)}, bf16[2,128,1024]{2,1,0:T(8,128)(2,1)}, u32[]{:S(2)}) copy-start(bf16[2,128,1024]{2,1,0:T(8,128)(2,1)} %param.13) | copy-start | bytes 1572868
  15.0 7.1 %copy-start.8 = (s32[32]{0:T(128)S(1)}, s32[32]{0:T(128)}, u32[]{:S(2)}) copy-start(s32[32]{0:T(128)} %param.16) | copy-start | bytes 388
  15.0 7.2 %copy-start.9 = (s32[32]{0:T(128)S(1)}, s32[32]{0:T(128)}, u32[]{:S(2)}) copy-start(s32[32]{0:T(128)} %param.17) | copy-start | bytes 388
  15.0 53.6 %all-to-all-start.1 = ((bf16[2,1024,8,128]{3,1,0,2:T(8,128)(2,1)}), bf16[2,1024,8,128]{3,1,0,2:T(8,128)(2,1)}, u32[]{:S(2)}, u32[]{:S(2)}) async-start(bf16[2,1024,8,128]{3,1,0,2:T(8,128)(2,1)} %copy.87), calls=%async_computation.1 | async-start | bytes 8388608 | tf_op jit(solution)/shard_map/all_to_all | solution.py:157
  22.4 59.2 %copy-start.7 = (s32[2]{0:T(128)}, s32[2]{0:T(128)S(1)}, u32[]{:S(2)}) copy-start(s32[2]{0:T(128)S(1)} %fusion.40.len_ref) | copy-start | bytes 28
  68.6 22.4 %all-to-all-start = ((bf16[2,128,8,128]{1,3,0,2:T(8,128)(2,1)}), bf16[2,128,8,128]{1,3,0,2:T(8,128)(2,1)S(1)}, u32[]{:S(2)}, u32[]{:S(2)}) async-start(bf16[2,128,8,128]{1,3,0,2:T(8,128)(2,1)} %copy.83), calls=%async_computation | async-start | bytes 1048576 | tf_op jit(solution)/shard_map/all_to_all | solution.py:159
  74.1 13.6 %copy-start.6 = (s32[2,128]{1,0:T(2,128)S(1)}, s32[2,128]{1,0:T(2,128)}, u32[]{:S(2)}) copy-start(s32[2,128]{1,0:T(2,128)} %param.23) | copy-start | bytes 3076
  91.0 11.8 %all-to-all-start.2 = ((bf16[2,128,8,128]{3,1,0,2:T(8,128)(2,1)}), bf16[2,128,8,128]{3,1,0,2:T(8,128)(2,1)S(1)}, u32[]{:S(2)}, u32[]{:S(2)}) async-start(bf16[2,128,8,128]{3,1,0,2:T(8,128)(2,1)} %copy.89), calls=%async_computation.2 | async-start | bytes 1048576 | tf_op jit(solution)/shard_map/all_to_all | solution.py:158
  102.7 28.1 %all-to-all-start.4 = ((s32[16,1,16]{2,1,0:T(1,128)}), s32[16,1,16]{2,1,0:T(1,128)S(1)}, u32[]{:S(2)}, u32[]{:S(2)}) async-start(s32[16,1,16]{2,1,0:T(1,128)} %all_to_all.74), calls=%async_computation.4 | async-start | bytes 16384 | tf_op jit(solution)/shard_map/all_to_all | solution.py:179
  130.9 6.2 %copy-start.3 = (s32[256,8]{0,1:T(8,128)S(1)}, s32[256,8]{0,1:T(8,128)}, u32[]{:S(2)}) copy-start(s32[256,8]{0,1:T(8,128)} %param.20) | copy-start | bytes 24580
  130.9 98.8 %all-to-all-start.3 = ((bf16[16,16,4,16,128]{4,3,2,1,0:T(8,128)(2,1)}), bf16[16,16,4,16,128]{4,3,2,1,0:T(8,128)(2,1)}, u32[]{:S(2)}, u32[]{:S(2)}) async-start(bf16[16,16,4,16,128]{4,3,2,1,0:T(8,128)(2,1)} %bitcast.179), calls=%async_computation.3 | async-start | bytes 8388608 | tf_op jit(solution)/shard_map/all_to_all | solution.py:178
  230.7 15.3 %copy-start.5 = (f32[1024]{0:T(1024)S(1)}, f32[1024]{0:T(1024)}, u32[]{:S(2)}) copy-start(f32[1024]{0:T(1024)} %param.19) | copy-start | bytes 12292
  230.7 11.7 %all-to-all-start.5 = ((bf16[2,256,4,128]{3,2,0,1:T(4,128)(2,1)}), bf16[2,256,4,128]{3,2,0,1:T(4,128)(2,1)S(1)}, u32[]{:S(2)}, u32[]{:S(2)}) async-start(bf16[2,256,4,128]{3,2,0,1:T(4,128)(2,1)} %copy.92), calls=%async_computation.5 | async-start | bytes 1048576 | tf_op jit(solution)/shard_map/all_to_all | solution.py:185
  251.3 98.1 %all-to-all-start.6 = ((bf16[8,512,1024]{2,1,0:T(8,128)(2,1)}), bf16[8,512,1024]{2,1,0:T(8,128)(2,1)}, u32[]{:S(2)}, u32[]{:S(2)}) async-start(bf16[8,512,1024]{2,1,0:T(8,128)(2,1)} %bitcast.177), calls=%async_computation.6 | async-start | bytes 16777216 | tf_op jit(solution)/shard_map/all_to_all | solution.py:226
  256.2 83.2 %all-gather.7.cloned.1.call-start = ((), (), s32[]{:S(2)}) async-start(), calls=%async_computation.9 | async-start | bytes 9437184 | tf_op jit(solution)/shard_map/all_gather | solution.py:165
  385.7 5.4 %copy-start.4 = (f32[256,8]{0,1:T(8,128)S(1)}, f32[256,8]{0,1:T(8,128)}, u32[]{:S(2)}) copy-start(f32[256,8]{0,1:T(8,128)} %param.21) | copy-start | bytes 24580
  385.7 98.3 %all-to-all-start.7 = ((bf16[8,512,1024]{2,1,0:T(8,128)(2,1)}), bf16[8,512,1024]{2,1,0:T(8,128)(2,1)}, u32[]{:S(2)}, u32[]{:S(2)}) async-start(bf16[8,512,1024]{2,1,0:T(8,128)(2,1)} %bitcast.176), calls=%async_computation.7 | async-start | bytes 16777216 | tf_op jit(solution)/shard_map/all_to_all | solution.py:241
  489.7 6.8 %copy-start.1 = (bf16[1024,1024]{1,0:T(8,128)(2,1)S(1)}, bf16[1024,1024]{1,0:T(8,128)(2,1)}, u32[]{:S(2)}) copy-start(bf16[1024,1024]{1,0:T(8,128)(2,1)} %param.18) | copy-start | bytes 6291460
Sparse Core Ops, SparseCore 0:
  10.1 77.6 all-gather.4
  258.6 80.7 all-gather.6

commit v11 on v9

--- a/solution.py
+++ b/solution.py
@@ -221,35 +221,40 @@
     slot_of = side_major(jnp.where(picks > 0, rank, -1).T)
     weight_of = side_major(pick_weight.T)
     selector = slot_of[:, None, :] == jnp.arange(capacity, dtype=jnp.int32)[None, :, None]
-    buffer = jnp.einsum(
-        "ect,td->ecd", selector.astype(jnp.bfloat16), normed, preferred_element_type=jnp.float32
-    ).astype(jnp.bfloat16)
     per_dev = halves * exp_dev
-    slot_block = lax.all_to_all(
-        buffer.reshape(side, per_dev * capacity, width_model), "rlow", split_axis=0, concat_axis=0, tiled=True
-    )
-    grouped = slot_block.reshape(side, halves, exp_dev, capacity, width_model)
     weights = full_weights.reshape(halves, kv_count, *w_experts.shape)
-    gate_act = jnp.einsum(
-        "szjcd,zkjdf->szjckf", grouped, weights[:, :, :, 0], preferred_element_type=jnp.float32
-    )
-    up_act = jnp.einsum(
-        "szjcd,zkjdf->szjckf", grouped, weights[:, :, :, 1], preferred_element_type=jnp.float32
-    )
-    activated = (jax.nn.silu(gate_act) * up_act).astype(jnp.bfloat16)
-    expert_out = jnp.einsum(
-        "szjckf,zkjdf->szjcd", activated, weights[:, :, :, 2], preferred_element_type=jnp.float32
-    ).astype(jnp.bfloat16)
-    returned = lax.all_to_all(
-        expert_out.reshape(side, per_dev * capacity, width_model), "rlow", split_axis=0, concat_axis=0, tiled=True
-    )
     combine = jnp.where(selector, weight_of[:, None, :], 0.0)
     combine_hi = combine.astype(jnp.bfloat16)
     combine_lo = (combine - combine_hi.astype(jnp.float32)).astype(jnp.bfloat16)
-    returned = returned.reshape(experts, capacity, width_model)
-    expert_sum = jnp.einsum(
-        "ect,ecd->td", combine_hi, returned, preferred_element_type=jnp.float32
-    ) + jnp.einsum("ect,ecd->td", combine_lo, returned, preferred_element_type=jnp.float32)
+    chunks = 2 if capacity % 16 == 0 else 1
+    size = capacity // chunks
+    expert_sum = jnp.zeros((row_count, width_model), jnp.float32)
+    for chunk in range(chunks):
+        rows = slice(chunk * size, (chunk + 1) * size)
+        buffer = jnp.einsum(
+            "ect,td->ecd", selector[:, rows].astype(jnp.bfloat16), normed,
+            preferred_element_type=jnp.float32,
+        ).astype(jnp.bfloat16)
+        slot_block = lax.all_to_all(
+            buffer.reshape(side, per_dev * size, width_model), "rlow", split_axis=0, concat_axis=0, tiled=True
+        )
+        grouped = slot_block.reshape(side, halves, exp_dev, size, width_model)
+        gate_act = jnp.einsum(
+            "szjcd,zkjdf->szjckf", grouped, weights[:, :, :, 0], preferred_element_type=jnp.float32
+        )
+        up_act = jnp.einsum(
+            "szjcd,zkjdf->szjckf", grouped, weights[:, :, :, 1], preferred_element_type=jnp.float32
+        )
+        activated = (jax.nn.silu(gate_act) * up_act).astype(jnp.bfloat16)
+        expert_out = jnp.einsum(
+            "szjckf,zkjdf->szjcd", activated, weights[:, :, :, 2], preferred_element_type=jnp.float32
+        ).astype(jnp.bfloat16)
+        returned = lax.all_to_all(
+            expert_out.reshape(side, per_dev * size, width_model), "rlow", split_axis=0, concat_axis=0, tiled=True
+        ).reshape(experts, size, width_model)
+        expert_sum = expert_sum + jnp.einsum(
+            "ect,ecd->td", combine_hi[:, rows], returned, preferred_element_type=jnp.float32
+        ) + jnp.einsum("ect,ecd->td", combine_lo[:, rows], returned, preferred_element_type=jnp.float32)
     layer_out = (
         (residual + expert_sum).astype(jnp.bfloat16).reshape(local_reqs, local_tokens, width_model)
     )

time: 504 us -> 479 us (0.950)
  blocking collectives: 97.2 us -> 0 us
  waiting for transfers between devices: 180 us -> 232 us
  matrix products: 46 us -> 63.7 us
  Pallas kernels: 43.4 us -> 29.6 us
  starting transfers between devices: 35.4 us -> 49.1 us
    all_to_all x1 -> x0, blocking collectives: 97.2 us -> none  [body(): lax.all_to_all(buffer.reshape(side, per_dev * capacity, width_model), 'rl...]
    all_to_all x1 -> x4, waiting for transfers between devices: 79 us -> 119 us  [the longest x2 70.5 us: body(): lax.all_to_all(buffer.reshape(side, per_dev * size, width_model), 'rlow',...]
    all_to_all x1 -> x4, starting transfers between devices: 5.07 us -> 19 us  [the longest x2 9.49 us: body(): lax.all_to_all(expert_out.reshape(side, per_dev * size, width_model), 'rl...]
    pallas_call x1, Pallas kernels: 43.4 us -> 29.6 us  [attend(): pl.pallas_call(functools.partial(attend_kernel, tk=tk, head_dim=head_dim)...]
    dot_general x4 -> x8, matrix products: 24.2 us -> 37.7 us  [the longest x2 14.4 us: body(): jnp.einsum('szjcd,zkjdf->szjckf', grouped, weights[:, :, :, 1], preferred...]
    all_gather x1, waiting for transfers between devices: 24.8 us -> 38.2 us  [body(): full_weights = lax.all_gather(pair_weights, 'kv', axis=1, tiled=False)]
    dot_general x1 -> x2, matrix products: 16.4 us -> 20.5 us  [body(): jnp.einsum('szjckf,zkjdf->szjcd', activated, weights[:, :, :, 2], preferr...]
    unnamed x27 -> x35, local copies, waits for them, and re-layouts: 16.4 us -> 13.3 us
  transfers between devices with their start and end apart: 9 -> 12, of which waited for: 7 -> 10; matrix products, arithmetic and copies ran while one was open for 14% -> 27% of each run, Pallas kernels for 9% -> 6%
where the time goes in v11:
time: 479 us; the launch traced here: 476 us
  waiting for transfers between devices  232 us (48%)
  local copies, waits for them, and re-layouts  65.6 us (14%)
  matrix products  63.7 us (13%)
  starting transfers between devices  49.1 us (10%)
  Pallas kernels  29.6 us (6%)
  other arithmetic  21.1 us (4%)
  between operations  14.4 us (3%)
    all_to_all x2, waiting for transfers between devices, body(): lax.all_to_all(buffer.reshape(side, per_dev * size, width_model), 'rlow',...  70.5 us
    all_to_all x2, waiting for transfers between devices, body(): lax.all_to_all(expert_out.reshape(side, per_dev * size, width_model), 'rl...  48.8 us
    all_to_all x1, waiting for transfers between devices, body(): lax.all_to_all(cache, 'kv', split_axis=2, concat_axis=1, tiled=True)  46.3 us
    all_gather x1, waiting for transfers between devices, body(): full_weights = lax.all_gather(pair_weights, 'kv', axis=1, tiled=False)  38.2 us
    pallas_call x1, Pallas kernels, attend(): pl.pallas_call(functools.partial(attend_kernel, tk=tk, head_dim=head_dim)...  29.6 us
    dot_general x2, matrix products, body(): jnp.einsum('szjckf,zkjdf->szjcd', activated, weights[:, :, :, 2], preferr...  20.5 us
    dot_general x2, matrix products, body(): jnp.einsum('szjcd,zkjdf->szjckf', grouped, weights[:, :, :, 1], preferred...  14.4 us
    unnamed x35, local copies, waits for them, and re-layouts  13.3 us
  transfers between devices with their start and end apart: 12, of which 10 were waited for; matrix products, arithmetic and copies ran while one was open for 27% of the time, Pallas kernels for 6%

profile of v11, /device:TPU:16, one launch (start us, length us, event | category | flops | bytes accessed | tf_op | source)
XLA Modules:
  0.0 476.0 jit_solution(6754125167132828867)
XLA Ops:
  10.0 5.0 %copy.116 = bf16[2,1024,8,128]{3,1,0,2:T(8,128)(2,1)} copy(bf16[2,1024,8,128]{3,2,1,0:T(8,128)(2,1)} %param.15) | data formatting | bytes 8388608 | tf_op args[3]
  15.0 6.0 %all-to-all-start.1 = ((bf16[2,1024,8,128]{3,1,0,2:T(8,128)(2,1)}), bf16[2,1024,8,128]{3,1,0,2:T(8,128)(2,1)}, u32[]{:S(2)}, u32[]{:S(2)}) async-start(bf16[2,1024,8,128]{3,1,0,2:T(8,128)(2,1)} %copy.116), calls=%async_computation.1 | async-start | bytes 8388608 | tf_op jit(solution)/shard_map/all_to_all | solution.py:157
  22.4 46.3 %all-to-all-done.1 = bf16[2,1024,8,128]{3,1,0,2:T(8,128)(2,1)} async-done(((bf16[2,1024,8,128]{3,1,0,2:T(8,128)(2,1)}), bf16[2,1024,8,128]{3,1,0,2:T(8,128)(2,1)}, u32[]{:S(2)}, u32[]{:S(2)}) %all-to-all-start.1) | async-done | bytes 4194336 | tf_op jit(solution)/shard_map/all_to_all | solution.py:157
  74.2 7.5 %copy.117 = bf16[2,2,1024,4,128]{4,3,2,1,0:T(4,128)(2,1)} copy(bf16[2,2,1024,4,128]{4,2,0,3,1:T(8,128)(2,1)} %bitcast.7) | data formatting | bytes 8388608 | tf_op jit(solution)/shard_map/all_to_all | solution.py:157
  81.6 6.2 %all-gather.5.cloned.1.call-done = bf16[2,3,1024,256]{2,3,0,1:T(8,128)(2,1)} async-done(((bf16[1,3,1024,256]{2,3,0,1:T(8,128)(2,1)}), bf16[2,3,1024,256]{2,3,0,1:T(8,128)(2,1)}) %all-gather.5.cloned.1.call-update) | async-done | bytes 3145744 | tf_op jit(solution)/shard_map/all_gather | solution.py:161
  97.1 5.6 %all-to-all-done.2 = bf16[2,128,8,128]{3,1,0,2:T(8,128)(2,1)S(1)} async-done(((bf16[2,128,8,128]{3,1,0,2:T(8,128)(2,1)}), bf16[2,128,8,128]{3,1,0,2:T(8,128)(2,1)S(1)}, u32[]{:S(2)}, u32[]{:S(2)}) %all-to-all-start.2) | async-done | bytes 524320 | tf_op jit(solution)/shard_map/all_to_all | solution.py:158
  102.7 7.3 %all-to-all-start.4 = ((s32[16,1,16]{2,1,0:T(1,128)}), s32[16,1,16]{2,1,0:T(1,128)S(1)}, u32[]{:S(2)}, u32[]{:S(2)}) async-start(s32[16,1,16]{2,1,0:T(1,128)} %all_to_all.80), calls=%async_computation.4 | async-start | bytes 16384 | tf_op jit(solution)/shard_map/all_to_all | solution.py:179
  110.0 12.5 %broadcast_select_fusion = bf16[2,2048,4,128]{3,2,1,0:T(4,128)(2,1)S(1)} fusion(bf16[2,2048,4,128]{3,2,1,0:T(4,128)(2,1)} %bitcast.245, pred[2,2048]{1,0:T(4,128)(4,1)S(1)} %iota_compare_fusion.4), kind=kLoop, calls=%fused_computation.25 | loop fusion | flops 2097152 | bytes 8392704 | tf_op jit(solution)/shard_map/jit(_where)/select_n | solution.py:168
  125.6 5.3 %gather_fusion = bf16[256,4,16,128]{3,2,1,0:T(8,128)(2,1)} fusion(bf16[256,4,16,128]{3,2,1,0:T(8,128)(2,1)} %bitcast.253, s32[1024]{0:T(1024)S(1)} %pad_clamp_fusion), kind=kCustom, calls=%fused_computation | custom fusion | bytes 8389632 | tf_op jit(solution)/shard_map/gather | solution.py:128
  131.0 6.2 %all-to-all-start.3 = ((bf16[16,16,4,16,128]{4,3,2,1,0:T(8,128)(2,1)}), bf16[16,16,4,16,128]{4,3,2,1,0:T(8,128)(2,1)}, u32[]{:S(2)}, u32[]{:S(2)}) async-start(bf16[16,16,4,16,128]{4,3,2,1,0:T(8,128)(2,1)} %bitcast.248), calls=%async_computation.3 | async-start | bytes 8388608 | tf_op jit(solution)/shard_map/all_to_all | solution.py:178
  143.4 7.5 %reshape.175.c_ref = bf16[2,2048,512]{2,1,0:T(8,128)(2,1)} reshape(bf16[2,2048,4,128]{3,2,1,0:T(4,128)(2,1)} %bitcast.246) | data formatting | bytes 8388608 | tf_op jit(solution)/shard_map/reshape | solution.py:100
  150.9 29.6 %shard_map.131 = bf16[2,256,512]{2,1,0:T(8,128)(2,1)} custom-call(s32[2]{0:T(128)} %copy-done.12, bf16[2,256,512]{2,1,0:T(8,128)(2,1)} %reshape.174.q_ref, bf16[2,2048,512]{2,1,0:T(8,128)(2,1)} %reshape.175.c_ref, bf16[2,256,512]{2,1,0:T(8,128)(2,1)} %reshape.176.s_ref), custom_call_target="tpu_custom_call" | custom-call | flops 7247757312 | bytes 5767168 | tf_op jit(solution)/shard_map/pallas_call | solution.py:103
  181.6 38.2 %all-gather.7.cloned.1.call-done = bf16[2,2,3,1024,256]{3,4,1,0,2:T(8,128)(2,1)} async-done(((bf16[2,1,3,1024,256]{3,4,1,0,2:T(8,128)(2,1)}), bf16[2,2,3,1024,256]{3,4,1,0,2:T(8,128)(2,1)}) %all-gather.7.cloned.1.call-update) | async-done | bytes 6291472 | tf_op jit(solution)/shard_map/all_gather | solution.py:165
  219.9 9.9 %all-to-all-done.3 = bf16[16,16,4,16,128]{4,3,2,1,0:T(8,128)(2,1)} async-done(((bf16[16,16,4,16,128]{4,3,2,1,0:T(8,128)(2,1)}), bf16[16,16,4,16,128]{4,3,2,1,0:T(8,128)(2,1)}, u32[]{:S(2)}, u32[]{:S(2)}) %all-to-all-start.3) | async-done | bytes 4194336 | tf_op jit(solution)/shard_map/all_to_all | solution.py:178
  235.9 6.4 %all-to-all-done.5 = bf16[2,256,4,128]{3,2,0,1:T(4,128)(2,1)S(1)} async-done(((bf16[2,256,4,128]{3,2,0,1:T(4,128)(2,1)}), bf16[2,256,4,128]{3,2,0,1:T(4,128)(2,1)S(1)}, u32[]{:S(2)}, u32[]{:S(2)}) %all-to-all-start.5) | async-done | bytes 524320 | tf_op jit(solution)/shard_map/all_to_all | solution.py:187
  257.5 44.8 %all-to-all-done.6 = bf16[8,256,1024]{2,1,0:T(8,128)(2,1)} async-done(((bf16[8,256,1024]{2,1,0:T(8,128)(2,1)}), bf16[8,256,1024]{2,1,0:T(8,128)(2,1)}, u32[]{:S(2)}, u32[]{:S(2)}) %all-to-all-start.6) | async-done | bytes 4194336 | tf_op jit(solution)/shard_map/all_to_all | solution.py:238
  307.1 7.2 %fusion.15 = f32[2,2,256,8,128]{4,2,3,1,0:T(8,128)} fusion(bf16[8,2,128,1024,1]{3,2,1,0,4:T(8,128)(2,1)} %bitcast.34, bf16[2,2,1,3,1024,256]{4,5,1,0,3,2:T(8,128)(2,1)} %bitcast.264), kind=kOutput, calls=%fused_computation.30 | convolution fusion | flops 2147483648 | bytes 10485760 | tf_op jit(solution)/shard_map/szjcd,zkjdf->szjckf/dot_general | solution.py:245
  314.3 10.2 %fusion.1 = bf16[8,2,1,128,1024]{4,3,0,1,2:T(8,128)(2,1)} fusion(f32[2,2,256,8,128]{4,2,3,1,0:T(8,128)} %fusion.15, bf16[2,2,1,3,1024,256]{4,5,1,0,3,2:T(8,128)(2,1)} %bitcast.265, bf16[8,2,128,1024,1]{3,2,1,0,4:T(8,128)(2,1)} %bitcast.34), kind=kOutput, calls=%fused_computation.8 | convolution fusion | flops 4303355904 | bytes 16777216 | tf_op jit(solution)/shard_map/szjckf,zkjdf->szjcd/dot_general | solution.py:249
  329.3 25.7 %all-to-all-done.8 = bf16[8,256,1024]{2,1,0:T(8,128)(2,1)} async-done(((bf16[8,256,1024]{2,1,0:T(8,128)(2,1)}), bf16[8,256,1024]{2,1,0:T(8,128)(2,1)}, u32[]{:S(2)}, u32[]{:S(2)}) %all-to-all-start.8) | async-done | bytes 4194336 | tf_op jit(solution)/shard_map/all_to_all | solution.py:238
  359.6 7.2 %fusion.11 = f32[2,2,256,8,128]{4,2,3,1,0:T(8,128)} fusion(bf16[8,2,128,1024,1]{3,2,1,0,4:T(8,128)(2,1)} %bitcast.58, bf16[2,2,1,3,1024,256]{4,5,1,0,3,2:T(8,128)(2,1)} %bitcast.266), kind=kOutput, calls=%fused_computation.26 | convolution fusion | flops 2147483648 | bytes 10485760 | tf_op jit(solution)/shard_map/szjcd,zkjdf->szjckf/dot_general | solution.py:245
  366.8 10.2 %fusion.2 = bf16[8,2,1,128,1024]{4,3,0,1,2:T(8,128)(2,1)} fusion(f32[2,2,256,8,128]{4,2,3,1,0:T(8,128)} %fusion.11, bf16[2,2,1,3,1024,256]{4,5,1,0,3,2:T(8,128)(2,1)} %bitcast.267, bf16[8,2,128,1024,1]{3,2,1,0,4:T(8,128)(2,1)} %bitcast.58), kind=kOutput, calls=%fused_computation.9 | convolution fusion | flops 4303355904 | bytes 16777216 | tf_op jit(solution)/shard_map/szjckf,zkjdf->szjcd/dot_general | solution.py:249
  381.8 25.9 %all-to-all-done.7 = bf16[8,256,1024]{2,1,0:T(8,128)(2,1)} async-done(((bf16[8,256,1024]{2,1,0:T(8,128)(2,1)}), bf16[8,256,1024]{2,1,0:T(8,128)(2,1)}, u32[]{:S(2)}, u32[]{:S(2)}) %all-to-all-start.7) | async-done | bytes 4194336 | tf_op jit(solution)/shard_map/all_to_all | solution.py:252
  415.6 7.3 %reshape.201 = bf16[256,8192]{1,0:T(8,128)(2,1)} reshape(bf16[16,16,4,16,128]{4,3,2,1,0:T(8,128)(2,1)} %all-to-all-done.3) | data formatting | bytes 8388608 | tf_op jit(solution)/shard_map/reshape | solution.py:195
  437.7 22.9 %all-to-all-done.9 = bf16[8,256,1024]{2,1,0:T(8,128)(2,1)} async-done(((bf16[8,256,1024]{2,1,0:T(8,128)(2,1)}), bf16[8,256,1024]{2,1,0:T(8,128)(2,1)}, u32[]{:S(2)}, u32[]{:S(2)}) %all-to-all-start.9) | async-done | bytes 4194336 | tf_op jit(solution)/shard_map/all_to_all | solution.py:252
  (95 shorter events, 100.6 us)
Async XLA Ops:
  7.2 236.8 %copy-start = (bf16[1024,1024]{1,0:T(8,128)(2,1)S(1)}, bf16[1024,1024]{1,0:T(8,128)(2,1)}, u32[]{:S(2)}) copy-start(bf16[1024,1024]{1,0:T(8,128)(2,1)} %param.18) | copy-start | bytes 6291460
  7.2 80.6 %all-gather.5.cloned.1.call-start = ((), (), s32[]{:S(2)}) async-start(), calls=%async_computation.10 | async-start | bytes 4718592 | tf_op jit(solution)/shard_map/all_gather | solution.py:161
  15.0 6.0 %copy-start.7 = (bf16[2,128,1024]{2,1,0:T(8,128)(2,1)S(1)}, bf16[2,128,1024]{2,1,0:T(8,128)(2,1)}, u32[]{:S(2)}) copy-start(bf16[2,128,1024]{2,1,0:T(8,128)(2,1)} %param.13) | copy-start | bytes 1572868
  15.0 7.1 %copy-start.13 = (s32[32]{0:T(128)S(1)}, s32[32]{0:T(128)}, u32[]{:S(2)}) copy-start(s32[32]{0:T(128)} %param.16) | copy-start | bytes 388
  15.0 7.2 %copy-start.14 = (s32[32]{0:T(128)S(1)}, s32[32]{0:T(128)}, u32[]{:S(2)}) copy-start(s32[32]{0:T(128)} %param.17) | copy-start | bytes 388
  15.0 53.6 %all-to-all-start.1 = ((bf16[2,1024,8,128]{3,1,0,2:T(8,128)(2,1)}), bf16[2,1024,8,128]{3,1,0,2:T(8,128)(2,1)}, u32[]{:S(2)}, u32[]{:S(2)}) async-start(bf16[2,1024,8,128]{3,1,0,2:T(8,128)(2,1)} %copy.116), calls=%async_computation.1 | async-start | bytes 8388608 | tf_op jit(solution)/shard_map/all_to_all | solution.py:157
  22.4 59.3 %copy-start.12 = (s32[2]{0:T(128)}, s32[2]{0:T(128)S(1)}, u32[]{:S(2)}) copy-start(s32[2]{0:T(128)S(1)} %fusion.68.len_ref) | copy-start | bytes 28
  68.6 22.3 %all-to-all-start = ((bf16[2,128,8,128]{1,3,0,2:T(8,128)(2,1)}), bf16[2,128,8,128]{1,3,0,2:T(8,128)(2,1)S(1)}, u32[]{:S(2)}, u32[]{:S(2)}) async-start(bf16[2,128,8,128]{1,3,0,2:T(8,128)(2,1)} %copy.112), calls=%async_computation | async-start | bytes 1048576 | tf_op jit(solution)/shard_map/all_to_all | solution.py:159
  74.2 13.6 %copy-start.11 = (s32[2,128]{1,0:T(2,128)S(1)}, s32[2,128]{1,0:T(2,128)}, u32[]{:S(2)}) copy-start(s32[2,128]{1,0:T(2,128)} %param.23) | copy-start | bytes 3076
  91.0 11.8 %all-to-all-start.2 = ((bf16[2,128,8,128]{3,1,0,2:T(8,128)(2,1)}), bf16[2,128,8,128]{3,1,0,2:T(8,128)(2,1)S(1)}, u32[]{:S(2)}, u32[]{:S(2)}) async-start(bf16[2,128,8,128]{3,1,0,2:T(8,128)(2,1)} %copy.118), calls=%async_computation.2 | async-start | bytes 1048576 | tf_op jit(solution)/shard_map/all_to_all | solution.py:158
  102.7 28.2 %all-to-all-start.4 = ((s32[16,1,16]{2,1,0:T(1,128)}), s32[16,1,16]{2,1,0:T(1,128)S(1)}, u32[]{:S(2)}, u32[]{:S(2)}) async-start(s32[16,1,16]{2,1,0:T(1,128)} %all_to_all.80), calls=%async_computation.4 | async-start | bytes 16384 | tf_op jit(solution)/shard_map/all_to_all | solution.py:179
  131.0 6.9 %copy-start.8 = (s32[256,8]{0,1:T(8,128)S(1)}, s32[256,8]{0,1:T(8,128)}, u32[]{:S(2)}) copy-start(s32[256,8]{0,1:T(8,128)} %param.20) | copy-start | bytes 24580
  131.0 98.8 %all-to-all-start.3 = ((bf16[16,16,4,16,128]{4,3,2,1,0:T(8,128)(2,1)}), bf16[16,16,4,16,128]{4,3,2,1,0:T(8,128)(2,1)}, u32[]{:S(2)}, u32[]{:S(2)}) async-start(bf16[16,16,4,16,128]{4,3,2,1,0:T(8,128)(2,1)} %bitcast.248), calls=%async_computation.3 | async-start | bytes 8388608 | tf_op jit(solution)/shard_map/all_to_all | solution.py:178
  137.1 82.8 %all-gather.7.cloned.1.call-start = ((), (), s32[]{:S(2)}) async-start(), calls=%async_computation.11 | async-start | bytes 9437184 | tf_op jit(solution)/shard_map/all_gather | solution.py:165
  230.8 11.5 %all-to-all-start.5 = ((bf16[2,256,4,128]{3,2,0,1:T(4,128)(2,1)}), bf16[2,256,4,128]{3,2,0,1:T(4,128)(2,1)S(1)}, u32[]{:S(2)}, u32[]{:S(2)}) async-start(bf16[2,256,4,128]{3,2,0,1:T(4,128)(2,1)} %copy.121), calls=%async_computation.5 | async-start | bytes 1048576 | tf_op jit(solution)/shard_map/all_to_all | solution.py:187
  234.3 11.8 %copy-start.9 = (f32[1024]{0:T(1024)S(1)}, f32[1024]{0:T(1024)}, u32[]{:S(2)}) copy-start(f32[1024]{0:T(1024)} %param.19) | copy-start | bytes 12292
  249.4 4.7 copy-start.3
  249.5 52.9 %all-to-all-start.6 = ((bf16[8,256,1024]{2,1,0:T(8,128)(2,1)}), bf16[8,256,1024]{2,1,0:T(8,128)(2,1)}, u32[]{:S(2)}, u32[]{:S(2)}) async-start(bf16[8,256,1024]{2,1,0:T(8,128)(2,1)} %bitcast.252), calls=%async_computation.6 | async-start | bytes 8388608 | tf_op jit(solution)/shard_map/all_to_all | solution.py:238
  302.3 52.7 %all-to-all-start.8 = ((bf16[8,256,1024]{2,1,0:T(8,128)(2,1)}), bf16[8,256,1024]{2,1,0:T(8,128)(2,1)}, u32[]{:S(2)}, u32[]{:S(2)}) async-start(bf16[8,256,1024]{2,1,0:T(8,128)(2,1)} %bitcast.250), calls=%async_computation.8 | async-start | bytes 8388608 | tf_op jit(solution)/shard_map/all_to_all | solution.py:238
  355.0 52.7 %all-to-all-start.7 = ((bf16[8,256,1024]{2,1,0:T(8,128)(2,1)}), bf16[8,256,1024]{2,1,0:T(8,128)(2,1)}, u32[]{:S(2)}, u32[]{:S(2)}) async-start(bf16[8,256,1024]{2,1,0:T(8,128)(2,1)} %bitcast.251), calls=%async_computation.7 | async-start | bytes 8388608 | tf_op jit(solution)/shard_map/all_to_all | solution.py:252
  407.8 5.0 %copy-start.10 = (f32[256,8]{0,1:T(8,128)S(1)}, f32[256,8]{0,1:T(8,128)}, u32[]{:S(2)}) copy-start(f32[256,8]{0,1:T(8,128)} %param.21) | copy-start | bytes 24580
  407.8 52.9 %all-to-all-start.9 = ((bf16[8,256,1024]{2,1,0:T(8,128)(2,1)}), bf16[8,256,1024]{2,1,0:T(8,128)(2,1)}, u32[]{:S(2)}, u32[]{:S(2)}) async-start(bf16[8,256,1024]{2,1,0:T(8,128)(2,1)} %bitcast.249), calls=%async_computation.9 | async-start | bytes 8388608 | tf_op jit(solution)/shard_map/all_to_all | solution.py:252
  413.5 16.1 %copy-start.4 = (bf16[16,256,256]{2,1,0:T(8,128)(2,1)}, bf16[16,256,256]{2,1,0:T(8,128)(2,1)S(1)}, u32[]{:S(2)}) copy-start(bf16[16,256,256]{2,1,0:T(8,128)(2,1)S(1)} %fusion) | copy-start | bytes 6291460
  460.6 8.5 %copy-start.1 = (bf16[1024,1024]{1,0:T(8,128)(2,1)S(1)}, bf16[1024,1024]{1,0:T(8,128)(2,1)}, u32[]{:S(2)}) copy-start(bf16[1024,1024]{1,0:T(8,128)(2,1)} %param.18) | copy-start | bytes 6291460
  (3 other events, 10.0 us)
Sparse Core Ops, SparseCore 0:
  10.1 77.6 all-gather.4
  139.5 80.3 all-gather.6

commit v12 on v11

--- a/solution.py
+++ b/solution.py
@@ -226,7 +226,7 @@
     combine = jnp.where(selector, weight_of[:, None, :], 0.0)
     combine_hi = combine.astype(jnp.bfloat16)
     combine_lo = (combine - combine_hi.astype(jnp.float32)).astype(jnp.bfloat16)
-    chunks = 2 if capacity % 16 == 0 else 1
+    chunks = 4 if capacity % 32 == 0 else 1
     size = capacity // chunks
     expert_sum = jnp.zeros((row_count, width_model), jnp.float32)
     for chunk in range(chunks):

time: 479 us -> 523 us (1.092); the launches traced: 476 us -> 513 us
  matrix products: 63.7 us -> 87.1 us
  starting transfers between devices: 49.1 us -> 63.9 us
    all_to_all x2 -> x4, waiting for transfers between devices: 48.8 us -> 31.3 us  [body(): lax.all_to_all(expert_out.reshape(side, per_dev * size, width_model), 'rl...]
    all_to_all x2 -> x4, waiting for transfers between devices: 70.5 us -> 81.3 us  [body(): lax.all_to_all(buffer.reshape(side, per_dev * size, width_model), 'rlow',...]
    dot_general x2 -> x4, matrix products: 20.5 us -> 29.2 us  [body(): jnp.einsum('szjckf,zkjdf->szjcd', activated, weights[:, :, :, 2], preferr...]
    all_to_all x2 -> x4, starting transfers between devices: 9.49 us -> 17.1 us  [body(): lax.all_to_all(expert_out.reshape(side, per_dev * size, width_model), 'rl...]
    all_to_all x2 -> x4, starting transfers between devices: 9.46 us -> 17 us  [body(): lax.all_to_all(buffer.reshape(side, per_dev * size, width_model), 'rlow',...]
    dot_general x2 -> x4, matrix products: 14.4 us -> 19.2 us  [body(): jnp.einsum('szjcd,zkjdf->szjckf', grouped, weights[:, :, :, 1], preferred...]
    dot_general x2 -> x4, matrix products: 8.68 us -> 13.2 us  [body(): jnp.einsum('ect,ecd->td', combine_hi[:, rows], returned, preferred_elemen...]
    dot_general x2 -> x4, matrix products: 7.88 us -> 11 us  [body(): jnp.einsum('ect,ecd->td', combine_lo[:, rows], returned, preferred_elemen...]
  transfers between devices with their start and end apart: 12 -> 16, of which waited for: 10 -> 13; matrix products, arithmetic and copies ran while one was open for 27% -> 31% of each run, Pallas kernels for 6% -> 5%
where the time goes in v12:
time: 523 us; the launch traced here: 513 us
  waiting for transfers between devices  233 us (45%)
  matrix products  87.1 us (17%)
  local copies, waits for them, and re-layouts  66.1 us (13%)
  starting transfers between devices  63.9 us (12%)
  Pallas kernels  26.1 us (5%)
  other arithmetic  22.6 us (4%)
  between operations  14.9 us (3%)
    all_to_all x4, waiting for transfers between devices, body(): lax.all_to_all(buffer.reshape(side, per_dev * size, width_model), 'rlow',...  81.3 us
    all_to_all x1, waiting for transfers between devices, body(): lax.all_to_all(cache, 'kv', split_axis=2, concat_axis=1, tiled=True)  46.2 us
    all_gather x1, waiting for transfers between devices, body(): full_weights = lax.all_gather(pair_weights, 'kv', axis=1, tiled=False)  41.8 us
    all_to_all x4, waiting for transfers between devices, body(): lax.all_to_all(expert_out.reshape(side, per_dev * size, width_model), 'rl...  31.3 us
    dot_general x4, matrix products, body(): jnp.einsum('szjckf,zkjdf->szjcd', activated, weights[:, :, :, 2], preferr...  29.2 us
    pallas_call x1, Pallas kernels, attend(): pl.pallas_call(functools.partial(attend_kernel, tk=tk, head_dim=head_dim)...  26.1 us
    dot_general x4, matrix products, body(): jnp.einsum('szjcd,zkjdf->szjckf', grouped, weights[:, :, :, 1], preferred...  19.2 us
    all_to_all x4, starting transfers between devices, body(): lax.all_to_all(expert_out.reshape(side, per_dev * size, width_model), 'rl...  17.1 us
  transfers between devices with their start and end apart: 16, of which 13 were waited for; matrix products, arithmetic and copies ran while one was open for 31% of the time, Pallas kernels for 5%

profile of v12, /device:TPU:16, one launch (start us, length us, event | category | flops | bytes accessed | tf_op | source)
XLA Modules:
  0.0 513.4 jit_solution(11650040391116438147)
XLA Ops:
  12.9 5.7 %all-to-all-start.1 = ((bf16[2,1024,8,128]{3,1,0,2:T(8,128)(2,1)}), bf16[2,1024,8,128]{3,1,0,2:T(8,128)(2,1)}, u32[]{:S(2)}, u32[]{:S(2)}) async-start(bf16[2,1024,8,128]{3,1,0,2:T(8,128)(2,1)} %copy.118), calls=%async_computation.1 | async-start | bytes 8388608 | tf_op jit(solution)/shard_map/all_to_all | solution.py:157
  20.1 46.2 %all-to-all-done.1 = bf16[2,1024,8,128]{3,1,0,2:T(8,128)(2,1)} async-done(((bf16[2,1024,8,128]{3,1,0,2:T(8,128)(2,1)}), bf16[2,1024,8,128]{3,1,0,2:T(8,128)(2,1)}, u32[]{:S(2)}, u32[]{:S(2)}) %all-to-all-start.1) | async-done | bytes 4194336 | tf_op jit(solution)/shard_map/all_to_all | solution.py:157
  70.8 7.5 %copy.119 = bf16[2,2,1024,4,128]{4,3,2,1,0:T(4,128)(2,1)} copy(bf16[2,2,1024,4,128]{4,2,0,3,1:T(8,128)(2,1)} %bitcast.8) | data formatting | bytes 8388608 | tf_op jit(solution)/shard_map/all_to_all | solution.py:157
  78.3 8.9 %all-gather.5.cloned.1.call-done = bf16[2,3,1024,256]{3,2,0,1:T(8,128)(2,1)} async-done(((bf16[1,3,1024,256]{3,2,0,1:T(8,128)(2,1)}), bf16[2,3,1024,256]{3,2,0,1:T(8,128)(2,1)}) %all-gather.5.cloned.1.call-update) | async-done | bytes 3145744 | tf_op jit(solution)/shard_map/all_gather | solution.py:161
  102.2 7.3 %all-to-all-start.4 = ((s32[16,1,16]{2,1,0:T(1,128)}), s32[16,1,16]{2,1,0:T(1,128)S(1)}, u32[]{:S(2)}, u32[]{:S(2)}) async-start(s32[16,1,16]{2,1,0:T(1,128)} %all_to_all.92), calls=%async_computation.4 | async-start | bytes 16384 | tf_op jit(solution)/shard_map/all_to_all | solution.py:179
  109.5 12.5 %broadcast_select_fusion = bf16[2,2048,4,128]{3,2,1,0:T(4,128)(2,1)S(1)} fusion(bf16[2,2048,4,128]{3,2,1,0:T(4,128)(2,1)} %bitcast.393, pred[2,2048]{1,0:T(4,128)(4,1)S(1)} %iota_compare_fusion.4), kind=kLoop, calls=%fused_computation.11 | loop fusion | flops 2097152 | bytes 8392704 | tf_op jit(solution)/shard_map/jit(_where)/select_n | solution.py:168
  130.5 6.0 %all-to-all-start.3 = ((bf16[16,16,4,16,128]{4,3,2,1,0:T(8,128)(2,1)}), bf16[16,16,4,16,128]{4,3,2,1,0:T(8,128)(2,1)}, u32[]{:S(2)}, u32[]{:S(2)}) async-start(bf16[16,16,4,16,128]{4,3,2,1,0:T(8,128)(2,1)} %bitcast.398), calls=%async_computation.3 | async-start | bytes 8388608 | tf_op jit(solution)/shard_map/all_to_all | solution.py:178
  142.7 7.4 %reshape.233.c_ref = bf16[2,2048,512]{2,1,0:T(8,128)(2,1)} reshape(bf16[2,2048,4,128]{3,2,1,0:T(4,128)(2,1)} %bitcast.394) | data formatting | bytes 8388608 | tf_op jit(solution)/shard_map/reshape | solution.py:100
  150.2 26.1 %shard_map.131 = bf16[2,256,512]{2,1,0:T(8,128)(2,1)} custom-call(s32[2]{0:T(128)} %copy-done.15, bf16[2,256,512]{2,1,0:T(8,128)(2,1)} %reshape.232.q_ref, bf16[2,2048,512]{2,1,0:T(8,128)(2,1)} %reshape.233.c_ref, bf16[2,256,512]{2,1,0:T(8,128)(2,1)} %reshape.234.s_ref), custom_call_target="tpu_custom_call" | custom-call | flops 7247757312 | bytes 5767168 | tf_op jit(solution)/shard_map/pallas_call | solution.py:103
  177.5 41.8 %all-gather.7.cloned.1.call-done = bf16[2,2,3,1024,256]{4,3,1,0,2:T(8,128)(2,1)} async-done(((bf16[2,1,3,1024,256]{4,3,1,0,2:T(8,128)(2,1)}), bf16[2,2,3,1024,256]{4,3,1,0,2:T(8,128)(2,1)}) %all-gather.7.cloned.1.call-update) | async-done | bytes 6291472 | tf_op jit(solution)/shard_map/all_gather | solution.py:165
  219.3 9.9 %all-to-all-done.3 = bf16[16,16,4,16,128]{4,3,2,1,0:T(8,128)(2,1)} async-done(((bf16[16,16,4,16,128]{4,3,2,1,0:T(8,128)(2,1)}), bf16[16,16,4,16,128]{4,3,2,1,0:T(8,128)(2,1)}, u32[]{:S(2)}, u32[]{:S(2)}) %all-to-all-start.3) | async-done | bytes 4194336 | tf_op jit(solution)/shard_map/all_to_all | solution.py:178
  235.3 6.4 %all-to-all-done.5 = bf16[2,256,4,128]{3,2,0,1:T(4,128)(2,1)S(1)} async-done(((bf16[2,256,4,128]{3,2,0,1:T(4,128)(2,1)}), bf16[2,256,4,128]{3,2,0,1:T(4,128)(2,1)S(1)}, u32[]{:S(2)}, u32[]{:S(2)}) %all-to-all-start.5) | async-done | bytes 524320 | tf_op jit(solution)/shard_map/all_to_all | solution.py:187
  255.1 23.7 %all-to-all-done.12 = bf16[8,128,1024]{2,1,0:T(8,128)(2,1)} async-done(((bf16[8,128,1024]{2,1,0:T(8,128)(2,1)}), bf16[8,128,1024]{2,1,0:T(8,128)(2,1)}, u32[]{:S(2)}, u32[]{:S(2)}) %all-to-all-start.12) | async-done | bytes 2097184 | tf_op jit(solution)/shard_map/all_to_all | solution.py:238
  285.1 23.7 %all-to-all-done.10 = bf16[8,128,1024]{2,1,0:T(8,128)(2,1)} async-done(((bf16[8,128,1024]{2,1,0:T(8,128)(2,1)}), bf16[8,128,1024]{2,1,0:T(8,128)(2,1)}, u32[]{:S(2)}, u32[]{:S(2)}) %all-to-all-start.10) | async-done | bytes 2097184 | tf_op jit(solution)/shard_map/all_to_all | solution.py:238
  315.2 23.6 %all-to-all-done.8 = bf16[8,128,1024]{2,1,0:T(8,128)(2,1)} async-done(((bf16[8,128,1024]{2,1,0:T(8,128)(2,1)}), bf16[8,128,1024]{2,1,0:T(8,128)(2,1)}, u32[]{:S(2)}, u32[]{:S(2)}) %all-to-all-start.8) | async-done | bytes 2097184 | tf_op jit(solution)/shard_map/all_to_all | solution.py:238
  347.4 7.3 %fusion.55 = bf16[8,2,1,64,1024]{4,3,0,1,2:T(8,128)(2,1)} fusion(bf16[2,2,1,3,1024,256]{5,4,1,0,3,2:T(8,128)(2,1)} %bitcast.423, f32[2,2,256,8,64]{2,4,3,1,0:T(8,128)} %fusion.16, bf16[8,2,64,1024,1]{3,2,1,0,4:T(8,128)(2,1)} %bitcast.99), kind=kOutput, calls=%fused_computation.76 | convolution fusion | flops 2151677952 | bytes 10485760 | tf_op jit(solution)/shard_map/szjckf,zkjdf->szjcd/dot_general | solution.py:249
  357.9 10.4 %all-to-all-done.6 = bf16[8,128,1024]{2,1,0:T(8,128)(2,1)S(1)} async-done(((bf16[8,128,1024]{2,1,0:T(8,128)(2,1)}), bf16[8,128,1024]{2,1,0:T(8,128)(2,1)S(1)}, u32[]{:S(2)}, u32[]{:S(2)}) %all-to-all-start.6) | async-done | bytes 2097184 | tf_op jit(solution)/shard_map/all_to_all | solution.py:238
  378.0 7.3 %fusion.52 = bf16[8,2,1,64,1024]{4,3,0,1,2:T(8,128)(2,1)} fusion(bf16[2,2,1,3,1024,256]{5,4,1,0,3,2:T(8,128)(2,1)} %bitcast.425, f32[2,2,256,8,64]{2,4,3,1,0:T(8,128)} %fusion.18, bf16[8,2,64,1024,1]{3,2,1,0,4:T(8,128)(2,1)} %bitcast.81), kind=kOutput, calls=%fused_computation.75 | convolution fusion | flops 2151677952 | bytes 10485760 | tf_op jit(solution)/shard_map/szjckf,zkjdf->szjcd/dot_general | solution.py:249
  388.4 10.4 %all-to-all-done.13 = bf16[8,128,1024]{2,1,0:T(8,128)(2,1)S(1)} async-done(((bf16[8,128,1024]{2,1,0:T(8,128)(2,1)}), bf16[8,128,1024]{2,1,0:T(8,128)(2,1)S(1)}, u32[]{:S(2)}, u32[]{:S(2)}) %all-to-all-start.13) | async-done | bytes 2097184 | tf_op jit(solution)/shard_map/all_to_all | solution.py:252
  407.9 7.3 %fusion.49 = bf16[8,2,1,64,1024]{4,3,0,1,2:T(8,128)(2,1)} fusion(bf16[2,2,1,3,1024,256]{5,4,1,0,3,2:T(8,128)(2,1)} %bitcast.427, f32[2,2,256,8,64]{2,4,3,1,0:T(8,128)} %fusion.20, bf16[8,2,64,1024,1]{3,2,1,0,4:T(8,128)(2,1)} %bitcast.61), kind=kOutput, calls=%fused_computation.74 | convolution fusion | flops 2151677952 | bytes 10485760 | tf_op jit(solution)/shard_map/szjckf,zkjdf->szjcd/dot_general | solution.py:249
  418.4 10.5 %all-to-all-done.11 = bf16[8,128,1024]{2,1,0:T(8,128)(2,1)} async-done(((bf16[8,128,1024]{2,1,0:T(8,128)(2,1)}), bf16[8,128,1024]{2,1,0:T(8,128)(2,1)}, u32[]{:S(2)}, u32[]{:S(2)}) %all-to-all-start.11) | async-done | bytes 2097184 | tf_op jit(solution)/shard_map/all_to_all | solution.py:252
  438.3 7.3 %fusion.46 = bf16[8,2,1,64,1024]{4,3,0,1,2:T(8,128)(2,1)} fusion(bf16[2,2,1,3,1024,256]{5,4,1,0,3,2:T(8,128)(2,1)} %bitcast.429, f32[2,2,256,8,64]{2,4,3,1,0:T(8,128)} %fusion.22, bf16[8,2,64,1024,1]{3,2,1,0,4:T(8,128)(2,1)} %bitcast.411), kind=kOutput, calls=%fused_computation.73 | convolution fusion | flops 2151677952 | bytes 10485760 | tf_op jit(solution)/shard_map/szjckf,zkjdf->szjcd/dot_general | solution.py:249
  448.7 10.4 %all-to-all-done.9 = bf16[8,128,1024]{2,1,0:T(8,128)(2,1)} async-done(((bf16[8,128,1024]{2,1,0:T(8,128)(2,1)}), bf16[8,128,1024]{2,1,0:T(8,128)(2,1)}, u32[]{:S(2)}, u32[]{:S(2)}) %all-to-all-start.9) | async-done | bytes 2097184 | tf_op jit(solution)/shard_map/all_to_all | solution.py:252
  467.8 7.3 %reshape.269 = bf16[256,8192]{1,0:T(8,128)(2,1)} reshape(bf16[16,16,4,16,128]{4,3,2,1,0:T(8,128)(2,1)} %all-to-all-done.3) | data formatting | bytes 8388608 | tf_op jit(solution)/shard_map/reshape | solution.py:195
  (121 shorter events, 163.5 us)
Async XLA Ops:
  7.2 236.2 %copy-start = (bf16[1024,1024]{1,0:T(8,128)(2,1)S(1)}, bf16[1024,1024]{1,0:T(8,128)(2,1)}, u32[]{:S(2)}) copy-start(bf16[1024,1024]{1,0:T(8,128)(2,1)} %param.18) | copy-start | bytes 6291460
  7.2 80.1 %all-gather.5.cloned.1.call-start = ((), (), s32[]{:S(2)}) async-start(), calls=%async_computation.14 | async-start | bytes 4718592 | tf_op jit(solution)/shard_map/all_gather | solution.py:161
  12.9 5.8 %copy-start.9 = (bf16[2,128,1024]{2,1,0:T(8,128)(2,1)S(1)}, bf16[2,128,1024]{2,1,0:T(8,128)(2,1)}, u32[]{:S(2)}) copy-start(bf16[2,128,1024]{2,1,0:T(8,128)(2,1)} %param.13) | copy-start | bytes 1572868
  12.9 53.4 %all-to-all-start.1 = ((bf16[2,1024,8,128]{3,1,0,2:T(8,128)(2,1)}), bf16[2,1024,8,128]{3,1,0,2:T(8,128)(2,1)}, u32[]{:S(2)}, u32[]{:S(2)}) async-start(bf16[2,1024,8,128]{3,1,0,2:T(8,128)(2,1)} %copy.118), calls=%async_computation.1 | async-start | bytes 8388608 | tf_op jit(solution)/shard_map/all_to_all | solution.py:157
  19.0 50.9 %copy-start.10 = (bf16[2,128,8,128]{3,2,1,0:T(8,128)(2,1)S(1)}, bf16[2,128,8,128]{3,2,1,0:T(8,128)(2,1)}, u32[]{:S(2)}) copy-start(bf16[2,128,8,128]{3,2,1,0:T(8,128)(2,1)} %param.14) | copy-start | bytes 1572868
  20.1 58.2 %copy-start.15 = (s32[2]{0:T(128)}, s32[2]{0:T(128)S(1)}, u32[]{:S(2)}) copy-start(s32[2]{0:T(128)S(1)} %fusion.134.len_ref) | copy-start | bytes 28
  66.3 24.1 %all-to-all-start = ((bf16[2,128,8,128]{1,3,0,2:T(8,128)(2,1)}), bf16[2,128,8,128]{1,3,0,2:T(8,128)(2,1)S(1)}, u32[]{:S(2)}, u32[]{:S(2)}) async-start(bf16[2,128,8,128]{1,3,0,2:T(8,128)(2,1)} %copy.114), calls=%async_computation | async-start | bytes 1048576 | tf_op jit(solution)/shard_map/all_to_all | solution.py:159
  70.8 16.4 %copy-start.14 = (s32[2,128]{1,0:T(2,128)S(1)}, s32[2,128]{1,0:T(2,128)}, u32[]{:S(2)}) copy-start(s32[2,128]{1,0:T(2,128)} %param.23) | copy-start | bytes 3076
  90.5 11.8 %all-to-all-start.2 = ((bf16[2,128,8,128]{3,1,0,2:T(8,128)(2,1)}), bf16[2,128,8,128]{3,1,0,2:T(8,128)(2,1)S(1)}, u32[]{:S(2)}, u32[]{:S(2)}) async-start(bf16[2,128,8,128]{3,1,0,2:T(8,128)(2,1)} %copy.120), calls=%async_computation.2 | async-start | bytes 1048576 | tf_op jit(solution)/shard_map/all_to_all | solution.py:158
  102.2 28.2 %all-to-all-start.4 = ((s32[16,1,16]{2,1,0:T(1,128)}), s32[16,1,16]{2,1,0:T(1,128)S(1)}, u32[]{:S(2)}, u32[]{:S(2)}) async-start(s32[16,1,16]{2,1,0:T(1,128)} %all_to_all.92), calls=%async_computation.4 | async-start | bytes 16384 | tf_op jit(solution)/shard_map/all_to_all | solution.py:179
  130.5 98.7 %all-to-all-start.3 = ((bf16[16,16,4,16,128]{4,3,2,1,0:T(8,128)(2,1)}), bf16[16,16,4,16,128]{4,3,2,1,0:T(8,128)(2,1)}, u32[]{:S(2)}, u32[]{:S(2)}) async-start(bf16[16,16,4,16,128]{4,3,2,1,0:T(8,128)(2,1)} %bitcast.398), calls=%async_computation.3 | async-start | bytes 8388608 | tf_op jit(solution)/shard_map/all_to_all | solution.py:178
  136.5 82.8 %all-gather.7.cloned.1.call-start = ((), (), s32[]{:S(2)}) async-start(), calls=%async_computation.15 | async-start | bytes 9437184 | tf_op jit(solution)/shard_map/all_gather | solution.py:165
  230.2 11.5 %all-to-all-start.5 = ((bf16[2,256,4,128]{3,2,0,1:T(4,128)(2,1)}), bf16[2,256,4,128]{3,2,0,1:T(4,128)(2,1)S(1)}, u32[]{:S(2)}, u32[]{:S(2)}) async-start(bf16[2,256,4,128]{3,2,0,1:T(4,128)(2,1)} %copy.123), calls=%async_computation.5 | async-start | bytes 1048576 | tf_op jit(solution)/shard_map/all_to_all | solution.py:187
  248.5 4.5 copy-start.7
  248.5 30.2 %all-to-all-start.12 = ((bf16[8,128,1024]{2,1,0:T(8,128)(2,1)}), bf16[8,128,1024]{2,1,0:T(8,128)(2,1)}, u32[]{:S(2)}, u32[]{:S(2)}) async-start(bf16[8,128,1024]{2,1,0:T(8,128)(2,1)} %bitcast.407), calls=%async_computation.12 | async-start | bytes 4194304 | tf_op jit(solution)/shard_map/all_to_all | solution.py:238
  278.7 30.1 %all-to-all-start.10 = ((bf16[8,128,1024]{2,1,0:T(8,128)(2,1)}), bf16[8,128,1024]{2,1,0:T(8,128)(2,1)}, u32[]{:S(2)}, u32[]{:S(2)}) async-start(bf16[8,128,1024]{2,1,0:T(8,128)(2,1)} %bitcast.406), calls=%async_computation.10 | async-start | bytes 4194304 | tf_op jit(solution)/shard_map/all_to_all | solution.py:238
  308.8 30.1 %all-to-all-start.8 = ((bf16[8,128,1024]{2,1,0:T(8,128)(2,1)}), bf16[8,128,1024]{2,1,0:T(8,128)(2,1)}, u32[]{:S(2)}, u32[]{:S(2)}) async-start(bf16[8,128,1024]{2,1,0:T(8,128)(2,1)} %bitcast.405), calls=%async_computation.8 | async-start | bytes 4194304 | tf_op jit(solution)/shard_map/all_to_all | solution.py:238
  338.8 29.4 %all-to-all-start.6 = ((bf16[8,128,1024]{2,1,0:T(8,128)(2,1)}), bf16[8,128,1024]{2,1,0:T(8,128)(2,1)S(1)}, u32[]{:S(2)}, u32[]{:S(2)}) async-start(bf16[8,128,1024]{2,1,0:T(8,128)(2,1)} %bitcast.401), calls=%async_computation.6 | async-start | bytes 4194304 | tf_op jit(solution)/shard_map/all_to_all | solution.py:238
  369.6 29.2 %all-to-all-start.13 = ((bf16[8,128,1024]{2,1,0:T(8,128)(2,1)}), bf16[8,128,1024]{2,1,0:T(8,128)(2,1)S(1)}, u32[]{:S(2)}, u32[]{:S(2)}) async-start(bf16[8,128,1024]{2,1,0:T(8,128)(2,1)} %bitcast.403), calls=%async_computation.13 | async-start | bytes 4194304 | tf_op jit(solution)/shard_map/all_to_all | solution.py:252
  398.8 30.1 %all-to-all-start.11 = ((bf16[8,128,1024]{2,1,0:T(8,128)(2,1)}), bf16[8,128,1024]{2,1,0:T(8,128)(2,1)}, u32[]{:S(2)}, u32[]{:S(2)}) async-start(bf16[8,128,1024]{2,1,0:T(8,128)(2,1)} %bitcast.404), calls=%async_computation.11 | async-start | bytes 4194304 | tf_op jit(solution)/shard_map/all_to_all | solution.py:252
  428.9 30.3 %all-to-all-start.9 = ((bf16[8,128,1024]{2,1,0:T(8,128)(2,1)}), bf16[8,128,1024]{2,1,0:T(8,128)(2,1)}, u32[]{:S(2)}, u32[]{:S(2)}) async-start(bf16[8,128,1024]{2,1,0:T(8,128)(2,1)} %bitcast.402), calls=%async_computation.9 | async-start | bytes 4194304 | tf_op jit(solution)/shard_map/all_to_all | solution.py:252
  459.2 4.5 copy-start.12
  459.2 39.5 %all-to-all-start.7 = ((bf16[8,128,1024]{2,1,0:T(8,128)(2,1)}), bf16[8,128,1024]{2,1,0:T(8,128)(2,1)}, u32[]{:S(2)}, u32[]{:S(2)}) async-start(bf16[8,128,1024]{2,1,0:T(8,128)(2,1)} %bitcast.400), calls=%async_computation.7 | async-start | bytes 4194304 | tf_op jit(solution)/shard_map/all_to_all | solution.py:252
  501.4 4.8 copy-start.1
  (10 other events, 19.4 us)
Sparse Core Ops, SparseCore 0:
  9.6 77.6 all-gather.4
  138.9 80.3 all-gather.6

commit v13 on v11

--- a/solution.py
+++ b/solution.py
@@ -181,9 +181,7 @@
         ),
     )
     attn_heads = attend(query_heads, cache_heads, span_heads, lengths)
-    attn_heads, full_weights, arrived, where_to = lax.optimization_barrier(
-        (attn_heads, full_weights, arrived, where_to)
-    )
+    attn_heads, arrived, where_to = lax.optimization_barrier((attn_heads, arrived, where_to))
     attn = lax.all_to_all(attn_heads, "kv", split_axis=1, concat_axis=2, tiled=True).reshape(
         row_count, kv_heads * group_width
     )

time: 479 us -> 484 us (1.010)
  waiting for transfers between devices: 232 us -> 245 us
  Pallas kernels: 29.6 us -> 22.6 us
    all_to_all x1, waiting for transfers between devices: 9.92 us -> 56.3 us  [body(): lax.all_to_all(outgoing, REQ, split_axis=0, concat_axis=0, tiled=True)]
    all_to_all x2, waiting for transfers between devices: 70.5 us -> 44 us  [body(): lax.all_to_all(buffer.reshape(side, per_dev * size, width_model), 'rlow',...]
    all_gather x1, waiting for transfers between devices: 38.2 us -> 30.3 us  [body(): full_weights = lax.all_gather(pair_weights, 'kv', axis=1, tiled=False)]
    pallas_call x1, Pallas kernels: 29.6 us -> 22.6 us  [attend(): pl.pallas_call(functools.partial(attend_kernel, tk=tk, head_dim=head_dim)...]
  transfers between devices with their start and end apart: 12 -> 12, of which waited for: 10 -> 9; matrix products, arithmetic and copies ran while one was open for 27% -> 27% of each run, Pallas kernels for 6% -> 5%
where the time goes in v13:
time: 484 us; the launch traced here: 480 us
  waiting for transfers between devices  245 us (51%)
  local copies, waits for them, and re-layouts  65.2 us (13%)
  matrix products  63.7 us (13%)
  starting transfers between devices  48.9 us (10%)
  Pallas kernels  22.6 us (5%)
  other arithmetic  21.1 us (4%)
  between operations  14.4 us (3%)
    all_to_all x1, waiting for transfers between devices, body(): lax.all_to_all(outgoing, REQ, split_axis=0, concat_axis=0, tiled=True)  56.3 us
    all_to_all x2, waiting for transfers between devices, body(): lax.all_to_all(expert_out.reshape(side, per_dev * size, width_model), 'rl...  48.8 us
    all_to_all x1, waiting for transfers between devices, body(): lax.all_to_all(cache, 'kv', split_axis=2, concat_axis=1, tiled=True)  46.3 us
    all_to_all x2, waiting for transfers between devices, body(): lax.all_to_all(buffer.reshape(side, per_dev * size, width_model), 'rlow',...  44 us
    all_gather x1, waiting for transfers between devices, body(): full_weights = lax.all_gather(pair_weights, 'kv', axis=1, tiled=False)  30.3 us
    pallas_call x1, Pallas kernels, attend(): pl.pallas_call(functools.partial(attend_kernel, tk=tk, head_dim=head_dim)...  22.6 us
    dot_general x2, matrix products, body(): jnp.einsum('szjckf,zkjdf->szjcd', activated, weights[:, :, :, 2], preferr...  20.5 us
    dot_general x2, matrix products, body(): jnp.einsum('szjcd,zkjdf->szjckf', grouped, weights[:, :, :, 1], preferred...  14.4 us
  transfers between devices with their start and end apart: 12, of which 9 were waited for; matrix products, arithmetic and copies ran while one was open for 27% of the time, Pallas kernels for 5%

profile of v13, /device:TPU:16, one launch (start us, length us, event | category | flops | bytes accessed | tf_op | source)
XLA Modules:
  0.0 480.4 jit_solution(4652933412765374957)
XLA Ops:
  10.0 5.0 %copy.116 = bf16[2,1024,8,128]{3,1,0,2:T(8,128)(2,1)} copy(bf16[2,1024,8,128]{3,2,1,0:T(8,128)(2,1)} %param.15) | data formatting | bytes 8388608 | tf_op args[3]
  15.0 6.0 %all-to-all-start.1 = ((bf16[2,1024,8,128]{3,1,0,2:T(8,128)(2,1)}), bf16[2,1024,8,128]{3,1,0,2:T(8,128)(2,1)}, u32[]{:S(2)}, u32[]{:S(2)}) async-start(bf16[2,1024,8,128]{3,1,0,2:T(8,128)(2,1)} %copy.116), calls=%async_computation.1 | async-start | bytes 8388608 | tf_op jit(solution)/shard_map/all_to_all | solution.py:157
  22.4 46.3 %all-to-all-done.1 = bf16[2,1024,8,128]{3,1,0,2:T(8,128)(2,1)} async-done(((bf16[2,1024,8,128]{3,1,0,2:T(8,128)(2,1)}), bf16[2,1024,8,128]{3,1,0,2:T(8,128)(2,1)}, u32[]{:S(2)}, u32[]{:S(2)}) %all-to-all-start.1) | async-done | bytes 4194336 | tf_op jit(solution)/shard_map/all_to_all | solution.py:157
  74.2 7.5 %copy.117 = bf16[2,2,1024,4,128]{4,3,2,1,0:T(4,128)(2,1)} copy(bf16[2,2,1024,4,128]{4,2,0,3,1:T(8,128)(2,1)} %bitcast.7) | data formatting | bytes 8388608 | tf_op jit(solution)/shard_map/all_to_all | solution.py:157
  81.6 6.2 %all-gather.5.cloned.1.call-done = bf16[2,3,1024,256]{2,3,0,1:T(8,128)(2,1)} async-done(((bf16[1,3,1024,256]{2,3,0,1:T(8,128)(2,1)}), bf16[2,3,1024,256]{2,3,0,1:T(8,128)(2,1)}) %all-gather.5.cloned.1.call-update) | async-done | bytes 3145744 | tf_op jit(solution)/shard_map/all_gather | solution.py:161
  97.1 5.6 %all-to-all-done.2 = bf16[2,128,8,128]{3,1,0,2:T(8,128)(2,1)S(1)} async-done(((bf16[2,128,8,128]{3,1,0,2:T(8,128)(2,1)}), bf16[2,128,8,128]{3,1,0,2:T(8,128)(2,1)S(1)}, u32[]{:S(2)}, u32[]{:S(2)}) %all-to-all-start.2) | async-done | bytes 524320 | tf_op jit(solution)/shard_map/all_to_all | solution.py:158
  102.7 7.3 %all-to-all-start.4 = ((s32[16,1,16]{2,1,0:T(1,128)}), s32[16,1,16]{2,1,0:T(1,128)S(1)}, u32[]{:S(2)}, u32[]{:S(2)}) async-start(s32[16,1,16]{2,1,0:T(1,128)} %all_to_all.80), calls=%async_computation.4 | async-start | bytes 16384 | tf_op jit(solution)/shard_map/all_to_all | solution.py:179
  110.0 12.5 %broadcast_select_fusion = bf16[2,2048,4,128]{3,2,1,0:T(4,128)(2,1)S(1)} fusion(bf16[2,2048,4,128]{3,2,1,0:T(4,128)(2,1)} %bitcast.242, pred[2,2048]{1,0:T(4,128)(4,1)S(1)} %iota_compare_fusion.4), kind=kLoop, calls=%fused_computation.25 | loop fusion | flops 2097152 | bytes 8392704 | tf_op jit(solution)/shard_map/jit(_where)/select_n | solution.py:168
  125.6 5.2 %gather_fusion = bf16[256,4,16,128]{3,2,1,0:T(8,128)(2,1)} fusion(bf16[256,4,16,128]{3,2,1,0:T(8,128)(2,1)} %bitcast.250, s32[1024]{0:T(1024)S(1)} %pad_clamp_fusion), kind=kCustom, calls=%fused_computation | custom fusion | bytes 8389632 | tf_op jit(solution)/shard_map/gather | solution.py:128
  130.9 6.2 %all-to-all-start.3 = ((bf16[16,16,4,16,128]{4,3,2,1,0:T(8,128)(2,1)}), bf16[16,16,4,16,128]{4,3,2,1,0:T(8,128)(2,1)}, u32[]{:S(2)}, u32[]{:S(2)}) async-start(bf16[16,16,4,16,128]{4,3,2,1,0:T(8,128)(2,1)} %bitcast.245), calls=%async_computation.3 | async-start | bytes 8388608 | tf_op jit(solution)/shard_map/all_to_all | solution.py:178
  142.5 7.2 %reshape.175.c_ref = bf16[2,2048,512]{2,1,0:T(8,128)(2,1)} reshape(bf16[2,2048,4,128]{3,2,1,0:T(4,128)(2,1)} %bitcast.243) | data formatting | bytes 8388608 | tf_op jit(solution)/shard_map/reshape | solution.py:100
  149.7 22.6 %shard_map.131 = bf16[2,256,512]{2,1,0:T(8,128)(2,1)} custom-call(s32[2]{0:T(128)} %copy-done.12, bf16[2,256,512]{2,1,0:T(8,128)(2,1)} %reshape.174.q_ref, bf16[2,2048,512]{2,1,0:T(8,128)(2,1)} %reshape.175.c_ref, bf16[2,256,512]{2,1,0:T(8,128)(2,1)} %reshape.176.s_ref), custom_call_target="tpu_custom_call" | custom-call | flops 7247757312 | bytes 5767168 | tf_op jit(solution)/shard_map/pallas_call | solution.py:103
  173.4 56.3 %all-to-all-done.3 = bf16[16,16,4,16,128]{4,3,2,1,0:T(8,128)(2,1)} async-done(((bf16[16,16,4,16,128]{4,3,2,1,0:T(8,128)(2,1)}), bf16[16,16,4,16,128]{4,3,2,1,0:T(8,128)(2,1)}, u32[]{:S(2)}, u32[]{:S(2)}) %all-to-all-start.3) | async-done | bytes 4194336 | tf_op jit(solution)/shard_map/all_to_all | solution.py:178
  235.8 6.4 %all-to-all-done.5 = bf16[2,256,4,128]{3,2,0,1:T(4,128)(2,1)S(1)} async-done(((bf16[2,256,4,128]{3,2,0,1:T(4,128)(2,1)}), bf16[2,256,4,128]{3,2,0,1:T(4,128)(2,1)S(1)}, u32[]{:S(2)}, u32[]{:S(2)}) %all-to-all-start.5) | async-done | bytes 524320 | tf_op jit(solution)/shard_map/all_to_all | solution.py:185
  258.2 44.0 %all-to-all-done.6 = bf16[8,256,1024]{2,1,0:T(8,128)(2,1)} async-done(((bf16[8,256,1024]{2,1,0:T(8,128)(2,1)}), bf16[8,256,1024]{2,1,0:T(8,128)(2,1)}, u32[]{:S(2)}, u32[]{:S(2)}) %all-to-all-start.6) | async-done | bytes 4194336 | tf_op jit(solution)/shard_map/all_to_all | solution.py:236
  307.0 30.3 %all-gather.7.cloned.1.call-done = bf16[2,2,3,1024,256]{3,4,1,0,2:T(8,128)(2,1)} async-done(((bf16[2,1,3,1024,256]{3,4,1,0,2:T(8,128)(2,1)}), bf16[2,2,3,1024,256]{3,4,1,0,2:T(8,128)(2,1)}) %all-gather.7.cloned.1.call-update) | async-done | bytes 6291472 | tf_op jit(solution)/shard_map/all_gather | solution.py:165
  337.3 7.2 %fusion.15 = f32[2,2,256,8,128]{4,2,3,1,0:T(8,128)} fusion(bf16[8,2,128,1024,1]{3,2,1,0,4:T(8,128)(2,1)} %bitcast.34, bf16[2,2,1,3,1024,256]{4,5,1,0,3,2:T(8,128)(2,1)} %bitcast.261), kind=kOutput, calls=%fused_computation.30 | convolution fusion | flops 2147483648 | bytes 10485760 | tf_op jit(solution)/shard_map/szjcd,zkjdf->szjckf/dot_general | solution.py:243
  344.5 10.2 %fusion.1 = bf16[8,2,1,128,1024]{4,3,0,1,2:T(8,128)(2,1)} fusion(f32[2,2,256,8,128]{4,2,3,1,0:T(8,128)} %fusion.15, bf16[2,2,1,3,1024,256]{4,5,1,0,3,2:T(8,128)(2,1)} %bitcast.262, bf16[8,2,128,1024,1]{3,2,1,0,4:T(8,128)(2,1)} %bitcast.34), kind=kOutput, calls=%fused_computation.8 | convolution fusion | flops 4303355904 | bytes 16777216 | tf_op jit(solution)/shard_map/szjckf,zkjdf->szjcd/dot_general | solution.py:247
  364.1 7.2 %fusion.11 = f32[2,2,256,8,128]{4,2,3,1,0:T(8,128)} fusion(bf16[8,2,128,1024,1]{3,2,1,0,4:T(8,128)(2,1)} %bitcast.58, bf16[2,2,1,3,1024,256]{4,5,1,0,3,2:T(8,128)(2,1)} %bitcast.263), kind=kOutput, calls=%fused_computation.26 | convolution fusion | flops 2147483648 | bytes 10485760 | tf_op jit(solution)/shard_map/szjcd,zkjdf->szjckf/dot_general | solution.py:243
  371.3 10.2 %fusion.2 = bf16[8,2,1,128,1024]{4,3,0,1,2:T(8,128)(2,1)} fusion(f32[2,2,256,8,128]{4,2,3,1,0:T(8,128)} %fusion.11, bf16[2,2,1,3,1024,256]{4,5,1,0,3,2:T(8,128)(2,1)} %bitcast.264, bf16[8,2,128,1024,1]{3,2,1,0,4:T(8,128)(2,1)} %bitcast.58), kind=kOutput, calls=%fused_computation.9 | convolution fusion | flops 4303355904 | bytes 16777216 | tf_op jit(solution)/shard_map/szjckf,zkjdf->szjcd/dot_general | solution.py:247
  386.3 25.9 %all-to-all-done.7 = bf16[8,256,1024]{2,1,0:T(8,128)(2,1)} async-done(((bf16[8,256,1024]{2,1,0:T(8,128)(2,1)}), bf16[8,256,1024]{2,1,0:T(8,128)(2,1)}, u32[]{:S(2)}, u32[]{:S(2)}) %all-to-all-start.7) | async-done | bytes 4194336 | tf_op jit(solution)/shard_map/all_to_all | solution.py:250
  412.2 4.9 %all-to-all-start.9 = ((bf16[8,256,1024]{2,1,0:T(8,128)(2,1)}), bf16[8,256,1024]{2,1,0:T(8,128)(2,1)}, u32[]{:S(2)}, u32[]{:S(2)}) async-start(bf16[8,256,1024]{2,1,0:T(8,128)(2,1)} %bitcast.246), calls=%async_computation.9 | async-start | bytes 8388608 | tf_op jit(solution)/shard_map/all_to_all | solution.py:250
  420.1 7.3 %reshape.201 = bf16[256,8192]{1,0:T(8,128)(2,1)} reshape(bf16[16,16,4,16,128]{4,3,2,1,0:T(8,128)(2,1)} %all-to-all-done.3) | data formatting | bytes 8388608 | tf_op jit(solution)/shard_map/reshape | solution.py:193
  442.2 22.9 %all-to-all-done.9 = bf16[8,256,1024]{2,1,0:T(8,128)(2,1)} async-done(((bf16[8,256,1024]{2,1,0:T(8,128)(2,1)}), bf16[8,256,1024]{2,1,0:T(8,128)(2,1)}, u32[]{:S(2)}, u32[]{:S(2)}) %all-to-all-start.9) | async-done | bytes 4194336 | tf_op jit(solution)/shard_map/all_to_all | solution.py:250
  (95 shorter events, 95.7 us)
Async XLA Ops:
  7.2 236.7 %copy-start = (bf16[1024,1024]{1,0:T(8,128)(2,1)S(1)}, bf16[1024,1024]{1,0:T(8,128)(2,1)}, u32[]{:S(2)}) copy-start(bf16[1024,1024]{1,0:T(8,128)(2,1)} %param.18) | copy-start | bytes 6291460
  7.2 80.6 %all-gather.5.cloned.1.call-start = ((), (), s32[]{:S(2)}) async-start(), calls=%async_computation.10 | async-start | bytes 4718592 | tf_op jit(solution)/shard_map/all_gather | solution.py:161
  15.0 6.0 %copy-start.7 = (bf16[2,128,1024]{2,1,0:T(8,128)(2,1)S(1)}, bf16[2,128,1024]{2,1,0:T(8,128)(2,1)}, u32[]{:S(2)}) copy-start(bf16[2,128,1024]{2,1,0:T(8,128)(2,1)} %param.13) | copy-start | bytes 1572868
  15.0 7.1 %copy-start.13 = (s32[32]{0:T(128)S(1)}, s32[32]{0:T(128)}, u32[]{:S(2)}) copy-start(s32[32]{0:T(128)} %param.16) | copy-start | bytes 388
  15.0 7.2 %copy-start.14 = (s32[32]{0:T(128)S(1)}, s32[32]{0:T(128)}, u32[]{:S(2)}) copy-start(s32[32]{0:T(128)} %param.17) | copy-start | bytes 388
  15.0 53.6 %all-to-all-start.1 = ((bf16[2,1024,8,128]{3,1,0,2:T(8,128)(2,1)}), bf16[2,1024,8,128]{3,1,0,2:T(8,128)(2,1)}, u32[]{:S(2)}, u32[]{:S(2)}) async-start(bf16[2,1024,8,128]{3,1,0,2:T(8,128)(2,1)} %copy.116), calls=%async_computation.1 | async-start | bytes 8388608 | tf_op jit(solution)/shard_map/all_to_all | solution.py:157
  22.4 59.3 %copy-start.12 = (s32[2]{0:T(128)}, s32[2]{0:T(128)S(1)}, u32[]{:S(2)}) copy-start(s32[2]{0:T(128)S(1)} %fusion.48.len_ref) | copy-start | bytes 28
  68.6 22.3 %all-to-all-start = ((bf16[2,128,8,128]{1,3,0,2:T(8,128)(2,1)}), bf16[2,128,8,128]{1,3,0,2:T(8,128)(2,1)S(1)}, u32[]{:S(2)}, u32[]{:S(2)}) async-start(bf16[2,128,8,128]{1,3,0,2:T(8,128)(2,1)} %copy.112), calls=%async_computation | async-start | bytes 1048576 | tf_op jit(solution)/shard_map/all_to_all | solution.py:159
  74.2 13.6 %copy-start.11 = (s32[2,128]{1,0:T(2,128)S(1)}, s32[2,128]{1,0:T(2,128)}, u32[]{:S(2)}) copy-start(s32[2,128]{1,0:T(2,128)} %param.23) | copy-start | bytes 3076
  91.0 11.8 %all-to-all-start.2 = ((bf16[2,128,8,128]{3,1,0,2:T(8,128)(2,1)}), bf16[2,128,8,128]{3,1,0,2:T(8,128)(2,1)S(1)}, u32[]{:S(2)}, u32[]{:S(2)}) async-start(bf16[2,128,8,128]{3,1,0,2:T(8,128)(2,1)} %copy.118), calls=%async_computation.2 | async-start | bytes 1048576 | tf_op jit(solution)/shard_map/all_to_all | solution.py:158
  102.7 28.1 %all-to-all-start.4 = ((s32[16,1,16]{2,1,0:T(1,128)}), s32[16,1,16]{2,1,0:T(1,128)S(1)}, u32[]{:S(2)}, u32[]{:S(2)}) async-start(s32[16,1,16]{2,1,0:T(1,128)} %all_to_all.80), calls=%async_computation.4 | async-start | bytes 16384 | tf_op jit(solution)/shard_map/all_to_all | solution.py:179
  130.9 6.2 %copy-start.8 = (s32[256,8]{0,1:T(8,128)S(1)}, s32[256,8]{0,1:T(8,128)}, u32[]{:S(2)}) copy-start(s32[256,8]{0,1:T(8,128)} %param.20) | copy-start | bytes 24580
  130.9 98.8 %all-to-all-start.3 = ((bf16[16,16,4,16,128]{4,3,2,1,0:T(8,128)(2,1)}), bf16[16,16,4,16,128]{4,3,2,1,0:T(8,128)(2,1)}, u32[]{:S(2)}, u32[]{:S(2)}) async-start(bf16[16,16,4,16,128]{4,3,2,1,0:T(8,128)(2,1)} %bitcast.245), calls=%async_computation.3 | async-start | bytes 8388608 | tf_op jit(solution)/shard_map/all_to_all | solution.py:178
  230.7 11.5 %all-to-all-start.5 = ((bf16[2,256,4,128]{3,2,0,1:T(4,128)(2,1)}), bf16[2,256,4,128]{3,2,0,1:T(4,128)(2,1)S(1)}, u32[]{:S(2)}, u32[]{:S(2)}) async-start(bf16[2,256,4,128]{3,2,0,1:T(4,128)(2,1)} %copy.121), calls=%async_computation.5 | async-start | bytes 1048576 | tf_op jit(solution)/shard_map/all_to_all | solution.py:185
  234.2 11.8 %copy-start.9 = (f32[1024]{0:T(1024)S(1)}, f32[1024]{0:T(1024)}, u32[]{:S(2)}) copy-start(f32[1024]{0:T(1024)} %param.19) | copy-start | bytes 12292
  249.4 5.4 %copy-start.3 = (pred[16,256,256]{2,1,0:T(32,128)(4,1)S(1)}, pred[16,256,256]{2,1,0:T(32,128)(4,1)}, u32[]{:S(2)}) copy-start(pred[16,256,256]{2,1,0:T(32,128)(4,1)} %iota_compare_fusion) | copy-start | bytes 3145732
  249.4 52.9 %all-to-all-start.6 = ((bf16[8,256,1024]{2,1,0:T(8,128)(2,1)}), bf16[8,256,1024]{2,1,0:T(8,128)(2,1)}, u32[]{:S(2)}, u32[]{:S(2)}) async-start(bf16[8,256,1024]{2,1,0:T(8,128)(2,1)} %bitcast.249), calls=%async_computation.6 | async-start | bytes 8388608 | tf_op jit(solution)/shard_map/all_to_all | solution.py:236
  254.1 83.2 %all-gather.7.cloned.1.call-start = ((), (), s32[]{:S(2)}) async-start(), calls=%async_computation.11 | async-start | bytes 9437184 | tf_op jit(solution)/shard_map/all_gather | solution.py:165
  302.2 57.3 %all-to-all-start.8 = ((bf16[8,256,1024]{2,1,0:T(8,128)(2,1)}), bf16[8,256,1024]{2,1,0:T(8,128)(2,1)}, u32[]{:S(2)}, u32[]{:S(2)}) async-start(bf16[8,256,1024]{2,1,0:T(8,128)(2,1)} %bitcast.247), calls=%async_computation.8 | async-start | bytes 8388608 | tf_op jit(solution)/shard_map/all_to_all | solution.py:236
  359.5 52.7 %all-to-all-start.7 = ((bf16[8,256,1024]{2,1,0:T(8,128)(2,1)}), bf16[8,256,1024]{2,1,0:T(8,128)(2,1)}, u32[]{:S(2)}, u32[]{:S(2)}) async-start(bf16[8,256,1024]{2,1,0:T(8,128)(2,1)} %bitcast.248), calls=%async_computation.7 | async-start | bytes 8388608 | tf_op jit(solution)/shard_map/all_to_all | solution.py:250
  412.2 5.0 %copy-start.10 = (f32[256,8]{0,1:T(8,128)S(1)}, f32[256,8]{0,1:T(8,128)}, u32[]{:S(2)}) copy-start(f32[256,8]{0,1:T(8,128)} %param.21) | copy-start | bytes 24580
  412.2 52.9 %all-to-all-start.9 = ((bf16[8,256,1024]{2,1,0:T(8,128)(2,1)}), bf16[8,256,1024]{2,1,0:T(8,128)(2,1)}, u32[]{:S(2)}, u32[]{:S(2)}) async-start(bf16[8,256,1024]{2,1,0:T(8,128)(2,1)} %bitcast.246), calls=%async_computation.9 | async-start | bytes 8388608 | tf_op jit(solution)/shard_map/all_to_all | solution.py:250
  418.0 16.1 %copy-start.4 = (bf16[16,256,256]{2,1,0:T(8,128)(2,1)}, bf16[16,256,256]{2,1,0:T(8,128)(2,1)S(1)}, u32[]{:S(2)}) copy-start(bf16[16,256,256]{2,1,0:T(8,128)(2,1)S(1)} %fusion) | copy-start | bytes 6291460
  465.1 8.5 %copy-start.1 = (bf16[1024,1024]{1,0:T(8,128)(2,1)S(1)}, bf16[1024,1024]{1,0:T(8,128)(2,1)}, u32[]{:S(2)}) copy-start(bf16[1024,1024]{1,0:T(8,128)(2,1)} %param.18) | copy-start | bytes 6291460
  (3 other events, 10.0 us)
Sparse Core Ops, SparseCore 0:
  10.1 77.6 all-gather.4
  256.4 80.7 all-gather.6

commit v14 on v12

--- a/solution.py
+++ b/solution.py
@@ -226,11 +226,12 @@
     combine = jnp.where(selector, weight_of[:, None, :], 0.0)
     combine_hi = combine.astype(jnp.bfloat16)
     combine_lo = (combine - combine_hi.astype(jnp.float32)).astype(jnp.bfloat16)
-    chunks = 4 if capacity % 32 == 0 else 1
-    size = capacity // chunks
+    edge = (capacity * 5 // 16) // 8 * 8
+    bounds = [0, edge, capacity - edge, capacity] if edge > 0 else [0, capacity]
     expert_sum = jnp.zeros((row_count, width_model), jnp.float32)
-    for chunk in range(chunks):
-        rows = slice(chunk * size, (chunk + 1) * size)
+    for lo, hi in zip(bounds[:-1], bounds[1:]):
+        rows = slice(lo, hi)
+        size = hi - lo
         buffer = jnp.einsum(
             "ect,td->ecd", selector[:, rows].astype(jnp.bfloat16), normed,
             preferred_element_type=jnp.float32,

time: 523 us -> 499 us (0.954)
  waiting for transfers between devices: 233 us -> 222 us
  matrix products: 87.1 us -> 77.4 us
  Pallas kernels: 26.1 us -> 32.9 us
  starting transfers between devices: 63.9 us -> 57.1 us
    all_gather x1, waiting for transfers between devices: 41.8 us -> 34.9 us  [body(): full_weights = lax.all_gather(pair_weights, 'kv', axis=1, tiled=False)]
    pallas_call x1, Pallas kernels: 26.1 us -> 32.9 us  [attend(): pl.pallas_call(functools.partial(attend_kernel, tk=tk, head_dim=head_dim)...]
    all_to_all x4 -> x3, waiting for transfers between devices: 81.3 us -> 77.2 us  [body(): lax.all_to_all(buffer.reshape(side, per_dev * size, width_model), 'rlow',...]
    all_to_all x4 -> x3, starting transfers between devices: 17.1 us -> 13.7 us  [body(): lax.all_to_all(expert_out.reshape(side, per_dev * size, width_model), 'rl...]
    all_to_all x4 -> x3, starting transfers between devices: 17 us -> 13.6 us  [body(): lax.all_to_all(buffer.reshape(side, per_dev * size, width_model), 'rlow',...]
    dot_general x4 -> x3, matrix products: 29.2 us -> 26.1 us  [body(): jnp.einsum('szjckf,zkjdf->szjcd', activated, weights[:, :, :, 2], preferr...]
    dot_general x4 -> x3, matrix products: 19.2 us -> 16.8 us  [body(): jnp.einsum('szjcd,zkjdf->szjckf', grouped, weights[:, :, :, 1], preferred...]
    dot_general x4 -> x3, matrix products: 13.2 us -> 11.3 us  [body(): jnp.einsum('ect,ecd->td', combine_hi[:, rows], returned, preferred_elemen...]
  transfers between devices with their start and end apart: 16 -> 14, of which waited for: 13 -> 12; matrix products, arithmetic and copies ran while one was open for 31% -> 30% of each run, Pallas kernels for 5% -> 7%
where the time goes in v14:
time: 499 us; the launch traced here: 490 us
  waiting for transfers between devices  222 us (44%)
  matrix products  77.4 us (16%)
  local copies, waits for them, and re-layouts  64.6 us (13%)
  starting transfers between devices  57.1 us (11%)
  Pallas kernels  32.9 us (7%)
  other arithmetic  21.3 us (4%)
  between operations  14.9 us (3%)
    all_to_all x3, waiting for transfers between devices, body(): lax.all_to_all(buffer.reshape(side, per_dev * size, width_model), 'rlow',...  77.2 us
    all_to_all x1, waiting for transfers between devices, body(): lax.all_to_all(cache, 'kv', split_axis=2, concat_axis=1, tiled=True)  46.3 us
    all_gather x1, waiting for transfers between devices, body(): full_weights = lax.all_gather(pair_weights, 'kv', axis=1, tiled=False)  34.9 us
    pallas_call x1, Pallas kernels, attend(): pl.pallas_call(functools.partial(attend_kernel, tk=tk, head_dim=head_dim)...  32.9 us
    all_to_all x3, waiting for transfers between devices, body(): lax.all_to_all(expert_out.reshape(side, per_dev * size, width_model), 'rl...  32.2 us
    dot_general x3, matrix products, body(): jnp.einsum('szjckf,zkjdf->szjcd', activated, weights[:, :, :, 2], preferr...  26.1 us
    dot_general x3, matrix products, body(): jnp.einsum('szjcd,zkjdf->szjckf', grouped, weights[:, :, :, 1], preferred...  16.8 us
    all_to_all x3, starting transfers between devices, body(): lax.all_to_all(expert_out.reshape(side, per_dev * size, width_model), 'rl...  13.7 us
  transfers between devices with their start and end apart: 14, of which 12 were waited for; matrix products, arithmetic and copies ran while one was open for 30% of the time, Pallas kernels for 7%

profile of v14, /device:TPU:16, one launch (start us, length us, event | category | flops | bytes accessed | tf_op | source)
XLA Modules:
  0.0 489.9 jit_solution(7035565098923090399)
XLA Ops:
  12.9 5.7 %all-to-all-start.1 = ((bf16[2,1024,8,128]{3,1,0,2:T(8,128)(2,1)}), bf16[2,1024,8,128]{3,1,0,2:T(8,128)(2,1)}, u32[]{:S(2)}, u32[]{:S(2)}) async-start(bf16[2,1024,8,128]{3,1,0,2:T(8,128)(2,1)} %copy.105), calls=%async_computation.1 | async-start | bytes 8388608 | tf_op jit(solution)/shard_map/all_to_all | solution.py:157
  20.1 46.3 %all-to-all-done.1 = bf16[2,1024,8,128]{3,1,0,2:T(8,128)(2,1)} async-done(((bf16[2,1024,8,128]{3,1,0,2:T(8,128)(2,1)}), bf16[2,1024,8,128]{3,1,0,2:T(8,128)(2,1)}, u32[]{:S(2)}, u32[]{:S(2)}) %all-to-all-start.1) | async-done | bytes 4194336 | tf_op jit(solution)/shard_map/all_to_all | solution.py:157
  71.9 7.5 %copy.106 = bf16[2,2,1024,4,128]{4,3,2,1,0:T(4,128)(2,1)} copy(bf16[2,2,1024,4,128]{4,2,0,3,1:T(8,128)(2,1)} %bitcast.8) | data formatting | bytes 8388608 | tf_op jit(solution)/shard_map/all_to_all | solution.py:157
  79.3 7.9 %all-gather.5.cloned.1.call-done = bf16[2,3,1024,256]{3,2,0,1:T(8,128)(2,1)} async-done(((bf16[1,3,1024,256]{3,2,0,1:T(8,128)(2,1)}), bf16[2,3,1024,256]{3,2,0,1:T(8,128)(2,1)}) %all-gather.5.cloned.1.call-update) | async-done | bytes 3145744 | tf_op jit(solution)/shard_map/all_gather | solution.py:161
  96.6 5.6 %all-to-all-done.2 = bf16[2,128,8,128]{3,1,0,2:T(8,128)(2,1)S(1)} async-done(((bf16[2,128,8,128]{3,1,0,2:T(8,128)(2,1)}), bf16[2,128,8,128]{3,1,0,2:T(8,128)(2,1)S(1)}, u32[]{:S(2)}, u32[]{:S(2)}) %all-to-all-start.2) | async-done | bytes 524320 | tf_op jit(solution)/shard_map/all_to_all | solution.py:158
  102.2 7.3 %all-to-all-start.4 = ((s32[16,1,16]{2,1,0:T(1,128)}), s32[16,1,16]{2,1,0:T(1,128)S(1)}, u32[]{:S(2)}, u32[]{:S(2)}) async-start(s32[16,1,16]{2,1,0:T(1,128)} %all_to_all.86), calls=%async_computation.4 | async-start | bytes 16384 | tf_op jit(solution)/shard_map/all_to_all | solution.py:179
  109.5 12.5 %broadcast_select_fusion = bf16[2,2048,4,128]{3,2,1,0:T(4,128)(2,1)S(1)} fusion(bf16[2,2048,4,128]{3,2,1,0:T(4,128)(2,1)} %bitcast.315, pred[2,2048]{1,0:T(4,128)(4,1)S(1)} %iota_compare_fusion.4), kind=kLoop, calls=%fused_computation.10 | loop fusion | flops 2097152 | bytes 8392704 | tf_op jit(solution)/shard_map/jit(_where)/select_n | solution.py:168
  130.3 6.0 %all-to-all-start.3 = ((bf16[16,16,4,16,128]{4,3,2,1,0:T(8,128)(2,1)}), bf16[16,16,4,16,128]{4,3,2,1,0:T(8,128)(2,1)}, u32[]{:S(2)}, u32[]{:S(2)}) async-start(bf16[16,16,4,16,128]{4,3,2,1,0:T(8,128)(2,1)} %bitcast.318), calls=%async_computation.3 | async-start | bytes 8388608 | tf_op jit(solution)/shard_map/all_to_all | solution.py:178
  142.6 7.5 %reshape.204.c_ref = bf16[2,2048,512]{2,1,0:T(8,128)(2,1)} reshape(bf16[2,2048,4,128]{3,2,1,0:T(4,128)(2,1)} %bitcast.316) | data formatting | bytes 8388608 | tf_op jit(solution)/shard_map/reshape | solution.py:100
  150.1 32.9 %shard_map.131 = bf16[2,256,512]{2,1,0:T(8,128)(2,1)} custom-call(s32[2]{0:T(128)} %copy-done.13, bf16[2,256,512]{2,1,0:T(8,128)(2,1)} %reshape.203.q_ref, bf16[2,2048,512]{2,1,0:T(8,128)(2,1)} %reshape.204.c_ref, bf16[2,256,512]{2,1,0:T(8,128)(2,1)} %reshape.205.s_ref), custom_call_target="tpu_custom_call" | custom-call | flops 7247757312 | bytes 5767168 | tf_op jit(solution)/shard_map/pallas_call | solution.py:103
  184.2 34.9 %all-gather.7.cloned.1.call-done = bf16[2,2,3,1024,256]{4,3,1,0,2:T(8,128)(2,1)} async-done(((bf16[2,1,3,1024,256]{4,3,1,0,2:T(8,128)(2,1)}), bf16[2,2,3,1024,256]{4,3,1,0,2:T(8,128)(2,1)}) %all-gather.7.cloned.1.call-update) | async-done | bytes 6291472 | tf_op jit(solution)/shard_map/all_gather | solution.py:165
  219.1 9.9 %all-to-all-done.3 = bf16[16,16,4,16,128]{4,3,2,1,0:T(8,128)(2,1)} async-done(((bf16[16,16,4,16,128]{4,3,2,1,0:T(8,128)(2,1)}), bf16[16,16,4,16,128]{4,3,2,1,0:T(8,128)(2,1)}, u32[]{:S(2)}, u32[]{:S(2)}) %all-to-all-start.3) | async-done | bytes 4194336 | tf_op jit(solution)/shard_map/all_to_all | solution.py:178
  235.1 6.4 %all-to-all-done.5 = bf16[2,256,4,128]{3,2,0,1:T(4,128)(2,1)S(1)} async-done(((bf16[2,256,4,128]{3,2,0,1:T(4,128)(2,1)}), bf16[2,256,4,128]{3,2,0,1:T(4,128)(2,1)S(1)}, u32[]{:S(2)}, u32[]{:S(2)}) %all-to-all-start.5) | async-done | bytes 524320 | tf_op jit(solution)/shard_map/all_to_all | solution.py:187
  255.6 29.0 %all-to-all-done.10 = bf16[8,160,1024]{2,1,0:T(8,128)(2,1)} async-done(((bf16[8,160,1024]{2,1,0:T(8,128)(2,1)}), bf16[8,160,1024]{2,1,0:T(8,128)(2,1)}, u32[]{:S(2)}, u32[]{:S(2)}) %all-to-all-start.10) | async-done | bytes 2621472 | tf_op jit(solution)/shard_map/all_to_all | solution.py:239
  291.6 28.7 %all-to-all-done.6 = bf16[8,160,1024]{2,1,0:T(8,128)(2,1)} async-done(((bf16[8,160,1024]{2,1,0:T(8,128)(2,1)}), bf16[8,160,1024]{2,1,0:T(8,128)(2,1)}, u32[]{:S(2)}, u32[]{:S(2)}) %all-to-all-start.6) | async-done | bytes 2621472 | tf_op jit(solution)/shard_map/all_to_all | solution.py:239
  330.4 8.3 %fusion.11 = bf16[8,2,1,80,1024]{4,3,0,1,2:T(8,128)(2,1)} fusion(bf16[2,2,1,3,1024,256]{5,4,1,0,3,2:T(8,128)(2,1)} %bitcast.339, f32[2,2,256,8,80]{2,4,3,1,0:T(8,128)} %fusion.20, bf16[8,2,80,1024,1]{3,2,1,0,4:T(8,128)(2,1)} %bitcast.81), kind=kOutput, calls=%fused_computation.24 | convolution fusion | flops 2689597440 | bytes 12058624 | tf_op jit(solution)/shard_map/szjckf,zkjdf->szjcd/dot_general | solution.py:250
  342.4 19.6 %all-to-all-done.8 = bf16[8,192,1024]{2,1,0:T(8,128)(2,1)} async-done(((bf16[8,192,1024]{2,1,0:T(8,128)(2,1)}), bf16[8,192,1024]{2,1,0:T(8,128)(2,1)}, u32[]{:S(2)}, u32[]{:S(2)}) %all-to-all-start.8) | async-done | bytes 3145760 | tf_op jit(solution)/shard_map/all_to_all | solution.py:239
  371.7 8.4 %fusion.10 = bf16[8,2,1,80,1024]{4,3,0,1,2:T(8,128)(2,1)} fusion(bf16[2,2,1,3,1024,256]{5,4,1,0,3,2:T(8,128)(2,1)} %bitcast.341, f32[2,2,256,8,80]{2,4,3,1,0:T(8,128)} %fusion.24, bf16[8,2,80,1024,1]{3,2,1,0,4:T(8,128)(2,1)} %bitcast.36), kind=kOutput, calls=%fused_computation.23 | convolution fusion | flops 2689597440 | bytes 12058624 | tf_op jit(solution)/shard_map/szjckf,zkjdf->szjcd/dot_general | solution.py:250
  383.7 13.9 %all-to-all-done.11 = bf16[8,160,1024]{2,1,0:T(8,128)(2,1)} async-done(((bf16[8,160,1024]{2,1,0:T(8,128)(2,1)}), bf16[8,160,1024]{2,1,0:T(8,128)(2,1)}, u32[]{:S(2)}, u32[]{:S(2)}) %all-to-all-start.11) | async-done | bytes 2621472 | tf_op jit(solution)/shard_map/all_to_all | solution.py:253
  402.1 6.0 %fusion.6 = f32[2,2,256,8,96]{2,4,3,1,0:T(8,128)} fusion(bf16[8,2,96,1024,1]{3,2,1,0,4:T(8,128)(2,1)} %bitcast.61, bf16[2,2,1,3,1024,256]{5,4,1,0,3,2:T(8,128)(2,1)} %bitcast.342), kind=kOutput, calls=%fused_computation.19 | convolution fusion | flops 1610612736 | bytes 8388608 | tf_op jit(solution)/shard_map/szjcd,zkjdf->szjckf/dot_general | solution.py:246
  408.1 9.4 %fusion.1 = bf16[8,2,1,96,1024]{4,3,0,1,2:T(8,128)(2,1)} fusion(bf16[2,2,1,3,1024,256]{5,4,1,0,3,2:T(8,128)(2,1)} %bitcast.343, f32[2,2,256,8,96]{2,4,3,1,0:T(8,128)} %fusion.6, bf16[8,2,96,1024,1]{3,2,1,0,4:T(8,128)(2,1)} %bitcast.61), kind=kOutput, calls=%fused_computation.11 | convolution fusion | flops 3227516928 | bytes 13631488 | tf_op jit(solution)/shard_map/szjckf,zkjdf->szjcd/dot_general | solution.py:250
  421.4 12.0 %all-to-all-done.7 = bf16[8,160,1024]{2,1,0:T(8,128)(2,1)} async-done(((bf16[8,160,1024]{2,1,0:T(8,128)(2,1)}), bf16[8,160,1024]{2,1,0:T(8,128)(2,1)}, u32[]{:S(2)}, u32[]{:S(2)}) %all-to-all-start.7) | async-done | bytes 2621472 | tf_op jit(solution)/shard_map/all_to_all | solution.py:253
  441.2 7.5 %reshape.235 = bf16[256,8192]{1,0:T(8,128)(2,1)} reshape(bf16[16,16,4,16,128]{4,3,2,1,0:T(8,128)(2,1)} %all-to-all-done.3) | data formatting | bytes 8388608 | tf_op jit(solution)/shard_map/reshape | solution.py:195
  468.8 6.3 %all-to-all-done.9 = bf16[8,192,1024]{2,1,0:T(8,128)(2,1)} async-done(((bf16[8,192,1024]{2,1,0:T(8,128)(2,1)}), bf16[8,192,1024]{2,1,0:T(8,128)(2,1)}, u32[]{:S(2)}, u32[]{:S(2)}) %all-to-all-start.9) | async-done | bytes 3145760 | tf_op jit(solution)/shard_map/all_to_all | solution.py:253
  (107 shorter events, 135.4 us)
Async XLA Ops:
  7.2 236.0 %copy-start = (bf16[1024,1024]{1,0:T(8,128)(2,1)S(1)}, bf16[1024,1024]{1,0:T(8,128)(2,1)}, u32[]{:S(2)}) copy-start(bf16[1024,1024]{1,0:T(8,128)(2,1)} %param.18) | copy-start | bytes 6291460
  7.2 80.1 %all-gather.5.cloned.1.call-start = ((), (), s32[]{:S(2)}) async-start(), calls=%async_computation.12 | async-start | bytes 4718592 | tf_op jit(solution)/shard_map/all_gather | solution.py:161
  12.9 5.8 %copy-start.8 = (bf16[2,128,1024]{2,1,0:T(8,128)(2,1)S(1)}, bf16[2,128,1024]{2,1,0:T(8,128)(2,1)}, u32[]{:S(2)}) copy-start(bf16[2,128,1024]{2,1,0:T(8,128)(2,1)} %param.13) | copy-start | bytes 1572868
  12.9 6.9 %copy-start.14 = (s32[32]{0:T(128)S(1)}, s32[32]{0:T(128)}, u32[]{:S(2)}) copy-start(s32[32]{0:T(128)} %param.16) | copy-start | bytes 388
  12.9 7.0 %copy-start.15 = (s32[32]{0:T(128)S(1)}, s32[32]{0:T(128)}, u32[]{:S(2)}) copy-start(s32[32]{0:T(128)} %param.17) | copy-start | bytes 388
  12.9 53.4 %all-to-all-start.1 = ((bf16[2,1024,8,128]{3,1,0,2:T(8,128)(2,1)}), bf16[2,1024,8,128]{3,1,0,2:T(8,128)(2,1)}, u32[]{:S(2)}, u32[]{:S(2)}) async-start(bf16[2,1024,8,128]{3,1,0,2:T(8,128)(2,1)} %copy.105), calls=%async_computation.1 | async-start | bytes 8388608 | tf_op jit(solution)/shard_map/all_to_all | solution.py:157
  20.1 59.3 %copy-start.13 = (s32[2]{0:T(128)}, s32[2]{0:T(128)S(1)}, u32[]{:S(2)}) copy-start(s32[2]{0:T(128)S(1)} %fusion.96.len_ref) | copy-start | bytes 28
  66.3 24.1 %all-to-all-start = ((bf16[2,128,8,128]{1,3,0,2:T(8,128)(2,1)}), bf16[2,128,8,128]{1,3,0,2:T(8,128)(2,1)S(1)}, u32[]{:S(2)}, u32[]{:S(2)}) async-start(bf16[2,128,8,128]{1,3,0,2:T(8,128)(2,1)} %copy.101), calls=%async_computation | async-start | bytes 1048576 | tf_op jit(solution)/shard_map/all_to_all | solution.py:159
  71.9 15.4 %copy-start.12 = (s32[2,128]{1,0:T(2,128)S(1)}, s32[2,128]{1,0:T(2,128)}, u32[]{:S(2)}) copy-start(s32[2,128]{1,0:T(2,128)} %param.23) | copy-start | bytes 3076
  90.4 11.8 %all-to-all-start.2 = ((bf16[2,128,8,128]{3,1,0,2:T(8,128)(2,1)}), bf16[2,128,8,128]{3,1,0,2:T(8,128)(2,1)S(1)}, u32[]{:S(2)}, u32[]{:S(2)}) async-start(bf16[2,128,8,128]{3,1,0,2:T(8,128)(2,1)} %copy.107), calls=%async_computation.2 | async-start | bytes 1048576 | tf_op jit(solution)/shard_map/all_to_all | solution.py:158
  102.2 28.1 %all-to-all-start.4 = ((s32[16,1,16]{2,1,0:T(1,128)}), s32[16,1,16]{2,1,0:T(1,128)S(1)}, u32[]{:S(2)}, u32[]{:S(2)}) async-start(s32[16,1,16]{2,1,0:T(1,128)} %all_to_all.86), calls=%async_computation.4 | async-start | bytes 16384 | tf_op jit(solution)/shard_map/all_to_all | solution.py:179
  130.3 98.7 %all-to-all-start.3 = ((bf16[16,16,4,16,128]{4,3,2,1,0:T(8,128)(2,1)}), bf16[16,16,4,16,128]{4,3,2,1,0:T(8,128)(2,1)}, u32[]{:S(2)}, u32[]{:S(2)}) async-start(bf16[16,16,4,16,128]{4,3,2,1,0:T(8,128)(2,1)} %bitcast.318), calls=%async_computation.3 | async-start | bytes 8388608 | tf_op jit(solution)/shard_map/all_to_all | solution.py:178
  136.3 82.8 %all-gather.7.cloned.1.call-start = ((), (), s32[]{:S(2)}) async-start(), calls=%async_computation.13 | async-start | bytes 9437184 | tf_op jit(solution)/shard_map/all_gather | solution.py:165
  230.0 11.5 %all-to-all-start.5 = ((bf16[2,256,4,128]{3,2,0,1:T(4,128)(2,1)}), bf16[2,256,4,128]{3,2,0,1:T(4,128)(2,1)S(1)}, u32[]{:S(2)}, u32[]{:S(2)}) async-start(bf16[2,256,4,128]{3,2,0,1:T(4,128)(2,1)} %copy.110), calls=%async_computation.5 | async-start | bytes 1048576 | tf_op jit(solution)/shard_map/all_to_all | solution.py:187
  248.7 4.6 copy-start.2
  248.7 35.9 %all-to-all-start.10 = ((bf16[8,160,1024]{2,1,0:T(8,128)(2,1)}), bf16[8,160,1024]{2,1,0:T(8,128)(2,1)}, u32[]{:S(2)}, u32[]{:S(2)}) async-start(bf16[8,160,1024]{2,1,0:T(8,128)(2,1)} %bitcast.325), calls=%async_computation.10 | async-start | bytes 5242880 | tf_op jit(solution)/shard_map/all_to_all | solution.py:239
  284.6 35.7 %all-to-all-start.6 = ((bf16[8,160,1024]{2,1,0:T(8,128)(2,1)}), bf16[8,160,1024]{2,1,0:T(8,128)(2,1)}, u32[]{:S(2)}, u32[]{:S(2)}) async-start(bf16[8,160,1024]{2,1,0:T(8,128)(2,1)} %bitcast.324), calls=%async_computation.6 | async-start | bytes 5242880 | tf_op jit(solution)/shard_map/all_to_all | solution.py:239
  320.3 41.6 %all-to-all-start.8 = ((bf16[8,192,1024]{2,1,0:T(8,128)(2,1)}), bf16[8,192,1024]{2,1,0:T(8,128)(2,1)}, u32[]{:S(2)}, u32[]{:S(2)}) async-start(bf16[8,192,1024]{2,1,0:T(8,128)(2,1)} %bitcast.321), calls=%async_computation.8 | async-start | bytes 6291456 | tf_op jit(solution)/shard_map/all_to_all | solution.py:239
  361.9 35.7 %all-to-all-start.11 = ((bf16[8,160,1024]{2,1,0:T(8,128)(2,1)}), bf16[8,160,1024]{2,1,0:T(8,128)(2,1)}, u32[]{:S(2)}, u32[]{:S(2)}) async-start(bf16[8,160,1024]{2,1,0:T(8,128)(2,1)} %bitcast.323), calls=%async_computation.11 | async-start | bytes 5242880 | tf_op jit(solution)/shard_map/all_to_all | solution.py:253
  397.7 35.7 %all-to-all-start.7 = ((bf16[8,160,1024]{2,1,0:T(8,128)(2,1)}), bf16[8,160,1024]{2,1,0:T(8,128)(2,1)}, u32[]{:S(2)}, u32[]{:S(2)}) async-start(bf16[8,160,1024]{2,1,0:T(8,128)(2,1)} %bitcast.322), calls=%async_computation.7 | async-start | bytes 5242880 | tf_op jit(solution)/shard_map/all_to_all | solution.py:253
  433.4 4.9 copy-start.10
  433.4 41.8 %all-to-all-start.9 = ((bf16[8,192,1024]{2,1,0:T(8,128)(2,1)}), bf16[8,192,1024]{2,1,0:T(8,128)(2,1)}, u32[]{:S(2)}, u32[]{:S(2)}) async-start(bf16[8,192,1024]{2,1,0:T(8,128)(2,1)} %bitcast.320), calls=%async_computation.9 | async-start | bytes 6291456 | tf_op jit(solution)/shard_map/all_to_all | solution.py:253
  441.1 24.1 %copy-start.3 = (bf16[16,256,256]{2,1,0:T(8,128)(2,1)}, bf16[16,256,256]{2,1,0:T(8,128)(2,1)S(1)}, u32[]{:S(2)}) copy-start(bf16[16,256,256]{2,1,0:T(8,128)(2,1)S(1)} %select_convert_fusion) | copy-start | bytes 6291460
  475.2 7.5 %copy-start.1 = (bf16[1024,1024]{1,0:T(8,128)(2,1)S(1)}, bf16[1024,1024]{1,0:T(8,128)(2,1)}, u32[]{:S(2)}) copy-start(bf16[1024,1024]{1,0:T(8,128)(2,1)} %param.18) | copy-start | bytes 6291460
  (6 other events, 17.1 us)
Sparse Core Ops, SparseCore 0:
  9.6 77.6 all-gather.4
  138.7 80.3 all-gather.6

commit v15 on v11

--- a/solution.py
+++ b/solution.py
@@ -174,12 +174,12 @@
     sorted_pages, local_slot = place_pages(page_rows, block_map.reshape(-1), slots_dev)
     per_owner = sorted_pages.shape[0] // req_count
     outgoing = sorted_pages.reshape(req_count, per_owner, group_count, BLOCK, head_pair)
-    arrived, where_to = (
-        lax.all_to_all(outgoing, REQ, split_axis=0, concat_axis=0, tiled=True),
-        lax.all_to_all(
-            local_slot.reshape(req_count, per_owner), REQ, split_axis=0, concat_axis=0, tiled=True
-        ),
-    )
+    arrived = lax.all_to_all(outgoing, REQ, split_axis=0, concat_axis=0, tiled=True)
+    every_map = lax.all_gather(block_map, REQ, axis=0, tiled=True).reshape(req_count, -1)
+    mine = every_map // slots_dev == lax.axis_index(REQ)
+    order = jnp.cumsum(mine.astype(jnp.int32), axis=1) - 1
+    hit = mine[:, :, None] & (order[:, :, None] == jnp.arange(per_owner, dtype=jnp.int32)[None, None, :])
+    where_to = jnp.sum(jnp.where(hit, (every_map % slots_dev)[:, :, None], 0), axis=1)
     attn_heads = attend(query_heads, cache_heads, span_heads, lengths)
     attn_heads, full_weights, arrived, where_to = lax.optimization_barrier(
         (attn_heads, full_weights, arrived, where_to)

time: 479 us -> 536 us (1.12)
  blocking collectives: 0 us -> 88.8 us
  waiting for transfers between devices: 232 us -> 181 us
  Pallas kernels: 29.6 us -> 57.2 us
    all_gather x0 -> x1, blocking collectives: none -> 88.8 us  [body(): lax.all_gather(block_map, REQ, axis=0, tiled=True).reshape(req_count, -1)]
    all_gather x1, waiting for transfers between devices: 38.2 us -> 0.02 us  [body(): full_weights = lax.all_gather(pair_weights, 'kv', axis=1, tiled=False)]
    pallas_call x1, Pallas kernels: 29.6 us -> 57.2 us  [attend(): pl.pallas_call(functools.partial(attend_kernel, tk=tk, head_dim=head_dim)...]
    all_to_all x1, waiting for transfers between devices: 9.92 us -> 0.01 us  [body(): lax.all_to_all(outgoing, REQ, split_axis=0, concat_axis=0, tiled=True)]
    all_to_all x1 -> x0, starting transfers between devices: 7.32 us -> none  [body(): lax.all_to_all(local_slot.reshape(req_count, per_owner), REQ, split_axis=...]
  transfers between devices with their start and end apart: 12 -> 11, of which waited for: 10 -> 8; matrix products, arithmetic and copies ran while one was open for 27% -> 24% of each run, Pallas kernels for 6% -> 11%
where the time goes in v15:
time: 536 us; the launch traced here: 537 us
  waiting for transfers between devices  181 us (34%)
  blocking collectives  88.8 us (17%)
  matrix products  63.7 us (12%)
  local copies, waits for them, and re-layouts  63.2 us (12%)
  Pallas kernels  57.2 us (11%)
  starting transfers between devices  46.4 us (9%)
  other arithmetic  22.2 us (4%)
  between operations  14.4 us (3%)
    all_gather x1, blocking collectives, body(): lax.all_gather(block_map, REQ, axis=0, tiled=True).reshape(req_count, -1)  88.8 us
    all_to_all x2, waiting for transfers between devices, body(): lax.all_to_all(buffer.reshape(side, per_dev * size, width_model), 'rlow',...  71.2 us
    pallas_call x1, Pallas kernels, attend(): pl.pallas_call(functools.partial(attend_kernel, tk=tk, head_dim=head_dim)...  57.2 us
    all_to_all x2, waiting for transfers between devices, body(): lax.all_to_all(expert_out.reshape(side, per_dev * size, width_model), 'rl...  48.9 us
    all_to_all x1, waiting for transfers between devices, body(): lax.all_to_all(cache, 'kv', split_axis=2, concat_axis=1, tiled=True)  44.2 us
    dot_general x2, matrix products, body(): jnp.einsum('szjckf,zkjdf->szjcd', activated, weights[:, :, :, 2], preferr...  20.4 us
    dot_general x2, matrix products, body(): jnp.einsum('szjcd,zkjdf->szjckf', grouped, weights[:, :, :, 1], preferred...  14.4 us
    unnamed x35, local copies, waits for them, and re-layouts  13.3 us
  transfers between devices with their start and end apart: 11, of which 8 were waited for; matrix products, arithmetic and copies ran while one was open for 24% of the time, Pallas kernels for 11%

profile of v15, /device:TPU:16, one launch (start us, length us, event | category | flops | bytes accessed | tf_op | source)
XLA Modules:
  0.0 536.8 jit_solution(8131150790733151808)
XLA Ops:
  10.0 5.0 copy.125
  15.0 6.0 %all-to-all-start.1 = ((bf16[2,1024,8,128]{3,1,0,2:T(8,128)(2,1)}), bf16[2,1024,8,128]{3,1,0,2:T(8,128)(2,1)}, u32[]{:S(2)}, u32[]{:S(2)}) async-start(bf16[2,1024,8,128]{3,1,0,2:T(8,128)(2,1)} %copy.125), calls=%async_computation.1 | async-start | bytes 8388608 | tf_op jit(solution)/shard_map/all_to_all | solution.py:157
  24.5 44.2 %all-to-all-done.1 = bf16[2,1024,8,128]{3,1,0,2:T(8,128)(2,1)} async-done(((bf16[2,1024,8,128]{3,1,0,2:T(8,128)(2,1)}), bf16[2,1024,8,128]{3,1,0,2:T(8,128)(2,1)}, u32[]{:S(2)}, u32[]{:S(2)}) %all-to-all-start.1) | async-done | bytes 4194336 | tf_op jit(solution)/shard_map/all_to_all | solution.py:157
  72.2 7.4 %copy.126 = bf16[2,2,1024,4,128]{4,3,2,1,0:T(4,128)(2,1)} copy(bf16[2,2,1024,4,128]{4,2,0,3,1:T(8,128)(2,1)} %bitcast.7) | data formatting | bytes 8388608 | tf_op jit(solution)/shard_map/all_to_all | solution.py:157
  79.6 8.2 %all-gather.6.cloned.1.call-done = bf16[2,3,1024,256]{2,3,0,1:T(8,128)(2,1)} async-done(((bf16[1,3,1024,256]{2,3,0,1:T(8,128)(2,1)}), bf16[2,3,1024,256]{2,3,0,1:T(8,128)(2,1)}) %all-gather.6.cloned.1.call-update) | async-done | bytes 3145744 | tf_op jit(solution)/shard_map/all_gather | solution.py:161
  87.8 12.5 %broadcast_select_fusion = bf16[2,2048,4,128]{3,2,1,0:T(4,128)(2,1)S(1)} fusion(bf16[2,2048,4,128]{3,2,1,0:T(4,128)(2,1)} %bitcast.265, pred[2,2048]{1,0:T(4,128)(4,1)S(1)} %iota_compare_fusion.5), kind=kLoop, calls=%fused_computation.24 | loop fusion | flops 2097152 | bytes 8392704 | tf_op jit(solution)/shard_map/jit(_where)/select_n | solution.py:168
  110.1 5.4 gather_fusion
  118.3 7.9 %all-to-all-start.3 = ((bf16[16,16,4,16,128]{4,3,2,1,0:T(8,128)(2,1)}), bf16[16,16,4,16,128]{4,3,2,1,0:T(8,128)(2,1)}, u32[]{:S(2)}, u32[]{:S(2)}) async-start(bf16[16,16,4,16,128]{4,3,2,1,0:T(8,128)(2,1)} %bitcast.268), calls=%async_computation.3 | async-start | bytes 8388608 | tf_op jit(solution)/shard_map/all_to_all | solution.py:177
  132.5 7.5 %reshape.255.c_ref = bf16[2,2048,512]{2,1,0:T(8,128)(2,1)} reshape(bf16[2,2048,4,128]{3,2,1,0:T(4,128)(2,1)} %bitcast.266) | data formatting | bytes 8388608 | tf_op jit(solution)/shard_map/reshape | solution.py:100
  140.0 88.8 %all-gather.2 = s32[16,2,128]{2,1,0:T(2,128)S(1)} all-gather(s32[1,2,128]{2,1,0:T(2,128)S(1)} %bitcast.285), channel_id=1, replica_groups=mesh['zhi'=2,'rlow'=8,'kv'=2] {'zhi','rlow'}, dimensions={0}, use_global_device_ids=true | all-gather | bytes 17408 | tf_op jit(solution)/shard_map/all_gather | solution.py:178
  229.7 57.2 %shard_map.131 = bf16[2,256,512]{2,1,0:T(8,128)(2,1)} custom-call(s32[2]{0:T(128)} %copy-done.12, bf16[2,256,512]{2,1,0:T(8,128)(2,1)} %reshape.254.q_ref, bf16[2,2048,512]{2,1,0:T(8,128)(2,1)} %reshape.255.c_ref, bf16[2,256,512]{2,1,0:T(8,128)(2,1)} %reshape.256.s_ref), custom_call_target="tpu_custom_call" | custom-call | flops 7247757312 | bytes 5767168 | tf_op jit(solution)/shard_map/pallas_call | solution.py:103
  294.6 4.9 all-to-all-done.4
  306.7 7.6 %all-to-all-start.5 = ((bf16[8,256,1024]{2,1,0:T(8,128)(2,1)}), bf16[8,256,1024]{2,1,0:T(8,128)(2,1)}, u32[]{:S(2)}, u32[]{:S(2)}) async-start(bf16[8,256,1024]{2,1,0:T(8,128)(2,1)} %bitcast.273), calls=%async_computation.5 | async-start | bytes 8388608 | tf_op jit(solution)/shard_map/all_to_all | solution.py:238
  317.7 45.4 %all-to-all-done.5 = bf16[8,256,1024]{2,1,0:T(8,128)(2,1)} async-done(((bf16[8,256,1024]{2,1,0:T(8,128)(2,1)}), bf16[8,256,1024]{2,1,0:T(8,128)(2,1)}, u32[]{:S(2)}, u32[]{:S(2)}) %all-to-all-start.5) | async-done | bytes 4194336 | tf_op jit(solution)/shard_map/all_to_all | solution.py:238
  367.9 7.2 %fusion.15 = f32[2,2,256,8,128]{4,2,3,1,0:T(8,128)} fusion(bf16[8,2,128,1024,1]{3,2,1,0,4:T(8,128)(2,1)} %bitcast.34, bf16[2,2,1,3,1024,256]{4,5,1,0,3,2:T(8,128)(2,1)} %bitcast.286), kind=kOutput, calls=%fused_computation.29 | convolution fusion | flops 2147483648 | bytes 10485760 | tf_op jit(solution)/shard_map/szjcd,zkjdf->szjckf/dot_general | solution.py:245
  375.2 10.2 %fusion.1 = bf16[8,2,1,128,1024]{4,3,0,1,2:T(8,128)(2,1)} fusion(f32[2,2,256,8,128]{4,2,3,1,0:T(8,128)} %fusion.15, bf16[2,2,1,3,1024,256]{4,5,1,0,3,2:T(8,128)(2,1)} %bitcast.287, bf16[8,2,128,1024,1]{3,2,1,0,4:T(8,128)(2,1)} %bitcast.34), kind=kOutput, calls=%fused_computation.7 | convolution fusion | flops 4303355904 | bytes 16777216 | tf_op jit(solution)/shard_map/szjckf,zkjdf->szjcd/dot_general | solution.py:249
  385.3 4.8 copy.146
  390.2 25.7 %all-to-all-done.7 = bf16[8,256,1024]{2,1,0:T(8,128)(2,1)} async-done(((bf16[8,256,1024]{2,1,0:T(8,128)(2,1)}), bf16[8,256,1024]{2,1,0:T(8,128)(2,1)}, u32[]{:S(2)}, u32[]{:S(2)}) %all-to-all-start.7) | async-done | bytes 4194336 | tf_op jit(solution)/shard_map/all_to_all | solution.py:238
  420.5 7.2 %fusion.11 = f32[2,2,256,8,128]{4,2,3,1,0:T(8,128)} fusion(bf16[8,2,128,1024,1]{3,2,1,0,4:T(8,128)(2,1)} %bitcast.58, bf16[2,2,1,3,1024,256]{4,5,1,0,3,2:T(8,128)(2,1)} %bitcast.288), kind=kOutput, calls=%fused_computation.25 | convolution fusion | flops 2147483648 | bytes 10485760 | tf_op jit(solution)/shard_map/szjcd,zkjdf->szjckf/dot_general | solution.py:245
  427.7 10.2 %fusion.2 = bf16[8,2,1,128,1024]{4,3,0,1,2:T(8,128)(2,1)} fusion(f32[2,2,256,8,128]{4,2,3,1,0:T(8,128)} %fusion.11, bf16[2,2,1,3,1024,256]{4,5,1,0,3,2:T(8,128)(2,1)} %bitcast.289, bf16[8,2,128,1024,1]{3,2,1,0,4:T(8,128)(2,1)} %bitcast.58), kind=kOutput, calls=%fused_computation.8 | convolution fusion | flops 4303355904 | bytes 16777216 | tf_op jit(solution)/shard_map/szjckf,zkjdf->szjcd/dot_general | solution.py:249
  442.7 26.0 %all-to-all-done.6 = bf16[8,256,1024]{2,1,0:T(8,128)(2,1)} async-done(((bf16[8,256,1024]{2,1,0:T(8,128)(2,1)}), bf16[8,256,1024]{2,1,0:T(8,128)(2,1)}, u32[]{:S(2)}, u32[]{:S(2)}) %all-to-all-start.6) | async-done | bytes 4194336 | tf_op jit(solution)/shard_map/all_to_all | solution.py:252
  468.6 4.9 all-to-all-start.8
  476.5 7.3 %reshape.284 = bf16[256,8192]{1,0:T(8,128)(2,1)} reshape(bf16[16,16,4,16,128]{4,3,2,1,0:T(8,128)(2,1)} %all-to-all-done.3) | data formatting | bytes 8388608 | tf_op jit(solution)/shard_map/reshape | solution.py:195
  498.6 22.9 %all-to-all-done.8 = bf16[8,256,1024]{2,1,0:T(8,128)(2,1)} async-done(((bf16[8,256,1024]{2,1,0:T(8,128)(2,1)}), bf16[8,256,1024]{2,1,0:T(8,128)(2,1)}, u32[]{:S(2)}, u32[]{:S(2)}) %all-to-all-start.8) | async-done | bytes 4194336 | tf_op jit(solution)/shard_map/all_to_all | solution.py:252
  (101 shorter events, 87.9 us)
Async XLA Ops:
  7.2 294.0 %copy-start = (bf16[1024,1024]{1,0:T(8,128)(2,1)S(1)}, bf16[1024,1024]{1,0:T(8,128)(2,1)}, u32[]{:S(2)}) copy-start(bf16[1024,1024]{1,0:T(8,128)(2,1)} %param.18) | copy-start | bytes 6291460
  7.2 80.6 %all-gather.6.cloned.1.call-start = ((), (), s32[]{:S(2)}) async-start(), calls=%async_computation.9 | async-start | bytes 4718592 | tf_op jit(solution)/shard_map/all_gather | solution.py:161
  15.0 6.0 %copy-start.7 = (bf16[2,128,1024]{2,1,0:T(8,128)(2,1)S(1)}, bf16[2,128,1024]{2,1,0:T(8,128)(2,1)}, u32[]{:S(2)}) copy-start(bf16[2,128,1024]{2,1,0:T(8,128)(2,1)} %param.13) | copy-start | bytes 1572868
  15.0 9.1 %copy-start.13 = (s32[32]{0:T(128)S(1)}, s32[32]{0:T(128)}, u32[]{:S(2)}) copy-start(s32[32]{0:T(128)} %param.16) | copy-start | bytes 388
  15.0 9.2 %copy-start.14 = (s32[32]{0:T(128)S(1)}, s32[32]{0:T(128)}, u32[]{:S(2)}) copy-start(s32[32]{0:T(128)} %param.17) | copy-start | bytes 388
  15.0 53.6 %all-to-all-start.1 = ((bf16[2,1024,8,128]{3,1,0,2:T(8,128)(2,1)}), bf16[2,1024,8,128]{3,1,0,2:T(8,128)(2,1)}, u32[]{:S(2)}, u32[]{:S(2)}) async-start(bf16[2,1024,8,128]{3,1,0,2:T(8,128)(2,1)} %copy.125), calls=%async_computation.1 | async-start | bytes 8388608 | tf_op jit(solution)/shard_map/all_to_all | solution.py:157
  24.4 55.2 %copy-start.12 = (s32[2]{0:T(128)}, s32[2]{0:T(128)S(1)}, u32[]{:S(2)}) copy-start(s32[2]{0:T(128)S(1)} %fusion.77.len_ref) | copy-start | bytes 28
  68.7 37.9 %all-to-all-start = ((bf16[2,128,8,128]{1,3,0,2:T(8,128)(2,1)}), bf16[2,128,8,128]{1,3,0,2:T(8,128)(2,1)S(1)}, u32[]{:S(2)}, u32[]{:S(2)}) async-start(bf16[2,128,8,128]{1,3,0,2:T(8,128)(2,1)} %copy.121), calls=%async_computation | async-start | bytes 1048576 | tf_op jit(solution)/shard_map/all_to_all | solution.py:159
  106.6 11.8 %all-to-all-start.2 = ((bf16[2,128,8,128]{3,1,0,2:T(8,128)(2,1)}), bf16[2,128,8,128]{3,1,0,2:T(8,128)(2,1)S(1)}, u32[]{:S(2)}, u32[]{:S(2)}) async-start(bf16[2,128,8,128]{3,1,0,2:T(8,128)(2,1)} %copy.127), calls=%async_computation.2 | async-start | bytes 1048576 | tf_op jit(solution)/shard_map/all_to_all | solution.py:158
  118.3 8.7 %copy-start.8 = (s32[256,8]{0,1:T(8,128)S(1)}, s32[256,8]{0,1:T(8,128)}, u32[]{:S(2)}) copy-start(s32[256,8]{0,1:T(8,128)} %param.20) | copy-start | bytes 24580
  118.3 170.2 %all-to-all-start.3 = ((bf16[16,16,4,16,128]{4,3,2,1,0:T(8,128)(2,1)}), bf16[16,16,4,16,128]{4,3,2,1,0:T(8,128)(2,1)}, u32[]{:S(2)}, u32[]{:S(2)}) async-start(bf16[16,16,4,16,128]{4,3,2,1,0:T(8,128)(2,1)} %bitcast.268), calls=%async_computation.3 | async-start | bytes 8388608 | tf_op jit(solution)/shard_map/all_to_all | solution.py:177
  126.3 162.2 %all-gather.8.cloned.1.call-start = ((), (), s32[]{:S(2)}) async-start(), calls=%async_computation.10 | async-start | bytes 9437184 | tf_op jit(solution)/shard_map/all_gather | solution.py:165
  289.5 10.1 %all-to-all-start.4 = ((bf16[2,256,4,128]{3,2,0,1:T(4,128)(2,1)}), bf16[2,256,4,128]{3,2,0,1:T(4,128)(2,1)S(1)}, u32[]{:S(2)}, u32[]{:S(2)}) async-start(bf16[2,256,4,128]{3,2,0,1:T(4,128)(2,1)} %copy.135), calls=%async_computation.4 | async-start | bytes 1048576 | tf_op jit(solution)/shard_map/all_to_all | solution.py:187
  293.0 10.3 %copy-start.9 = (f32[1024]{0:T(1024)S(1)}, f32[1024]{0:T(1024)}, u32[]{:S(2)}) copy-start(f32[1024]{0:T(1024)} %param.19) | copy-start | bytes 12292
  306.7 7.6 %copy-start.3 = (pred[16,256,256]{2,1,0:T(32,128)(4,1)S(1)}, pred[16,256,256]{2,1,0:T(32,128)(4,1)}, u32[]{:S(2)}) copy-start(pred[16,256,256]{2,1,0:T(32,128)(4,1)} %iota_compare_fusion) | copy-start | bytes 3145732
  306.7 56.5 %all-to-all-start.5 = ((bf16[8,256,1024]{2,1,0:T(8,128)(2,1)}), bf16[8,256,1024]{2,1,0:T(8,128)(2,1)}, u32[]{:S(2)}, u32[]{:S(2)}) async-start(bf16[8,256,1024]{2,1,0:T(8,128)(2,1)} %bitcast.273), calls=%async_computation.5 | async-start | bytes 8388608 | tf_op jit(solution)/shard_map/all_to_all | solution.py:238
  363.1 52.7 %all-to-all-start.7 = ((bf16[8,256,1024]{2,1,0:T(8,128)(2,1)}), bf16[8,256,1024]{2,1,0:T(8,128)(2,1)}, u32[]{:S(2)}, u32[]{:S(2)}) async-start(bf16[8,256,1024]{2,1,0:T(8,128)(2,1)} %bitcast.271), calls=%async_computation.7 | async-start | bytes 8388608 | tf_op jit(solution)/shard_map/all_to_all | solution.py:238
  415.9 52.8 %all-to-all-start.6 = ((bf16[8,256,1024]{2,1,0:T(8,128)(2,1)}), bf16[8,256,1024]{2,1,0:T(8,128)(2,1)}, u32[]{:S(2)}, u32[]{:S(2)}) async-start(bf16[8,256,1024]{2,1,0:T(8,128)(2,1)} %bitcast.272), calls=%async_computation.6 | async-start | bytes 8388608 | tf_op jit(solution)/shard_map/all_to_all | solution.py:252
  468.6 4.9 copy-start.10
  468.6 52.8 %all-to-all-start.8 = ((bf16[8,256,1024]{2,1,0:T(8,128)(2,1)}), bf16[8,256,1024]{2,1,0:T(8,128)(2,1)}, u32[]{:S(2)}, u32[]{:S(2)}) async-start(bf16[8,256,1024]{2,1,0:T(8,128)(2,1)} %bitcast.269), calls=%async_computation.8 | async-start | bytes 8388608 | tf_op jit(solution)/shard_map/all_to_all | solution.py:252
  474.4 16.1 %copy-start.4 = (bf16[16,256,256]{2,1,0:T(8,128)(2,1)}, bf16[16,256,256]{2,1,0:T(8,128)(2,1)S(1)}, u32[]{:S(2)}) copy-start(bf16[16,256,256]{2,1,0:T(8,128)(2,1)S(1)} %fusion) | copy-start | bytes 6291460
  490.5 3.6 copy-start.6
  521.5 4.2 copy-start.5
  521.5 8.5 %copy-start.1 = (bf16[1024,1024]{1,0:T(8,128)(2,1)S(1)}, bf16[1024,1024]{1,0:T(8,128)(2,1)}, u32[]{:S(2)}) copy-start(bf16[1024,1024]{1,0:T(8,128)(2,1)} %param.18) | copy-start | bytes 6291460
  (2 other events, 5.2 us)
Sparse Core Ops, SparseCore 0:
  10.1 77.6 all-gather.5
  128.7 80.3 all-gather.7
